TPU v7x, 256 devices: a whole 4x4x8 slice. The times are simulated.
256 devices in a mesh: segment: 2 (over y_hi), blk: 32 (over z, x), mp: 4 (over y_lo, core).
Axes of the slice: x: 4, y: 4 (y_hi: 2, y_lo: 2; y = y_hi * 2 + y_lo), z: 8, core: 2. Of those that a mesh axis runs over, the one named last changes fastest.
Arguments:
- section_input: bfloat16 [2, 8192, 1536], P('segment', 'blk', 'mp'), may hold values from -36 to 36
- row_code: int32 [2, 8192], P('segment', 'blk'), may hold values from 0 to 255
- code_table: bfloat16 [2, 256, 1536], P('segment', None, 'mp'), may hold values from -6 to 6
- self_gain: float32 [2, 1536], P('segment'), may hold values from 0.1 to 1.9
- self_weights: bfloat16 [2, 3, 1536, 1536], P('segment', None, None, 'mp'), may hold values from -0.22963966 to 0.22963966
- self_out: bfloat16 [2, 1536, 1536], P('segment', 'mp'), may hold values from -0.15625 to 0.15625
- cross_gain: float32 [1536], replicated, may hold values from 0.1 to 1.9
- memory_gain: float32 [1536], replicated, may hold values from 0.1 to 1.9
- cross_weights: bfloat16 [3, 1536, 1536], P(None, None, 'mp'), may hold values from -0.22963966 to 0.22963966
- cross_out: bfloat16 [1536, 1536], P('mp'), may hold values from -0.15625 to 0.15625
Outputs:
- sections: bfloat16 [2, 8192, 1536], P('segment', 'blk', 'mp')
All inputs are finite; a program needn't handle non-finite values.
Results may differ from a plain program's by a relative error of at most 0.0085.
Values may be sent and summed in bfloat16 or wider, within the bound.
No kernel may reach another device: no remote copies, remote signals or barrier semaphores. Data moves between devices by JAX's collectives and lax.ppermute only.
A program may use at most 128 MiB of HBM per device.

v0:
```python
import math

import jax
import jax.numpy as jnp
from jax import lax
from jax.sharding import PartitionSpec as P

HEAD_DIM = 128


def shifted(value, axis, steps):
    count = lax.axis_size(axis)
    initial, last = (max(0, -steps), min(count, count - steps))
    return lax.ppermute(value, axis, [(source, source + steps) for source in range(initial, last)])


def rms_norm(values, gain):
    widened = values.astype(jnp.float32)
    meansq = jnp.mean(widened * widened, axis=-1, keepdims=True)
    return (widened * lax.rsqrt(meansq + 1e-05) * gain).astype(jnp.bfloat16)


def project(normed, weight):
    return jnp.dot(normed, weight, preferred_element_type=jnp.float32).astype(jnp.bfloat16)


def make_fold(queries):
    row_count = queries.shape[0]
    head_count = queries.shape[1] // HEAD_DIM
    grouped = queries.reshape(row_count, head_count, HEAD_DIM)
    factor = 1.0 / math.sqrt(HEAD_DIM)

    def fold(running, piece, start):
        piece_rows = piece.shape[1]
        block_rows = math.gcd(piece_rows, 1024)
        key_blocks = piece[0].reshape(piece_rows // block_rows, block_rows, head_count, HEAD_DIM)
        value_blocks = piece[1].reshape(piece_rows // block_rows, block_rows, head_count, HEAD_DIM)

        def absorb(current, blocks):
            running_max, running_sum, running_out = current
            key_block, value_block = blocks
            scores = (
                jnp.einsum("qhd,khd->qhk", grouped, key_block, preferred_element_type=jnp.float32)
                * factor
            )
            new_max = jnp.maximum(running_max, jnp.max(scores, axis=2))
            shrink = jnp.exp(running_max - new_max)
            weights = jnp.exp(scores - new_max[:, :, None])
            new_sum = running_sum * shrink + jnp.sum(weights, axis=2)
            new_out = running_out * shrink[:, :, None] + jnp.einsum(
                "qhk,khd->qhd",
                weights.astype(jnp.bfloat16),
                value_block,
                preferred_element_type=jnp.float32,
            )
            return ((new_max, new_sum, new_out), None)

        result, unused = lax.scan(absorb, running, (key_blocks, value_blocks))
        return result

    start_state = (
        jnp.full((row_count, head_count), -1e30, jnp.float32),
        jnp.zeros((row_count, head_count), jnp.float32),
        jnp.zeros((row_count, head_count, HEAD_DIM), jnp.float32),
    )
    return (fold, start_state)


def finish(running):
    running_max, running_sum, running_out = running
    merged = running_out / running_sum[:, :, None]
    return merged.reshape(merged.shape[0], merged.shape[1] * merged.shape[2]).astype(jnp.bfloat16)


def memory_projection(memory_full, memory_gain, cross_weights):
    memory_normed = rms_norm(memory_full, memory_gain)
    return jnp.stack(
        [project(memory_normed, cross_weights[1]), project(memory_normed, cross_weights[2])]
    )


def on_device(
    section_input,
    row_code,
    code_table,
    self_gain,
    self_weights,
    self_out,
    cross_gain,
    memory_gain,
    cross_weights,
    cross_out,
):
    local_rows = section_input.shape[1]
    codes_total = code_table.shape[1]
    matches = (
        row_code[0][:, None] == lax.broadcasted_iota(jnp.int32, (local_rows, codes_total), 1)
    ).astype(jnp.bfloat16)
    looked = jnp.dot(matches, code_table[0], preferred_element_type=jnp.float32)
    embedded = (section_input[0].astype(jnp.float32) + looked).astype(jnp.bfloat16)
    embedded_full = lax.all_gather(embedded, "mp", axis=1, tiled=True)
    normed = rms_norm(embedded_full, self_gain[0])
    self_queries = project(normed, self_weights[0, 0])
    self_pairs = jnp.stack(
        [project(normed, self_weights[0, 1]), project(normed, self_weights[0, 2])]
    )
    fold_self, self_start = make_fold(self_queries)
    self_running = fold_self(
        self_start, lax.all_gather(self_pairs, "blk", axis=1, tiled=True), jnp.int32(0)
    )
    partial_out = jnp.dot(finish(self_running), self_out[0], preferred_element_type=jnp.float32)
    reduced = lax.psum_scatter(
        partial_out.astype(jnp.bfloat16), "mp", scatter_dimension=1, tiled=True
    ).astype(jnp.float32)
    hidden_part = (embedded.astype(jnp.float32) + reduced).astype(jnp.bfloat16)
    hidden_full = lax.all_gather(hidden_part, "mp", axis=1, tiled=True)
    cross_queries = project(rms_norm(hidden_full, cross_gain), cross_weights[0])
    fold_cross, cross_start = make_fold(cross_queries)
    arrived = shifted(hidden_part, "segment", 1)
    memory_full = lax.all_gather(arrived, "mp", axis=1, tiled=True)
    memory_pairs = memory_projection(memory_full, memory_gain, cross_weights)
    crossed = fold_cross(
        cross_start, lax.all_gather(memory_pairs, "blk", axis=1, tiled=True), jnp.int32(0)
    )
    cross_partial = jnp.dot(finish(crossed), cross_out, preferred_element_type=jnp.float32)
    cross_reduced = lax.psum_scatter(
        cross_partial.astype(jnp.bfloat16), "mp", scatter_dimension=1, tiled=True
    ).astype(jnp.float32)
    decoded = (hidden_part.astype(jnp.float32) + cross_reduced).astype(jnp.bfloat16)
    chosen = jnp.where(lax.axis_index("segment") == 0, hidden_part, decoded)
    return chosen[None]


def solution(mesh):
    return jax.shard_map(
        on_device,
        mesh=mesh,
        in_specs=(
            P("segment", "blk", "mp"),
            P("segment", "blk"),
            P("segment", None, "mp"),
            P("segment", None),
            P("segment", None, None, "mp"),
            P("segment", "mp", None),
            P(),
            P(),
            P(None, None, "mp"),
            P("mp", None),
        ),
        out_specs=P("segment", "blk", "mp"),
        check_vma=False,
    )
```

profile of v0, /device:TPU:1, one launch (start us, length us, event | category | flops | bytes accessed | tf_op | source)
XLA Modules:
  0.0 598.6 jit_solution(17165010562332060110)
XLA Ops:
  8.0 10.3 %all_gather.15 = bf16[256,1536]{1,0:T(8,128)(2,1)S(1)} all-gather(bf16[256,384]{1,0:T(8,128)(2,1)S(1)} %fusion.90), channel_id=1, replica_groups=mesh['segment'=2,'blk'=32,'mp'=4] {'mp'}, dimensions={1}, use_global_device_ids=true | all-gather | bytes 983040 | tf_op jit(solution)/shard_map/all_gather | solution.py:101
  19.2 1.9 fusion.100
  21.1 1.9 fusion.97
  26.1 117.8 %all-gather.3.cloned.1.call-done = bf16[2,8192,384]{2,1,0:T(8,128)(2,1)} async-done(((bf16[2,256,384]{2,1,0:T(8,128)(2,1)}), bf16[2,8192,384]{2,1,0:T(8,128)(2,1)}) %all-gather.3.cloned.1.call-update) | async-done | bytes 12582928 | tf_op jit(solution)/shard_map/all_gather | solution.py:109
  143.9 10.2 %fusion.116 = (bf16[1,8192,384]{2,1,0:T(8,128)(2,1)}, bf16[1,8192,384]{2,1,0:T(8,128)(2,1)}) fusion(bf16[2,8192,384]{2,1,0:T(8,128)(2,1)} %all-gather.3.cloned.1.call-done), kind=kLoop, calls=%fused_computation.111 | loop fusion | bytes 25165824 | tf_op jit(solution)/shard_map/slice | solution.py:37
  154.1 16.6 %reshape.48 = bf16[8,1024,3,128]{3,2,1,0:T(4,128)(2,1)} reshape(bf16[1,8192,384]{2,1,0:T(8,128)(2,1)} %get-tuple-element.214) | data formatting | bytes 12582912 | tf_op jit(solution)/shard_map/reshape;squeeze | solution.py:36
  170.8 7.7 %copy.38 = bf16[8,1024,3,128]{3,1,2,0:T(8,128)(2,1)} copy(bf16[8,1024,3,128]{3,2,1,0:T(4,128)(2,1)} %reshape.48) | data formatting | bytes 12582912
  178.4 16.6 %reshape.49 = bf16[8,1024,3,128]{3,2,1,0:T(4,128)(2,1)} reshape(bf16[1,8192,384]{2,1,0:T(8,128)(2,1)} %get-tuple-element.213) | data formatting | bytes 12582912 | tf_op jit(solution)/shard_map/reshape;squeeze | solution.py:37
  195.1 13.0 %copy.40 = bf16[8,1024,3,128]{1,3,2,0:T(8,128)(2,1)} copy(bf16[8,1024,3,128]{3,2,1,0:T(4,128)(2,1)} %reshape.49) | data formatting | bytes 12582912
  208.1 65.1 %while.30 = (s32[]{:T(128)}, f32[256,3]{0,1:T(4,128)S(1)}, f32[256,3]{0,1:T(4,128)S(1)}, f32[256,3,128]{0,2,1:T(8,128)S(1)}, bf16[8,1024,3,128]{3,1,2,0:T(8,128)...) while((s32[]{:T(128)}, f32[256,3]{0,1:T(4,128)S(1)}, ...), condition=%wide.region_4.5_spmd.clone, body=%wide.region_1.4_spmd.clone.sunk | while | flops 409243392 | bytes 24626308 | solution.py:58
  208.1 3.4 bitcast_reduce_fusion.4
  211.5 2.6 fusion.137
  216.2 3.4 bitcast_reduce_fusion.4
  219.6 2.6 fusion.137
  224.4 3.4 bitcast_reduce_fusion.4
  227.8 2.6 fusion.137
  232.5 3.4 bitcast_reduce_fusion.4
  235.9 2.6 fusion.137
  240.6 3.4 bitcast_reduce_fusion.4
  244.0 2.6 fusion.137
  248.8 3.4 bitcast_reduce_fusion.4
  252.2 2.6 fusion.137
  256.9 3.4 bitcast_reduce_fusion.4
  260.3 2.6 fusion.137
  265.0 3.4 bitcast_reduce_fusion.4
  268.4 2.6 fusion.137
  275.1 20.2 %reduce-scatter.7.cloned.1.call-done = bf16[384,256]{1,0:T(8,128)(2,1)} async-done(((bf16[1536,256]{1,0:T(8,128)(2,1)}), bf16[384,256]{1,0:T(8,128)(2,1)}) %reduce-scatter.7.cloned.1.call-update) | async-done | bytes 196624
  296.4 4.5 collective-permute-start
  300.9 4.1 collective-permute-done
  305.0 8.7 %all_gather.17 = bf16[256,1536]{1,0:T(8,128)(2,1)S(1)} all-gather(bf16[256,384]{1,0:T(8,128)(2,1)S(1)} %collective-permute-done), channel_id=1, replica_groups=mesh['segment'=2,'blk'=32,'mp'=4] {'mp'}, dimensions={1}, use_global_device_ids=true | all-gather | bytes 983040 | tf_op jit(solution)/shard_map/all_gather | solution.py:120
  314.0 1.9 fusion.94
  315.9 1.9 fusion.91
  318.7 8.9 %all_gather.19 = bf16[256,1536]{1,0:T(8,128)(2,1)S(1)} all-gather(bf16[256,384]{1,0:T(8,128)(2,1)S(1)} %add_convert_fusion.1), channel_id=1, replica_groups=mesh['segment'=2,'blk'=32,'mp'=4] {'mp'}, dimensions={1}, use_global_device_ids=true | all-gather | bytes 983040 | tf_op jit(solution)/shard_map/all_gather | solution.py:116
  327.8 1.9 fusion.87
  330.0 108.6 %all-gather.5.cloned.1.call-done = bf16[2,8192,384]{2,1,0:T(8,128)(2,1)} async-done(((bf16[2,256,384]{2,1,0:T(8,128)(2,1)}), bf16[2,8192,384]{2,1,0:T(8,128)(2,1)}) %all-gather.5.cloned.1.call-update) | async-done | bytes 12582928 | tf_op jit(solution)/shard_map/all_gather | solution.py:123
  438.6 10.2 %fusion.115 = (bf16[1,8192,384]{2,1,0:T(8,128)(2,1)}, bf16[1,8192,384]{2,1,0:T(8,128)(2,1)}) fusion(bf16[2,8192,384]{2,1,0:T(8,128)(2,1)} %all-gather.5.cloned.1.call-done), kind=kLoop, calls=%fused_computation.110 | loop fusion | bytes 25165824 | tf_op jit(solution)/shard_map/slice | solution.py:37
  448.8 16.6 %reshape.50 = bf16[8,1024,3,128]{3,2,1,0:T(4,128)(2,1)} reshape(bf16[1,8192,384]{2,1,0:T(8,128)(2,1)} %get-tuple-element.212) | data formatting | bytes 12582912 | tf_op jit(solution)/shard_map/reshape;squeeze | solution.py:36
  465.5 7.7 %copy.44 = bf16[8,1024,3,128]{3,1,2,0:T(8,128)(2,1)} copy(bf16[8,1024,3,128]{3,2,1,0:T(4,128)(2,1)} %reshape.50) | data formatting | bytes 12582912
  473.1 16.6 %reshape.51 = bf16[8,1024,3,128]{3,2,1,0:T(4,128)(2,1)} reshape(bf16[1,8192,384]{2,1,0:T(8,128)(2,1)} %get-tuple-element.211) | data formatting | bytes 12582912 | tf_op jit(solution)/shard_map/reshape;squeeze | solution.py:37
  489.8 13.0 %copy.46 = bf16[8,1024,3,128]{1,3,2,0:T(8,128)(2,1)} copy(bf16[8,1024,3,128]{3,2,1,0:T(4,128)(2,1)} %reshape.51) | data formatting | bytes 12582912
  502.8 65.2 %while.31 = (s32[]{:T(128)}, f32[256,3]{0,1:T(4,128)S(1)}, f32[256,3]{0,1:T(4,128)S(1)}, f32[256,3,128]{0,2,1:T(8,128)S(1)}, bf16[8,1024,3,128]{3,1,2,0:T(8,128)...) while((s32[]{:T(128)}, f32[256,3]{0,1:T(4,128)S(1)}, ...), condition=%wide.region_11.12_spmd.clone, body=%wide.region_8.11_spmd.clone.sunk | while | flops 409243392 | bytes 24626308 | solution.py:58
  502.8 3.5 bitcast_reduce_fusion.5
  506.3 2.6 fusion.143
  509.1 1.9 fusion.145
  511.1 3.4 bitcast_reduce_fusion.5
  514.4 2.6 fusion.143
  517.3 1.9 fusion.145
  519.2 3.4 bitcast_reduce_fusion.5
  522.6 2.6 fusion.143
  525.4 1.9 fusion.145
  527.3 3.4 bitcast_reduce_fusion.5
  530.7 2.6 fusion.143
  533.5 1.9 fusion.145
  535.5 3.4 bitcast_reduce_fusion.5
  538.8 2.6 fusion.143
  543.6 3.4 bitcast_reduce_fusion.5
  547.0 2.6 fusion.143
  551.7 3.4 bitcast_reduce_fusion.5
  555.1 2.6 fusion.143
  557.9 1.9 fusion.145
  559.9 3.4 bitcast_reduce_fusion.5
  563.2 2.6 fusion.143
  566.1 1.9 fusion.145
  569.8 20.4 %reduce-scatter.9.cloned.1.call-done = bf16[384,256]{1,0:T(8,128)(2,1)} async-done(((bf16[1536,256]{1,0:T(8,128)(2,1)}), bf16[384,256]{1,0:T(8,128)(2,1)}) %reduce-scatter.9.cloned.1.call-update) | async-done | bytes 196624
  (139 shorter events, 36.7 us)
Async XLA Ops:
  6.5 266.7 %copy-start = (bf16[1,384,1536]{2,1,0:T(8,128)(2,1)S(1)}, bf16[1,384,1536]{2,1,0:T(8,128)(2,1)}, u32[]{:S(2)}) copy-start(bf16[1,384,1536]{2,1,0:T(8,128)(2,1)} %param.19) | copy-start | bytes 3538948
  6.5 137.4 %all-gather.3.cloned.1.call-start = ((), (), s32[]{:S(2)}) async-start(), calls=%async_computation.2 | async-start | bytes 12976128 | tf_op jit(solution)/shard_map/all_gather | solution.py:109
  23.8 271.5 %reduce-scatter.7.cloned.1.call-start = ((), (), s32[]{:S(2)}) async-start(), calls=%async_computation.4 | async-start | bytes 983040
  211.5 2.8 copy-start.2
  219.6 2.8 copy-start.2
  227.8 2.8 copy-start.2
  235.9 2.8 copy-start.2
  244.0 2.8 copy-start.2
  252.2 2.8 copy-start.2
  260.3 2.8 copy-start.2
  268.4 2.8 copy-start.2
  273.2 40.8 %copy-start.5 = (f32[1536]{0:T(1024)S(1)}, f32[1536]{0:T(1024)}, u32[]{:S(2)}) copy-start(f32[1536]{0:T(1024)} %param.21) | copy-start | bytes 18436
  275.0 163.6 %all-gather.5.cloned.1.call-start = ((), (), s32[]{:S(2)}) async-start(), calls=%async_computation.3 | async-start | bytes 12976128 | tf_op jit(solution)/shard_map/all_gather | solution.py:123
  296.4 8.6 %collective-permute-start = (bf16[256,384]{1,0:T(8,128)(2,1)S(1)}, bf16[256,384]{1,0:T(8,128)(2,1)S(1)}, u32[]{:S(2)}, u32[]{:S(2)}) collective-permute-start(bf16[256,384]{1,0:T(8,128)(2,1)S(1)} %add_convert_fusion.1), channel_id=1, source_target_pairs={{0,128},{1,129},{2,130},{3,131},{4,132},{5,133},{6,134},{7,135},{8... | collective-permute-start | bytes 589832 | tf_op jit(solution)/shard_map/ppermute | solution.py:14
  315.9 11.9 %copy-start.6 = (f32[1536]{0:T(1024)S(1)}, f32[1536]{0:T(1024)}, u32[]{:S(2)}) copy-start(f32[1536]{0:T(1024)} %param.20) | copy-start | bytes 18436
  318.6 271.6 %reduce-scatter.9.cloned.1.call-start = ((), (), s32[]{:S(2)}) async-start(), calls=%async_computation.5 | async-start | bytes 983040
  502.8 65.2 %copy-start.4 = (bf16[384,1536]{1,0:T(8,128)(2,1)S(1)}, bf16[384,1536]{1,0:T(8,128)(2,1)}, u32[]{:S(2)}) copy-start(bf16[384,1536]{1,0:T(8,128)(2,1)} %param.23) | copy-start | bytes 3538948
  506.3 2.8 copy-start.3
  514.4 2.8 copy-start.3
  522.6 2.8 copy-start.3
  530.7 2.8 copy-start.3
  538.8 2.8 copy-start.3
  547.0 2.8 copy-start.3
  555.1 2.8 copy-start.3
  563.2 2.8 copy-start.3
  568.0 24.1 %copy-start.1 = (bf16[1,384,1536]{2,1,0:T(8,128)(2,1)S(1)}, bf16[1,384,1536]{2,1,0:T(8,128)(2,1)}, u32[]{:S(2)}) copy-start(bf16[1,384,1536]{2,1,0:T(8,128)(2,1)} %param.19) | copy-start | bytes 3538948
Sparse Core Ops, SparseCore 0:
  23.9 119.9 all-gather.2
  275.1 20.1 reduce-scatter.6
  318.7 119.8 all-gather.4
  569.9 20.2 reduce-scatter.8
where the time goes:
time: 603 us; the launch traced here: 599 us
  waiting for transfers between devices  271 us (45%)
  local copies, waits for them, and re-layouts  137 us (23%)
  matrix products  98.3 us (16%)
  other arithmetic  45.4 us (8%)
  blocking collectives  27.8 us (5%)
  between operations  13.4 us (2%)
    all_gather x1, waiting for transfers between devices, on_device(): lax.all_gather(self_pairs, 'blk', axis=1, tiled=True)  118 us
    all_gather x1, waiting for transfers between devices, on_device(): lax.all_gather(memory_pairs, 'blk', axis=1, tiled=True)  109 us
    dot_general x16, matrix products, absorb(): jnp.einsum('qhd,khd->qhk', grouped, key_block, preferred_element_type=jnp...  54.2 us
    unnamed x20, local copies, waits for them, and re-layouts  46.3 us
    reduce_sum x16, other arithmetic, absorb(): new_sum = running_sum * shrink + jnp.sum(weights, axis=2)  41.1 us
    unnamed x6, waiting for transfers between devices  40.7 us
    another operation x2, local copies, waits for them, and re-layouts, fold(): piece[0].reshape(piece_rows // block_rows, block_rows, head_count, HEAD_DIM)  33.3 us
    another operation x2, local copies, waits for them, and re-layouts, fold(): piece[1].reshape(piece_rows // block_rows, block_rows, head_count, HEAD_DIM)  33.3 us
  transfers between devices with their start and end apart: 5, of which 5 were waited for; matrix products, arithmetic and copies ran while one was open for 1% of the time, Pallas kernels for 0%

commit v1 on v0

--- a/solution.py
+++ b/solution.py
@@ -4,6 +4,8 @@
 import jax.numpy as jnp
 from jax import lax
 from jax.sharding import PartitionSpec as P
+from jax.experimental import pallas as pl
+from jax.experimental.pallas import tpu as pltpu
 
 HEAD_DIM = 128
 
@@ -72,6 +74,35 @@
     return merged.reshape(merged.shape[0], merged.shape[1] * merged.shape[2]).astype(jnp.bfloat16)
 
 
+def attend_kernel(q_ref, k_ref, v_ref, o_ref):
+    scores = lax.dot_general(
+        q_ref[...], k_ref[...], (((1,), (1,)), ((), ())), preferred_element_type=jnp.float32
+    ) * (1.0 / math.sqrt(HEAD_DIM))
+    largest = jnp.max(scores, axis=1, keepdims=True)
+    weights = jnp.exp(scores - largest)
+    summed = jnp.sum(weights, axis=1, keepdims=True)
+    result = jnp.dot(weights.astype(jnp.bfloat16), v_ref[...], preferred_element_type=jnp.float32)
+    o_ref[...] = (result / summed).astype(o_ref.dtype)
+
+
+def attend(queries, pairs):
+    rows, width = queries.shape
+    keys = pairs.shape[1]
+    heads = width // HEAD_DIM
+    return pl.pallas_call(
+        attend_kernel,
+        grid=(heads,),
+        in_specs=[
+            pl.BlockSpec((rows, HEAD_DIM), lambda h: (0, h)),
+            pl.BlockSpec((None, keys, HEAD_DIM), lambda h: (0, 0, h)),
+            pl.BlockSpec((None, keys, HEAD_DIM), lambda h: (1, 0, h)),
+        ],
+        out_specs=pl.BlockSpec((rows, HEAD_DIM), lambda h: (0, h)),
+        out_shape=jax.ShapeDtypeStruct((rows, width), jnp.bfloat16),
+        compiler_params=pltpu.CompilerParams(vmem_limit_bytes=48 * 1024 * 1024),
+    )(queries, pairs, pairs)
+
+
 def memory_projection(memory_full, memory_gain, cross_weights):
     memory_normed = rms_norm(memory_full, memory_gain)
     return jnp.stack(
@@ -104,25 +135,19 @@
     self_pairs = jnp.stack(
         [project(normed, self_weights[0, 1]), project(normed, self_weights[0, 2])]
     )
-    fold_self, self_start = make_fold(self_queries)
-    self_running = fold_self(
-        self_start, lax.all_gather(self_pairs, "blk", axis=1, tiled=True), jnp.int32(0)
-    )
-    partial_out = jnp.dot(finish(self_running), self_out[0], preferred_element_type=jnp.float32)
+    self_attended = attend(self_queries, lax.all_gather(self_pairs, "blk", axis=1, tiled=True))
+    partial_out = jnp.dot(self_attended, self_out[0], preferred_element_type=jnp.float32)
     reduced = lax.psum_scatter(
         partial_out.astype(jnp.bfloat16), "mp", scatter_dimension=1, tiled=True
     ).astype(jnp.float32)
     hidden_part = (embedded.astype(jnp.float32) + reduced).astype(jnp.bfloat16)
     hidden_full = lax.all_gather(hidden_part, "mp", axis=1, tiled=True)
     cross_queries = project(rms_norm(hidden_full, cross_gain), cross_weights[0])
-    fold_cross, cross_start = make_fold(cross_queries)
     arrived = shifted(hidden_part, "segment", 1)
     memory_full = lax.all_gather(arrived, "mp", axis=1, tiled=True)
     memory_pairs = memory_projection(memory_full, memory_gain, cross_weights)
-    crossed = fold_cross(
-        cross_start, lax.all_gather(memory_pairs, "blk", axis=1, tiled=True), jnp.int32(0)
-    )
-    cross_partial = jnp.dot(finish(crossed), cross_out, preferred_element_type=jnp.float32)
+    crossed = attend(cross_queries, lax.all_gather(memory_pairs, "blk", axis=1, tiled=True))
+    cross_partial = jnp.dot(crossed, cross_out, preferred_element_type=jnp.float32)
     cross_reduced = lax.psum_scatter(
         cross_partial.astype(jnp.bfloat16), "mp", scatter_dimension=1, tiled=True
     ).astype(jnp.float32)

time: 603 us -> 368 us (0.61)
  local copies, waits for them, and re-layouts: 137 us -> 4.52 us
  matrix products: 98.3 us -> 13.9 us
  other arithmetic: 45.4 us -> 3.17 us
  Pallas kernels: 0 us -> 28.2 us
    dot_general x34 -> x2, matrix products: 85.5 us -> 1.14 us  [the longest x1 0.57 us: on_device(): jnp.dot(self_attended, self_out[0], preferred_element_type=jnp.float32)]
    another operation x4 -> x0, local copies, waits for them, and re-layouts: 66.5 us -> none  [the longest x2 33.3 us: fold(): piece[0].reshape(piece_rows // block_rows, block_rows, head_count, HEAD_DIM)]
    unnamed x20 -> x14, local copies, waits for them, and re-layouts: 46.3 us -> 4.52 us
    reduce_sum x16 -> x0, other arithmetic: 41.1 us -> none  [absorb(): new_sum = running_sum * shrink + jnp.sum(weights, axis=2)]
    pallas_call x0 -> x2, Pallas kernels: none -> 28.2 us  [attend(): pl.pallas_call(attend_kernel, grid=(heads,), in_specs=[pl.BlockSpec((rows...]
    slice x2 -> x0, local copies, waits for them, and re-layouts: 20.4 us -> none  [fold(): piece[1].reshape(piece_rows // block_rows, block_rows, head_count, HEAD_DIM)]
where the time goes in v1:
time: 368 us
  waiting for transfers between devices  272 us (74%)
  Pallas kernels  28.2 us (8%)
  blocking collectives  27.8 us (8%)
  matrix products  13.9 us (4%)
  between operations  13.3 us (4%)
  starting transfers between devices  4.57 us (1%)
  local copies, waits for them, and re-layouts  4.52 us (1%)
    all_gather x1, waiting for transfers between devices, on_device(): lax.all_gather(self_pairs, 'blk', axis=1, tiled=True)  118 us
    all_gather x1, waiting for transfers between devices, on_device(): lax.all_gather(memory_pairs, 'blk', axis=1, tiled=True)  109 us
    unnamed x6, waiting for transfers between devices  40.7 us
    pallas_call x2, Pallas kernels, attend(): pl.pallas_call(attend_kernel, grid=(heads,), in_specs=[pl.BlockSpec((rows...  28.2 us
    dot_general x6, matrix products, project(): jnp.dot(normed, weight, preferred_element_type=jnp.float32)  11.4 us
    all_gather x1, blocking collectives, on_device(): embedded_full = lax.all_gather(embedded, 'mp', axis=1, tiled=True)  10.3 us
    all_gather x1, blocking collectives, on_device(): hidden_full = lax.all_gather(hidden_part, 'mp', axis=1, tiled=True)  8.89 us
    all_gather x1, blocking collectives, on_device(): memory_full = lax.all_gather(arrived, 'mp', axis=1, tiled=True)  8.69 us
  transfers between devices with their start and end apart: 5, of which 5 were waited for; matrix products, arithmetic and copies ran while one was open for 1% of the time, Pallas kernels for 0%

profile of v1, /device:TPU:1, one launch (start us, length us, event | category | flops | bytes accessed | tf_op | source)
XLA Modules:
  0.0 367.5 jit_solution(17183074126242886081)
XLA Ops:
  6.5 0.0 copy-start
  6.5 0.0 copy-start.2
  6.5 0.0 all-gather.3.cloned.1.call-start
  6.5 1.4 fusion.46
  8.0 10.3 %all_gather.15 = bf16[256,1536]{1,0:T(8,128)(2,1)S(1)} all-gather(bf16[256,384]{1,0:T(8,128)(2,1)S(1)} %fusion.46), channel_id=1, replica_groups=mesh['segment'=2,'blk'=32,'mp'=4] {'mp'}, dimensions={1}, use_global_device_ids=true | all-gather | bytes 983040 | tf_op jit(solution)/shard_map/all_gather | solution.py:132
  18.2 0.2 fusion
  18.5 0.0 copy-done.2
  18.5 1.9 fusion.53
  20.4 1.9 fusion.56
  22.3 0.8 pad_maximum_fusion
  23.1 0.0 all-gather.3.cloned.1.call-update
  23.2 0.0 reduce-scatter.7.cloned.1.call-start
  23.2 1.9 fusion.28.q_ref
  25.1 118.2 %all-gather.3.cloned.1.call-done.k_ref.v_ref = bf16[2,8192,384]{2,1,0:T(8,128)(2,1)} async-done(((bf16[2,256,384]{2,1,0:T(8,128)(2,1)}), bf16[2,8192,384]{2,1,0:T(8,128)(2,1)}) %all-gather.3.cloned.1.call-update) | async-done | bytes 12582928 | tf_op jit(solution)/shard_map/all_gather | solution.py:138
  143.3 14.1 %shard_map.100 = bf16[256,384]{1,0:T(8,128)(2,1)S(1)} custom-call(bf16[256,384]{1,0:T(8,128)(2,1)S(1)} %fusion.28.q_ref, bf16[2,8192,384]{2,1,0:T(8,128)(2,1)} %all-gather.3.cloned.1.call-done.k_ref.v_ref, bf16[2,8192,384]{2,1,0:T(8,128)(2,1)} %all-gather.3.cloned.1.call-done.k_ref.v_ref), custom_call_target="tpu_custom_call" | custom-call | tf_op jit(solution)/shard_map/pallas_call | solution.py:92
  157.4 0.0 copy-done
  157.5 0.6 convolution_convert_fusion.1
  158.0 1.2 copy.11
  159.2 0.0 reduce-scatter.7.cloned.1.call-update
  159.2 0.0 copy-start.3
  159.2 0.0 all-gather.5.cloned.1.call-start
  159.3 20.3 %reduce-scatter.7.cloned.1.call-done = bf16[384,256]{1,0:T(8,128)(2,1)} async-done(((bf16[1536,256]{1,0:T(8,128)(2,1)}), bf16[384,256]{1,0:T(8,128)(2,1)}) %reduce-scatter.7.cloned.1.call-update) | async-done | bytes 196624
  179.5 1.1 copy.12
  180.6 0.1 add_convert_fusion.1
  180.7 4.4 %collective-permute-start = (bf16[256,384]{1,0:T(8,128)(2,1)S(1)}, bf16[256,384]{1,0:T(8,128)(2,1)S(1)}, u32[]{:S(2)}, u32[]{:S(2)}) collective-permute-start(bf16[256,384]{1,0:T(8,128)(2,1)S(1)} %add_convert_fusion.1), channel_id=1, source_target_pairs={{0,128},{1,129},{2,130},{3,131},{4,132},{5,133},{6,134},{7,135},{8... | collective-permute-start | bytes 589832 | tf_op jit(solution)/shard_map/ppermute | solution.py:16
  185.1 4.1 %collective-permute-done = bf16[256,384]{1,0:T(8,128)(2,1)S(1)} collective-permute-done((bf16[256,384]{1,0:T(8,128)(2,1)S(1)}, bf16[256,384]{1,0:T(8,128)(2,1)S(1)}, u32[]{:S(2)}, u32[]{:S(2)}) %collective-permute-start) | collective-permute-done | bytes 196640 | tf_op jit(solution)/shard_map/ppermute | solution.py:16
  189.3 8.7 %all_gather.18 = bf16[256,1536]{1,0:T(8,128)(2,1)S(1)} all-gather(bf16[256,384]{1,0:T(8,128)(2,1)S(1)} %collective-permute-done), channel_id=1, replica_groups=mesh['segment'=2,'blk'=32,'mp'=4] {'mp'}, dimensions={1}, use_global_device_ids=true | all-gather | bytes 983040 | tf_op jit(solution)/shard_map/all_gather | solution.py:147
  198.0 0.2 fusion.6
  198.2 0.0 copy-done.3
  198.2 1.9 fusion.47
  200.1 1.9 fusion.50
  202.0 0.0 copy-start.4
  202.0 0.8 pad_maximum_fusion.1
  202.8 0.0 all-gather.5.cloned.1.call-update
  202.9 0.0 reduce-scatter.9.cloned.1.call-start
  202.9 8.9 %all_gather.17 = bf16[256,1536]{1,0:T(8,128)(2,1)S(1)} all-gather(bf16[256,384]{1,0:T(8,128)(2,1)S(1)} %add_convert_fusion.1), channel_id=1, replica_groups=mesh['segment'=2,'blk'=32,'mp'=4] {'mp'}, dimensions={1}, use_global_device_ids=true | all-gather | bytes 983040 | tf_op jit(solution)/shard_map/all_gather | solution.py:144
  211.8 0.2 fusion.3
  212.0 0.0 copy-done.4
  212.1 1.9 fusion.37.q_ref
  214.0 0.0 copy-start.1
  214.0 108.9 %all-gather.5.cloned.1.call-done.k_ref.v_ref = bf16[2,8192,384]{2,1,0:T(8,128)(2,1)} async-done(((bf16[2,256,384]{2,1,0:T(8,128)(2,1)}), bf16[2,8192,384]{2,1,0:T(8,128)(2,1)}) %all-gather.5.cloned.1.call-update) | async-done | bytes 12582928 | tf_op jit(solution)/shard_map/all_gather | solution.py:149
  322.8 14.1 %shard_map.101 = bf16[256,384]{1,0:T(8,128)(2,1)S(1)} custom-call(bf16[256,384]{1,0:T(8,128)(2,1)S(1)} %fusion.37.q_ref, bf16[2,8192,384]{2,1,0:T(8,128)(2,1)} %all-gather.5.cloned.1.call-done.k_ref.v_ref, bf16[2,8192,384]{2,1,0:T(8,128)(2,1)} %all-gather.5.cloned.1.call-done.k_ref.v_ref), custom_call_target="tpu_custom_call" | custom-call | tf_op jit(solution)/shard_map/pallas_call | solution.py:92
  336.9 0.0 copy-done.1
  337.0 0.6 convolution_convert_fusion
  337.5 1.2 copy.13
  338.7 0.0 reduce-scatter.9.cloned.1.call-update
  338.7 20.4 %reduce-scatter.9.cloned.1.call-done = bf16[384,256]{1,0:T(8,128)(2,1)} async-done(((bf16[1536,256]{1,0:T(8,128)(2,1)}), bf16[384,256]{1,0:T(8,128)(2,1)}) %reduce-scatter.9.cloned.1.call-update) | async-done | bytes 196624
  359.1 1.1 copy.14
  360.2 0.7 fusion.65
  (4 shorter events, 0.0 us)
Async XLA Ops:
  6.5 150.9 %copy-start = (bf16[1,384,1536]{2,1,0:T(8,128)(2,1)S(1)}, bf16[1,384,1536]{2,1,0:T(8,128)(2,1)}, u32[]{:S(2)}) copy-start(bf16[1,384,1536]{2,1,0:T(8,128)(2,1)} %param.15) | copy-start | bytes 3538948
  6.5 11.9 %copy-start.2 = (f32[1,1536]{1,0:T(1,128)S(1)}, f32[1,1536]{1,0:T(1,128)}, u32[]{:S(2)}) copy-start(f32[1,1536]{1,0:T(1,128)} %param.13) | copy-start | bytes 18436
  6.5 136.8 %all-gather.3.cloned.1.call-start = ((), (), s32[]{:S(2)}) async-start(), calls=%async_computation.2 | async-start | bytes 12976128 | tf_op jit(solution)/shard_map/all_gather | solution.py:138
  23.2 156.4 %reduce-scatter.7.cloned.1.call-start = ((), (), s32[]{:S(2)}) async-start(), calls=%async_computation.4 | async-start | bytes 983040
  159.2 39.0 %copy-start.3 = (f32[1536]{0:T(1024)S(1)}, f32[1536]{0:T(1024)}, u32[]{:S(2)}) copy-start(f32[1536]{0:T(1024)} %param.17) | copy-start | bytes 18436
  159.2 163.6 %all-gather.5.cloned.1.call-start = ((), (), s32[]{:S(2)}) async-start(), calls=%async_computation.3 | async-start | bytes 12976128 | tf_op jit(solution)/shard_map/all_gather | solution.py:149
  180.7 8.6 %collective-permute-start = (bf16[256,384]{1,0:T(8,128)(2,1)S(1)}, bf16[256,384]{1,0:T(8,128)(2,1)S(1)}, u32[]{:S(2)}, u32[]{:S(2)}) collective-permute-start(bf16[256,384]{1,0:T(8,128)(2,1)S(1)} %add_convert_fusion.1), channel_id=1, source_target_pairs={{0,128},{1,129},{2,130},{3,131},{4,132},{5,133},{6,134},{7,135},{8... | collective-permute-start | bytes 589832 | tf_op jit(solution)/shard_map/ppermute | solution.py:16
  202.0 10.0 %copy-start.4 = (f32[1536]{0:T(1024)S(1)}, f32[1536]{0:T(1024)}, u32[]{:S(2)}) copy-start(f32[1536]{0:T(1024)} %param.16) | copy-start | bytes 18436
  202.9 156.3 %reduce-scatter.9.cloned.1.call-start = ((), (), s32[]{:S(2)}) async-start(), calls=%async_computation.5 | async-start | bytes 983040
  214.0 123.0 %copy-start.1 = (bf16[384,1536]{1,0:T(8,128)(2,1)S(1)}, bf16[384,1536]{1,0:T(8,128)(2,1)}, u32[]{:S(2)}) copy-start(bf16[384,1536]{1,0:T(8,128)(2,1)} %param.19) | copy-start | bytes 3538948
Sparse Core Ops, SparseCore 0:
  23.3 119.9 all-gather.2
  159.3 20.1 reduce-scatter.6
  203.0 119.8 all-gather.4
  338.8 20.2 reduce-scatter.8

commit v2 on v0

v2 whole, which is shorter than its diff:
```python
import math

import jax
import jax.numpy as jnp
from jax import lax
from jax.experimental import pallas as pl
from jax.experimental.pallas import tpu as pltpu
from jax.sharding import Mesh
from jax.sharding import PartitionSpec as P

HEAD_DIM = 128
X_SIZE = 4
TILE = 256
STATS = 128


def shifted(value, axis, steps):
    count = lax.axis_size(axis)
    initial, last = (max(0, -steps), min(count, count - steps))
    return lax.ppermute(value, axis, [(source, source + steps) for source in range(initial, last)])


def rms_norm(values, gain):
    widened = values.astype(jnp.float32)
    meansq = jnp.mean(widened * widened, axis=-1, keepdims=True)
    return (widened * lax.rsqrt(meansq + 1e-05) * gain).astype(jnp.bfloat16)


def project(normed, weight):
    return jnp.dot(normed, weight, preferred_element_type=jnp.float32).astype(jnp.bfloat16)


def partial_kernel(q_ref, k_ref, v_ref, o_ref):
    heads = q_ref.shape[1] // HEAD_DIM
    rows = q_ref.shape[0]
    lane = lax.broadcasted_iota(jnp.int32, (rows, STATS), 1)
    stats = jnp.zeros((rows, STATS), jnp.float32)
    for h in range(heads):
        cols = slice(h * HEAD_DIM, (h + 1) * HEAD_DIM)
        scores = lax.dot_general(
            q_ref[:, cols], k_ref[:, cols], (((1,), (1,)), ((), ())),
            preferred_element_type=jnp.float32,
        ) * (1.0 / math.sqrt(HEAD_DIM))
        largest = jnp.max(scores, axis=1, keepdims=True)
        weights = jnp.exp(scores - largest)
        summed = jnp.sum(weights, axis=1, keepdims=True)
        o_ref[:, cols] = jnp.dot(
            weights.astype(jnp.bfloat16), v_ref[:, cols], preferred_element_type=jnp.float32
        )
        stats = jnp.where(lane == h, largest, stats)
        stats = jnp.where(lane == heads + h, summed, stats)
    o_ref[:, heads * HEAD_DIM:] = stats


def partial_attend(queries, pairs):
    rows, width = queries.shape
    keys = pairs.shape[1]
    return pl.pallas_call(
        partial_kernel,
        grid=(rows // TILE,),
        in_specs=[
            pl.BlockSpec((TILE, width), lambda i: (i, 0)),
            pl.BlockSpec((None, keys, width), lambda i: (0, 0, 0)),
            pl.BlockSpec((None, keys, width), lambda i: (1, 0, 0)),
        ],
        out_specs=pl.BlockSpec((TILE, width + STATS), lambda i: (i, 0)),
        out_shape=jax.ShapeDtypeStruct((rows, width + STATS), jnp.float32),
        compiler_params=pltpu.CompilerParams(vmem_limit_bytes=48 * 1024 * 1024),
    )(queries, pairs, pairs)


def attend(queries, pairs):
    rows, width = queries.shape
    heads = width // HEAD_DIM
    query_block = lax.all_gather(queries, "bx", axis=0, tiled=True)
    key_block = lax.all_gather(pairs, "bz", axis=1, tiled=True)
    partial = partial_attend(query_block, key_block)
    parts = lax.all_to_all(partial, "bx", 0, 0, tiled=True)
    parts = parts.reshape(-1, rows, width + STATS)
    outs = parts[:, :, :width].reshape(-1, rows, heads, HEAD_DIM)
    maxes = parts[:, :, width:width + heads]
    sums = parts[:, :, width + heads:width + 2 * heads]
    top = jnp.max(maxes, axis=0)
    scale = jnp.exp(maxes - top[None])
    total = jnp.sum(sums * scale, axis=0)
    merged = jnp.sum(outs * scale[..., None], axis=0) / total[..., None]
    return merged.reshape(rows, width).astype(jnp.bfloat16)


def memory_projection(memory_full, memory_gain, cross_weights):
    memory_normed = rms_norm(memory_full, memory_gain)
    return jnp.stack(
        [project(memory_normed, cross_weights[1]), project(memory_normed, cross_weights[2])]
    )


def on_device(
    section_input,
    row_code,
    code_table,
    self_gain,
    self_weights,
    self_out,
    cross_gain,
    memory_gain,
    cross_weights,
    cross_out,
):
    local_rows = section_input.shape[1]
    codes_total = code_table.shape[1]
    matches = (
        row_code[0][:, None] == lax.broadcasted_iota(jnp.int32, (local_rows, codes_total), 1)
    ).astype(jnp.bfloat16)
    looked = jnp.dot(matches, code_table[0], preferred_element_type=jnp.float32)
    embedded = (section_input[0].astype(jnp.float32) + looked).astype(jnp.bfloat16)
    embedded_full = lax.all_gather(embedded, "mp", axis=1, tiled=True)
    normed = rms_norm(embedded_full, self_gain[0])
    self_queries = project(normed, self_weights[0, 0])
    self_pairs = jnp.stack(
        [project(normed, self_weights[0, 1]), project(normed, self_weights[0, 2])]
    )
    self_attended = attend(self_queries, self_pairs)
    partial_out = jnp.dot(self_attended, self_out[0], preferred_element_type=jnp.float32)
    reduced = lax.psum_scatter(
        partial_out.astype(jnp.bfloat16), "mp", scatter_dimension=1, tiled=True
    ).astype(jnp.float32)
    hidden_part = (embedded.astype(jnp.float32) + reduced).astype(jnp.bfloat16)
    hidden_full = lax.all_gather(hidden_part, "mp", axis=1, tiled=True)
    cross_queries = project(rms_norm(hidden_full, cross_gain), cross_weights[0])
    arrived = shifted(hidden_part, "segment", 1)
    memory_full = lax.all_gather(arrived, "mp", axis=1, tiled=True)
    memory_pairs = memory_projection(memory_full, memory_gain, cross_weights)
    crossed = attend(cross_queries, memory_pairs)
    cross_partial = jnp.dot(crossed, cross_out, preferred_element_type=jnp.float32)
    cross_reduced = lax.psum_scatter(
        cross_partial.astype(jnp.bfloat16), "mp", scatter_dimension=1, tiled=True
    ).astype(jnp.float32)
    decoded = (hidden_part.astype(jnp.float32) + cross_reduced).astype(jnp.bfloat16)
    chosen = jnp.where(lax.axis_index("segment") == 0, hidden_part, decoded)
    return chosen[None]


def solution(mesh):
    segments, blocks, parts = (mesh.shape["segment"], mesh.shape["blk"], mesh.shape["mp"])
    split = Mesh(
        mesh.devices.reshape(segments, blocks // X_SIZE, X_SIZE, parts),
        ("segment", "bz", "bx", "mp"),
    )
    rows = ("bz", "bx")
    return jax.shard_map(
        on_device,
        mesh=split,
        in_specs=(
            P("segment", rows, "mp"),
            P("segment", rows),
            P("segment", None, "mp"),
            P("segment", None),
            P("segment", None, None, "mp"),
            P("segment", "mp", None),
            P(),
            P(),
            P(None, None, "mp"),
            P("mp", None),
        ),
        out_specs=P("segment", rows, "mp"),
        check_vma=False,
    )
```

time: 603 us -> 288 us (0.48)
  waiting for transfers between devices: 271 us -> 102 us
  local copies, waits for them, and re-layouts: 137 us -> 16 us
  matrix products: 98.3 us -> 13.9 us
  blocking collectives: 27.8 us -> 110 us
  other arithmetic: 45.4 us -> 3.53 us
  Pallas kernels: 0 us -> 23.6 us
    all_gather x2, waiting for transfers between devices: 226 us -> 54.7 us  [attend(): key_block = lax.all_gather(pairs, 'bz', axis=1, tiled=True)]
    dot_general x34 -> x2, matrix products: 85.5 us -> 1.18 us  [the longest x1 0.59 us: on_device(): jnp.dot(self_attended, self_out[0], preferred_element_type=jnp.float32)]
    another operation x4 -> x0, local copies, waits for them, and re-layouts: 66.5 us -> none  [the longest x2 33.3 us: fold(): piece[0].reshape(piece_rows // block_rows, block_rows, head_count, HEAD_DIM)]
    all_to_all x0 -> x2, blocking collectives: none -> 57.2 us  [attend(): parts = lax.all_to_all(partial, 'bx', 0, 0, tiled=True)]
    reduce_sum x16 -> x4, other arithmetic: 41.1 us -> 0.31 us  [the longest x2 0.26 us: attend(): merged = jnp.sum(outs * scale[..., None], axis=0) / total[..., None]]
    unnamed x20 -> x26, local copies, waits for them, and re-layouts: 46.3 us -> 12.3 us
    all_gather x0 -> x2, blocking collectives: none -> 25.4 us  [attend(): query_block = lax.all_gather(queries, 'bx', axis=0, tiled=True)]
    pallas_call x0 -> x2, Pallas kernels: none -> 23.6 us  [partial_attend(): pl.pallas_call(partial_kernel, grid=(rows // TILE,), in_specs=[pl.BlockSp...]
where the time goes in v2:
time: 288 us; the launch traced here: 287 us
  blocking collectives  110 us (38%)
  waiting for transfers between devices  102 us (35%)
  Pallas kernels  23.6 us (8%)
  local copies, waits for them, and re-layouts  16 us (6%)
  matrix products  13.9 us (5%)
  between operations  13.3 us (5%)
  starting transfers between devices  4.41 us (2%)
  other arithmetic  3.53 us (1%)
    all_to_all x2, blocking collectives, attend(): parts = lax.all_to_all(partial, 'bx', 0, 0, tiled=True)  57.2 us
    all_gather x2, waiting for transfers between devices, attend(): key_block = lax.all_gather(pairs, 'bz', axis=1, tiled=True)  54.7 us
    unnamed x6, waiting for transfers between devices  43.2 us
    all_gather x2, blocking collectives, attend(): query_block = lax.all_gather(queries, 'bx', axis=0, tiled=True)  25.4 us
    pallas_call x2, Pallas kernels, partial_attend(): pl.pallas_call(partial_kernel, grid=(rows // TILE,), in_specs=[pl.BlockSp...  23.6 us
    unnamed x26, local copies, waits for them, and re-layouts  12.3 us
    dot_general x6, matrix products, project(): jnp.dot(normed, weight, preferred_element_type=jnp.float32)  11.3 us
    all_gather x1, blocking collectives, on_device(): embedded_full = lax.all_gather(embedded, 'mp', axis=1, tiled=True)  10.2 us
  transfers between devices with their start and end apart: 5, of which 5 were waited for; matrix products, arithmetic and copies ran while one was open for 1% of the time, Pallas kernels for 0%

profile of v2, /device:TPU:1, one launch (start us, length us, event | category | flops | bytes accessed | tf_op | source)
XLA Modules:
  0.0 287.1 jit_solution(13144329391409440854)
XLA Ops:
  6.5 0.0 copy-start
  6.5 0.0 all-gather.3.cloned.1.call-start
  6.5 1.4 fusion.48
  8.0 0.0 copy-start.5
  8.0 0.7 copy-done.5
  8.6 10.2 %all_gather.21 = bf16[256,1536]{1,0:T(8,128)(2,1)S(1)} all-gather(bf16[256,384]{1,0:T(8,128)(2,1)S(1)} %fusion.48), channel_id=1, replica_groups=mesh['segment'=2,'bz'=8,'bx'=4,'mp'=4] {'mp'}, dimensions={1}, use_global_device_ids=true | all-gather | bytes 983040 | tf_op jit(solution)/shard_map/all_gather | solution.py:116
  18.9 0.2 fusion
  19.1 0.0 copy-done.8
  19.2 1.9 fusion.55
  21.1 1.9 fusion.58
  23.0 0.8 pad_maximum_fusion
  23.8 0.0 all-gather.3.cloned.1.call-update
  23.8 0.0 reduce-scatter.7.cloned.1.call-start
  23.8 1.9 fusion.30
  25.7 12.3 %all_gather.22.q_ref = bf16[1024,384]{1,0:T(8,128)(2,1)} all-gather(bf16[256,384]{1,0:T(8,128)(2,1)S(1)} %fusion.30), channel_id=1, replica_groups=mesh['segment'=2,'bz'=8,'bx'=4,'mp'=4] {'bx'}, dimensions={0}, use_global_device_ids=true | all-gather | bytes 983040 | tf_op jit(solution)/shard_map/all_gather | solution.py:75
  38.1 32.2 %all-gather.3.cloned.1.call-done.k_ref.v_ref = bf16[2,2048,384]{2,1,0:T(8,128)(2,1)} async-done(((bf16[2,256,384]{2,1,0:T(8,128)(2,1)}), bf16[2,2048,384]{2,1,0:T(8,128)(2,1)}) %all-gather.3.cloned.1.call-update) | async-done | bytes 3145744 | tf_op jit(solution)/shard_map/all_gather | solution.py:76
  70.3 0.0 copy-start.2
  70.3 1.9 copy-done.2
  72.2 1.1 copy-done.3
  73.3 11.8 %shard_map.100 = f32[1024,512]{1,0:T(8,128)S(1)} custom-call(bf16[1024,384]{1,0:T(8,128)(2,1)S(1)} %copy-done.3, bf16[2,2048,384]{2,1,0:T(8,128)(2,1)S(1)} %copy-done.2, bf16[2,2048,384]{2,1,0:T(8,128)(2,1)S(1)} %copy-done.2), custom_call_target="tpu_custom_call" | custom-call | tf_op jit(solution)/shard_map/pallas_call | solution.py:58
  85.1 1.9 copy.13
  87.0 28.6 %all_to_all.18 = f32[4,256,512]{1,2,0:T(8,128)S(1)} all-to-all(f32[4,256,512]{1,2,0:T(8,128)} %copy.13), channel_id=1, replica_groups=mesh['segment'=2,'bz'=8,'bx'=4,'mp'=4] {'bx'}, dimensions={0} | all-to-all | bytes 4194304 | tf_op jit(solution)/shard_map/all_to_all | solution.py:78
  115.7 0.1 fusion.10
  115.8 0.0 copy-done
  115.9 0.6 convolution_convert_fusion.1
  116.4 0.0 copy-start.6
  116.5 1.2 copy.15
  117.6 0.0 reduce-scatter.7.cloned.1.call-update
  117.6 0.0 copy-start.9
  117.6 0.0 all-gather.5.cloned.1.call-start
  117.7 21.5 %reduce-scatter.7.cloned.1.call-done = bf16[384,256]{1,0:T(8,128)(2,1)} async-done(((bf16[1536,256]{1,0:T(8,128)(2,1)}), bf16[384,256]{1,0:T(8,128)(2,1)}) %reduce-scatter.7.cloned.1.call-update) | async-done | bytes 196624
  139.2 1.1 copy.16
  140.3 0.0 copy-done.6
  140.3 0.1 add_convert_fusion.1
  140.4 4.3 %collective-permute-start = (bf16[256,384]{1,0:T(8,128)(2,1)S(1)}, bf16[256,384]{1,0:T(8,128)(2,1)S(1)}, u32[]{:S(2)}, u32[]{:S(2)}) collective-permute-start(bf16[256,384]{1,0:T(8,128)(2,1)S(1)} %add_convert_fusion.1), channel_id=1, source_target_pairs={{0,128},{1,129},{2,130},{3,131},{4,132},{5,133},{6,134},{7,135},{8... | collective-permute-start | bytes 589832 | tf_op jit(solution)/shard_map/ppermute | solution.py:20
  144.7 4.1 %collective-permute-done = bf16[256,384]{1,0:T(8,128)(2,1)S(1)} collective-permute-done((bf16[256,384]{1,0:T(8,128)(2,1)S(1)}, bf16[256,384]{1,0:T(8,128)(2,1)S(1)}, u32[]{:S(2)}, u32[]{:S(2)}) %collective-permute-start) | collective-permute-done | bytes 196640 | tf_op jit(solution)/shard_map/ppermute | solution.py:20
  148.8 8.7 %all_gather.26 = bf16[256,1536]{1,0:T(8,128)(2,1)S(1)} all-gather(bf16[256,384]{1,0:T(8,128)(2,1)S(1)} %collective-permute-done), channel_id=1, replica_groups=mesh['segment'=2,'bz'=8,'bx'=4,'mp'=4] {'mp'}, dimensions={1}, use_global_device_ids=true | all-gather | bytes 983040 | tf_op jit(solution)/shard_map/all_gather | solution.py:131
  157.5 0.2 fusion.6
  157.8 0.0 copy-done.9
  157.8 1.9 fusion.52
  159.7 1.9 fusion.49
  161.6 0.0 copy-start.10
  161.6 0.8 pad_maximum_fusion.1
  162.4 0.0 all-gather.5.cloned.1.call-update
  162.4 0.0 reduce-scatter.9.cloned.1.call-start
  162.5 8.7 %all_gather.24 = bf16[256,1536]{1,0:T(8,128)(2,1)S(1)} all-gather(bf16[256,384]{1,0:T(8,128)(2,1)S(1)} %add_convert_fusion.1), channel_id=1, replica_groups=mesh['segment'=2,'bz'=8,'bx'=4,'mp'=4] {'mp'}, dimensions={1}, use_global_device_ids=true | all-gather | bytes 983040 | tf_op jit(solution)/shard_map/all_gather | solution.py:128
  171.2 0.2 fusion.3
  171.4 0.0 copy-done.10
  171.4 1.9 fusion.39
  173.3 13.0 %all_gather.25.q_ref = bf16[1024,384]{1,0:T(8,128)(2,1)} all-gather(bf16[256,384]{1,0:T(8,128)(2,1)S(1)} %fusion.39), channel_id=1, replica_groups=mesh['segment'=2,'bz'=8,'bx'=4,'mp'=4] {'bx'}, dimensions={0}, use_global_device_ids=true | all-gather | bytes 983040 | tf_op jit(solution)/shard_map/all_gather | solution.py:75
  186.4 22.5 %all-gather.5.cloned.1.call-done.k_ref.v_ref = bf16[2,2048,384]{2,1,0:T(8,128)(2,1)} async-done(((bf16[2,256,384]{2,1,0:T(8,128)(2,1)}), bf16[2,2048,384]{2,1,0:T(8,128)(2,1)}) %all-gather.5.cloned.1.call-update) | async-done | bytes 3145744 | tf_op jit(solution)/shard_map/all_gather | solution.py:76
  208.8 1.9 copy-done.1
  210.7 1.1 copy-done.4
  211.8 11.8 %shard_map.101 = f32[1024,512]{1,0:T(8,128)S(1)} custom-call(bf16[1024,384]{1,0:T(8,128)(2,1)S(1)} %copy-done.4, bf16[2,2048,384]{2,1,0:T(8,128)(2,1)S(1)} %copy-done.1, bf16[2,2048,384]{2,1,0:T(8,128)(2,1)S(1)} %copy-done.1), custom_call_target="tpu_custom_call" | custom-call | tf_op jit(solution)/shard_map/pallas_call | solution.py:58
  223.6 1.9 copy.14
  225.5 28.6 %all_to_all.19 = f32[4,256,512]{1,2,0:T(8,128)S(1)} all-to-all(f32[4,256,512]{1,2,0:T(8,128)} %copy.14), channel_id=1, replica_groups=mesh['segment'=2,'bz'=8,'bx'=4,'mp'=4] {'bx'}, dimensions={0} | all-to-all | bytes 4194304 | tf_op jit(solution)/shard_map/all_to_all | solution.py:78
  254.2 0.1 fusion.9
  254.4 1.1 copy-done.7
  255.4 0.6 convolution_convert_fusion
  256.0 1.2 copy.17
  257.2 0.0 reduce-scatter.9.cloned.1.call-update
  257.2 21.6 %reduce-scatter.9.cloned.1.call-done = bf16[384,256]{1,0:T(8,128)(2,1)} async-done(((bf16[1536,256]{1,0:T(8,128)(2,1)}), bf16[384,256]{1,0:T(8,128)(2,1)}) %reduce-scatter.9.cloned.1.call-update) | async-done | bytes 196624
  278.8 1.1 copy.18
  279.9 0.7 fusion.68
  (15 shorter events, 0.2 us)
Async XLA Ops:
  6.5 109.3 %copy-start = (bf16[1,384,1536]{2,1,0:T(8,128)(2,1)S(1)}, bf16[1,384,1536]{2,1,0:T(8,128)(2,1)}, u32[]{:S(2)}) copy-start(bf16[1,384,1536]{2,1,0:T(8,128)(2,1)} %param.15) | copy-start | bytes 3538948
  6.5 12.6 %copy-start.8 = (f32[1,1536]{1,0:T(1,128)S(1)}, f32[1,1536]{1,0:T(1,128)}, u32[]{:S(2)}) copy-start(f32[1,1536]{1,0:T(1,128)} %param.13) | copy-start | bytes 18436
  6.5 63.8 %all-gather.3.cloned.1.call-start = ((), (), s32[]{:S(2)}) async-start(), calls=%async_computation.4 | async-start | bytes 3538944 | tf_op jit(solution)/shard_map/all_gather | solution.py:76
  8.0 0.7 copy-start.5
  23.8 115.5 %reduce-scatter.7.cloned.1.call-start = ((), (), s32[]{:S(2)}) async-start(), calls=%async_computation.6 | async-start | bytes 983040
  70.3 1.9 copy-start.2
  72.2 1.1 copy-start.3
  116.4 23.9 %copy-start.6 = (bf16[256,384]{1,0:T(8,128)(2,1)S(1)}, bf16[256,384]{1,0:T(8,128)(2,1)}, u32[]{:S(2)}) copy-start(bf16[256,384]{1,0:T(8,128)(2,1)} %copy-done.5) | copy-start | bytes 589828
  117.6 40.1 %copy-start.9 = (f32[1536]{0:T(1024)S(1)}, f32[1536]{0:T(1024)}, u32[]{:S(2)}) copy-start(f32[1536]{0:T(1024)} %param.17) | copy-start | bytes 18436
  117.6 91.2 %all-gather.5.cloned.1.call-start = ((), (), s32[]{:S(2)}) async-start(), calls=%async_computation.5 | async-start | bytes 3538944 | tf_op jit(solution)/shard_map/all_gather | solution.py:76
  140.4 8.4 %collective-permute-start = (bf16[256,384]{1,0:T(8,128)(2,1)S(1)}, bf16[256,384]{1,0:T(8,128)(2,1)S(1)}, u32[]{:S(2)}, u32[]{:S(2)}) collective-permute-start(bf16[256,384]{1,0:T(8,128)(2,1)S(1)} %add_convert_fusion.1), channel_id=1, source_target_pairs={{0,128},{1,129},{2,130},{3,131},{4,132},{5,133},{6,134},{7,135},{8... | collective-permute-start | bytes 589832 | tf_op jit(solution)/shard_map/ppermute | solution.py:20
  161.6 9.8 %copy-start.10 = (f32[1536]{0:T(1024)S(1)}, f32[1536]{0:T(1024)}, u32[]{:S(2)}) copy-start(f32[1536]{0:T(1024)} %param.16) | copy-start | bytes 18436
  162.4 116.4 %reduce-scatter.9.cloned.1.call-start = ((), (), s32[]{:S(2)}) async-start(), calls=%async_computation.7 | async-start | bytes 983040
  208.8 1.9 copy-start.1
  210.7 1.1 copy-start.4
  254.1 1.3 copy-start.7
Sparse Core Ops, SparseCore 0:
  23.9 46.3 all-gather.2
  117.8 21.4 reduce-scatter.6
  162.5 46.2 all-gather.4
  257.3 21.4 reduce-scatter.8

commit v3 on v2

--- a/solution.py
+++ b/solution.py
@@ -69,11 +69,13 @@
     )(queries, pairs, pairs)
 
 
-def attend(queries, pairs):
+def attend(queries, pairs, riders=None):
     rows, width = queries.shape
     heads = width // HEAD_DIM
     query_block = lax.all_gather(queries, "bx", axis=0, tiled=True)
     key_block = lax.all_gather(pairs, "bz", axis=1, tiled=True)
+    if riders is not None:
+        key_block, riders = lax.optimization_barrier((key_block, riders))
     partial = partial_attend(query_block, key_block)
     parts = lax.all_to_all(partial, "bx", 0, 0, tiled=True)
     parts = parts.reshape(-1, rows, width + STATS)
@@ -84,14 +86,29 @@
     scale = jnp.exp(maxes - top[None])
     total = jnp.sum(sums * scale, axis=0)
     merged = jnp.sum(outs * scale[..., None], axis=0) / total[..., None]
-    return merged.reshape(rows, width).astype(jnp.bfloat16)
+    merged = merged.reshape(rows, width).astype(jnp.bfloat16)
+    return merged if riders is None else (merged, riders)
 
 
-def memory_projection(memory_full, memory_gain, cross_weights):
-    memory_normed = rms_norm(memory_full, memory_gain)
-    return jnp.stack(
-        [project(memory_normed, cross_weights[1]), project(memory_normed, cross_weights[2])]
-    )
+def spread(block_of):
+    count = lax.axis_size("mp")
+    me = lax.axis_index("mp")
+    blocks = [(me, block_of(me))]
+    for step in range(1, count):
+        piece = block_of((me + step) % count)
+        received = lax.ppermute(piece, "mp", [(j, (j + step) % count) for j in range(count)])
+        blocks.append(((me - step + count) % count, received))
+    return blocks
+
+
+def project_out(attended_full, blocks):
+    width = blocks[0][1].shape[0]
+    total = None
+    for source, block in blocks:
+        piece = lax.dynamic_slice_in_dim(attended_full, source * width, width, axis=1)
+        term = jnp.dot(piece, block, preferred_element_type=jnp.float32)
+        total = term if total is None else total + term
+    return total
 
 
 def on_device(
@@ -107,7 +124,13 @@
     cross_out,
 ):
     local_rows = section_input.shape[1]
+    local_width = section_input.shape[2]
     codes_total = code_table.shape[1]
+    me = lax.axis_index("mp")
+    self_blocks = spread(lambda target: self_out[0])
+    cross_blocks = spread(
+        lambda target: lax.dynamic_slice_in_dim(cross_out, target * local_width, local_width, axis=1)
+    )
     matches = (
         row_code[0][:, None] == lax.broadcasted_iota(jnp.int32, (local_rows, codes_total), 1)
     ).astype(jnp.bfloat16)
@@ -119,23 +142,24 @@
     self_pairs = jnp.stack(
         [project(normed, self_weights[0, 1]), project(normed, self_weights[0, 2])]
     )
-    self_attended = attend(self_queries, self_pairs)
-    partial_out = jnp.dot(self_attended, self_out[0], preferred_element_type=jnp.float32)
-    reduced = lax.psum_scatter(
-        partial_out.astype(jnp.bfloat16), "mp", scatter_dimension=1, tiled=True
-    ).astype(jnp.float32)
-    hidden_part = (embedded.astype(jnp.float32) + reduced).astype(jnp.bfloat16)
-    hidden_full = lax.all_gather(hidden_part, "mp", axis=1, tiled=True)
+    self_local, (self_blocks, cross_blocks) = attend(
+        self_queries, self_pairs, (self_blocks, cross_blocks)
+    )
+    self_attended = lax.all_gather(self_local, "mp", axis=1, tiled=True)
+    hidden_full = (
+        embedded_full.astype(jnp.float32) + project_out(self_attended, self_blocks)
+    ).astype(jnp.bfloat16)
+    hidden_part = lax.dynamic_slice_in_dim(hidden_full, me * local_width, local_width, axis=1)
     cross_queries = project(rms_norm(hidden_full, cross_gain), cross_weights[0])
-    arrived = shifted(hidden_part, "segment", 1)
-    memory_full = lax.all_gather(arrived, "mp", axis=1, tiled=True)
-    memory_pairs = memory_projection(memory_full, memory_gain, cross_weights)
-    crossed = attend(cross_queries, memory_pairs)
-    cross_partial = jnp.dot(crossed, cross_out, preferred_element_type=jnp.float32)
-    cross_reduced = lax.psum_scatter(
-        cross_partial.astype(jnp.bfloat16), "mp", scatter_dimension=1, tiled=True
-    ).astype(jnp.float32)
-    decoded = (hidden_part.astype(jnp.float32) + cross_reduced).astype(jnp.bfloat16)
+    memory_normed = rms_norm(hidden_full, memory_gain)
+    memory_pairs = jnp.stack(
+        [project(memory_normed, cross_weights[1]), project(memory_normed, cross_weights[2])]
+    )
+    arrived = shifted(memory_pairs, "segment", 1)
+    crossed = lax.all_gather(attend(cross_queries, arrived), "mp", axis=1, tiled=True)
+    decoded = (
+        hidden_part.astype(jnp.float32) + project_out(crossed, cross_blocks)
+    ).astype(jnp.bfloat16)
     chosen = jnp.where(lax.axis_index("segment") == 0, hidden_part, decoded)
     return chosen[None]
 

time: 288 us -> 287 us (level)
  blocking collectives: 110 us -> 56.1 us
  waiting for transfers between devices: 102 us -> 140 us
  starting transfers between devices: 4.41 us -> 17.6 us
  matrix products: 13.9 us -> 18.5 us
    all_to_all x2 -> x0, blocking collectives: 57.2 us -> none  [attend(): parts = lax.all_to_all(partial, 'bx', 0, 0, tiled=True)]
    ppermute x0 -> x6, waiting for transfers between devices: none -> 49.5 us  [spread(): lax.ppermute(piece, 'mp', [(j, (j + step) % count) for j in range(count)])]
    all_to_all x0 -> x2, waiting for transfers between devices: none -> 48.5 us  [attend(): parts = lax.all_to_all(partial, 'bx', 0, 0, tiled=True)]
    unnamed x6 -> x2, waiting for transfers between devices: 43.2 us -> 0.03 us
    all_gather x2, waiting for transfers between devices: 54.7 us -> 34.2 us  [attend(): key_block = lax.all_gather(pairs, 'bz', axis=1, tiled=True)]
    all_to_all x0 -> x2, starting transfers between devices: none -> 7.57 us  [attend(): parts = lax.all_to_all(partial, 'bx', 0, 0, tiled=True)]
    dot_general x2 -> x8, matrix products: 1.18 us -> 8.5 us  [project_out(): term = jnp.dot(piece, block, preferred_element_type=jnp.float32)]
    ppermute x0 -> x6, starting transfers between devices: none -> 6.17 us  [spread(): lax.ppermute(piece, 'mp', [(j, (j + step) % count) for j in range(count)])]
  transfers between devices with their start and end apart: 5 -> 11, of which waited for: 5 -> 5; matrix products, arithmetic and copies ran while one was open for 1% -> 2% of each run, Pallas kernels for 0% -> 0%
where the time goes in v3:
time: 287 us; the launch traced here: 286 us
  waiting for transfers between devices  140 us (49%)
  blocking collectives  56.1 us (20%)
  Pallas kernels  23.6 us (8%)
  matrix products  18.5 us (6%)
  starting transfers between devices  17.6 us (6%)
  local copies, waits for them, and re-layouts  14.3 us (5%)
  between operations  13.8 us (5%)
    ppermute x6, waiting for transfers between devices, spread(): lax.ppermute(piece, 'mp', [(j, (j + step) % count) for j in range(count)])  49.5 us
    all_to_all x2, waiting for transfers between devices, attend(): parts = lax.all_to_all(partial, 'bx', 0, 0, tiled=True)  48.5 us
    all_gather x2, waiting for transfers between devices, attend(): key_block = lax.all_gather(pairs, 'bz', axis=1, tiled=True)  34.2 us
    pallas_call x2, Pallas kernels, partial_attend(): pl.pallas_call(partial_kernel, grid=(rows // TILE,), in_specs=[pl.BlockSp...  23.6 us
    all_gather x2, blocking collectives, attend(): query_block = lax.all_gather(queries, 'bx', axis=0, tiled=True)  22.5 us
    all_gather x1, blocking collectives, on_device(): self_attended = lax.all_gather(self_local, 'mp', axis=1, tiled=True)  12.3 us
    all_gather x1, blocking collectives, on_device(): lax.all_gather(attend(cross_queries, arrived), 'mp', axis=1, tiled=True)  10.9 us
    all_gather x1, blocking collectives, on_device(): embedded_full = lax.all_gather(embedded, 'mp', axis=1, tiled=True)  10.3 us
  transfers between devices with their start and end apart: 11, of which 5 were waited for; matrix products, arithmetic and copies ran while one was open for 2% of the time, Pallas kernels for 0%

profile of v3, /device:TPU:1, one launch (start us, length us, event | category | flops | bytes accessed | tf_op | source)
XLA Modules:
  0.0 285.9 jit_solution(2706208886554460808)
XLA Ops:
  6.5 0.9 copy-done
  7.5 1.2 fusion.54
  8.7 10.3 %all_gather.21 = bf16[256,1536]{1,0:T(8,128)(2,1)S(1)} all-gather(bf16[256,384]{1,0:T(8,128)(2,1)S(1)} %fusion.54), channel_id=1, replica_groups=mesh['segment'=2,'bz'=8,'bx'=4,'mp'=4] {'mp'}, dimensions={1}, use_global_device_ids=true | all-gather | bytes 983040 | tf_op jit(solution)/shard_map/all_gather | solution.py:139
  19.0 0.2 fusion.9
  19.2 1.9 fusion.63
  21.1 1.9 fusion.66
  23.0 0.8 pad_maximum_fusion
  23.8 0.0 all-gather.3.cloned.1.call-update
  23.8 1.7 collective-permute-start
  25.6 0.1 collective-permute-start.1
  25.7 0.7 collective-permute-start.2
  26.3 2.1 constant_dynamic-slice_fusion
  28.4 1.1 collective-permute-start.3
  29.5 1.4 collective-permute-start.4
  30.9 1.9 fusion.35
  32.8 49.5 %collective-permute-done.3 = bf16[384,384]{1,0:T(8,128)(2,1)S(1)} collective-permute-done((bf16[384,384]{1,0:T(8,128)(2,1)S(1)}, bf16[384,384]{1,0:T(8,128)(2,1)S(1)}, u32[]{:S(2)}, u32[]{:S(2)}) %collective-permute-start.3) | collective-permute-done | bytes 294944 | tf_op jit(solution)/shard_map/ppermute | solution.py:99
  82.3 1.2 collective-permute-start.5
  83.5 11.7 %all_gather.22.q_ref = bf16[1024,384]{1,0:T(8,128)(2,1)S(1)} all-gather(bf16[256,384]{1,0:T(8,128)(2,1)S(1)} %fusion.35), channel_id=1, replica_groups=mesh['segment'=2,'bz'=8,'bx'=4,'mp'=4] {'bx'}, dimensions={0}, use_global_device_ids=true | all-gather | bytes 983040 | tf_op jit(solution)/shard_map/all_gather | solution.py:75
  95.2 0.0 collective-permute-done.4
  95.2 0.0 collective-permute-done.5
  95.2 0.0 copy-start.16
  95.2 0.0 collective-permute-done
  95.2 0.0 collective-permute-done.1
  95.2 0.7 copy-done.14
  95.9 0.2 copy-done.16
  96.1 0.0 collective-permute-done.2
  96.1 0.4 copy-done.6
  96.5 0.6 copy-done.8
  97.1 1.9 copy-done.1
  99.0 11.8 %shard_map.100 = f32[1024,512]{1,0:T(8,128)S(1)} custom-call(bf16[1024,384]{1,0:T(8,128)(2,1)S(1)} %all_gather.22.q_ref, bf16[2,2048,384]{2,1,0:T(8,128)(2,1)S(1)} %copy-done.1, bf16[2,2048,384]{2,1,0:T(8,128)(2,1)S(1)} %copy-done.1), custom_call_target="tpu_custom_call" | custom-call | tf_op jit(solution)/shard_map/pallas_call | solution.py:58
  110.8 1.8 copy.11
  112.6 3.6 %all-to-all-start = ((f32[4,256,512]{1,2,0:T(8,128)}), f32[4,256,512]{1,2,0:T(8,128)S(1)}, u32[]{:S(2)}, u32[]{:S(2)}) async-start(f32[4,256,512]{1,2,0:T(8,128)} %copy.11), calls=%async_computation | async-start | bytes 4194304 | tf_op jit(solution)/shard_map/all_to_all | solution.py:80
  116.3 0.0 all-gather.5.cloned.1.call-start
  116.3 23.6 %all-to-all-done = f32[4,256,512]{1,2,0:T(8,128)S(1)} async-done(((f32[4,256,512]{1,2,0:T(8,128)}), f32[4,256,512]{1,2,0:T(8,128)S(1)}, u32[]{:S(2)}, u32[]{:S(2)}) %all-to-all-start) | async-done | bytes 2097184 | tf_op jit(solution)/shard_map/all_to_all | solution.py:80
  140.0 0.1 fusion.13
  140.2 12.3 %all_gather.24 = bf16[256,1536]{0,1:T(8,128)(2,1)S(1)} all-gather(bf16[256,384]{0,1:T(8,128)(2,1)S(1)} %fusion.73), channel_id=1, replica_groups=mesh['segment'=2,'bz'=8,'bx'=4,'mp'=4] {'mp'}, dimensions={1}, use_global_device_ids=true | all-gather | bytes 983040 | tf_op jit(solution)/shard_map/all_gather | solution.py:148
  152.5 2.0 fusion.84
  154.5 0.6 fusion.86
  155.1 0.7 copy-done.7
  155.8 0.6 fusion.88
  156.4 0.5 copy-done.4
  156.9 2.4 fusion.8
  159.3 0.6 fusion.57
  160.0 0.0 copy-start.21
  160.0 0.6 fusion.60
  160.7 3.8 %collective-permute-start.6 = (bf16[2,256,384]{2,1,0:T(8,128)(2,1)S(1)}, bf16[2,256,384]{2,1,0:T(8,128)(2,1)S(1)}, u32[]{:S(2)}, u32[]{:S(2)}) collective-permute-start(bf16[2,256,384]{2,1,0:T(8,128)(2,1)S(1)} %pad_maximum_fusion.1), channel_id=1, source_target_pairs={{0,128},{1,129},{2,130},{3,131},{4,132},{5,133},{6,134},{7,135},{8... | collective-permute-start | bytes 1179656 | tf_op jit(solution)/shard_map/ppermute | solution.py:20
  164.5 8.3 %collective-permute-done.6 = bf16[2,256,384]{2,1,0:T(8,128)(2,1)S(1)} collective-permute-done((bf16[2,256,384]{2,1,0:T(8,128)(2,1)S(1)}, bf16[2,256,384]{2,1,0:T(8,128)(2,1)S(1)}, u32[]{:S(2)}, u32[]{:S(2)}) %collective-permute-start.6) | collective-permute-done | bytes 393248 | tf_op jit(solution)/shard_map/ppermute | solution.py:20
  172.8 0.7 copy-done.11
  173.5 0.0 all-gather.5.cloned.1.call-update
  173.5 1.9 fusion.44
  175.4 10.8 %all_gather.25.q_ref = bf16[1024,384]{1,0:T(8,128)(2,1)S(1)} all-gather(bf16[256,384]{1,0:T(8,128)(2,1)S(1)} %fusion.44), channel_id=1, replica_groups=mesh['segment'=2,'bz'=8,'bx'=4,'mp'=4] {'bx'}, dimensions={0}, use_global_device_ids=true | all-gather | bytes 983040 | tf_op jit(solution)/shard_map/all_gather | solution.py:75
  186.3 34.1 %all-gather.5.cloned.1.call-done.k_ref.v_ref = bf16[2,2048,384]{2,1,0:T(8,128)(2,1)} async-done(((bf16[2,256,384]{2,1,0:T(8,128)(2,1)}), bf16[2,2048,384]{2,1,0:T(8,128)(2,1)}) %all-gather.5.cloned.1.call-update) | async-done | bytes 3145744 | tf_op jit(solution)/shard_map/all_gather | solution.py:76
  220.4 1.9 copy-done.2
  222.3 11.8 %shard_map.101 = f32[1024,512]{1,0:T(8,128)S(1)} custom-call(bf16[1024,384]{1,0:T(8,128)(2,1)S(1)} %all_gather.25.q_ref, bf16[2,2048,384]{2,1,0:T(8,128)(2,1)S(1)} %copy-done.2, bf16[2,2048,384]{2,1,0:T(8,128)(2,1)S(1)} %copy-done.2), custom_call_target="tpu_custom_call" | custom-call | tf_op jit(solution)/shard_map/pallas_call | solution.py:58
  234.1 1.8 copy.12
  236.0 4.0 %all-to-all-start.1 = ((f32[4,256,512]{1,2,0:T(8,128)}), f32[4,256,512]{1,2,0:T(8,128)S(1)}, u32[]{:S(2)}, u32[]{:S(2)}) async-start(f32[4,256,512]{1,2,0:T(8,128)} %copy.12), calls=%async_computation.1 | async-start | bytes 4194304 | tf_op jit(solution)/shard_map/all_to_all | solution.py:80
  239.9 24.9 %all-to-all-done.1 = f32[4,256,512]{1,2,0:T(8,128)S(1)} async-done(((f32[4,256,512]{1,2,0:T(8,128)}), f32[4,256,512]{1,2,0:T(8,128)S(1)}, u32[]{:S(2)}, u32[]{:S(2)}) %all-to-all-start.1) | async-done | bytes 2097184 | tf_op jit(solution)/shard_map/all_to_all | solution.py:80
  264.9 0.1 fusion.12
  265.0 0.0 copy-start.15
  265.1 10.9 %all_gather.27 = bf16[256,1536]{0,1:T(8,128)(2,1)S(1)} all-gather(bf16[256,384]{0,1:T(8,128)(2,1)S(1)} %fusion.72), channel_id=1, replica_groups=mesh['segment'=2,'bz'=8,'bx'=4,'mp'=4] {'mp'}, dimensions={1}, use_global_device_ids=true | all-gather | bytes 983040 | tf_op jit(solution)/shard_map/all_gather | solution.py:159
  276.0 0.3 fusion.77
  276.4 0.3 fusion.79
  276.7 0.3 fusion.81
  277.0 2.0 fusion.56
  (43 shorter events, 0.3 us)
Async XLA Ops:
  6.5 0.9 copy-start
  6.5 12.7 %copy-start.18 = (f32[1,1536]{1,0:T(1,128)S(1)}, f32[1,1536]{1,0:T(1,128)}, u32[]{:S(2)}) copy-start(f32[1,1536]{1,0:T(1,128)} %param.13) | copy-start | bytes 18436
  6.5 89.5 %all-gather.3.cloned.1.call-start = ((), (), s32[]{:S(2)}) async-start(), calls=%async_computation.2 | async-start | bytes 3538944 | tf_op jit(solution)/shard_map/all_gather | solution.py:76
  19.0 12.0 %copy-start.3 = (bf16[256,1536]{1,0:T(8,128)(2,1)}, bf16[256,1536]{1,0:T(8,128)(2,1)S(1)}, u32[]{:S(2)}) copy-start(bf16[256,1536]{1,0:T(8,128)(2,1)S(1)} %all_gather.21) | copy-start | bytes 2359300
  23.8 71.4 %collective-permute-start = (bf16[384,1536]{1,0:T(8,128)(2,1)}, bf16[384,1536]{1,0:T(8,128)(2,1)S(1)}, u32[]{:S(2)}, u32[]{:S(2)}) collective-permute-start(bf16[384,1536]{1,0:T(8,128)(2,1)} %bitcast.8), channel_id=1, source_target_pairs={{0,1},{1,2},{2,3},{3,0},{4,5},{5,6},{6,7},{7,4},{8,9},{9,10},{10,1... | collective-permute-start | bytes 3538952 | tf_op jit(solution)/shard_map/ppermute | solution.py:99
  25.6 69.6 %collective-permute-start.1 = (bf16[384,1536]{1,0:T(8,128)(2,1)}, bf16[384,1536]{1,0:T(8,128)(2,1)S(1)}, u32[]{:S(2)}, u32[]{:S(2)}) collective-permute-start(bf16[384,1536]{1,0:T(8,128)(2,1)} %bitcast.8), channel_id=1, source_target_pairs={{0,2},{1,3},{2,0},{3,1},{4,6},{5,7},{6,4},{7,5},{8,10},{9,11},{10,... | collective-permute-start | bytes 3538952 | tf_op jit(solution)/shard_map/ppermute | solution.py:99
  25.7 70.4 %collective-permute-start.2 = (bf16[384,1536]{1,0:T(8,128)(2,1)}, bf16[384,1536]{1,0:T(8,128)(2,1)}, u32[]{:S(2)}, u32[]{:S(2)}) collective-permute-start(bf16[384,1536]{1,0:T(8,128)(2,1)} %bitcast.8), channel_id=1, source_target_pairs={{0,3},{1,0},{2,1},{3,2},{4,7},{5,4},{6,5},{7,6},{8,11},{9,8},{10,9... | collective-permute-start | bytes 3538952 | tf_op jit(solution)/shard_map/ppermute | solution.py:99
  28.4 53.8 %collective-permute-start.3 = (bf16[384,384]{1,0:T(8,128)(2,1)S(1)}, bf16[384,384]{1,0:T(8,128)(2,1)S(1)}, u32[]{:S(2)}, u32[]{:S(2)}) collective-permute-start(bf16[384,384]{1,0:T(8,128)(2,1)S(1)} %get-tuple-element.44), channel_id=1, source_target_pairs={{0,1},{1,2},{2,3},{3,0},{4,5},{5,6},{6,7},{7,4},{8,9},{9,10},{10,1... | collective-permute-start | bytes 884744 | tf_op jit(solution)/shard_map/ppermute | solution.py:99
  29.5 65.7 %collective-permute-start.4 = (bf16[384,384]{1,0:T(8,128)(2,1)S(1)}, bf16[384,384]{1,0:T(8,128)(2,1)S(1)}, u32[]{:S(2)}, u32[]{:S(2)}) collective-permute-start(bf16[384,384]{1,0:T(8,128)(2,1)S(1)} %get-tuple-element.46), channel_id=1, source_target_pairs={{0,2},{1,3},{2,0},{3,1},{4,6},{5,7},{6,4},{7,5},{8,10},{9,11},{10,... | collective-permute-start | bytes 884744 | tf_op jit(solution)/shard_map/ppermute | solution.py:99
  82.3 13.0 %copy-start.12 = (bf16[384,384]{1,0:T(8,128)(2,1)}, bf16[384,384]{1,0:T(8,128)(2,1)S(1)}, u32[]{:S(2)}) copy-start(bf16[384,384]{1,0:T(8,128)(2,1)S(1)} %collective-permute-done.3) | copy-start | bytes 884740
  82.3 12.9 %collective-permute-start.5 = (bf16[384,384]{1,0:T(8,128)(2,1)S(1)}, bf16[384,384]{1,0:T(8,128)(2,1)S(1)}, u32[]{:S(2)}, u32[]{:S(2)}) collective-permute-start(bf16[384,384]{1,0:T(8,128)(2,1)S(1)} %get-tuple-element.43), channel_id=1, source_target_pairs={{0,3},{1,0},{2,1},{3,2},{4,7},{5,4},{6,5},{7,6},{8,11},{9,8},{10,9... | collective-permute-start | bytes 884744 | tf_op jit(solution)/shard_map/ppermute | solution.py:99
  95.2 0.7 copy-start.14
  95.2 0.9 copy-start.16
  95.2 1.3 copy-start.6
  96.1 1.0 copy-start.8
  97.1 1.9 copy-start.1
  112.6 27.3 %all-to-all-start = ((f32[4,256,512]{1,2,0:T(8,128)}), f32[4,256,512]{1,2,0:T(8,128)S(1)}, u32[]{:S(2)}, u32[]{:S(2)}) async-start(f32[4,256,512]{1,2,0:T(8,128)} %copy.11), calls=%async_computation | async-start | bytes 4194304 | tf_op jit(solution)/shard_map/all_to_all | solution.py:80
  116.3 104.2 %all-gather.5.cloned.1.call-start = ((), (), s32[]{:S(2)}) async-start(), calls=%async_computation.3 | async-start | bytes 3538944 | tf_op jit(solution)/shard_map/all_gather | solution.py:76
  152.5 2.0 copy-start.9
  154.5 1.3 copy-start.7
  155.8 1.1 copy-start.4
  156.9 2.4 copy-start.19
  156.9 2.4 copy-start.20
  159.3 14.2 %copy-start.5 = (bf16[256,1536]{1,0:T(8,128)(2,1)}, bf16[256,1536]{1,0:T(8,128)(2,1)S(1)}, u32[]{:S(2)}) copy-start(bf16[256,1536]{1,0:T(8,128)(2,1)S(1)} %get-tuple-element.48) | copy-start | bytes 2359300
  160.0 13.6 %copy-start.21 = (f32[1536]{0:T(1024)S(1)}, f32[1536]{0:T(1024)}, u32[]{:S(2)}) copy-start(f32[1536]{0:T(1024)} %param.16) | copy-start | bytes 18436
  160.7 12.1 %collective-permute-start.6 = (bf16[2,256,384]{2,1,0:T(8,128)(2,1)S(1)}, bf16[2,256,384]{2,1,0:T(8,128)(2,1)S(1)}, u32[]{:S(2)}, u32[]{:S(2)}) collective-permute-start(bf16[2,256,384]{2,1,0:T(8,128)(2,1)S(1)} %pad_maximum_fusion.1), channel_id=1, source_target_pairs={{0,128},{1,129},{2,130},{3,131},{4,132},{5,133},{6,134},{7,135},{8... | collective-permute-start | bytes 1179656 | tf_op jit(solution)/shard_map/ppermute | solution.py:20
  172.8 0.7 copy-start.11
  220.4 1.9 copy-start.2
  236.0 28.9 %all-to-all-start.1 = ((f32[4,256,512]{1,2,0:T(8,128)}), f32[4,256,512]{1,2,0:T(8,128)S(1)}, u32[]{:S(2)}, u32[]{:S(2)}) async-start(f32[4,256,512]{1,2,0:T(8,128)} %copy.12), calls=%async_computation.1 | async-start | bytes 4194304 | tf_op jit(solution)/shard_map/all_to_all | solution.py:80
  264.9 11.1 %copy-start.17 = (bf16[384,384]{1,0:T(8,128)(2,1)S(1)}, bf16[384,384]{1,0:T(8,128)(2,1)}, u32[]{:S(2)}) copy-start(bf16[384,384]{1,0:T(8,128)(2,1)} %copy-done.16) | copy-start | bytes 884740
  265.0 11.3 %copy-start.15 = (bf16[384,384]{1,0:T(8,128)(2,1)S(1)}, bf16[384,384]{1,0:T(8,128)(2,1)}, u32[]{:S(2)}) copy-start(bf16[384,384]{1,0:T(8,128)(2,1)} %copy-done.14) | copy-start | bytes 884740
  265.0 11.7 %copy-start.13 = (bf16[384,384]{1,0:T(8,128)(2,1)S(1)}, bf16[384,384]{1,0:T(8,128)(2,1)}, u32[]{:S(2)}) copy-start(bf16[384,384]{1,0:T(8,128)(2,1)} %copy-done.12) | copy-start | bytes 884740
  276.0 1.0 copy-start.10
Sparse Core Ops, SparseCore 0:
  24.0 46.3 all-gather.2
  173.6 46.7 all-gather.4

commit v4 on v3

--- a/solution.py
+++ b/solution.py
@@ -12,6 +12,7 @@
 X_SIZE = 4
 TILE = 256
 STATS = 128
+STAT_ROWS = 8
 
 
 def shifted(value, axis, steps):
@@ -30,7 +31,7 @@
     return jnp.dot(normed, weight, preferred_element_type=jnp.float32).astype(jnp.bfloat16)
 
 
-def partial_kernel(q_ref, k_ref, v_ref, o_ref):
+def partial_kernel(q_ref, k_ref, v_ref, o_ref, s_ref):
     heads = q_ref.shape[1] // HEAD_DIM
     rows = q_ref.shape[0]
     lane = lax.broadcasted_iota(jnp.int32, (rows, STATS), 1)
@@ -46,10 +47,10 @@
         summed = jnp.sum(weights, axis=1, keepdims=True)
         o_ref[:, cols] = jnp.dot(
             weights.astype(jnp.bfloat16), v_ref[:, cols], preferred_element_type=jnp.float32
-        )
+        ).astype(o_ref.dtype)
         stats = jnp.where(lane == h, largest, stats)
         stats = jnp.where(lane == heads + h, summed, stats)
-    o_ref[:, heads * HEAD_DIM:] = stats
+    s_ref[...] = jnp.transpose(stats)[: s_ref.shape[0]]
 
 
 def partial_attend(queries, pairs):
@@ -63,8 +64,14 @@
             pl.BlockSpec((None, keys, width), lambda i: (0, 0, 0)),
             pl.BlockSpec((None, keys, width), lambda i: (1, 0, 0)),
         ],
-        out_specs=pl.BlockSpec((TILE, width + STATS), lambda i: (i, 0)),
-        out_shape=jax.ShapeDtypeStruct((rows, width + STATS), jnp.float32),
+        out_specs=[
+            pl.BlockSpec((TILE, width), lambda i: (i, 0)),
+            pl.BlockSpec((STAT_ROWS, TILE), lambda i: (0, i)),
+        ],
+        out_shape=[
+            jax.ShapeDtypeStruct((rows, width), jnp.bfloat16),
+            jax.ShapeDtypeStruct((STAT_ROWS, rows), jnp.float32),
+        ],
         compiler_params=pltpu.CompilerParams(vmem_limit_bytes=48 * 1024 * 1024),
     )(queries, pairs, pairs)
 
@@ -74,20 +81,21 @@
     heads = width // HEAD_DIM
     query_block = lax.all_gather(queries, "bx", axis=0, tiled=True)
     key_block = lax.all_gather(pairs, "bz", axis=1, tiled=True)
-    if riders is not None:
-        key_block, riders = lax.optimization_barrier((key_block, riders))
-    partial = partial_attend(query_block, key_block)
-    parts = lax.all_to_all(partial, "bx", 0, 0, tiled=True)
-    parts = parts.reshape(-1, rows, width + STATS)
-    outs = parts[:, :, :width].reshape(-1, rows, heads, HEAD_DIM)
-    maxes = parts[:, :, width:width + heads]
-    sums = parts[:, :, width + heads:width + 2 * heads]
+    partial, stats = partial_attend(query_block, key_block)
+    outs = lax.all_to_all(partial, "bx", 0, 0, tiled=True)
+    stats = lax.all_to_all(stats, "bx", 1, 1, tiled=True)
+    outs = outs.reshape(-1, rows, heads, HEAD_DIM).astype(jnp.float32)
+    stats = stats.reshape(STAT_ROWS, -1, rows)
+    maxes = jnp.transpose(stats[:heads], (1, 2, 0))
+    sums = jnp.transpose(stats[heads:2 * heads], (1, 2, 0))
     top = jnp.max(maxes, axis=0)
     scale = jnp.exp(maxes - top[None])
     total = jnp.sum(sums * scale, axis=0)
     merged = jnp.sum(outs * scale[..., None], axis=0) / total[..., None]
     merged = merged.reshape(rows, width).astype(jnp.bfloat16)
-    return merged if riders is None else (merged, riders)
+    if riders is None:
+        return merged
+    return lax.optimization_barrier((merged, riders))
 
 
 def spread(block_of):

time: 287 us -> 247 us (0.86)
  waiting for transfers between devices: 140 us -> 89.5 us
  starting transfers between devices: 17.6 us -> 27.1 us
  matrix products: 18.5 us -> 24.5 us
  local copies, waits for them, and re-layouts: 14.3 us -> 9.03 us
    ppermute x6, waiting for transfers between devices: 49.5 us -> 2.73 us  [spread(): lax.ppermute(piece, 'mp', [(j, (j + step) % count) for j in range(count)])]
    all_to_all x2 -> x4, waiting for transfers between devices: 48.5 us -> 20.6 us  [the longest x2 14.3 us: attend(): outs = lax.all_to_all(partial, 'bx', 0, 0, tiled=True)]
    all_gather x2, waiting for transfers between devices: 34.2 us -> 57.9 us  [attend(): key_block = lax.all_gather(pairs, 'bz', axis=1, tiled=True)]
    all_to_all x2 -> x4, starting transfers between devices: 7.57 us -> 14.9 us  [the longest x2 7.93 us: attend(): stats = lax.all_to_all(stats, 'bx', 1, 1, tiled=True)]
    dot_general x8, matrix products: 8.5 us -> 14.1 us  [project_out(): term = jnp.dot(piece, block, preferred_element_type=jnp.float32)]
    unnamed x44 -> x34, local copies, waits for them, and re-layouts: 8.57 us -> 5.73 us
  transfers between devices with their start and end apart: 11 -> 13, of which waited for: 5 -> 8; matrix products, arithmetic and copies ran while one was open for 2% -> 3% of each run, Pallas kernels for 0% -> 5%
where the time goes in v4:
time: 247 us; the launch traced here: 246 us
  waiting for transfers between devices  89.5 us (36%)
  blocking collectives  56.5 us (23%)
  starting transfers between devices  27.1 us (11%)
  matrix products  24.5 us (10%)
  Pallas kernels  24.5 us (10%)
  between operations  13.7 us (6%)
  local copies, waits for them, and re-layouts  9.03 us (4%)
    all_gather x2, waiting for transfers between devices, attend(): key_block = lax.all_gather(pairs, 'bz', axis=1, tiled=True)  57.9 us
    pallas_call x2, Pallas kernels, partial_attend(): pl.pallas_call(partial_kernel, grid=(rows // TILE,), in_specs=[pl.BlockSp...  24.5 us
    all_gather x2, blocking collectives, attend(): query_block = lax.all_gather(queries, 'bx', axis=0, tiled=True)  24.1 us
    all_to_all x2, waiting for transfers between devices, attend(): outs = lax.all_to_all(partial, 'bx', 0, 0, tiled=True)  14.3 us
    dot_general x8, matrix products, project_out(): term = jnp.dot(piece, block, preferred_element_type=jnp.float32)  14.1 us
    all_gather x1, blocking collectives, on_device(): lax.all_gather(attend(cross_queries, arrived), 'mp', axis=1, tiled=True)  12.4 us
    all_gather x1, blocking collectives, on_device(): embedded_full = lax.all_gather(embedded, 'mp', axis=1, tiled=True)  10.3 us
    all_gather x1, blocking collectives, on_device(): self_attended = lax.all_gather(self_local, 'mp', axis=1, tiled=True)  9.75 us
  transfers between devices with their start and end apart: 13, of which 8 were waited for; matrix products, arithmetic and copies ran while one was open for 3% of the time, Pallas kernels for 5%

profile of v4, /device:TPU:1, one launch (start us, length us, event | category | flops | bytes accessed | tf_op | source)
XLA Modules:
  0.0 246.5 jit_solution(13922676378483870525)
XLA Ops:
  6.5 0.9 copy-done
  7.5 1.2 fusion.54
  8.7 10.3 %all_gather.21 = bf16[256,1536]{1,0:T(8,128)(2,1)S(1)} all-gather(bf16[256,384]{1,0:T(8,128)(2,1)S(1)} %fusion.54), channel_id=1, replica_groups=mesh['segment'=2,'bz'=8,'bx'=4,'mp'=4] {'mp'}, dimensions={1}, use_global_device_ids=true | all-gather | bytes 983040 | tf_op jit(solution)/shard_map/all_gather | solution.py:147
  19.0 0.2 fusion.9
  19.2 1.9 fusion.63
  21.1 0.0 copy-start.4
  21.1 2.0 fusion.66
  23.1 0.8 pad_maximum_fusion
  24.0 0.0 all-gather.3.cloned.1.call-update
  24.0 1.7 collective-permute-start
  25.7 0.1 collective-permute-start.1
  25.8 0.7 collective-permute-start.2
  26.5 0.9 constant_dynamic-slice_fusion
  27.4 1.1 collective-permute-start.3
  28.5 1.9 fusion.35
  30.4 12.2 %all_gather.22.q_ref = bf16[1024,384]{1,0:T(8,128)(2,1)S(1)} all-gather(bf16[256,384]{1,0:T(8,128)(2,1)S(1)} %fusion.35), channel_id=1, replica_groups=mesh['segment'=2,'bz'=8,'bx'=4,'mp'=4] {'bx'}, dimensions={0}, use_global_device_ids=true | all-gather | bytes 983040 | tf_op jit(solution)/shard_map/all_gather | solution.py:82
  42.6 27.9 %all-gather.3.cloned.1.call-done.k_ref.v_ref = bf16[2,2048,384]{2,1,0:T(8,128)(2,1)} async-done(((bf16[2,256,384]{2,1,0:T(8,128)(2,1)}), bf16[2,2048,384]{2,1,0:T(8,128)(2,1)}) %all-gather.3.cloned.1.call-update) | async-done | bytes 3145744 | tf_op jit(solution)/shard_map/all_gather | solution.py:83
  70.5 1.9 copy-done.1
  72.4 12.2 %shard_map.100 = (bf16[1024,384]{1,0:T(8,128)(2,1)S(1)}, f32[8,1024]{1,0:T(8,128)}) custom-call(bf16[1024,384]{1,0:T(8,128)(2,1)S(1)} %all_gather.22.q_ref, bf16[2,2048,384]{2,1,0:T(8,128)(2,1)S(1)} %copy-done.1, bf16[2,2048,384]{2,1,0:T(8,128)(2,1)S(1)} %copy-done.1), custom_call_target="tpu_custom_call" | custom-call | tf_op jit(solution)/shard_map/pallas_call | solution.py:59
  84.6 4.0 %all-to-all-start.1 = ((f32[8,4,256]{2,0,1:T(8,128)}), f32[8,4,256]{2,0,1:T(8,128)S(1)}, u32[]{:S(2)}, u32[]{:S(2)}) async-start(f32[8,4,256]{2,0,1:T(8,128)} %bitcast.9), calls=%async_computation.1 | async-start | bytes 65536 | tf_op jit(solution)/shard_map/all_to_all | solution.py:86
  88.6 1.2 copy.13
  89.8 3.1 %all-to-all-done.1 = f32[8,4,256]{2,0,1:T(8,128)S(1)} async-done(((f32[8,4,256]{2,0,1:T(8,128)}), f32[8,4,256]{2,0,1:T(8,128)S(1)}, u32[]{:S(2)}, u32[]{:S(2)}) %all-to-all-start.1) | async-done | bytes 32800 | tf_op jit(solution)/shard_map/all_to_all | solution.py:86
  92.9 3.5 %all-to-all-start = ((bf16[4,256,384]{1,2,0:T(8,128)(2,1)}), bf16[4,256,384]{1,2,0:T(8,128)(2,1)S(1)}, u32[]{:S(2)}, u32[]{:S(2)}) async-start(bf16[4,256,384]{1,2,0:T(8,128)(2,1)} %copy.13), calls=%async_computation | async-start | bytes 1572864 | tf_op jit(solution)/shard_map/all_to_all | solution.py:85
  96.4 0.0 all-gather.5.cloned.1.call-start
  96.4 1.3 collective-permute-start.4
  97.7 0.0 collective-permute-done.3
  97.7 2.9 %collective-permute-start.5 = (bf16[384,384]{1,0:T(8,128)(2,1)S(1)}, bf16[384,384]{1,0:T(8,128)(2,1)S(1)}, u32[]{:S(2)}, u32[]{:S(2)}) collective-permute-start(bf16[384,384]{1,0:T(8,128)(2,1)S(1)} %get-tuple-element.51), channel_id=1, source_target_pairs={{0,3},{1,0},{2,1},{3,2},{4,7},{5,4},{6,5},{7,6},{8,11},{9,8},{10,9... | collective-permute-start | bytes 884744 | tf_op jit(solution)/shard_map/ppermute | solution.py:107
  100.7 5.0 %all-to-all-done = bf16[4,256,384]{1,2,0:T(8,128)(2,1)S(1)} async-done(((bf16[4,256,384]{1,2,0:T(8,128)(2,1)}), bf16[4,256,384]{1,2,0:T(8,128)(2,1)S(1)}, u32[]{:S(2)}, u32[]{:S(2)}) %all-to-all-start) | async-done | bytes 786464 | tf_op jit(solution)/shard_map/all_to_all | solution.py:85
  105.8 0.2 fusion.13
  106.0 0.0 collective-permute-done.4
  106.0 2.7 %collective-permute-done.5 = bf16[384,384]{1,0:T(8,128)(2,1)S(1)} collective-permute-done((bf16[384,384]{1,0:T(8,128)(2,1)S(1)}, bf16[384,384]{1,0:T(8,128)(2,1)S(1)}, u32[]{:S(2)}, u32[]{:S(2)}) %collective-permute-start.5) | collective-permute-done | bytes 294944 | tf_op jit(solution)/shard_map/ppermute | solution.py:107
  108.7 0.0 collective-permute-done
  108.7 0.0 collective-permute-done.1
  108.7 0.0 collective-permute-done.2
  108.8 9.8 %all_gather.24 = bf16[256,1536]{0,1:T(8,128)(2,1)S(1)} all-gather(bf16[256,384]{0,1:T(8,128)(2,1)S(1)} %fusion.73), channel_id=1, replica_groups=mesh['segment'=2,'bz'=8,'bx'=4,'mp'=4] {'mp'}, dimensions={1}, use_global_device_ids=true | all-gather | bytes 983040 | tf_op jit(solution)/shard_map/all_gather | solution.py:156
  118.5 1.9 fusion.84
  120.4 3.0 %fusion.86 = f32[256,1536]{1,0:T(8,128)} fusion(bf16[384,1536]{1,0:T(8,128)(2,1)} %collective-permute-done.1, bf16[256,1536]{0,1:T(8,128)(2,1)S(1)} %all_gather.24, s32[]{:T(128)S(6)} %select_n.82), kind=kOutput, calls=%fused_computation.77 | convolution fusion | flops 301989888 | bytes 2949124 | tf_op jit(solution)/shard_map/dot_general | solution.py:117
  123.4 3.1 %fusion.88 = f32[256,1536]{1,0:T(8,128)} fusion(bf16[384,1536]{1,0:T(8,128)(2,1)} %collective-permute-done, bf16[256,1536]{0,1:T(8,128)(2,1)S(1)} %all_gather.24, s32[]{:T(128)S(6)} %select_n.81), kind=kOutput, calls=%fused_computation.79 | convolution fusion | flops 301989888 | bytes 2949124 | tf_op jit(solution)/shard_map/dot_general | solution.py:117
  126.5 3.2 %fusion.8 = (f32[256]{0:T(256)S(1)}, bf16[256,1536]{1,0:T(8,128)(2,1)S(1)}) fusion(f32[256,1536]{1,0:T(8,128)S(1)} %fusion.84, f32[256,1536]{1,0:T(8,128)} %fusion.86, f32[256,1536]{1,0:T(8,128)} %fusion.88, bf16[384,1536]{1,0:T(8,128)(2,1)} %bitcast.14, bf16[256,1536]{0,1:T(8,128)(2,1)S(1)} %all_gather.24, s32[]{:T(128)S(6)} %select_n.80, ...), kind=kOutput, calls=%fused_computation.13 | convolution fusion | flops 305528576 | bytes 7668740 | tf_op jit(solution)/shard_map/dot_general | solution.py:117
  129.7 0.0 copy-done.14
  129.8 0.6 fusion.57
  130.4 0.2 copy-done.3
  130.6 0.6 fusion.60
  131.3 4.4 %collective-permute-start.6 = (bf16[2,256,384]{2,1,0:T(8,128)(2,1)S(1)}, bf16[2,256,384]{2,1,0:T(8,128)(2,1)S(1)}, u32[]{:S(2)}, u32[]{:S(2)}) collective-permute-start(bf16[2,256,384]{2,1,0:T(8,128)(2,1)S(1)} %pad_maximum_fusion.1), channel_id=1, source_target_pairs={{0,128},{1,129},{2,130},{3,131},{4,132},{5,133},{6,134},{7,135},{8... | collective-permute-start | bytes 1179656 | tf_op jit(solution)/shard_map/ppermute | solution.py:21
  135.7 8.3 %collective-permute-done.6 = bf16[2,256,384]{2,1,0:T(8,128)(2,1)S(1)} collective-permute-done((bf16[2,256,384]{2,1,0:T(8,128)(2,1)S(1)}, bf16[2,256,384]{2,1,0:T(8,128)(2,1)S(1)}, u32[]{:S(2)}, u32[]{:S(2)}) %collective-permute-start.6) | collective-permute-done | bytes 393248 | tf_op jit(solution)/shard_map/ppermute | solution.py:21
  144.0 0.7 copy-done.6
  144.7 0.0 all-gather.5.cloned.1.call-update
  144.7 2.1 fusion.44
  146.9 11.9 %all_gather.25.q_ref = bf16[1024,384]{1,0:T(8,128)(2,1)S(1)} all-gather(bf16[256,384]{1,0:T(8,128)(2,1)S(1)} %fusion.44), channel_id=1, replica_groups=mesh['segment'=2,'bz'=8,'bx'=4,'mp'=4] {'bx'}, dimensions={0}, use_global_device_ids=true | all-gather | bytes 983040 | tf_op jit(solution)/shard_map/all_gather | solution.py:82
  158.8 30.0 %all-gather.5.cloned.1.call-done.k_ref.v_ref = bf16[2,2048,384]{2,1,0:T(8,128)(2,1)} async-done(((bf16[2,256,384]{2,1,0:T(8,128)(2,1)}), bf16[2,2048,384]{2,1,0:T(8,128)(2,1)}) %all-gather.5.cloned.1.call-update) | async-done | bytes 3145744 | tf_op jit(solution)/shard_map/all_gather | solution.py:83
  188.7 1.9 copy-done.2
  190.6 12.2 %shard_map.101 = (bf16[1024,384]{1,0:T(8,128)(2,1)S(1)}, f32[8,1024]{1,0:T(8,128)}) custom-call(bf16[1024,384]{1,0:T(8,128)(2,1)S(1)} %all_gather.25.q_ref, bf16[2,2048,384]{2,1,0:T(8,128)(2,1)S(1)} %copy-done.2, bf16[2,2048,384]{2,1,0:T(8,128)(2,1)S(1)} %copy-done.2), custom_call_target="tpu_custom_call" | custom-call | tf_op jit(solution)/shard_map/pallas_call | solution.py:59
  202.9 4.0 %all-to-all-start.3 = ((f32[8,4,256]{2,0,1:T(8,128)}), f32[8,4,256]{2,0,1:T(8,128)S(1)}, u32[]{:S(2)}, u32[]{:S(2)}) async-start(f32[8,4,256]{2,0,1:T(8,128)} %bitcast.21), calls=%async_computation.3 | async-start | bytes 65536 | tf_op jit(solution)/shard_map/all_to_all | solution.py:86
  206.8 1.2 copy.14
  208.0 3.1 %all-to-all-done.3 = f32[8,4,256]{2,0,1:T(8,128)S(1)} async-done(((f32[8,4,256]{2,0,1:T(8,128)}), f32[8,4,256]{2,0,1:T(8,128)S(1)}, u32[]{:S(2)}, u32[]{:S(2)}) %all-to-all-start.3) | async-done | bytes 32800 | tf_op jit(solution)/shard_map/all_to_all | solution.py:86
  211.1 3.5 %all-to-all-start.2 = ((bf16[4,256,384]{1,2,0:T(8,128)(2,1)}), bf16[4,256,384]{1,2,0:T(8,128)(2,1)S(1)}, u32[]{:S(2)}, u32[]{:S(2)}) async-start(bf16[4,256,384]{1,2,0:T(8,128)(2,1)} %copy.14), calls=%async_computation.2 | async-start | bytes 1572864 | tf_op jit(solution)/shard_map/all_to_all | solution.py:85
  214.7 9.3 %all-to-all-done.2 = bf16[4,256,384]{1,2,0:T(8,128)(2,1)S(1)} async-done(((bf16[4,256,384]{1,2,0:T(8,128)(2,1)}), bf16[4,256,384]{1,2,0:T(8,128)(2,1)S(1)}, u32[]{:S(2)}, u32[]{:S(2)}) %all-to-all-start.2) | async-done | bytes 786464 | tf_op jit(solution)/shard_map/all_to_all | solution.py:85
  224.0 0.2 fusion.12
  224.2 12.4 %all_gather.27 = bf16[256,1536]{0,1:T(8,128)(2,1)S(1)} all-gather(bf16[256,384]{0,1:T(8,128)(2,1)S(1)} %fusion.72), channel_id=1, replica_groups=mesh['segment'=2,'bz'=8,'bx'=4,'mp'=4] {'mp'}, dimensions={1}, use_global_device_ids=true | all-gather | bytes 983040 | tf_op jit(solution)/shard_map/all_gather | solution.py:167
  236.6 0.3 fusion.77
  237.0 0.0 copy-done.10
  237.0 0.3 fusion.79
  237.3 0.3 fusion.81
  237.6 2.0 fusion.56
  (37 shorter events, 0.3 us)
Async XLA Ops:
  6.5 0.9 copy-start
  6.5 12.7 %copy-start.13 = (f32[1,1536]{1,0:T(1,128)S(1)}, f32[1,1536]{1,0:T(1,128)}, u32[]{:S(2)}) copy-start(f32[1,1536]{1,0:T(1,128)} %param.13) | copy-start | bytes 18436
  6.5 63.9 %all-gather.3.cloned.1.call-start = ((), (), s32[]{:S(2)}) async-start(), calls=%async_computation.4 | async-start | bytes 3538944 | tf_op jit(solution)/shard_map/all_gather | solution.py:83
  21.1 5.4 %copy-start.4 = (bf16[384,1536]{1,0:T(8,128)(2,1)S(1)}, bf16[384,1536]{1,0:T(8,128)(2,1)}, u32[]{:S(2)}) copy-start(bf16[384,1536]{1,0:T(8,128)(2,1)} %param.19) | copy-start | bytes 3538948
  24.0 84.7 %collective-permute-start = (bf16[384,1536]{1,0:T(8,128)(2,1)}, bf16[384,1536]{1,0:T(8,128)(2,1)}, u32[]{:S(2)}, u32[]{:S(2)}) collective-permute-start(bf16[384,1536]{1,0:T(8,128)(2,1)} %bitcast.14), channel_id=1, source_target_pairs={{0,1},{1,2},{2,3},{3,0},{4,5},{5,6},{6,7},{7,4},{8,9},{9,10},{10,1... | collective-permute-start | bytes 3538952 | tf_op jit(solution)/shard_map/ppermute | solution.py:107
  25.7 83.0 %collective-permute-start.1 = (bf16[384,1536]{1,0:T(8,128)(2,1)}, bf16[384,1536]{1,0:T(8,128)(2,1)}, u32[]{:S(2)}, u32[]{:S(2)}) collective-permute-start(bf16[384,1536]{1,0:T(8,128)(2,1)} %bitcast.14), channel_id=1, source_target_pairs={{0,2},{1,3},{2,0},{3,1},{4,6},{5,7},{6,4},{7,5},{8,10},{9,11},{10,... | collective-permute-start | bytes 3538952 | tf_op jit(solution)/shard_map/ppermute | solution.py:107
  25.8 82.9 %collective-permute-start.2 = (bf16[384,1536]{1,0:T(8,128)(2,1)}, bf16[384,1536]{1,0:T(8,128)(2,1)}, u32[]{:S(2)}, u32[]{:S(2)}) collective-permute-start(bf16[384,1536]{1,0:T(8,128)(2,1)} %bitcast.14), channel_id=1, source_target_pairs={{0,3},{1,0},{2,1},{3,2},{4,7},{5,4},{6,5},{7,6},{8,11},{9,8},{10,9... | collective-permute-start | bytes 3538952 | tf_op jit(solution)/shard_map/ppermute | solution.py:107
  27.4 70.3 %collective-permute-start.3 = (bf16[384,384]{1,0:T(8,128)(2,1)}, bf16[384,384]{1,0:T(8,128)(2,1)S(1)}, u32[]{:S(2)}, u32[]{:S(2)}) collective-permute-start(bf16[384,384]{1,0:T(8,128)(2,1)} %get-tuple-element.52), channel_id=1, source_target_pairs={{0,1},{1,2},{2,3},{3,0},{4,5},{5,6},{6,7},{7,4},{8,9},{9,10},{10,1... | collective-permute-start | bytes 884744 | tf_op jit(solution)/shard_map/ppermute | solution.py:107
  70.5 1.9 copy-start.1
  84.6 8.3 %all-to-all-start.1 = ((f32[8,4,256]{2,0,1:T(8,128)}), f32[8,4,256]{2,0,1:T(8,128)S(1)}, u32[]{:S(2)}, u32[]{:S(2)}) async-start(f32[8,4,256]{2,0,1:T(8,128)} %bitcast.9), calls=%async_computation.1 | async-start | bytes 65536 | tf_op jit(solution)/shard_map/all_to_all | solution.py:86
  92.9 12.9 %all-to-all-start = ((bf16[4,256,384]{1,2,0:T(8,128)(2,1)}), bf16[4,256,384]{1,2,0:T(8,128)(2,1)S(1)}, u32[]{:S(2)}, u32[]{:S(2)}) async-start(bf16[4,256,384]{1,2,0:T(8,128)(2,1)} %copy.13), calls=%async_computation | async-start | bytes 1572864 | tf_op jit(solution)/shard_map/all_to_all | solution.py:85
  96.4 92.4 %all-gather.5.cloned.1.call-start = ((), (), s32[]{:S(2)}) async-start(), calls=%async_computation.5 | async-start | bytes 3538944 | tf_op jit(solution)/shard_map/all_gather | solution.py:83
  96.4 9.5 %collective-permute-start.4 = (bf16[384,384]{1,0:T(8,128)(2,1)S(1)}, bf16[384,384]{1,0:T(8,128)(2,1)S(1)}, u32[]{:S(2)}, u32[]{:S(2)}) collective-permute-start(bf16[384,384]{1,0:T(8,128)(2,1)S(1)} %get-tuple-element.54), channel_id=1, source_target_pairs={{0,2},{1,3},{2,0},{3,1},{4,6},{5,7},{6,4},{7,5},{8,10},{9,11},{10,... | collective-permute-start | bytes 884744 | tf_op jit(solution)/shard_map/ppermute | solution.py:107
  97.7 20.8 %copy-start.7 = (bf16[384,384]{1,0:T(8,128)(2,1)}, bf16[384,384]{1,0:T(8,128)(2,1)S(1)}, u32[]{:S(2)}) copy-start(bf16[384,384]{1,0:T(8,128)(2,1)S(1)} %collective-permute-done.3) | copy-start | bytes 884740
  97.7 11.0 %collective-permute-start.5 = (bf16[384,384]{1,0:T(8,128)(2,1)S(1)}, bf16[384,384]{1,0:T(8,128)(2,1)S(1)}, u32[]{:S(2)}, u32[]{:S(2)}) collective-permute-start(bf16[384,384]{1,0:T(8,128)(2,1)S(1)} %get-tuple-element.51), channel_id=1, source_target_pairs={{0,3},{1,0},{2,1},{3,2},{4,7},{5,4},{6,5},{7,6},{8,11},{9,8},{10,9... | collective-permute-start | bytes 884744 | tf_op jit(solution)/shard_map/ppermute | solution.py:107
  106.0 12.5 %copy-start.9 = (bf16[384,384]{1,0:T(8,128)(2,1)}, bf16[384,384]{1,0:T(8,128)(2,1)S(1)}, u32[]{:S(2)}) copy-start(bf16[384,384]{1,0:T(8,128)(2,1)S(1)} %collective-permute-done.4) | copy-start | bytes 884740
  108.7 9.8 %copy-start.11 = (bf16[384,384]{1,0:T(8,128)(2,1)}, bf16[384,384]{1,0:T(8,128)(2,1)S(1)}, u32[]{:S(2)}) copy-start(bf16[384,384]{1,0:T(8,128)(2,1)S(1)} %collective-permute-done.5) | copy-start | bytes 884740
  126.5 3.3 %copy-start.14 = (bf16[3,1536,384]{2,1,0:T(8,128)(2,1)S(1)}, bf16[3,1536,384]{2,1,0:T(8,128)(2,1)}, u32[]{:S(2)}) copy-start(bf16[3,1536,384]{2,1,0:T(8,128)(2,1)} %param.18) | copy-start | bytes 10616836
  126.5 3.3 %copy-start.15 = (f32[1536]{0:T(1024)S(1)}, f32[1536]{0:T(1024)}, u32[]{:S(2)}) copy-start(f32[1536]{0:T(1024)} %param.17) | copy-start | bytes 18436
  129.7 0.9 copy-start.3
  130.6 14.1 %copy-start.16 = (f32[1536]{0:T(1024)S(1)}, f32[1536]{0:T(1024)}, u32[]{:S(2)}) copy-start(f32[1536]{0:T(1024)} %param.16) | copy-start | bytes 18436
  131.3 12.7 %collective-permute-start.6 = (bf16[2,256,384]{2,1,0:T(8,128)(2,1)S(1)}, bf16[2,256,384]{2,1,0:T(8,128)(2,1)S(1)}, u32[]{:S(2)}, u32[]{:S(2)}) collective-permute-start(bf16[2,256,384]{2,1,0:T(8,128)(2,1)S(1)} %pad_maximum_fusion.1), channel_id=1, source_target_pairs={{0,128},{1,129},{2,130},{3,131},{4,132},{5,133},{6,134},{7,135},{8... | collective-permute-start | bytes 1179656 | tf_op jit(solution)/shard_map/ppermute | solution.py:21
  144.0 0.7 copy-start.6
  188.7 1.9 copy-start.2
  202.9 8.3 %all-to-all-start.3 = ((f32[8,4,256]{2,0,1:T(8,128)}), f32[8,4,256]{2,0,1:T(8,128)S(1)}, u32[]{:S(2)}, u32[]{:S(2)}) async-start(f32[8,4,256]{2,0,1:T(8,128)} %bitcast.21), calls=%async_computation.3 | async-start | bytes 65536 | tf_op jit(solution)/shard_map/all_to_all | solution.py:86
  211.1 12.9 %all-to-all-start.2 = ((bf16[4,256,384]{1,2,0:T(8,128)(2,1)}), bf16[4,256,384]{1,2,0:T(8,128)(2,1)S(1)}, u32[]{:S(2)}, u32[]{:S(2)}) async-start(bf16[4,256,384]{1,2,0:T(8,128)(2,1)} %copy.14), calls=%async_computation.2 | async-start | bytes 1572864 | tf_op jit(solution)/shard_map/all_to_all | solution.py:85
  214.6 22.0 %copy-start.12 = (bf16[384,384]{1,0:T(8,128)(2,1)S(1)}, bf16[384,384]{1,0:T(8,128)(2,1)}, u32[]{:S(2)}) copy-start(bf16[384,384]{1,0:T(8,128)(2,1)} %copy-done.11) | copy-start | bytes 884740
  224.0 12.9 %copy-start.10 = (bf16[384,384]{1,0:T(8,128)(2,1)S(1)}, bf16[384,384]{1,0:T(8,128)(2,1)}, u32[]{:S(2)}) copy-start(bf16[384,384]{1,0:T(8,128)(2,1)} %copy-done.9) | copy-start | bytes 884740
  224.2 13.1 %copy-start.8 = (bf16[384,384]{1,0:T(8,128)(2,1)S(1)}, bf16[384,384]{1,0:T(8,128)(2,1)}, u32[]{:S(2)}) copy-start(bf16[384,384]{1,0:T(8,128)(2,1)} %copy-done.7) | copy-start | bytes 884740
  236.6 1.0 copy-start.5
Sparse Core Ops, SparseCore 0:
  24.1 46.3 all-gather.2
  144.9 43.8 all-gather.4

commit v5 on v4

--- a/solution.py
+++ b/solution.py
@@ -9,7 +9,9 @@
 from jax.sharding import PartitionSpec as P
 
 HEAD_DIM = 128
+MP = ("my", "mc")
 X_SIZE = 4
+CORES = 2
 TILE = 256
 STATS = 128
 STAT_ROWS = 8
@@ -98,25 +100,38 @@
     return lax.optimization_barrier((merged, riders))
 
 
+def mp_index():
+    return lax.axis_index("my") * lax.axis_size("mc") + lax.axis_index("mc")
+
+
+def mp_gather(value):
+    across = lax.all_gather(value, "my", axis=1, tiled=True)
+    both = lax.all_gather(across, "mc", axis=1, tiled=True)
+    rows, width = value.shape
+    grouped = both.reshape(rows, lax.axis_size("mc"), lax.axis_size("my"), width)
+    return grouped.transpose(0, 2, 1, 3).reshape(rows, -1)
+
+
 def spread(block_of):
-    count = lax.axis_size("mp")
-    me = lax.axis_index("mp")
-    blocks = [(me, block_of(me))]
+    count = lax.axis_size("my") * lax.axis_size("mc")
+    me = mp_index()
+    sources, blocks = [me], [block_of(me)]
     for step in range(1, count):
         piece = block_of((me + step) % count)
-        received = lax.ppermute(piece, "mp", [(j, (j + step) % count) for j in range(count)])
-        blocks.append(((me - step + count) % count, received))
-    return blocks
-
-
-def project_out(attended_full, blocks):
-    width = blocks[0][1].shape[0]
-    total = None
-    for source, block in blocks:
-        piece = lax.dynamic_slice_in_dim(attended_full, source * width, width, axis=1)
-        term = jnp.dot(piece, block, preferred_element_type=jnp.float32)
-        total = term if total is None else total + term
-    return total
+        received = lax.ppermute(piece, MP, [(j, (j + step) % count) for j in range(count)])
+        sources.append((me - step + count) % count)
+        blocks.append(received)
+    return jnp.stack(sources), jnp.concatenate(blocks, axis=0)
+
+
+def project_out(attended_full, spread_weight):
+    sources, weight = spread_weight
+    width = weight.shape[0] // sources.shape[0]
+    pieces = [
+        lax.dynamic_slice_in_dim(attended_full, sources[i] * width, width, axis=1)
+        for i in range(sources.shape[0])
+    ]
+    return jnp.dot(jnp.concatenate(pieces, axis=1), weight, preferred_element_type=jnp.float32)
 
 
 def on_device(
@@ -134,7 +149,7 @@
     local_rows = section_input.shape[1]
     local_width = section_input.shape[2]
     codes_total = code_table.shape[1]
-    me = lax.axis_index("mp")
+    me = mp_index()
     self_blocks = spread(lambda target: self_out[0])
     cross_blocks = spread(
         lambda target: lax.dynamic_slice_in_dim(cross_out, target * local_width, local_width, axis=1)
@@ -144,7 +159,7 @@
     ).astype(jnp.bfloat16)
     looked = jnp.dot(matches, code_table[0], preferred_element_type=jnp.float32)
     embedded = (section_input[0].astype(jnp.float32) + looked).astype(jnp.bfloat16)
-    embedded_full = lax.all_gather(embedded, "mp", axis=1, tiled=True)
+    embedded_full = mp_gather(embedded)
     normed = rms_norm(embedded_full, self_gain[0])
     self_queries = project(normed, self_weights[0, 0])
     self_pairs = jnp.stack(
@@ -153,7 +168,7 @@
     self_local, (self_blocks, cross_blocks) = attend(
         self_queries, self_pairs, (self_blocks, cross_blocks)
     )
-    self_attended = lax.all_gather(self_local, "mp", axis=1, tiled=True)
+    self_attended = mp_gather(self_local)
     hidden_full = (
         embedded_full.astype(jnp.float32) + project_out(self_attended, self_blocks)
     ).astype(jnp.bfloat16)
@@ -164,7 +179,7 @@
         [project(memory_normed, cross_weights[1]), project(memory_normed, cross_weights[2])]
     )
     arrived = shifted(memory_pairs, "segment", 1)
-    crossed = lax.all_gather(attend(cross_queries, arrived), "mp", axis=1, tiled=True)
+    crossed = mp_gather(attend(cross_queries, arrived))
     decoded = (
         hidden_part.astype(jnp.float32) + project_out(crossed, cross_blocks)
     ).astype(jnp.bfloat16)
@@ -175,25 +190,25 @@
 def solution(mesh):
     segments, blocks, parts = (mesh.shape["segment"], mesh.shape["blk"], mesh.shape["mp"])
     split = Mesh(
-        mesh.devices.reshape(segments, blocks // X_SIZE, X_SIZE, parts),
-        ("segment", "bz", "bx", "mp"),
+        mesh.devices.reshape(segments, blocks // X_SIZE, X_SIZE, parts // CORES, CORES),
+        ("segment", "bz", "bx", "my", "mc"),
     )
     rows = ("bz", "bx")
     return jax.shard_map(
         on_device,
         mesh=split,
         in_specs=(
-            P("segment", rows, "mp"),
+            P("segment", rows, MP),
             P("segment", rows),
-            P("segment", None, "mp"),
+            P("segment", None, MP),
             P("segment", None),
-            P("segment", None, None, "mp"),
-            P("segment", "mp", None),
+            P("segment", None, None, MP),
+            P("segment", MP, None),
             P(),
             P(),
-            P(None, None, "mp"),
-            P("mp", None),
+            P(None, None, MP),
+            P(MP, None),
         ),
-        out_specs=P("segment", rows, "mp"),
+        out_specs=P("segment", rows, MP),
         check_vma=False,
     )

time: 247 us -> 277 us (1.12)
  waiting for transfers between devices: 89.5 us -> 106 us
  matrix products: 24.5 us -> 15.7 us
  other arithmetic: 1.61 us -> 10.4 us
  local copies, waits for them, and re-layouts: 9.03 us -> 17.8 us
  between operations: 13.7 us -> 18.8 us
  starting transfers between devices: 27.1 us -> 22.5 us
  blocking collectives: 56.5 us -> 60.2 us
    ppermute x6, waiting for transfers between devices: 2.73 us -> 50.1 us  [spread(): lax.ppermute(piece, MP, [(j, (j + step) % count) for j in range(count)])]
    all_gather x2, waiting for transfers between devices: 57.9 us -> 34.1 us  [attend(): key_block = lax.all_gather(pairs, 'bz', axis=1, tiled=True)]
    dot_general x8 -> x2, matrix products: 14.1 us -> 5.26 us  [project_out(): jnp.dot(jnp.concatenate(pieces, axis=1), weight, preferred_element_type=j...]
    concatenate x0 -> x2, other arithmetic: none -> 7.57 us  [spread(): return (jnp.stack(sources), jnp.concatenate(blocks, axis=0))]
    convert_element_type x0 -> x4, local copies, waits for them, and re-layouts: none -> 5.52 us  [on_device(): embedded_full.astype(jnp.float32) + project_out(self_attended, self_blocks)]
    all_gather x3 -> x6, blocking collectives: 32.4 us -> 37.7 us  [the longest x3 21.2 us: mp_gather(): both = lax.all_gather(across, 'mc', axis=1, tiled=True)]
    all_to_all x2, waiting for transfers between devices: 14.3 us -> 9.63 us  [attend(): outs = lax.all_to_all(partial, 'bx', 0, 0, tiled=True)]
    ppermute x6, starting transfers between devices: 7.79 us -> 3.57 us  [spread(): lax.ppermute(piece, MP, [(j, (j + step) % count) for j in range(count)])]
  transfers between devices with their start and end apart: 13 -> 13, of which waited for: 8 -> 7; matrix products, arithmetic and copies ran while one was open for 3% -> 7% of each run, Pallas kernels for 5% -> 4%
where the time goes in v5:
time: 277 us; the launch traced here: 276 us
  waiting for transfers between devices  106 us (38%)
  blocking collectives  60.2 us (22%)
  Pallas kernels  24.6 us (9%)
  starting transfers between devices  22.5 us (8%)
  between operations  18.8 us (7%)
  local copies, waits for them, and re-layouts  17.8 us (6%)
  matrix products  15.7 us (6%)
  other arithmetic  10.4 us (4%)
    ppermute x6, waiting for transfers between devices, spread(): lax.ppermute(piece, MP, [(j, (j + step) % count) for j in range(count)])  50.1 us
    all_gather x2, waiting for transfers between devices, attend(): key_block = lax.all_gather(pairs, 'bz', axis=1, tiled=True)  34.1 us
    pallas_call x2, Pallas kernels, partial_attend(): pl.pallas_call(partial_kernel, grid=(rows // TILE,), in_specs=[pl.BlockSp...  24.6 us
    all_gather x2, blocking collectives, attend(): query_block = lax.all_gather(queries, 'bx', axis=0, tiled=True)  22.5 us
    all_gather x3, blocking collectives, mp_gather(): both = lax.all_gather(across, 'mc', axis=1, tiled=True)  21.2 us
    all_gather x3, blocking collectives, mp_gather(): across = lax.all_gather(value, 'my', axis=1, tiled=True)  16.6 us
    all_to_all x2, waiting for transfers between devices, attend(): outs = lax.all_to_all(partial, 'bx', 0, 0, tiled=True)  9.63 us
    dot_general x6, matrix products, project(): jnp.dot(normed, weight, preferred_element_type=jnp.float32)  9.2 us
  transfers between devices with their start and end apart: 13, of which 7 were waited for; matrix products, arithmetic and copies ran while one was open for 7% of the time, Pallas kernels for 4%

profile of v5, /device:TPU:1, one launch (start us, length us, event | category | flops | bytes accessed | tf_op | source)
XLA Modules:
  0.0 276.0 jit_solution(5680802412972339535)
XLA Ops:
  6.5 0.9 copy-done
  7.5 1.2 fusion.45
  8.7 6.2 %all_gather.30 = bf16[256,768]{1,0:T(8,128)(2,1)S(1)} all-gather(bf16[256,384]{1,0:T(8,128)(2,1)S(1)} %fusion.45), channel_id=1, replica_groups=mesh['segment'=2,'bz'=8,'bx'=4,'my'=2,'mc'=2] {'my'}, dimensions={1}, use_global_device_ids=true | all-gather | bytes 589824 | tf_op jit(solution)/shard_map/all_gather | solution.py:108
  14.9 5.3 %all_gather.31 = bf16[256,1536]{1,0:T(8,128)(2,1)S(1)} all-gather(bf16[256,768]{1,0:T(8,128)(2,1)S(1)} %all_gather.30), channel_id=1, replica_groups=mesh['segment'=2,'bz'=8,'bx'=4,'my'=2,'mc'=2] {'mc'}, dimensions={1}, use_global_device_ids=true | all-gather | bytes 1179648 | tf_op jit(solution)/shard_map/all_gather | solution.py:109
  20.2 1.1 reshape.141
  21.3 1.2 copy.16
  22.5 1.2 multiply_reduce_fusion
  23.7 0.3 fusion.8
  24.0 2.2 fusion.55
  26.2 2.0 fusion.58
  28.2 0.8 pad_maximum_fusion.2
  28.9 0.0 all-gather.3.cloned.1.call-update
  29.0 0.5 collective-permute-start.2
  29.4 0.6 collective-permute-start.1
  30.0 1.6 collective-permute-start
  31.6 1.1 constant_dynamic-slice_fusion.11
  32.7 0.9 collective-permute-start.4
  33.6 0.1 pad_add_fusion
  33.7 0.8 copy.15
  34.5 2.5 reshape.139
  37.0 1.9 fusion.27
  38.9 50.1 %collective-permute-done.5 = bf16[384,384]{1,0:T(8,128)(2,1)} collective-permute-done((bf16[384,384]{1,0:T(8,128)(2,1)}, bf16[384,384]{1,0:T(8,128)(2,1)}, u32[]{:S(2)}, u32[]{:S(2)}) %collective-permute-start.5) | collective-permute-done | bytes 294944 | tf_op jit(solution)/shard_map/ppermute | solution.py:121
  89.0 11.5 %all_gather.32.q_ref = bf16[1024,384]{1,0:T(8,128)(2,1)S(1)} all-gather(bf16[256,384]{1,0:T(8,128)(2,1)S(1)} %fusion.27), channel_id=1, replica_groups=mesh['segment'=2,'bz'=8,'bx'=4,'my'=2,'mc'=2] {'bx'}, dimensions={0}, use_global_device_ids=true | all-gather | bytes 983040 | tf_op jit(solution)/shard_map/all_gather | solution.py:84
  100.5 1.9 copy-done.1
  102.4 12.3 %shard_map.100 = (bf16[1024,384]{1,0:T(8,128)(2,1)S(1)}, f32[8,1024]{1,0:T(8,128)}) custom-call(bf16[1024,384]{1,0:T(8,128)(2,1)S(1)} %all_gather.32.q_ref, bf16[2,2048,384]{2,1,0:T(8,128)(2,1)S(1)} %copy-done.1, bf16[2,2048,384]{2,1,0:T(8,128)(2,1)S(1)} %copy-done.1), custom_call_target="tpu_custom_call" | custom-call | tf_op jit(solution)/shard_map/pallas_call | solution.py:61
  114.7 3.3 %all-to-all-start.1 = ((f32[8,4,256]{2,0,1:T(8,128)}), f32[8,4,256]{2,0,1:T(8,128)S(1)}, u32[]{:S(2)}, u32[]{:S(2)}) async-start(f32[8,4,256]{2,0,1:T(8,128)} %bitcast.12), calls=%async_computation.1 | async-start | bytes 65536 | tf_op jit(solution)/shard_map/all_to_all | solution.py:88
  118.0 2.2 pad_maximum_fusion.1
  120.2 1.2 copy.17
  121.4 0.9 all-to-all-done.1
  122.3 3.5 %all-to-all-start = ((bf16[4,256,384]{1,2,0:T(8,128)(2,1)}), bf16[4,256,384]{1,2,0:T(8,128)(2,1)S(1)}, u32[]{:S(2)}, u32[]{:S(2)}) async-start(bf16[4,256,384]{1,2,0:T(8,128)(2,1)} %copy.17), calls=%async_computation | async-start | bytes 1572864 | tf_op jit(solution)/shard_map/all_to_all | solution.py:87
  125.8 0.0 all-gather.5.cloned.1.call-start
  125.9 5.4 %pad_maximum_fusion = bf16[1536,1536]{1,0:T(8,128)(2,1)} fusion(bf16[384,1536]{1,0:T(8,128)(2,1)} %collective-permute-done.2, bf16[384,1536]{1,0:T(8,128)(2,1)} %collective-permute-done.1, bf16[384,1536]{1,0:T(8,128)(2,1)} %collective-permute-done, bf16[384,1536]{1,0:T(8,128)(2,1)} %bitcast.21), kind=kLoop, calls=%fused_computation | loop fusion | flops 18874368 | bytes 9437184 | tf_op jit(solution)/shard_map/concatenate | solution.py:124
  131.3 2.8 %all-to-all-done = bf16[4,256,384]{1,2,0:T(8,128)(2,1)S(1)} async-done(((bf16[4,256,384]{1,2,0:T(8,128)(2,1)}), bf16[4,256,384]{1,2,0:T(8,128)(2,1)S(1)}, u32[]{:S(2)}, u32[]{:S(2)}) %all-to-all-start) | async-done | bytes 786464 | tf_op jit(solution)/shard_map/all_to_all | solution.py:87
  134.1 0.2 fusion.7
  134.3 0.7 fusion.92
  137.5 5.2 %all_gather.34 = bf16[256,768]{0,1:T(8,128)(2,1)S(1)} all-gather(bf16[256,384]{0,1:T(8,128)(2,1)S(1)} %fusion.79), channel_id=1, replica_groups=mesh['segment'=2,'bz'=8,'bx'=4,'my'=2,'mc'=2] {'my'}, dimensions={1}, use_global_device_ids=true | all-gather | bytes 589824 | tf_op jit(solution)/shard_map/all_gather | solution.py:108
  142.7 8.9 %all_gather.35 = bf16[256,1536]{0,1:T(8,128)(2,1)S(1)} all-gather(bf16[256,768]{0,1:T(8,128)(2,1)S(1)} %all_gather.34), channel_id=1, replica_groups=mesh['segment'=2,'bz'=8,'bx'=4,'my'=2,'mc'=2] {'mc'}, dimensions={1}, use_global_device_ids=true | all-gather | bytes 1179648 | tf_op jit(solution)/shard_map/all_gather | solution.py:109
  151.6 0.1 copy.18
  151.7 0.1 constant_dynamic-slice_fusion.7
  151.8 1.3 copy-done.3
  153.0 4.0 %fusion.5 = (f32[256]{0:T(256)S(1)}, bf16[256,1536]{1,0:T(8,128)(2,1)S(1)}) fusion(f32[256,1536]{1,0:T(8,128)S(1)} %copy-done.3, bf16[1536,1536]{1,0:T(8,128)(2,1)} %pad_maximum_fusion, bf16[256,384]{0,1:T(8,128)(2,1)S(1)} %get-tuple-element.36, bf16[256,384]{0,1:T(8,128)(2,1)S(1)} %get-tuple-element.37, bf16[256,384]{0,1:T(8,128)(2,1)S(1)} %get-tuple-element.38, ...), kind=kOutput, calls=%fused_computation.9 | convolution fusion | flops 1213071104 | bytes 7865344 | tf_op jit(solution)/shard_map/dot_general | solution.py:134
  157.0 0.6 fusion.49
  157.7 0.6 fusion.52
  158.3 4.7 %collective-permute-start.6 = (bf16[2,256,384]{2,1,0:T(8,128)(2,1)S(1)}, bf16[2,256,384]{2,1,0:T(8,128)(2,1)S(1)}, u32[]{:S(2)}, u32[]{:S(2)}) collective-permute-start(bf16[2,256,384]{2,1,0:T(8,128)(2,1)S(1)} %pad_maximum_fusion.3), channel_id=1, source_target_pairs={{0,128},{1,129},{2,130},{3,131},{4,132},{5,133},{6,134},{7,135},{8... | collective-permute-start | bytes 1179656 | tf_op jit(solution)/shard_map/ppermute | solution.py:23
  163.0 8.1 %collective-permute-done.6 = bf16[2,256,384]{2,1,0:T(8,128)(2,1)S(1)} collective-permute-done((bf16[2,256,384]{2,1,0:T(8,128)(2,1)S(1)}, bf16[2,256,384]{2,1,0:T(8,128)(2,1)S(1)}, u32[]{:S(2)}, u32[]{:S(2)}) %collective-permute-start.6) | collective-permute-done | bytes 393248 | tf_op jit(solution)/shard_map/ppermute | solution.py:23
  171.1 0.8 copy-done.9
  171.9 0.0 all-gather.5.cloned.1.call-update
  171.9 1.9 fusion.36
  173.8 11.0 %all_gather.36.q_ref = bf16[1024,384]{1,0:T(8,128)(2,1)S(1)} all-gather(bf16[256,384]{1,0:T(8,128)(2,1)S(1)} %fusion.36), channel_id=1, replica_groups=mesh['segment'=2,'bz'=8,'bx'=4,'my'=2,'mc'=2] {'bx'}, dimensions={0}, use_global_device_ids=true | all-gather | bytes 983040 | tf_op jit(solution)/shard_map/all_gather | solution.py:84
  184.8 34.1 %all-gather.5.cloned.1.call-done.k_ref.v_ref = bf16[2,2048,384]{2,1,0:T(8,128)(2,1)} async-done(((bf16[2,256,384]{2,1,0:T(8,128)(2,1)}), bf16[2,2048,384]{2,1,0:T(8,128)(2,1)}) %all-gather.5.cloned.1.call-update) | async-done | bytes 3145744 | tf_op jit(solution)/shard_map/all_gather | solution.py:85
  218.9 1.9 copy-done.2
  220.8 12.2 %shard_map.101 = (bf16[1024,384]{1,0:T(8,128)(2,1)S(1)}, f32[8,1024]{1,0:T(8,128)}) custom-call(bf16[1024,384]{1,0:T(8,128)(2,1)S(1)} %all_gather.36.q_ref, bf16[2,2048,384]{2,1,0:T(8,128)(2,1)S(1)} %copy-done.2, bf16[2,2048,384]{2,1,0:T(8,128)(2,1)S(1)} %copy-done.2), custom_call_target="tpu_custom_call" | custom-call | tf_op jit(solution)/shard_map/pallas_call | solution.py:61
  233.1 4.0 %all-to-all-start.3 = ((f32[8,4,256]{2,0,1:T(8,128)}), f32[8,4,256]{2,0,1:T(8,128)S(1)}, u32[]{:S(2)}, u32[]{:S(2)}) async-start(f32[8,4,256]{2,0,1:T(8,128)} %bitcast.36), calls=%async_computation.3 | async-start | bytes 65536 | tf_op jit(solution)/shard_map/all_to_all | solution.py:88
  237.0 1.2 copy.19
  238.2 3.1 %all-to-all-done.3 = f32[8,4,256]{2,0,1:T(8,128)S(1)} async-done(((f32[8,4,256]{2,0,1:T(8,128)}), f32[8,4,256]{2,0,1:T(8,128)S(1)}, u32[]{:S(2)}, u32[]{:S(2)}) %all-to-all-start.3) | async-done | bytes 32800 | tf_op jit(solution)/shard_map/all_to_all | solution.py:88
  241.3 3.5 %all-to-all-start.2 = ((bf16[4,256,384]{1,2,0:T(8,128)(2,1)}), bf16[4,256,384]{1,2,0:T(8,128)(2,1)S(1)}, u32[]{:S(2)}, u32[]{:S(2)}) async-start(bf16[4,256,384]{1,2,0:T(8,128)(2,1)} %copy.19), calls=%async_computation.2 | async-start | bytes 1572864 | tf_op jit(solution)/shard_map/all_to_all | solution.py:87
  247.4 6.8 %all-to-all-done.2 = bf16[4,256,384]{1,2,0:T(8,128)(2,1)S(1)} async-done(((bf16[4,256,384]{1,2,0:T(8,128)(2,1)}), bf16[4,256,384]{1,2,0:T(8,128)(2,1)S(1)}, u32[]{:S(2)}, u32[]{:S(2)}) %all-to-all-start.2) | async-done | bytes 786464 | tf_op jit(solution)/shard_map/all_to_all | solution.py:87
  254.2 0.2 fusion.6
  254.4 5.2 %all_gather.38 = bf16[256,768]{0,1:T(8,128)(2,1)S(1)} all-gather(bf16[256,384]{0,1:T(8,128)(2,1)S(1)} %fusion.78), channel_id=1, replica_groups=mesh['segment'=2,'bz'=8,'bx'=4,'my'=2,'mc'=2] {'my'}, dimensions={1}, use_global_device_ids=true | all-gather | bytes 589824 | tf_op jit(solution)/shard_map/all_gather | solution.py:108
  259.6 7.0 %all_gather.39 = bf16[256,1536]{0,1:T(8,128)(2,1)S(1)} all-gather(bf16[256,768]{0,1:T(8,128)(2,1)S(1)} %all_gather.38), channel_id=1, replica_groups=mesh['segment'=2,'bz'=8,'bx'=4,'my'=2,'mc'=2] {'mc'}, dimensions={1}, use_global_device_ids=true | all-gather | bytes 1179648 | tf_op jit(solution)/shard_map/all_gather | solution.py:109
  266.6 0.1 copy.20
  266.6 0.1 constant_dynamic-slice_fusion.3
  266.7 1.1 copy-done.5
  267.8 1.3 fusion.48
  (44 shorter events, 0.3 us)
Async XLA Ops:
  6.5 0.9 copy-start
  6.5 94.0 %all-gather.3.cloned.1.call-start = ((), (), s32[]{:S(2)}) async-start(), calls=%async_computation.4 | async-start | bytes 3538944 | tf_op jit(solution)/shard_map/all_gather | solution.py:85
  22.5 1.2 copy-start.11
  24.0 4.2 %copy-start.7 = (bf16[256,2,2,384]{0,3,2,1:T(8,128)(2,1)}, bf16[256,2,2,384]{0,3,2,1:T(8,128)(2,1)S(1)}, u32[]{:S(2)}) copy-start(bf16[256,2,2,384]{0,3,2,1:T(8,128)(2,1)S(1)} %fusion.8) | copy-start | bytes 2359300
  26.2 5.5 %copy-start.6 = (bf16[384,1536]{1,0:T(8,128)(2,1)S(1)}, bf16[384,1536]{1,0:T(8,128)(2,1)}, u32[]{:S(2)}) copy-start(bf16[384,1536]{1,0:T(8,128)(2,1)} %param.19) | copy-start | bytes 3538948
  29.0 96.9 %collective-permute-start.2 = (bf16[384,1536]{1,0:T(8,128)(2,1)}, bf16[384,1536]{1,0:T(8,128)(2,1)}, u32[]{:S(2)}, u32[]{:S(2)}) collective-permute-start(bf16[384,1536]{1,0:T(8,128)(2,1)} %bitcast.21), channel_id=1, source_target_pairs={{0,3},{1,0},{2,1},{3,2},{4,7},{5,4},{6,5},{7,6},{8,11},{9,8},{10,9... | collective-permute-start | bytes 3538952 | tf_op jit(solution)/shard_map/ppermute | solution.py:121
  29.4 96.4 %collective-permute-start.1 = (bf16[384,1536]{1,0:T(8,128)(2,1)}, bf16[384,1536]{1,0:T(8,128)(2,1)}, u32[]{:S(2)}, u32[]{:S(2)}) collective-permute-start(bf16[384,1536]{1,0:T(8,128)(2,1)} %bitcast.21), channel_id=1, source_target_pairs={{0,2},{1,3},{2,0},{3,1},{4,6},{5,7},{6,4},{7,5},{8,10},{9,11},{10,... | collective-permute-start | bytes 3538952 | tf_op jit(solution)/shard_map/ppermute | solution.py:121
  30.0 95.9 %collective-permute-start = (bf16[384,1536]{1,0:T(8,128)(2,1)}, bf16[384,1536]{1,0:T(8,128)(2,1)}, u32[]{:S(2)}, u32[]{:S(2)}) collective-permute-start(bf16[384,1536]{1,0:T(8,128)(2,1)} %bitcast.21), channel_id=1, source_target_pairs={{0,1},{1,2},{2,3},{3,0},{4,5},{5,6},{6,7},{7,4},{8,9},{9,10},{10,1... | collective-permute-start | bytes 3538952 | tf_op jit(solution)/shard_map/ppermute | solution.py:121
  32.7 56.3 %collective-permute-start.5 = (bf16[384,384]{1,0:T(8,128)(2,1)}, bf16[384,384]{1,0:T(8,128)(2,1)}, u32[]{:S(2)}, u32[]{:S(2)}) collective-permute-start(bf16[384,384]{1,0:T(8,128)(2,1)} %get-tuple-element.29), channel_id=1, source_target_pairs={{0,3},{1,0},{2,1},{3,2},{4,7},{5,4},{6,5},{7,6},{8,11},{9,8},{10,9... | collective-permute-start | bytes 884744 | tf_op jit(solution)/shard_map/ppermute | solution.py:121
  32.7 85.3 %collective-permute-start.4 = (bf16[384,384]{1,0:T(8,128)(2,1)}, bf16[384,384]{1,0:T(8,128)(2,1)}, u32[]{:S(2)}, u32[]{:S(2)}) collective-permute-start(bf16[384,384]{1,0:T(8,128)(2,1)} %get-tuple-element.30), channel_id=1, source_target_pairs={{0,2},{1,3},{2,0},{3,1},{4,6},{5,7},{6,4},{7,5},{8,10},{9,11},{10,... | collective-permute-start | bytes 884744 | tf_op jit(solution)/shard_map/ppermute | solution.py:121
  34.5 2.5 copy-start.8
  37.0 52.0 %copy-start.10 = (bf16[384,384]{1,0:T(8,128)(2,1)S(1)}, bf16[384,384]{1,0:T(8,128)(2,1)}, u32[]{:S(2)}) copy-start(bf16[384,384]{1,0:T(8,128)(2,1)} %get-tuple-element.28) | copy-start | bytes 884740
  89.0 29.0 %collective-permute-start.3 = (bf16[384,384]{1,0:T(8,128)(2,1)S(1)}, bf16[384,384]{1,0:T(8,128)(2,1)S(1)}, u32[]{:S(2)}, u32[]{:S(2)}) collective-permute-start(bf16[384,384]{1,0:T(8,128)(2,1)S(1)} %copy-done.10), channel_id=1, source_target_pairs={{0,1},{1,2},{2,3},{3,0},{4,5},{5,6},{6,7},{7,4},{8,9},{9,10},{10,1... | collective-permute-start | bytes 884744 | tf_op jit(solution)/shard_map/ppermute | solution.py:121
  100.5 1.9 copy-start.1
  102.4 15.6 %copy-start.4 = (bf16[384,384]{1,0:T(8,128)(2,1)S(1)}, bf16[384,384]{1,0:T(8,128)(2,1)}, u32[]{:S(2)}) copy-start(bf16[384,384]{1,0:T(8,128)(2,1)} %get-tuple-element.27) | copy-start | bytes 884740
  114.7 7.5 %all-to-all-start.1 = ((f32[8,4,256]{2,0,1:T(8,128)}), f32[8,4,256]{2,0,1:T(8,128)S(1)}, u32[]{:S(2)}, u32[]{:S(2)}) async-start(f32[8,4,256]{2,0,1:T(8,128)} %bitcast.12), calls=%async_computation.1 | async-start | bytes 65536 | tf_op jit(solution)/shard_map/all_to_all | solution.py:88
  122.3 11.8 %all-to-all-start = ((bf16[4,256,384]{1,2,0:T(8,128)(2,1)}), bf16[4,256,384]{1,2,0:T(8,128)(2,1)S(1)}, u32[]{:S(2)}, u32[]{:S(2)}) async-start(bf16[4,256,384]{1,2,0:T(8,128)(2,1)} %copy.17), calls=%async_computation | async-start | bytes 1572864 | tf_op jit(solution)/shard_map/all_to_all | solution.py:87
  125.8 93.1 %all-gather.5.cloned.1.call-start = ((), (), s32[]{:S(2)}) async-start(), calls=%async_computation.5 | async-start | bytes 3538944 | tf_op jit(solution)/shard_map/all_gather | solution.py:85
  151.6 1.4 copy-start.3
  153.0 4.0 %copy-start.12 = (bf16[3,1536,384]{2,1,0:T(8,128)(2,1)S(1)}, bf16[3,1536,384]{2,1,0:T(8,128)(2,1)}, u32[]{:S(2)}) copy-start(bf16[3,1536,384]{2,1,0:T(8,128)(2,1)} %param.18) | copy-start | bytes 10616836
  153.0 4.0 %copy-start.13 = (f32[1536]{0:T(1024)S(1)}, f32[1536]{0:T(1024)}, u32[]{:S(2)}) copy-start(f32[1536]{0:T(1024)} %param.17) | copy-start | bytes 18436
  157.7 14.2 %copy-start.14 = (f32[1536]{0:T(1024)S(1)}, f32[1536]{0:T(1024)}, u32[]{:S(2)}) copy-start(f32[1536]{0:T(1024)} %param.16) | copy-start | bytes 18436
  158.3 12.8 %collective-permute-start.6 = (bf16[2,256,384]{2,1,0:T(8,128)(2,1)S(1)}, bf16[2,256,384]{2,1,0:T(8,128)(2,1)S(1)}, u32[]{:S(2)}, u32[]{:S(2)}) collective-permute-start(bf16[2,256,384]{2,1,0:T(8,128)(2,1)S(1)} %pad_maximum_fusion.3), channel_id=1, source_target_pairs={{0,128},{1,129},{2,130},{3,131},{4,132},{5,133},{6,134},{7,135},{8... | collective-permute-start | bytes 1179656 | tf_op jit(solution)/shard_map/ppermute | solution.py:23
  171.1 0.8 copy-start.9
  218.9 1.9 copy-start.2
  233.1 8.3 %all-to-all-start.3 = ((f32[8,4,256]{2,0,1:T(8,128)}), f32[8,4,256]{2,0,1:T(8,128)S(1)}, u32[]{:S(2)}, u32[]{:S(2)}) async-start(f32[8,4,256]{2,0,1:T(8,128)} %bitcast.36), calls=%async_computation.3 | async-start | bytes 65536 | tf_op jit(solution)/shard_map/all_to_all | solution.py:88
  241.3 12.9 %all-to-all-start.2 = ((bf16[4,256,384]{1,2,0:T(8,128)(2,1)}), bf16[4,256,384]{1,2,0:T(8,128)(2,1)S(1)}, u32[]{:S(2)}, u32[]{:S(2)}) async-start(bf16[4,256,384]{1,2,0:T(8,128)(2,1)} %copy.19), calls=%async_computation.2 | async-start | bytes 1572864 | tf_op jit(solution)/shard_map/all_to_all | solution.py:87
  266.6 1.3 copy-start.5
Sparse Core Ops, SparseCore 0:
  29.1 46.3 all-gather.2
  172.0 46.8 all-gather.4

commit v6 on v3

--- a/solution.py
+++ b/solution.py
@@ -12,6 +12,7 @@
 X_SIZE = 4
 TILE = 256
 STATS = 128
+PARTS = 3
 
 
 def shifted(value, axis, steps):
@@ -28,6 +29,16 @@
 
 def project(normed, weight):
     return jnp.dot(normed, weight, preferred_element_type=jnp.float32).astype(jnp.bfloat16)
+
+
+def split_parts(value, count):
+    parts = []
+    rest = value
+    for unused in range(count):
+        part = rest.astype(jnp.bfloat16).astype(jnp.float32)
+        parts.append(part)
+        rest = rest - part
+    return parts
 
 
 def partial_kernel(q_ref, k_ref, v_ref, o_ref):
@@ -46,10 +57,12 @@
         summed = jnp.sum(weights, axis=1, keepdims=True)
         o_ref[:, cols] = jnp.dot(
             weights.astype(jnp.bfloat16), v_ref[:, cols], preferred_element_type=jnp.float32
-        )
-        stats = jnp.where(lane == h, largest, stats)
-        stats = jnp.where(lane == heads + h, summed, stats)
-    o_ref[:, heads * HEAD_DIM:] = stats
+        ).astype(o_ref.dtype)
+        for kind, value in enumerate((largest, summed)):
+            for piece, part in enumerate(split_parts(value, PARTS)):
+                slot = (kind * heads + h) * PARTS + piece
+                stats = jnp.where(lane == slot, part, stats)
+    o_ref[:, heads * HEAD_DIM:] = stats.astype(o_ref.dtype)
 
 
 def partial_attend(queries, pairs):
@@ -64,7 +77,7 @@
             pl.BlockSpec((None, keys, width), lambda i: (1, 0, 0)),
         ],
         out_specs=pl.BlockSpec((TILE, width + STATS), lambda i: (i, 0)),
-        out_shape=jax.ShapeDtypeStruct((rows, width + STATS), jnp.float32),
+        out_shape=jax.ShapeDtypeStruct((rows, width + STATS), jnp.bfloat16),
         compiler_params=pltpu.CompilerParams(vmem_limit_bytes=48 * 1024 * 1024),
     )(queries, pairs, pairs)
 
@@ -74,20 +87,22 @@
     heads = width // HEAD_DIM
     query_block = lax.all_gather(queries, "bx", axis=0, tiled=True)
     key_block = lax.all_gather(pairs, "bz", axis=1, tiled=True)
-    if riders is not None:
-        key_block, riders = lax.optimization_barrier((key_block, riders))
     partial = partial_attend(query_block, key_block)
     parts = lax.all_to_all(partial, "bx", 0, 0, tiled=True)
-    parts = parts.reshape(-1, rows, width + STATS)
+    parts = parts.reshape(-1, rows, width + STATS).astype(jnp.float32)
     outs = parts[:, :, :width].reshape(-1, rows, heads, HEAD_DIM)
-    maxes = parts[:, :, width:width + heads]
-    sums = parts[:, :, width + heads:width + 2 * heads]
+    stats = parts[:, :, width:width + 2 * heads * PARTS].reshape(-1, rows, 2, heads, PARTS)
+    stats = jnp.sum(stats, axis=-1)
+    maxes = stats[:, :, 0]
+    sums = stats[:, :, 1]
     top = jnp.max(maxes, axis=0)
     scale = jnp.exp(maxes - top[None])
     total = jnp.sum(sums * scale, axis=0)
     merged = jnp.sum(outs * scale[..., None], axis=0) / total[..., None]
     merged = merged.reshape(rows, width).astype(jnp.bfloat16)
-    return merged if riders is None else (merged, riders)
+    if riders is None:
+        return merged
+    return lax.optimization_barrier((merged, riders))
 
 
 def spread(block_of):

time: 287 us -> 246 us (0.86)
  waiting for transfers between devices: 140 us -> 97.7 us
  matrix products: 18.5 us -> 25.4 us
  local copies, waits for them, and re-layouts: 14.3 us -> 9.37 us
  blocking collectives: 56.1 us -> 51.3 us
  starting transfers between devices: 17.6 us -> 20.8 us
    ppermute x6, waiting for transfers between devices: 49.5 us -> 5.17 us  [spread(): lax.ppermute(piece, 'mp', [(j, (j + step) % count) for j in range(count)])]
    all_gather x2, waiting for transfers between devices: 34.2 us -> 60.7 us  [attend(): key_block = lax.all_gather(pairs, 'bz', axis=1, tiled=True)]
    all_to_all x2, waiting for transfers between devices: 48.5 us -> 23.5 us  [attend(): parts = lax.all_to_all(partial, 'bx', 0, 0, tiled=True)]
    dot_general x8, matrix products: 8.5 us -> 15.1 us  [project_out(): term = jnp.dot(piece, block, preferred_element_type=jnp.float32)]
    all_gather x1, blocking collectives: 12.3 us -> 7.83 us  [on_device(): self_attended = lax.all_gather(self_local, 'mp', axis=1, tiled=True)]
    unnamed x44 -> x30, local copies, waits for them, and re-layouts: 8.57 us -> 5.72 us
  transfers between devices with their start and end apart: 11 -> 11, of which waited for: 5 -> 6; matrix products, arithmetic and copies ran while one was open for 2% -> 3% of each run, Pallas kernels for 0% -> 5%
where the time goes in v6:
time: 246 us; the launch traced here: 245 us
  waiting for transfers between devices  97.7 us (40%)
  blocking collectives  51.3 us (21%)
  matrix products  25.4 us (10%)
  Pallas kernels  24.6 us (10%)
  starting transfers between devices  20.8 us (8%)
  between operations  13.8 us (6%)
  local copies, waits for them, and re-layouts  9.37 us (4%)
    all_gather x2, waiting for transfers between devices, attend(): key_block = lax.all_gather(pairs, 'bz', axis=1, tiled=True)  60.7 us
    pallas_call x2, Pallas kernels, partial_attend(): pl.pallas_call(partial_kernel, grid=(rows // TILE,), in_specs=[pl.BlockSp...  24.6 us
    all_to_all x2, waiting for transfers between devices, attend(): parts = lax.all_to_all(partial, 'bx', 0, 0, tiled=True)  23.5 us
    all_gather x2, blocking collectives, attend(): query_block = lax.all_gather(queries, 'bx', axis=0, tiled=True)  22.3 us
    dot_general x8, matrix products, project_out(): term = jnp.dot(piece, block, preferred_element_type=jnp.float32)  15.1 us
    all_gather x1, blocking collectives, on_device(): lax.all_gather(attend(cross_queries, arrived), 'mp', axis=1, tiled=True)  10.9 us
    all_gather x1, blocking collectives, on_device(): embedded_full = lax.all_gather(embedded, 'mp', axis=1, tiled=True)  10.3 us
    dot_general x6, matrix products, project(): jnp.dot(normed, weight, preferred_element_type=jnp.float32)  9.07 us
  transfers between devices with their start and end apart: 11, of which 6 were waited for; matrix products, arithmetic and copies ran while one was open for 3% of the time, Pallas kernels for 5%

profile of v6, /device:TPU:1, one launch (start us, length us, event | category | flops | bytes accessed | tf_op | source)
XLA Modules:
  0.0 244.9 jit_solution(6951442370787447321)
XLA Ops:
  6.5 0.0 copy-start
  6.5 0.0 all-gather.3.cloned.1.call-start
  6.5 0.9 copy-done
  7.5 1.2 fusion.54
  8.7 10.3 %all_gather.21 = bf16[256,1536]{1,0:T(8,128)(2,1)S(1)} all-gather(bf16[256,384]{1,0:T(8,128)(2,1)S(1)} %fusion.54), channel_id=1, replica_groups=mesh['segment'=2,'bz'=8,'bx'=4,'mp'=4] {'mp'}, dimensions={1}, use_global_device_ids=true | all-gather | bytes 983040 | tf_op jit(solution)/shard_map/all_gather | solution.py:154
  19.0 0.2 fusion.9
  19.2 0.0 copy-done.11
  19.2 1.9 fusion.63
  21.1 1.9 fusion.66
  23.0 0.8 pad_maximum_fusion
  23.8 0.0 all-gather.3.cloned.1.call-update
  23.9 1.7 collective-permute-start
  25.6 0.0 collective-permute-start.1
  25.7 0.7 collective-permute-start.2
  26.3 1.9 fusion.35
  28.2 11.4 %all_gather.22.q_ref = bf16[1024,384]{1,0:T(8,128)(2,1)S(1)} all-gather(bf16[256,384]{1,0:T(8,128)(2,1)S(1)} %fusion.35), channel_id=1, replica_groups=mesh['segment'=2,'bz'=8,'bx'=4,'mp'=4] {'bx'}, dimensions={0}, use_global_device_ids=true | all-gather | bytes 983040 | tf_op jit(solution)/shard_map/all_gather | solution.py:88
  39.7 30.7 %all-gather.3.cloned.1.call-done.k_ref.v_ref = bf16[2,2048,384]{2,1,0:T(8,128)(2,1)} async-done(((bf16[2,256,384]{2,1,0:T(8,128)(2,1)}), bf16[2,2048,384]{2,1,0:T(8,128)(2,1)}) %all-gather.3.cloned.1.call-update) | async-done | bytes 3145744 | tf_op jit(solution)/shard_map/all_gather | solution.py:89
  70.4 1.9 copy-done.1
  72.3 12.3 %shard_map.100 = bf16[1024,512]{1,0:T(8,128)(2,1)S(1)} custom-call(bf16[1024,384]{1,0:T(8,128)(2,1)S(1)} %all_gather.22.q_ref, bf16[2,2048,384]{2,1,0:T(8,128)(2,1)S(1)} %copy-done.1, bf16[2,2048,384]{2,1,0:T(8,128)(2,1)S(1)} %copy-done.1), custom_call_target="tpu_custom_call" | custom-call | tf_op jit(solution)/shard_map/pallas_call | solution.py:71
  84.6 1.3 copy.15
  85.9 4.1 %all-to-all-start = ((bf16[4,256,512]{1,2,0:T(8,128)(2,1)}), bf16[4,256,512]{1,2,0:T(8,128)(2,1)S(1)}, u32[]{:S(2)}, u32[]{:S(2)}) async-start(bf16[4,256,512]{1,2,0:T(8,128)(2,1)} %copy.15), calls=%async_computation | async-start | bytes 2097152 | tf_op jit(solution)/shard_map/all_to_all | solution.py:91
  90.0 1.0 constant_dynamic-slice_fusion
  90.9 2.6 %collective-permute-start.3 = (bf16[384,384]{1,0:T(8,128)(2,1)}, bf16[384,384]{1,0:T(8,128)(2,1)S(1)}, u32[]{:S(2)}, u32[]{:S(2)}) collective-permute-start(bf16[384,384]{1,0:T(8,128)(2,1)} %get-tuple-element.44), channel_id=1, source_target_pairs={{0,1},{1,2},{2,3},{3,0},{4,5},{5,6},{6,7},{7,4},{8,9},{9,10},{10,1... | collective-permute-start | bytes 884744 | tf_op jit(solution)/shard_map/ppermute | solution.py:114
  93.5 0.3 collective-permute-start.4
  93.8 9.8 %all-to-all-done = bf16[4,256,512]{1,2,0:T(8,128)(2,1)S(1)} async-done(((bf16[4,256,512]{1,2,0:T(8,128)(2,1)}), bf16[4,256,512]{1,2,0:T(8,128)(2,1)S(1)}, u32[]{:S(2)}, u32[]{:S(2)}) %all-to-all-start) | async-done | bytes 1048608 | tf_op jit(solution)/shard_map/all_to_all | solution.py:91
  103.7 0.0 collective-permute-done.3
  103.7 2.5 %collective-permute-start.5 = (bf16[384,384]{1,0:T(8,128)(2,1)S(1)}, bf16[384,384]{1,0:T(8,128)(2,1)}, u32[]{:S(2)}, u32[]{:S(2)}) collective-permute-start(bf16[384,384]{1,0:T(8,128)(2,1)S(1)} %get-tuple-element.43), channel_id=1, source_target_pairs={{0,3},{1,0},{2,1},{3,2},{4,7},{5,4},{6,5},{7,6},{8,11},{9,8},{10,9... | collective-permute-start | bytes 884744 | tf_op jit(solution)/shard_map/ppermute | solution.py:114
  106.3 0.2 convert_element_type.74
  106.5 0.1 fusion.13
  106.6 0.0 collective-permute-done.4
  106.6 0.0 copy-start.9
  106.6 5.2 %collective-permute-done.5 = bf16[384,384]{1,0:T(8,128)(2,1)} collective-permute-done((bf16[384,384]{1,0:T(8,128)(2,1)S(1)}, bf16[384,384]{1,0:T(8,128)(2,1)}, u32[]{:S(2)}, u32[]{:S(2)}) %collective-permute-start.5) | collective-permute-done | bytes 294944 | tf_op jit(solution)/shard_map/ppermute | solution.py:114
  111.8 0.0 collective-permute-done
  111.8 0.0 collective-permute-done.1
  111.8 0.0 collective-permute-done.2
  111.8 7.8 %all_gather.24 = bf16[256,1536]{0,1:T(8,128)(2,1)S(1)} all-gather(bf16[256,384]{0,1:T(8,128)(2,1)S(1)} %fusion.73), channel_id=1, replica_groups=mesh['segment'=2,'bz'=8,'bx'=4,'mp'=4] {'mp'}, dimensions={1}, use_global_device_ids=true | all-gather | bytes 983040 | tf_op jit(solution)/shard_map/all_gather | solution.py:163
  119.7 1.9 fusion.84
  121.5 3.0 %fusion.86 = f32[256,1536]{1,0:T(8,128)} fusion(bf16[384,1536]{1,0:T(8,128)(2,1)} %collective-permute-done.1, bf16[256,1536]{0,1:T(8,128)(2,1)S(1)} %all_gather.24, s32[]{:T(128)S(6)} %select_n.82), kind=kOutput, calls=%fused_computation.77 | convolution fusion | flops 301989888 | bytes 2949124 | tf_op jit(solution)/shard_map/dot_general | solution.py:124
  124.6 3.0 %fusion.88 = f32[256,1536]{1,0:T(8,128)} fusion(bf16[384,1536]{1,0:T(8,128)(2,1)} %collective-permute-done, bf16[256,1536]{0,1:T(8,128)(2,1)S(1)} %all_gather.24, s32[]{:T(128)S(6)} %select_n.81), kind=kOutput, calls=%fused_computation.79 | convolution fusion | flops 301989888 | bytes 2949124 | tf_op jit(solution)/shard_map/dot_general | solution.py:124
  127.6 3.2 %fusion.8 = (f32[256]{0:T(256)S(1)}, bf16[256,1536]{1,0:T(8,128)(2,1)S(1)}) fusion(f32[256,1536]{1,0:T(8,128)S(1)} %fusion.84, f32[256,1536]{1,0:T(8,128)} %fusion.86, f32[256,1536]{1,0:T(8,128)} %fusion.88, bf16[384,1536]{1,0:T(8,128)(2,1)} %bitcast.14, bf16[256,1536]{0,1:T(8,128)(2,1)S(1)} %all_gather.24, s32[]{:T(128)S(6)} %select_n.80, ...), kind=kOutput, calls=%fused_computation.13 | convolution fusion | flops 305528576 | bytes 7668740 | tf_op jit(solution)/shard_map/dot_general | solution.py:124
  130.9 0.0 copy-done.12
  130.9 0.0 copy-done.13
  130.9 0.6 fusion.57
  131.5 0.2 copy-done.3
  131.7 0.6 fusion.60
  132.4 4.9 %collective-permute-start.6 = (bf16[2,256,384]{2,1,0:T(8,128)(2,1)S(1)}, bf16[2,256,384]{2,1,0:T(8,128)(2,1)S(1)}, u32[]{:S(2)}, u32[]{:S(2)}) collective-permute-start(bf16[2,256,384]{2,1,0:T(8,128)(2,1)S(1)} %pad_maximum_fusion.1), channel_id=1, source_target_pairs={{0,128},{1,129},{2,130},{3,131},{4,132},{5,133},{6,134},{7,135},{8... | collective-permute-start | bytes 1179656 | tf_op jit(solution)/shard_map/ppermute | solution.py:21
  137.4 8.3 %collective-permute-done.6 = bf16[2,256,384]{2,1,0:T(8,128)(2,1)S(1)} collective-permute-done((bf16[2,256,384]{2,1,0:T(8,128)(2,1)S(1)}, bf16[2,256,384]{2,1,0:T(8,128)(2,1)S(1)}, u32[]{:S(2)}, u32[]{:S(2)}) %collective-permute-start.6) | collective-permute-done | bytes 393248 | tf_op jit(solution)/shard_map/ppermute | solution.py:21
  145.7 0.8 copy-done.6
  146.4 0.0 all-gather.5.cloned.1.call-update
  146.4 2.1 fusion.44
  148.6 10.8 %all_gather.25.q_ref = bf16[1024,384]{1,0:T(8,128)(2,1)S(1)} all-gather(bf16[256,384]{1,0:T(8,128)(2,1)S(1)} %fusion.44), channel_id=1, replica_groups=mesh['segment'=2,'bz'=8,'bx'=4,'mp'=4] {'bx'}, dimensions={0}, use_global_device_ids=true | all-gather | bytes 983040 | tf_op jit(solution)/shard_map/all_gather | solution.py:88
  159.4 30.0 %all-gather.5.cloned.1.call-done.k_ref.v_ref = bf16[2,2048,384]{2,1,0:T(8,128)(2,1)} async-done(((bf16[2,256,384]{2,1,0:T(8,128)(2,1)}), bf16[2,2048,384]{2,1,0:T(8,128)(2,1)}) %all-gather.5.cloned.1.call-update) | async-done | bytes 3145744 | tf_op jit(solution)/shard_map/all_gather | solution.py:89
  189.4 1.9 copy-done.2
  191.3 12.3 %shard_map.101 = bf16[1024,512]{1,0:T(8,128)(2,1)S(1)} custom-call(bf16[1024,384]{1,0:T(8,128)(2,1)S(1)} %all_gather.25.q_ref, bf16[2,2048,384]{2,1,0:T(8,128)(2,1)S(1)} %copy-done.2, bf16[2,2048,384]{2,1,0:T(8,128)(2,1)S(1)} %copy-done.2), custom_call_target="tpu_custom_call" | custom-call | tf_op jit(solution)/shard_map/pallas_call | solution.py:71
  203.6 1.3 copy.18
  204.9 4.0 %all-to-all-start.1 = ((bf16[4,256,512]{1,2,0:T(8,128)(2,1)}), bf16[4,256,512]{1,2,0:T(8,128)(2,1)S(1)}, u32[]{:S(2)}, u32[]{:S(2)}) async-start(bf16[4,256,512]{1,2,0:T(8,128)(2,1)} %copy.18), calls=%async_computation.1 | async-start | bytes 2097152 | tf_op jit(solution)/shard_map/all_to_all | solution.py:91
  208.9 13.7 %all-to-all-done.1 = bf16[4,256,512]{1,2,0:T(8,128)(2,1)S(1)} async-done(((bf16[4,256,512]{1,2,0:T(8,128)(2,1)}), bf16[4,256,512]{1,2,0:T(8,128)(2,1)S(1)}, u32[]{:S(2)}, u32[]{:S(2)}) %all-to-all-start.1) | async-done | bytes 1048608 | tf_op jit(solution)/shard_map/all_to_all | solution.py:91
  222.7 0.2 convert_element_type.84
  222.9 0.1 fusion.12
  223.1 10.9 %all_gather.27 = bf16[256,1536]{0,1:T(8,128)(2,1)S(1)} all-gather(bf16[256,384]{0,1:T(8,128)(2,1)S(1)} %fusion.72), channel_id=1, replica_groups=mesh['segment'=2,'bz'=8,'bx'=4,'mp'=4] {'mp'}, dimensions={1}, use_global_device_ids=true | all-gather | bytes 983040 | tf_op jit(solution)/shard_map/all_gather | solution.py:174
  234.0 1.3 fusion.77
  235.3 0.3 fusion.79
  235.7 0.3 fusion.81
  236.0 2.0 fusion.56
  (39 shorter events, 0.4 us)
Async XLA Ops:
  6.5 0.9 copy-start
  6.5 12.7 %copy-start.11 = (f32[1,1536]{1,0:T(1,128)S(1)}, f32[1,1536]{1,0:T(1,128)}, u32[]{:S(2)}) copy-start(f32[1,1536]{1,0:T(1,128)} %param.13) | copy-start | bytes 18436
  6.5 63.8 %all-gather.3.cloned.1.call-start = ((), (), s32[]{:S(2)}) async-start(), calls=%async_computation.2 | async-start | bytes 3538944 | tf_op jit(solution)/shard_map/all_gather | solution.py:89
  23.9 87.9 %collective-permute-start = (bf16[384,1536]{1,0:T(8,128)(2,1)}, bf16[384,1536]{1,0:T(8,128)(2,1)}, u32[]{:S(2)}, u32[]{:S(2)}) collective-permute-start(bf16[384,1536]{1,0:T(8,128)(2,1)} %bitcast.14), channel_id=1, source_target_pairs={{0,1},{1,2},{2,3},{3,0},{4,5},{5,6},{6,7},{7,4},{8,9},{9,10},{10,1... | collective-permute-start | bytes 3538952 | tf_op jit(solution)/shard_map/ppermute | solution.py:114
  25.6 86.2 %collective-permute-start.1 = (bf16[384,1536]{1,0:T(8,128)(2,1)}, bf16[384,1536]{1,0:T(8,128)(2,1)}, u32[]{:S(2)}, u32[]{:S(2)}) collective-permute-start(bf16[384,1536]{1,0:T(8,128)(2,1)} %bitcast.14), channel_id=1, source_target_pairs={{0,2},{1,3},{2,0},{3,1},{4,6},{5,7},{6,4},{7,5},{8,10},{9,11},{10,... | collective-permute-start | bytes 3538952 | tf_op jit(solution)/shard_map/ppermute | solution.py:114
  25.7 86.2 %collective-permute-start.2 = (bf16[384,1536]{1,0:T(8,128)(2,1)}, bf16[384,1536]{1,0:T(8,128)(2,1)}, u32[]{:S(2)}, u32[]{:S(2)}) collective-permute-start(bf16[384,1536]{1,0:T(8,128)(2,1)} %bitcast.14), channel_id=1, source_target_pairs={{0,3},{1,0},{2,1},{3,2},{4,7},{5,4},{6,5},{7,6},{8,11},{9,8},{10,9... | collective-permute-start | bytes 3538952 | tf_op jit(solution)/shard_map/ppermute | solution.py:114
  70.4 1.9 copy-start.1
  85.9 4.1 %copy-start.4 = (bf16[384,1536]{1,0:T(8,128)(2,1)S(1)}, bf16[384,1536]{1,0:T(8,128)(2,1)}, u32[]{:S(2)}) copy-start(bf16[384,1536]{1,0:T(8,128)(2,1)} %param.19) | copy-start | bytes 3538948
  85.9 17.8 %all-to-all-start = ((bf16[4,256,512]{1,2,0:T(8,128)(2,1)}), bf16[4,256,512]{1,2,0:T(8,128)(2,1)S(1)}, u32[]{:S(2)}, u32[]{:S(2)}) async-start(bf16[4,256,512]{1,2,0:T(8,128)(2,1)} %copy.15), calls=%async_computation | async-start | bytes 2097152 | tf_op jit(solution)/shard_map/all_to_all | solution.py:91
  90.0 99.4 %all-gather.5.cloned.1.call-start = ((), (), s32[]{:S(2)}) async-start(), calls=%async_computation.3 | async-start | bytes 3538944 | tf_op jit(solution)/shard_map/all_gather | solution.py:89
  90.9 12.8 %collective-permute-start.3 = (bf16[384,384]{1,0:T(8,128)(2,1)}, bf16[384,384]{1,0:T(8,128)(2,1)S(1)}, u32[]{:S(2)}, u32[]{:S(2)}) collective-permute-start(bf16[384,384]{1,0:T(8,128)(2,1)} %get-tuple-element.44), channel_id=1, source_target_pairs={{0,1},{1,2},{2,3},{3,0},{4,5},{5,6},{6,7},{7,4},{8,9},{9,10},{10,1... | collective-permute-start | bytes 884744 | tf_op jit(solution)/shard_map/ppermute | solution.py:114
  93.5 13.1 %collective-permute-start.4 = (bf16[384,384]{1,0:T(8,128)(2,1)}, bf16[384,384]{1,0:T(8,128)(2,1)S(1)}, u32[]{:S(2)}, u32[]{:S(2)}) collective-permute-start(bf16[384,384]{1,0:T(8,128)(2,1)} %get-tuple-element.46), channel_id=1, source_target_pairs={{0,2},{1,3},{2,0},{3,1},{4,6},{5,7},{6,4},{7,5},{8,10},{9,11},{10,... | collective-permute-start | bytes 884744 | tf_op jit(solution)/shard_map/ppermute | solution.py:114
  103.7 2.7 %copy-start.7 = (bf16[384,384]{1,0:T(8,128)(2,1)}, bf16[384,384]{1,0:T(8,128)(2,1)S(1)}, u32[]{:S(2)}) copy-start(bf16[384,384]{1,0:T(8,128)(2,1)S(1)} %collective-permute-done.3) | copy-start | bytes 884740
  103.7 8.1 %collective-permute-start.5 = (bf16[384,384]{1,0:T(8,128)(2,1)S(1)}, bf16[384,384]{1,0:T(8,128)(2,1)}, u32[]{:S(2)}, u32[]{:S(2)}) collective-permute-start(bf16[384,384]{1,0:T(8,128)(2,1)S(1)} %get-tuple-element.43), channel_id=1, source_target_pairs={{0,3},{1,0},{2,1},{3,2},{4,7},{5,4},{6,5},{7,6},{8,11},{9,8},{10,9... | collective-permute-start | bytes 884744 | tf_op jit(solution)/shard_map/ppermute | solution.py:114
  106.6 5.2 %copy-start.9 = (bf16[384,384]{1,0:T(8,128)(2,1)}, bf16[384,384]{1,0:T(8,128)(2,1)S(1)}, u32[]{:S(2)}) copy-start(bf16[384,384]{1,0:T(8,128)(2,1)S(1)} %collective-permute-done.4) | copy-start | bytes 884740
  127.6 3.3 %copy-start.12 = (bf16[3,1536,384]{2,1,0:T(8,128)(2,1)S(1)}, bf16[3,1536,384]{2,1,0:T(8,128)(2,1)}, u32[]{:S(2)}) copy-start(bf16[3,1536,384]{2,1,0:T(8,128)(2,1)} %param.18) | copy-start | bytes 10616836
  127.6 3.3 %copy-start.13 = (f32[1536]{0:T(1024)S(1)}, f32[1536]{0:T(1024)}, u32[]{:S(2)}) copy-start(f32[1536]{0:T(1024)} %param.17) | copy-start | bytes 18436
  130.9 0.9 copy-start.3
  131.7 14.7 %copy-start.14 = (f32[1536]{0:T(1024)S(1)}, f32[1536]{0:T(1024)}, u32[]{:S(2)}) copy-start(f32[1536]{0:T(1024)} %param.16) | copy-start | bytes 18436
  132.4 13.2 %collective-permute-start.6 = (bf16[2,256,384]{2,1,0:T(8,128)(2,1)S(1)}, bf16[2,256,384]{2,1,0:T(8,128)(2,1)S(1)}, u32[]{:S(2)}, u32[]{:S(2)}) collective-permute-start(bf16[2,256,384]{2,1,0:T(8,128)(2,1)S(1)} %pad_maximum_fusion.1), channel_id=1, source_target_pairs={{0,128},{1,129},{2,130},{3,131},{4,132},{5,133},{6,134},{7,135},{8... | collective-permute-start | bytes 1179656 | tf_op jit(solution)/shard_map/ppermute | solution.py:21
  145.7 0.8 copy-start.6
  189.4 1.9 copy-start.2
  204.9 17.6 %all-to-all-start.1 = ((bf16[4,256,512]{1,2,0:T(8,128)(2,1)}), bf16[4,256,512]{1,2,0:T(8,128)(2,1)S(1)}, u32[]{:S(2)}, u32[]{:S(2)}) async-start(bf16[4,256,512]{1,2,0:T(8,128)(2,1)} %copy.18), calls=%async_computation.1 | async-start | bytes 2097152 | tf_op jit(solution)/shard_map/all_to_all | solution.py:91
  223.0 12.3 %copy-start.10 = (bf16[384,384]{1,0:T(8,128)(2,1)S(1)}, bf16[384,384]{1,0:T(8,128)(2,1)}, u32[]{:S(2)}) copy-start(bf16[384,384]{1,0:T(8,128)(2,1)} %copy-done.9) | copy-start | bytes 884740
  223.0 12.7 %copy-start.8 = (bf16[384,384]{1,0:T(8,128)(2,1)S(1)}, bf16[384,384]{1,0:T(8,128)(2,1)}, u32[]{:S(2)}) copy-start(bf16[384,384]{1,0:T(8,128)(2,1)} %copy-done.7) | copy-start | bytes 884740
  234.0 2.0 copy-start.5
Sparse Core Ops, SparseCore 0:
  24.0 46.3 all-gather.2
  146.6 42.8 all-gather.4

commit v7 on v6

--- a/solution.py
+++ b/solution.py
@@ -88,6 +88,8 @@
     query_block = lax.all_gather(queries, "bx", axis=0, tiled=True)
     key_block = lax.all_gather(pairs, "bz", axis=1, tiled=True)
     partial = partial_attend(query_block, key_block)
+    if riders is not None:
+        partial, riders = lax.optimization_barrier((partial, riders))
     parts = lax.all_to_all(partial, "bx", 0, 0, tiled=True)
     parts = parts.reshape(-1, rows, width + STATS).astype(jnp.float32)
     outs = parts[:, :, :width].reshape(-1, rows, heads, HEAD_DIM)
@@ -100,9 +102,7 @@
     total = jnp.sum(sums * scale, axis=0)
     merged = jnp.sum(outs * scale[..., None], axis=0) / total[..., None]
     merged = merged.reshape(rows, width).astype(jnp.bfloat16)
-    if riders is None:
-        return merged
-    return lax.optimization_barrier((merged, riders))
+    return merged if riders is None else (merged, riders)
 
 
 def spread(block_of):
@@ -118,12 +118,12 @@
 
 def project_out(attended_full, blocks):
     width = blocks[0][1].shape[0]
-    total = None
-    for source, block in blocks:
-        piece = lax.dynamic_slice_in_dim(attended_full, source * width, width, axis=1)
-        term = jnp.dot(piece, block, preferred_element_type=jnp.float32)
-        total = term if total is None else total + term
-    return total
+    pieces = [
+        lax.dynamic_slice_in_dim(attended_full, source * width, width, axis=1)
+        for source, unused in blocks
+    ]
+    weight = jnp.concatenate([block for unused, block in blocks], axis=0)
+    return jnp.dot(jnp.concatenate(pieces, axis=1), weight, preferred_element_type=jnp.float32)
 
 
 def on_device(

time: 246 us -> 261 us (1.061)
  waiting for transfers between devices: 97.7 us -> 123 us
  matrix products: 25.4 us -> 16.2 us
    ppermute x6, waiting for transfers between devices: 5.17 us -> 51.9 us  [spread(): lax.ppermute(piece, 'mp', [(j, (j + step) % count) for j in range(count)])]
    all_gather x2, waiting for transfers between devices: 60.7 us -> 34.1 us  [attend(): key_block = lax.all_gather(pairs, 'bz', axis=1, tiled=True)]
    dot_general x8 -> x2, matrix products: 15.1 us -> 6.01 us  [project_out(): jnp.dot(jnp.concatenate(pieces, axis=1), weight, preferred_element_type=j...]
    all_to_all x2, waiting for transfers between devices: 23.5 us -> 28.2 us  [attend(): parts = lax.all_to_all(partial, 'bx', 0, 0, tiled=True)]
    unnamed x30 -> x24, local copies, waits for them, and re-layouts: 5.72 us -> 5.48 us
  transfers between devices with their start and end apart: 11 -> 11, of which waited for: 6 -> 5; matrix products, arithmetic and copies ran while one was open for 3% -> 2% of each run, Pallas kernels for 5% -> 5%
where the time goes in v7:
time: 261 us
  waiting for transfers between devices  123 us (47%)
  blocking collectives  53.6 us (21%)
  Pallas kernels  24.7 us (9%)
  starting transfers between devices  18.7 us (7%)
  matrix products  16.2 us (6%)
  between operations  13.8 us (5%)
  local copies, waits for them, and re-layouts  9.12 us (3%)
    ppermute x6, waiting for transfers between devices, spread(): lax.ppermute(piece, 'mp', [(j, (j + step) % count) for j in range(count)])  51.9 us
    all_gather x2, waiting for transfers between devices, attend(): key_block = lax.all_gather(pairs, 'bz', axis=1, tiled=True)  34.1 us
    all_to_all x2, waiting for transfers between devices, attend(): parts = lax.all_to_all(partial, 'bx', 0, 0, tiled=True)  28.2 us
    pallas_call x2, Pallas kernels, partial_attend(): pl.pallas_call(partial_kernel, grid=(rows // TILE,), in_specs=[pl.BlockSp...  24.7 us
    all_gather x2, blocking collectives, attend(): query_block = lax.all_gather(queries, 'bx', axis=0, tiled=True)  23.4 us
    all_gather x1, blocking collectives, on_device(): lax.all_gather(attend(cross_queries, arrived), 'mp', axis=1, tiled=True)  10.9 us
    all_gather x1, blocking collectives, on_device(): embedded_full = lax.all_gather(embedded, 'mp', axis=1, tiled=True)  10.3 us
    all_gather x1, blocking collectives, on_device(): self_attended = lax.all_gather(self_local, 'mp', axis=1, tiled=True)  9.02 us
  transfers between devices with their start and end apart: 11, of which 5 were waited for; matrix products, arithmetic and copies ran while one was open for 2% of the time, Pallas kernels for 5%

profile of v7, /device:TPU:1, one launch (start us, length us, event | category | flops | bytes accessed | tf_op | source)
XLA Modules:
  0.0 260.5 jit_solution(7277077627137697655)
XLA Ops:
  6.5 0.0 copy-start
  6.5 0.0 all-gather.3.cloned.1.call-start
  6.5 0.9 copy-done
  7.5 1.2 fusion.67
  8.7 10.3 %all_gather.21 = bf16[256,1536]{1,0:T(8,128)(2,1)S(1)} all-gather(bf16[256,384]{1,0:T(8,128)(2,1)S(1)} %fusion.67), channel_id=1, replica_groups=mesh['segment'=2,'bz'=8,'bx'=4,'mp'=4] {'mp'}, dimensions={1}, use_global_device_ids=true | all-gather | bytes 983040 | tf_op jit(solution)/shard_map/all_gather | solution.py:154
  19.0 0.2 fusion.19
  19.2 0.0 copy-done.5
  19.2 1.9 fusion.80
  21.1 0.0 copy-start.3
  21.2 2.0 fusion.77
  23.1 0.8 pad_maximum_fusion
  24.0 0.0 all-gather.3.cloned.1.call-update
  24.0 0.2 collective-permute-start.2
  24.2 1.6 collective-permute-start.1
  25.8 1.9 collective-permute-start
  27.7 0.0 copy-done.3
  27.7 0.8 constant_dynamic-slice_fusion.8
  28.5 0.0 collective-permute-start.5
  28.5 1.7 collective-permute-start.3
  30.3 1.9 fusion.49
  32.2 51.8 %collective-permute-done.5 = bf16[384,384]{1,0:T(8,128)(2,1)S(1)} collective-permute-done((bf16[384,384]{1,0:T(8,128)(2,1)S(1)}, bf16[384,384]{1,0:T(8,128)(2,1)S(1)}, u32[]{:S(2)}, u32[]{:S(2)}) %collective-permute-start.5) | collective-permute-done | bytes 294944 | tf_op jit(solution)/shard_map/ppermute | solution.py:114
  84.0 1.3 collective-permute-start.4
  85.3 12.6 %all_gather.22.q_ref = bf16[1024,384]{1,0:T(8,128)(2,1)S(1)} all-gather(bf16[256,384]{1,0:T(8,128)(2,1)S(1)} %fusion.49), channel_id=1, replica_groups=mesh['segment'=2,'bz'=8,'bx'=4,'mp'=4] {'bx'}, dimensions={0}, use_global_device_ids=true | all-gather | bytes 983040 | tf_op jit(solution)/shard_map/all_gather | solution.py:88
  97.9 0.0 copy-done.8
  97.9 1.9 copy-done.1
  99.8 12.4 %shard_map.100 = bf16[1024,512]{1,0:T(8,128)(2,1)S(1)} custom-call(bf16[1024,384]{1,0:T(8,128)(2,1)S(1)} %all_gather.22.q_ref, bf16[2,2048,384]{2,1,0:T(8,128)(2,1)S(1)} %copy-done.1, bf16[2,2048,384]{2,1,0:T(8,128)(2,1)S(1)} %copy-done.1), custom_call_target="tpu_custom_call" | custom-call | tf_op jit(solution)/shard_map/pallas_call | solution.py:71
  112.2 0.0 collective-permute-done.3
  112.2 0.0 collective-permute-done.4
  112.2 0.0 collective-permute-done.2
  112.2 0.0 collective-permute-done.1
  112.2 0.0 collective-permute-done
  112.2 1.3 copy.15
  113.5 3.5 %all-to-all-start = ((bf16[4,256,512]{1,2,0:T(8,128)(2,1)}), bf16[4,256,512]{1,2,0:T(8,128)(2,1)S(1)}, u32[]{:S(2)}, u32[]{:S(2)}) async-start(bf16[4,256,512]{1,2,0:T(8,128)(2,1)} %copy.15), calls=%async_computation | async-start | bytes 2097152 | tf_op jit(solution)/shard_map/all_to_all | solution.py:93
  117.1 0.0 all-gather.5.cloned.1.call-start
  117.1 14.5 %all-to-all-done = bf16[4,256,512]{1,2,0:T(8,128)(2,1)S(1)} async-done(((bf16[4,256,512]{1,2,0:T(8,128)(2,1)}), bf16[4,256,512]{1,2,0:T(8,128)(2,1)S(1)}, u32[]{:S(2)}, u32[]{:S(2)}) %all-to-all-start) | async-done | bytes 1048608 | tf_op jit(solution)/shard_map/all_to_all | solution.py:93
  131.8 0.2 convert_element_type.74
  132.0 0.1 fusion.23
  132.1 0.0 copy-start.7
  132.2 9.0 %all_gather.24 = bf16[256,1536]{0,1:T(8,128)(2,1)S(1)} all-gather(bf16[256,384]{0,1:T(8,128)(2,1)S(1)} %fusion.107), channel_id=1, replica_groups=mesh['segment'=2,'bz'=8,'bx'=4,'mp'=4] {'mp'}, dimensions={1}, use_global_device_ids=true | all-gather | bytes 983040 | tf_op jit(solution)/shard_map/all_gather | solution.py:163
  141.2 0.1 constant_dynamic-slice_fusion.7
  141.3 0.0 copy-start.6
  141.3 0.0 copy-start.10
  141.3 3.7 %fusion.18 = (f32[256]{0:T(256)S(1)}, bf16[256,1536]{1,0:T(8,128)(2,1)S(1)}) fusion(bf16[384,1536]{1,0:T(8,128)(2,1)} %collective-permute-done.2, bf16[384,1536]{1,0:T(8,128)(2,1)} %collective-permute-done.1, bf16[384,1536]{1,0:T(8,128)(2,1)} %collective-permute-done, bf16[384,1536]{1,0:T(8,128)(2,1)S(1)} %bitcast.102, ...), kind=kOutput, calls=%fused_computation.18 | convolution fusion | flops 1232338688 | bytes 7078912 | tf_op jit(solution)/shard_map/dot_general | solution.py:126
  145.0 0.6 fusion.71
  145.6 0.0 copy-start.11
  145.7 0.6 fusion.74
  146.3 4.4 %collective-permute-start.6 = (bf16[2,256,384]{2,1,0:T(8,128)(2,1)S(1)}, bf16[2,256,384]{2,1,0:T(8,128)(2,1)S(1)}, u32[]{:S(2)}, u32[]{:S(2)}) collective-permute-start(bf16[2,256,384]{2,1,0:T(8,128)(2,1)S(1)} %pad_maximum_fusion.1), channel_id=1, source_target_pairs={{0,128},{1,129},{2,130},{3,131},{4,132},{5,133},{6,134},{7,135},{8... | collective-permute-start | bytes 1179656 | tf_op jit(solution)/shard_map/ppermute | solution.py:21
  150.8 8.3 %collective-permute-done.6 = bf16[2,256,384]{2,1,0:T(8,128)(2,1)S(1)} collective-permute-done((bf16[2,256,384]{2,1,0:T(8,128)(2,1)S(1)}, bf16[2,256,384]{2,1,0:T(8,128)(2,1)S(1)}, u32[]{:S(2)}, u32[]{:S(2)}) %collective-permute-start.6) | collective-permute-done | bytes 393248 | tf_op jit(solution)/shard_map/ppermute | solution.py:21
  159.0 0.7 copy-done.4
  159.8 0.0 all-gather.5.cloned.1.call-update
  159.8 0.0 copy-done.11
  159.8 1.9 fusion.58
  161.7 10.8 %all_gather.25.q_ref = bf16[1024,384]{1,0:T(8,128)(2,1)S(1)} all-gather(bf16[256,384]{1,0:T(8,128)(2,1)S(1)} %fusion.58), channel_id=1, replica_groups=mesh['segment'=2,'bz'=8,'bx'=4,'mp'=4] {'bx'}, dimensions={0}, use_global_device_ids=true | all-gather | bytes 983040 | tf_op jit(solution)/shard_map/all_gather | solution.py:88
  172.5 34.1 %all-gather.5.cloned.1.call-done.k_ref.v_ref = bf16[2,2048,384]{2,1,0:T(8,128)(2,1)} async-done(((bf16[2,256,384]{2,1,0:T(8,128)(2,1)}), bf16[2,2048,384]{2,1,0:T(8,128)(2,1)}) %all-gather.5.cloned.1.call-update) | async-done | bytes 3145744 | tf_op jit(solution)/shard_map/all_gather | solution.py:89
  206.6 1.9 copy-done.2
  208.5 12.3 %shard_map.101 = bf16[1024,512]{1,0:T(8,128)(2,1)S(1)} custom-call(bf16[1024,384]{1,0:T(8,128)(2,1)S(1)} %all_gather.25.q_ref, bf16[2,2048,384]{2,1,0:T(8,128)(2,1)S(1)} %copy-done.2, bf16[2,2048,384]{2,1,0:T(8,128)(2,1)S(1)} %copy-done.2), custom_call_target="tpu_custom_call" | custom-call | tf_op jit(solution)/shard_map/pallas_call | solution.py:71
  220.8 1.3 copy.18
  222.2 4.0 %all-to-all-start.1 = ((bf16[4,256,512]{1,2,0:T(8,128)(2,1)}), bf16[4,256,512]{1,2,0:T(8,128)(2,1)S(1)}, u32[]{:S(2)}, u32[]{:S(2)}) async-start(bf16[4,256,512]{1,2,0:T(8,128)(2,1)} %copy.18), calls=%async_computation.1 | async-start | bytes 2097152 | tf_op jit(solution)/shard_map/all_to_all | solution.py:93
  226.1 13.7 %all-to-all-done.1 = bf16[4,256,512]{1,2,0:T(8,128)(2,1)S(1)} async-done(((bf16[4,256,512]{1,2,0:T(8,128)(2,1)}), bf16[4,256,512]{1,2,0:T(8,128)(2,1)S(1)}, u32[]{:S(2)}, u32[]{:S(2)}) %all-to-all-start.1) | async-done | bytes 1048608 | tf_op jit(solution)/shard_map/all_to_all | solution.py:93
  239.9 0.2 convert_element_type.84
  240.1 0.1 fusion.22
  240.3 10.9 %all_gather.27 = bf16[256,1536]{0,1:T(8,128)(2,1)S(1)} all-gather(bf16[256,384]{0,1:T(8,128)(2,1)S(1)} %fusion.106), channel_id=1, replica_groups=mesh['segment'=2,'bz'=8,'bx'=4,'mp'=4] {'mp'}, dimensions={1}, use_global_device_ids=true | all-gather | bytes 983040 | tf_op jit(solution)/shard_map/all_gather | solution.py:174
  251.2 0.1 constant_dynamic-slice_fusion.3
  251.3 2.4 fusion.86
  (29 shorter events, 0.4 us)
Async XLA Ops:
  6.5 0.9 copy-start
  6.5 12.7 %copy-start.5 = (f32[1,1536]{1,0:T(1,128)S(1)}, f32[1,1536]{1,0:T(1,128)}, u32[]{:S(2)}) copy-start(f32[1,1536]{1,0:T(1,128)} %param.13) | copy-start | bytes 18436
  6.5 91.4 %all-gather.3.cloned.1.call-start = ((), (), s32[]{:S(2)}) async-start(), calls=%async_computation.2 | async-start | bytes 3538944 | tf_op jit(solution)/shard_map/all_gather | solution.py:89
  21.1 6.6 %copy-start.3 = (bf16[384,1536]{1,0:T(8,128)(2,1)S(1)}, bf16[384,1536]{1,0:T(8,128)(2,1)}, u32[]{:S(2)}) copy-start(bf16[384,1536]{1,0:T(8,128)(2,1)} %param.19) | copy-start | bytes 3538948
  24.0 88.2 %collective-permute-start.2 = (bf16[384,1536]{1,0:T(8,128)(2,1)}, bf16[384,1536]{1,0:T(8,128)(2,1)}, u32[]{:S(2)}, u32[]{:S(2)}) collective-permute-start(bf16[384,1536]{1,0:T(8,128)(2,1)} %bitcast.99), channel_id=1, source_target_pairs={{0,3},{1,0},{2,1},{3,2},{4,7},{5,4},{6,5},{7,6},{8,11},{9,8},{10,9... | collective-permute-start | bytes 3538952 | tf_op jit(solution)/shard_map/ppermute | solution.py:114
  24.2 88.0 %collective-permute-start.1 = (bf16[384,1536]{1,0:T(8,128)(2,1)}, bf16[384,1536]{1,0:T(8,128)(2,1)}, u32[]{:S(2)}, u32[]{:S(2)}) collective-permute-start(bf16[384,1536]{1,0:T(8,128)(2,1)} %bitcast.100), channel_id=1, source_target_pairs={{0,2},{1,3},{2,0},{3,1},{4,6},{5,7},{6,4},{7,5},{8,10},{9,11},{10,... | collective-permute-start | bytes 3538952 | tf_op jit(solution)/shard_map/ppermute | solution.py:114
  25.8 86.4 %collective-permute-start = (bf16[384,1536]{1,0:T(8,128)(2,1)}, bf16[384,1536]{1,0:T(8,128)(2,1)}, u32[]{:S(2)}, u32[]{:S(2)}) collective-permute-start(bf16[384,1536]{1,0:T(8,128)(2,1)} %bitcast.101), channel_id=1, source_target_pairs={{0,1},{1,2},{2,3},{3,0},{4,5},{5,6},{6,7},{7,4},{8,9},{9,10},{10,1... | collective-permute-start | bytes 3538952 | tf_op jit(solution)/shard_map/ppermute | solution.py:114
  28.5 55.5 %collective-permute-start.5 = (bf16[384,384]{1,0:T(8,128)(2,1)S(1)}, bf16[384,384]{1,0:T(8,128)(2,1)S(1)}, u32[]{:S(2)}, u32[]{:S(2)}) collective-permute-start(bf16[384,384]{1,0:T(8,128)(2,1)S(1)} %get-tuple-element.43), channel_id=1, source_target_pairs={{0,3},{1,0},{2,1},{3,2},{4,7},{5,4},{6,5},{7,6},{8,11},{9,8},{10,9... | collective-permute-start | bytes 884744 | tf_op jit(solution)/shard_map/ppermute | solution.py:114
  28.5 83.6 %collective-permute-start.3 = (bf16[384,384]{1,0:T(8,128)(2,1)}, bf16[384,384]{1,0:T(8,128)(2,1)}, u32[]{:S(2)}, u32[]{:S(2)}) collective-permute-start(bf16[384,384]{1,0:T(8,128)(2,1)} %get-tuple-element.44), channel_id=1, source_target_pairs={{0,1},{1,2},{2,3},{3,0},{4,5},{5,6},{6,7},{7,4},{8,9},{9,10},{10,1... | collective-permute-start | bytes 884744 | tf_op jit(solution)/shard_map/ppermute | solution.py:114
  84.0 13.9 %copy-start.8 = (bf16[384,384]{1,0:T(8,128)(2,1)}, bf16[384,384]{1,0:T(8,128)(2,1)S(1)}, u32[]{:S(2)}) copy-start(bf16[384,384]{1,0:T(8,128)(2,1)S(1)} %collective-permute-done.5) | copy-start | bytes 884740
  84.0 28.2 %collective-permute-start.4 = (bf16[384,384]{1,0:T(8,128)(2,1)S(1)}, bf16[384,384]{1,0:T(8,128)(2,1)}, u32[]{:S(2)}, u32[]{:S(2)}) collective-permute-start(bf16[384,384]{1,0:T(8,128)(2,1)S(1)} %get-tuple-element.46), channel_id=1, source_target_pairs={{0,2},{1,3},{2,0},{3,1},{4,6},{5,7},{6,4},{7,5},{8,10},{9,11},{10,... | collective-permute-start | bytes 884744 | tf_op jit(solution)/shard_map/ppermute | solution.py:114
  97.9 1.9 copy-start.1
  113.5 18.1 %all-to-all-start = ((bf16[4,256,512]{1,2,0:T(8,128)(2,1)}), bf16[4,256,512]{1,2,0:T(8,128)(2,1)S(1)}, u32[]{:S(2)}, u32[]{:S(2)}) async-start(bf16[4,256,512]{1,2,0:T(8,128)(2,1)} %copy.15), calls=%async_computation | async-start | bytes 2097152 | tf_op jit(solution)/shard_map/all_to_all | solution.py:93
  117.1 89.6 %all-gather.5.cloned.1.call-start = ((), (), s32[]{:S(2)}) async-start(), calls=%async_computation.3 | async-start | bytes 3538944 | tf_op jit(solution)/shard_map/all_gather | solution.py:89
  132.1 9.1 %copy-start.7 = (bf16[1,384,1536]{2,1,0:T(8,128)(2,1)S(1)}, bf16[1,384,1536]{2,1,0:T(8,128)(2,1)}, u32[]{:S(2)}) copy-start(bf16[1,384,1536]{2,1,0:T(8,128)(2,1)} %param.15) | copy-start | bytes 3538948
  141.3 3.7 %copy-start.6 = (bf16[3,1536,384]{2,1,0:T(8,128)(2,1)S(1)}, bf16[3,1536,384]{2,1,0:T(8,128)(2,1)}, u32[]{:S(2)}) copy-start(bf16[3,1536,384]{2,1,0:T(8,128)(2,1)} %param.18) | copy-start | bytes 10616836
  141.3 3.7 %copy-start.10 = (f32[1536]{0:T(1024)S(1)}, f32[1536]{0:T(1024)}, u32[]{:S(2)}) copy-start(f32[1536]{0:T(1024)} %param.17) | copy-start | bytes 18436
  145.6 14.1 %copy-start.11 = (f32[1536]{0:T(1024)S(1)}, f32[1536]{0:T(1024)}, u32[]{:S(2)}) copy-start(f32[1536]{0:T(1024)} %param.16) | copy-start | bytes 18436
  146.3 12.7 %collective-permute-start.6 = (bf16[2,256,384]{2,1,0:T(8,128)(2,1)S(1)}, bf16[2,256,384]{2,1,0:T(8,128)(2,1)S(1)}, u32[]{:S(2)}, u32[]{:S(2)}) collective-permute-start(bf16[2,256,384]{2,1,0:T(8,128)(2,1)S(1)} %pad_maximum_fusion.1), channel_id=1, source_target_pairs={{0,128},{1,129},{2,130},{3,131},{4,132},{5,133},{6,134},{7,135},{8... | collective-permute-start | bytes 1179656 | tf_op jit(solution)/shard_map/ppermute | solution.py:21
  159.0 0.7 copy-start.4
  206.6 1.9 copy-start.2
  222.2 17.6 %all-to-all-start.1 = ((bf16[4,256,512]{1,2,0:T(8,128)(2,1)}), bf16[4,256,512]{1,2,0:T(8,128)(2,1)S(1)}, u32[]{:S(2)}, u32[]{:S(2)}) async-start(bf16[4,256,512]{1,2,0:T(8,128)(2,1)} %copy.18), calls=%async_computation.1 | async-start | bytes 2097152 | tf_op jit(solution)/shard_map/all_to_all | solution.py:93
  240.2 11.1 %copy-start.9 = (bf16[384,384]{1,0:T(8,128)(2,1)S(1)}, bf16[384,384]{1,0:T(8,128)(2,1)}, u32[]{:S(2)}) copy-start(bf16[384,384]{1,0:T(8,128)(2,1)} %copy-done.8) | copy-start | bytes 884740
Sparse Core Ops, SparseCore 0:
  24.1 46.3 all-gather.2
  159.9 46.6 all-gather.4

commit v8 on v7

--- a/solution.py
+++ b/solution.py
@@ -9,7 +9,9 @@
 from jax.sharding import PartitionSpec as P
 
 HEAD_DIM = 128
+MP = ("my", "mc")
 X_SIZE = 4
+CORES = 2
 TILE = 256
 STATS = 128
 PARTS = 3
@@ -106,14 +108,32 @@
 
 
 def spread(block_of):
-    count = lax.axis_size("mp")
-    me = lax.axis_index("mp")
+    count = lax.axis_size(MP)
+    me = lax.axis_index(MP)
     blocks = [(me, block_of(me))]
     for step in range(1, count):
         piece = block_of((me + step) % count)
-        received = lax.ppermute(piece, "mp", [(j, (j + step) % count) for j in range(count)])
+        received = lax.ppermute(piece, MP, [(j, (j + step) % count) for j in range(count)])
         blocks.append(((me - step + count) % count, received))
     return blocks
+
+
+def spread_rows(block):
+    other = lax.ppermute(block, "my", [(0, 1), (1, 0)])
+    near = lax.ppermute(block, "mc", [(0, 1), (1, 0)])
+    return other, near
+
+
+def rows_in_order(block, other, near):
+    my, mc = lax.axis_index("my"), lax.axis_index("mc")
+    cores = lax.axis_size("mc")
+    far = lax.ppermute(other, "mc", [(0, 1), (1, 0)])
+    return [
+        (my * cores + mc, block),
+        ((1 - my) * cores + mc, other),
+        (my * cores + 1 - mc, near),
+        ((1 - my) * cores + 1 - mc, far),
+    ]
 
 
 def project_out(attended_full, blocks):
@@ -141,8 +161,8 @@
     local_rows = section_input.shape[1]
     local_width = section_input.shape[2]
     codes_total = code_table.shape[1]
-    me = lax.axis_index("mp")
-    self_blocks = spread(lambda target: self_out[0])
+    me = lax.axis_index(MP)
+    self_other, self_near = spread_rows(self_out[0])
     cross_blocks = spread(
         lambda target: lax.dynamic_slice_in_dim(cross_out, target * local_width, local_width, axis=1)
     )
@@ -151,16 +171,17 @@
     ).astype(jnp.bfloat16)
     looked = jnp.dot(matches, code_table[0], preferred_element_type=jnp.float32)
     embedded = (section_input[0].astype(jnp.float32) + looked).astype(jnp.bfloat16)
-    embedded_full = lax.all_gather(embedded, "mp", axis=1, tiled=True)
+    embedded_full = lax.all_gather(embedded, MP, axis=1, tiled=True)
     normed = rms_norm(embedded_full, self_gain[0])
     self_queries = project(normed, self_weights[0, 0])
     self_pairs = jnp.stack(
         [project(normed, self_weights[0, 1]), project(normed, self_weights[0, 2])]
     )
-    self_local, (self_blocks, cross_blocks) = attend(
-        self_queries, self_pairs, (self_blocks, cross_blocks)
-    )
-    self_attended = lax.all_gather(self_local, "mp", axis=1, tiled=True)
+    self_local, (self_other, self_near, cross_blocks) = attend(
+        self_queries, self_pairs, (self_other, self_near, cross_blocks)
+    )
+    self_blocks = rows_in_order(self_out[0], self_other, self_near)
+    self_attended = lax.all_gather(self_local, MP, axis=1, tiled=True)
     hidden_full = (
         embedded_full.astype(jnp.float32) + project_out(self_attended, self_blocks)
     ).astype(jnp.bfloat16)
@@ -171,7 +192,7 @@
         [project(memory_normed, cross_weights[1]), project(memory_normed, cross_weights[2])]
     )
     arrived = shifted(memory_pairs, "segment", 1)
-    crossed = lax.all_gather(attend(cross_queries, arrived), "mp", axis=1, tiled=True)
+    crossed = lax.all_gather(attend(cross_queries, arrived), MP, axis=1, tiled=True)
     decoded = (
         hidden_part.astype(jnp.float32) + project_out(crossed, cross_blocks)
     ).astype(jnp.bfloat16)
@@ -182,25 +203,25 @@
 def solution(mesh):
     segments, blocks, parts = (mesh.shape["segment"], mesh.shape["blk"], mesh.shape["mp"])
     split = Mesh(
-        mesh.devices.reshape(segments, blocks // X_SIZE, X_SIZE, parts),
-        ("segment", "bz", "bx", "mp"),
+        mesh.devices.reshape(segments, blocks // X_SIZE, X_SIZE, parts // CORES, CORES),
+        ("segment", "bz", "bx", "my", "mc"),
     )
     rows = ("bz", "bx")
     return jax.shard_map(
         on_device,
         mesh=split,
         in_specs=(
-            P("segment", rows, "mp"),
+            P("segment", rows, MP),
             P("segment", rows),
-            P("segment", None, "mp"),
+            P("segment", None, MP),
             P("segment", None),
-            P("segment", None, None, "mp"),
-            P("segment", "mp", None),
+            P("segment", None, None, MP),
+            P("segment", MP, None),
             P(),
             P(),
-            P(None, None, "mp"),
-            P("mp", None),
+            P(None, None, MP),
+            P(MP, None),
         ),
-        out_specs=P("segment", rows, "mp"),
+        out_specs=P("segment", rows, MP),
         check_vma=False,
     )

time: 261 us -> 231 us (0.89)
  waiting for transfers between devices: 123 us -> 92.3 us
    ppermute x6, waiting for transfers between devices: 51.9 us -> 0.02 us  [the longest x3 0.01 us: spread(): lax.ppermute(piece, MP, [(j, (j + step) % count) for j in range(count)])]
    all_gather x2, waiting for transfers between devices: 34.1 us -> 58.1 us  [attend(): key_block = lax.all_gather(pairs, 'bz', axis=1, tiled=True)]
    unnamed x24 -> x20, local copies, waits for them, and re-layouts: 5.48 us -> 5.49 us
where the time goes in v8:
time: 231 us
  waiting for transfers between devices  92.3 us (40%)
  blocking collectives  54.9 us (24%)
  Pallas kernels  24.7 us (11%)
  starting transfers between devices  17.7 us (8%)
  matrix products  16.2 us (7%)
  between operations  13.7 us (6%)
  local copies, waits for them, and re-layouts  9.29 us (4%)
    all_gather x2, waiting for transfers between devices, attend(): key_block = lax.all_gather(pairs, 'bz', axis=1, tiled=True)  58.1 us
    all_to_all x2, waiting for transfers between devices, attend(): parts = lax.all_to_all(partial, 'bx', 0, 0, tiled=True)  25.8 us
    pallas_call x2, Pallas kernels, partial_attend(): pl.pallas_call(partial_kernel, grid=(rows // TILE,), in_specs=[pl.BlockSp...  24.7 us
    all_gather x2, blocking collectives, attend(): query_block = lax.all_gather(queries, 'bx', axis=0, tiled=True)  22.7 us
    all_gather x1, blocking collectives, on_device(): self_attended = lax.all_gather(self_local, MP, axis=1, tiled=True)  11.1 us
    all_gather x1, blocking collectives, on_device(): lax.all_gather(attend(cross_queries, arrived), MP, axis=1, tiled=True)  10.8 us
    all_gather x1, blocking collectives, on_device(): embedded_full = lax.all_gather(embedded, MP, axis=1, tiled=True)  10.3 us
    dot_general x6, matrix products, project(): jnp.dot(normed, weight, preferred_element_type=jnp.float32)  8.93 us
  transfers between devices with their start and end apart: 11, of which 5 were waited for; matrix products, arithmetic and copies ran while one was open for 2% of the time, Pallas kernels for 5%

profile of v8, /device:TPU:1, one launch (start us, length us, event | category | flops | bytes accessed | tf_op | source)
XLA Modules:
  0.0 230.7 jit_solution(1672699993970364608)
XLA Ops:
  6.5 0.0 copy-start
  6.5 0.0 all-gather.3.cloned.1.call-start
  6.5 0.9 copy-done
  7.5 1.2 fusion.68
  8.7 10.3 %all_gather.21 = bf16[256,1536]{1,0:T(8,128)(2,1)S(1)} all-gather(bf16[256,384]{1,0:T(8,128)(2,1)S(1)} %fusion.68), channel_id=1, replica_groups=mesh['segment'=2,'bz'=8,'bx'=4,'my'=2,'mc'=2] {'my','mc'}, dimensions={1}, use_global_device_ids=true | all-gather | bytes 983040 | tf_op jit(solution)/shard_map/all_gather | solution.py:174
  19.0 0.2 fusion.19
  19.2 0.0 copy-done.5
  19.2 1.9 fusion.78
  21.1 0.0 copy-start.3
  21.2 2.0 fusion.75
  23.1 0.8 pad_maximum_fusion
  24.0 0.0 all-gather.3.cloned.1.call-update
  24.0 0.2 collective-permute-start.1
  24.3 1.6 collective-permute-start
  25.9 0.0 copy-done.3
  25.9 1.0 constant_dynamic-slice_fusion.8
  26.8 0.6 collective-permute-start.4
  27.5 1.1 collective-permute-start.2
  28.6 0.2 collective-permute-start.3
  28.8 1.9 fusion.50
  30.7 11.9 %all_gather.22.q_ref = bf16[1024,384]{1,0:T(8,128)(2,1)S(1)} all-gather(bf16[256,384]{1,0:T(8,128)(2,1)S(1)} %fusion.50), channel_id=1, replica_groups=mesh['segment'=2,'bz'=8,'bx'=4,'my'=2,'mc'=2] {'bx'}, dimensions={0}, use_global_device_ids=true | all-gather | bytes 983040 | tf_op jit(solution)/shard_map/all_gather | solution.py:90
  42.6 27.9 %all-gather.3.cloned.1.call-done.k_ref.v_ref = bf16[2,2048,384]{2,1,0:T(8,128)(2,1)} async-done(((bf16[2,256,384]{2,1,0:T(8,128)(2,1)}), bf16[2,2048,384]{2,1,0:T(8,128)(2,1)}) %all-gather.3.cloned.1.call-update) | async-done | bytes 3145744 | tf_op jit(solution)/shard_map/all_gather | solution.py:91
  70.5 1.9 copy-done.1
  72.4 12.4 %shard_map.100 = bf16[1024,512]{1,0:T(8,128)(2,1)S(1)} custom-call(bf16[1024,384]{1,0:T(8,128)(2,1)S(1)} %all_gather.22.q_ref, bf16[2,2048,384]{2,1,0:T(8,128)(2,1)S(1)} %copy-done.1, bf16[2,2048,384]{2,1,0:T(8,128)(2,1)S(1)} %copy-done.1), custom_call_target="tpu_custom_call" | custom-call | tf_op jit(solution)/shard_map/pallas_call | solution.py:73
  84.8 0.0 collective-permute-done.4
  84.8 0.0 collective-permute-done.2
  84.8 0.0 collective-permute-done.3
  84.8 0.0 collective-permute-done.1
  84.8 0.0 collective-permute-done
  84.8 1.3 copy.15
  86.1 4.0 %all-to-all-start = ((bf16[4,256,512]{1,2,0:T(8,128)(2,1)}), bf16[4,256,512]{1,2,0:T(8,128)(2,1)S(1)}, u32[]{:S(2)}, u32[]{:S(2)}) async-start(bf16[4,256,512]{1,2,0:T(8,128)(2,1)} %copy.15), calls=%async_computation | async-start | bytes 2097152 | tf_op jit(solution)/shard_map/all_to_all | solution.py:95
  90.1 0.0 all-gather.5.cloned.1.call-start
  90.1 1.5 collective-permute-start.5
  91.6 12.1 %all-to-all-done = bf16[4,256,512]{1,2,0:T(8,128)(2,1)S(1)} async-done(((bf16[4,256,512]{1,2,0:T(8,128)(2,1)}), bf16[4,256,512]{1,2,0:T(8,128)(2,1)S(1)}, u32[]{:S(2)}, u32[]{:S(2)}) %all-to-all-start) | async-done | bytes 1048608 | tf_op jit(solution)/shard_map/all_to_all | solution.py:95
  103.9 0.2 convert_element_type.74
  104.1 0.1 fusion.23
  104.2 0.0 copy-start.7
  104.3 11.1 %all_gather.24 = bf16[256,1536]{0,1:T(8,128)(2,1)S(1)} all-gather(bf16[256,384]{0,1:T(8,128)(2,1)S(1)} %fusion.99), channel_id=1, replica_groups=mesh['segment'=2,'bz'=8,'bx'=4,'my'=2,'mc'=2] {'my','mc'}, dimensions={1}, use_global_device_ids=true | all-gather | bytes 983040 | tf_op jit(solution)/shard_map/all_gather | solution.py:184
  115.4 0.1 constant_dynamic-slice_fusion.7
  115.5 0.0 collective-permute-done.5
  115.5 0.0 copy-done.7
  115.5 0.0 copy-start.6
  115.5 0.0 copy-start.8
  115.5 3.7 %fusion.18 = (f32[256]{0:T(256)S(1)}, bf16[256,1536]{1,0:T(8,128)(2,1)S(1)}) fusion(bf16[384,1536]{1,0:T(8,128)(2,1)} %collective-permute-done.5, bf16[384,1536]{1,0:T(8,128)(2,1)} %collective-permute-done.1, bf16[384,1536]{1,0:T(8,128)(2,1)} %collective-permute-done, bf16[384,1536]{1,0:T(8,128)(2,1)S(1)} %bitcast.101, ...), kind=kOutput, calls=%fused_computation.18 | convolution fusion | flops 1232338688 | bytes 7078912 | tf_op jit(solution)/shard_map/dot_general | solution.py:146
  119.2 0.6 fusion.69
  119.9 0.0 copy-start.9
  119.9 0.6 fusion.72
  120.6 4.4 %collective-permute-start.6 = (bf16[2,256,384]{2,1,0:T(8,128)(2,1)S(1)}, bf16[2,256,384]{2,1,0:T(8,128)(2,1)S(1)}, u32[]{:S(2)}, u32[]{:S(2)}) collective-permute-start(bf16[2,256,384]{2,1,0:T(8,128)(2,1)S(1)} %pad_maximum_fusion.1), channel_id=1, source_target_pairs={{0,128},{1,129},{2,130},{3,131},{4,132},{5,133},{6,134},{7,135},{8... | collective-permute-start | bytes 1179656 | tf_op jit(solution)/shard_map/ppermute | solution.py:23
  124.9 8.3 %collective-permute-done.6 = bf16[2,256,384]{2,1,0:T(8,128)(2,1)S(1)} collective-permute-done((bf16[2,256,384]{2,1,0:T(8,128)(2,1)S(1)}, bf16[2,256,384]{2,1,0:T(8,128)(2,1)S(1)}, u32[]{:S(2)}, u32[]{:S(2)}) %collective-permute-start.6) | collective-permute-done | bytes 393248 | tf_op jit(solution)/shard_map/ppermute | solution.py:23
  133.2 0.8 copy-done.4
  133.9 0.0 all-gather.5.cloned.1.call-update
  134.0 1.9 fusion.59
  135.9 10.8 %all_gather.25.q_ref = bf16[1024,384]{1,0:T(8,128)(2,1)S(1)} all-gather(bf16[256,384]{1,0:T(8,128)(2,1)S(1)} %fusion.59), channel_id=1, replica_groups=mesh['segment'=2,'bz'=8,'bx'=4,'my'=2,'mc'=2] {'bx'}, dimensions={0}, use_global_device_ids=true | all-gather | bytes 983040 | tf_op jit(solution)/shard_map/all_gather | solution.py:90
  146.7 30.2 %all-gather.5.cloned.1.call-done.k_ref.v_ref = bf16[2,2048,384]{2,1,0:T(8,128)(2,1)} async-done(((bf16[2,256,384]{2,1,0:T(8,128)(2,1)}), bf16[2,2048,384]{2,1,0:T(8,128)(2,1)}) %all-gather.5.cloned.1.call-update) | async-done | bytes 3145744 | tf_op jit(solution)/shard_map/all_gather | solution.py:91
  176.9 1.9 copy-done.2
  178.8 12.3 %shard_map.101 = bf16[1024,512]{1,0:T(8,128)(2,1)S(1)} custom-call(bf16[1024,384]{1,0:T(8,128)(2,1)S(1)} %all_gather.25.q_ref, bf16[2,2048,384]{2,1,0:T(8,128)(2,1)S(1)} %copy-done.2, bf16[2,2048,384]{2,1,0:T(8,128)(2,1)S(1)} %copy-done.2), custom_call_target="tpu_custom_call" | custom-call | tf_op jit(solution)/shard_map/pallas_call | solution.py:73
  191.1 1.3 copy.18
  192.5 4.0 %all-to-all-start.1 = ((bf16[4,256,512]{1,2,0:T(8,128)(2,1)}), bf16[4,256,512]{1,2,0:T(8,128)(2,1)S(1)}, u32[]{:S(2)}, u32[]{:S(2)}) async-start(bf16[4,256,512]{1,2,0:T(8,128)(2,1)} %copy.18), calls=%async_computation.1 | async-start | bytes 2097152 | tf_op jit(solution)/shard_map/all_to_all | solution.py:95
  196.4 13.7 %all-to-all-done.1 = bf16[4,256,512]{1,2,0:T(8,128)(2,1)S(1)} async-done(((bf16[4,256,512]{1,2,0:T(8,128)(2,1)}), bf16[4,256,512]{1,2,0:T(8,128)(2,1)S(1)}, u32[]{:S(2)}, u32[]{:S(2)}) %all-to-all-start.1) | async-done | bytes 1048608 | tf_op jit(solution)/shard_map/all_to_all | solution.py:95
  210.2 0.2 convert_element_type.84
  210.4 0.1 fusion.22
  210.6 10.8 %all_gather.27 = bf16[256,1536]{0,1:T(8,128)(2,1)S(1)} all-gather(bf16[256,384]{0,1:T(8,128)(2,1)S(1)} %fusion.98), channel_id=1, replica_groups=mesh['segment'=2,'bz'=8,'bx'=4,'my'=2,'mc'=2] {'my','mc'}, dimensions={1}, use_global_device_ids=true | all-gather | bytes 983040 | tf_op jit(solution)/shard_map/all_gather | solution.py:195
  221.4 0.1 constant_dynamic-slice_fusion.3
  221.5 2.4 %fusion.103 = bf16[1,256,384]{2,1,0:T(8,128)(2,1)} fusion(bf16[256,1536]{1,0:T(8,128)(2,1)S(1)} %get-tuple-element.44, s32[]{:T(128)S(6)} %select_n.65, pred[]{:T(512)S(6)} %eq.20, bf16[384,384]{1,0:T(8,128)(2,1)} %collective-permute-done.4, bf16[384,384]{1,0:T(8,128)(2,1)} %collective-permute-done.3, bf16[384,384]{1,0:T(8,128)(2,1)} %collective-permute-done.2, ...), kind=kOutput, calls=%fused_computation.89 | convolution fusion | flops 310247424 | bytes 2359301 | tf_op jit(solution)/shard_map/dot_general | solution.py:146
  (25 shorter events, 0.4 us)
Async XLA Ops:
  6.5 0.9 copy-start
  6.5 12.7 %copy-start.5 = (f32[1,1536]{1,0:T(1,128)S(1)}, f32[1,1536]{1,0:T(1,128)}, u32[]{:S(2)}) copy-start(f32[1,1536]{1,0:T(1,128)} %param.13) | copy-start | bytes 18436
  6.5 64.0 %all-gather.3.cloned.1.call-start = ((), (), s32[]{:S(2)}) async-start(), calls=%async_computation.2 | async-start | bytes 3538944 | tf_op jit(solution)/shard_map/all_gather | solution.py:91
  21.1 4.7 %copy-start.3 = (bf16[384,1536]{1,0:T(8,128)(2,1)S(1)}, bf16[384,1536]{1,0:T(8,128)(2,1)}, u32[]{:S(2)}) copy-start(bf16[384,1536]{1,0:T(8,128)(2,1)} %param.19) | copy-start | bytes 3538948
  24.0 60.8 %collective-permute-start.1 = (bf16[384,1536]{1,0:T(8,128)(2,1)}, bf16[384,1536]{1,0:T(8,128)(2,1)}, u32[]{:S(2)}, u32[]{:S(2)}) collective-permute-start(bf16[384,1536]{1,0:T(8,128)(2,1)} %bitcast.99), channel_id=1, source_target_pairs={{0,1},{1,0},{2,3},{3,2},{4,5},{5,4},{6,7},{7,6},{8,9},{9,8},{10,11... | collective-permute-start | bytes 3538952 | tf_op jit(solution)/shard_map/ppermute | solution.py:123
  24.3 60.5 %collective-permute-start = (bf16[384,1536]{1,0:T(8,128)(2,1)}, bf16[384,1536]{1,0:T(8,128)(2,1)}, u32[]{:S(2)}, u32[]{:S(2)}) collective-permute-start(bf16[384,1536]{1,0:T(8,128)(2,1)} %bitcast.100), channel_id=1, source_target_pairs={{0,2},{2,0},{1,3},{3,1},{4,6},{6,4},{5,7},{7,5},{8,10},{10,8},{9,1... | collective-permute-start | bytes 3538952 | tf_op jit(solution)/shard_map/ppermute | solution.py:122
  26.8 57.9 %collective-permute-start.4 = (bf16[384,384]{1,0:T(8,128)(2,1)}, bf16[384,384]{1,0:T(8,128)(2,1)}, u32[]{:S(2)}, u32[]{:S(2)}) collective-permute-start(bf16[384,384]{1,0:T(8,128)(2,1)} %get-tuple-element.31), channel_id=1, source_target_pairs={{0,3},{1,0},{2,1},{3,2},{4,7},{5,4},{6,5},{7,6},{8,11},{9,8},{10,9... | collective-permute-start | bytes 884744 | tf_op jit(solution)/shard_map/ppermute | solution.py:116
  27.5 57.3 %collective-permute-start.2 = (bf16[384,384]{1,0:T(8,128)(2,1)}, bf16[384,384]{1,0:T(8,128)(2,1)}, u32[]{:S(2)}, u32[]{:S(2)}) collective-permute-start(bf16[384,384]{1,0:T(8,128)(2,1)} %get-tuple-element.32), channel_id=1, source_target_pairs={{0,1},{1,2},{2,3},{3,0},{4,5},{5,6},{6,7},{7,4},{8,9},{9,10},{10,1... | collective-permute-start | bytes 884744 | tf_op jit(solution)/shard_map/ppermute | solution.py:116
  28.6 56.2 %collective-permute-start.3 = (bf16[384,384]{1,0:T(8,128)(2,1)S(1)}, bf16[384,384]{1,0:T(8,128)(2,1)}, u32[]{:S(2)}, u32[]{:S(2)}) collective-permute-start(bf16[384,384]{1,0:T(8,128)(2,1)S(1)} %get-tuple-element.34), channel_id=1, source_target_pairs={{0,2},{1,3},{2,0},{3,1},{4,6},{5,7},{6,4},{7,5},{8,10},{9,11},{10,... | collective-permute-start | bytes 884744 | tf_op jit(solution)/shard_map/ppermute | solution.py:116
  70.5 1.9 copy-start.1
  86.1 17.6 %all-to-all-start = ((bf16[4,256,512]{1,2,0:T(8,128)(2,1)}), bf16[4,256,512]{1,2,0:T(8,128)(2,1)S(1)}, u32[]{:S(2)}, u32[]{:S(2)}) async-start(bf16[4,256,512]{1,2,0:T(8,128)(2,1)} %copy.15), calls=%async_computation | async-start | bytes 2097152 | tf_op jit(solution)/shard_map/all_to_all | solution.py:95
  90.1 86.8 %all-gather.5.cloned.1.call-start = ((), (), s32[]{:S(2)}) async-start(), calls=%async_computation.3 | async-start | bytes 3538944 | tf_op jit(solution)/shard_map/all_gather | solution.py:91
  90.1 25.4 %collective-permute-start.5 = (bf16[384,1536]{1,0:T(8,128)(2,1)}, bf16[384,1536]{1,0:T(8,128)(2,1)}, u32[]{:S(2)}, u32[]{:S(2)}) collective-permute-start(bf16[384,1536]{1,0:T(8,128)(2,1)} %collective-permute-done), channel_id=1, source_target_pairs={{0,1},{1,0},{2,3},{3,2},{4,5},{5,4},{6,7},{7,6},{8,9},{9,8},{10,11... | collective-permute-start | bytes 3538952 | tf_op jit(solution)/shard_map/ppermute | solution.py:130
  104.2 11.3 %copy-start.7 = (bf16[1,384,1536]{2,1,0:T(8,128)(2,1)S(1)}, bf16[1,384,1536]{2,1,0:T(8,128)(2,1)}, u32[]{:S(2)}) copy-start(bf16[1,384,1536]{2,1,0:T(8,128)(2,1)} %param.15) | copy-start | bytes 3538948
  115.5 3.7 %copy-start.6 = (bf16[3,1536,384]{2,1,0:T(8,128)(2,1)S(1)}, bf16[3,1536,384]{2,1,0:T(8,128)(2,1)}, u32[]{:S(2)}) copy-start(bf16[3,1536,384]{2,1,0:T(8,128)(2,1)} %param.18) | copy-start | bytes 10616836
  115.5 3.7 %copy-start.8 = (f32[1536]{0:T(1024)S(1)}, f32[1536]{0:T(1024)}, u32[]{:S(2)}) copy-start(f32[1536]{0:T(1024)} %param.17) | copy-start | bytes 18436
  119.9 14.1 %copy-start.9 = (f32[1536]{0:T(1024)S(1)}, f32[1536]{0:T(1024)}, u32[]{:S(2)}) copy-start(f32[1536]{0:T(1024)} %param.16) | copy-start | bytes 18436
  120.6 12.6 %collective-permute-start.6 = (bf16[2,256,384]{2,1,0:T(8,128)(2,1)S(1)}, bf16[2,256,384]{2,1,0:T(8,128)(2,1)S(1)}, u32[]{:S(2)}, u32[]{:S(2)}) collective-permute-start(bf16[2,256,384]{2,1,0:T(8,128)(2,1)S(1)} %pad_maximum_fusion.1), channel_id=1, source_target_pairs={{0,128},{1,129},{2,130},{3,131},{4,132},{5,133},{6,134},{7,135},{8... | collective-permute-start | bytes 1179656 | tf_op jit(solution)/shard_map/ppermute | solution.py:23
  133.2 0.8 copy-start.4
  176.9 1.9 copy-start.2
  192.5 17.6 %all-to-all-start.1 = ((bf16[4,256,512]{1,2,0:T(8,128)(2,1)}), bf16[4,256,512]{1,2,0:T(8,128)(2,1)S(1)}, u32[]{:S(2)}, u32[]{:S(2)}) async-start(bf16[4,256,512]{1,2,0:T(8,128)(2,1)} %copy.18), calls=%async_computation.1 | async-start | bytes 2097152 | tf_op jit(solution)/shard_map/all_to_all | solution.py:95
Sparse Core Ops, SparseCore 0:
  24.1 46.3 all-gather.2
  134.1 42.7 all-gather.4

commit v9 on v8

--- a/solution.py
+++ b/solution.py
@@ -92,8 +92,15 @@
     partial = partial_attend(query_block, key_block)
     if riders is not None:
         partial, riders = lax.optimization_barrier((partial, riders))
-    parts = lax.all_to_all(partial, "bx", 0, 0, tiled=True)
-    parts = parts.reshape(-1, rows, width + STATS).astype(jnp.float32)
+    count = lax.axis_size("bx")
+    me = lax.axis_index("bx")
+    chunks = [lax.dynamic_slice_in_dim(partial, me * rows, rows, axis=0)]
+    for step in range(1, count):
+        piece = lax.dynamic_slice_in_dim(partial, ((me + step) % count) * rows, rows, axis=0)
+        chunks.append(
+            lax.ppermute(piece, "bx", [(j, (j + step) % count) for j in range(count)])
+        )
+    parts = jnp.stack(chunks).astype(jnp.float32)
     outs = parts[:, :, :width].reshape(-1, rows, heads, HEAD_DIM)
     stats = parts[:, :, width:width + 2 * heads * PARTS].reshape(-1, rows, 2, heads, PARTS)
     stats = jnp.sum(stats, axis=-1)
@@ -191,7 +198,9 @@
     memory_pairs = jnp.stack(
         [project(memory_normed, cross_weights[1]), project(memory_normed, cross_weights[2])]
     )
-    arrived = shifted(memory_pairs, "segment", 1)
+    arrived = jnp.stack(
+        [shifted(memory_pairs[0], "segment", 1), shifted(memory_pairs[1], "segment", 1)]
+    )
     crossed = lax.all_gather(attend(cross_queries, arrived), MP, axis=1, tiled=True)
     decoded = (
         hidden_part.astype(jnp.float32) + project_out(crossed, cross_blocks)

time: 231 us -> 235 us (1.017)
  waiting for transfers between devices: 92.3 us -> 83.1 us
  other arithmetic: 1.99 us -> 6.66 us
  local copies, waits for them, and re-layouts: 9.29 us -> 13.3 us
  starting transfers between devices: 17.7 us -> 21.1 us
    all_to_all x2 -> x0, waiting for transfers between devices: 25.8 us -> none  [attend(): parts = lax.all_to_all(partial, 'bx', 0, 0, tiled=True)]
    ppermute x0 -> x6, waiting for transfers between devices: none -> 17.3 us  [attend(): lax.ppermute(piece, 'bx', [(j, (j + step) % count) for j in range(count)])]
    ppermute x0 -> x6, starting transfers between devices: none -> 9.7 us  [attend(): lax.ppermute(piece, 'bx', [(j, (j + step) % count) for j in range(count)])]
    all_to_all x2 -> x0, starting transfers between devices: 7.93 us -> none  [attend(): parts = lax.all_to_all(partial, 'bx', 0, 0, tiled=True)]
    mul x0 -> x4, local copies, waits for them, and re-layouts: none -> 4.9 us  [attend(): merged = jnp.sum(outs * scale[..., None], axis=0) / total[..., None]]
    all_to_all x2 -> x0, local copies, waits for them, and re-layouts: 2.65 us -> none  [attend(): parts = lax.all_to_all(partial, 'bx', 0, 0, tiled=True)]
    ppermute x1 -> x2, starting transfers between devices: 4.36 us -> 5.66 us  [shifted(): lax.ppermute(value, axis, [(source, source + steps) for source in range(i...]
    ppermute x1 -> x2, waiting for transfers between devices: 8.27 us -> 6.97 us  [shifted(): lax.ppermute(value, axis, [(source, source + steps) for source in range(i...]
  transfers between devices with their start and end apart: 11 -> 16, of which waited for: 5 -> 10; matrix products, arithmetic and copies ran while one was open for 2% -> 3% of each run, Pallas kernels for 5% -> 5%
where the time goes in v9:
time: 235 us; the launch traced here: 234 us
  waiting for transfers between devices  83.1 us (35%)
  blocking collectives  55.4 us (24%)
  Pallas kernels  24.6 us (10%)
  starting transfers between devices  21.1 us (9%)
  matrix products  15.9 us (7%)
  between operations  13.9 us (6%)
  local copies, waits for them, and re-layouts  13.3 us (6%)
  other arithmetic  6.66 us (3%)
    all_gather x2, waiting for transfers between devices, attend(): key_block = lax.all_gather(pairs, 'bz', axis=1, tiled=True)  58.8 us
    pallas_call x2, Pallas kernels, partial_attend(): pl.pallas_call(partial_kernel, grid=(rows // TILE,), in_specs=[pl.BlockSp...  24.6 us
    all_gather x2, blocking collectives, attend(): query_block = lax.all_gather(queries, 'bx', axis=0, tiled=True)  23.8 us
    ppermute x6, waiting for transfers between devices, attend(): lax.ppermute(piece, 'bx', [(j, (j + step) % count) for j in range(count)])  17.3 us
    all_gather x1, blocking collectives, on_device(): lax.all_gather(attend(cross_queries, arrived), MP, axis=1, tiled=True)  10.7 us
    all_gather x1, blocking collectives, on_device(): self_attended = lax.all_gather(self_local, MP, axis=1, tiled=True)  10.7 us
    all_gather x1, blocking collectives, on_device(): embedded_full = lax.all_gather(embedded, MP, axis=1, tiled=True)  10.3 us
    ppermute x6, starting transfers between devices, attend(): lax.ppermute(piece, 'bx', [(j, (j + step) % count) for j in range(count)])  9.7 us
  transfers between devices with their start and end apart: 16, of which 10 were waited for; matrix products, arithmetic and copies ran while one was open for 3% of the time, Pallas kernels for 5%

profile of v9, /device:TPU:1, one launch (start us, length us, event | category | flops | bytes accessed | tf_op | source)
XLA Modules:
  0.0 234.0 jit_solution(5447579490163547156)
XLA Ops:
  6.5 0.9 copy-done
  7.5 1.2 fusion.68
  8.7 10.3 %all_gather.21 = bf16[256,1536]{1,0:T(8,128)(2,1)S(1)} all-gather(bf16[256,384]{1,0:T(8,128)(2,1)S(1)} %fusion.68), channel_id=1, replica_groups=mesh['segment'=2,'bz'=8,'bx'=4,'my'=2,'mc'=2] {'my','mc'}, dimensions={1}, use_global_device_ids=true | all-gather | bytes 983040 | tf_op jit(solution)/shard_map/all_gather | solution.py:181
  19.0 0.2 fusion.19
  19.2 1.9 fusion.69
  21.1 2.0 fusion.72
  23.1 0.8 pad_maximum_fusion
  24.0 1.7 collective-permute-start
  25.7 0.4 collective-permute-start.1
  26.2 0.8 constant_dynamic-slice_fusion.14
  27.1 1.4 collective-permute-start.3
  28.4 1.9 fusion.50
  30.3 11.8 %all_gather.22.q_ref = bf16[1024,384]{1,0:T(8,128)(2,1)S(1)} all-gather(bf16[256,384]{1,0:T(8,128)(2,1)S(1)} %fusion.50), channel_id=1, replica_groups=mesh['segment'=2,'bz'=8,'bx'=4,'my'=2,'mc'=2] {'bx'}, dimensions={0}, use_global_device_ids=true | all-gather | bytes 983040 | tf_op jit(solution)/shard_map/all_gather | solution.py:90
  42.1 28.4 %all-gather.3.cloned.1.call-done.k_ref.v_ref = bf16[2,2048,384]{2,1,0:T(8,128)(2,1)} async-done(((bf16[2,256,384]{2,1,0:T(8,128)(2,1)}), bf16[2,2048,384]{2,1,0:T(8,128)(2,1)}) %all-gather.3.cloned.1.call-update) | async-done | bytes 3145744 | tf_op jit(solution)/shard_map/all_gather | solution.py:91
  70.5 1.9 copy-done.1
  72.4 12.3 %shard_map.100 = bf16[1024,512]{1,0:T(8,128)(2,1)S(1)} custom-call(bf16[1024,384]{1,0:T(8,128)(2,1)S(1)} %all_gather.22.q_ref, bf16[2,2048,384]{2,1,0:T(8,128)(2,1)S(1)} %copy-done.1, bf16[2,2048,384]{2,1,0:T(8,128)(2,1)S(1)} %copy-done.1), custom_call_target="tpu_custom_call" | custom-call | tf_op jit(solution)/shard_map/pallas_call | solution.py:73
  84.7 0.8 copy-done.20
  85.6 1.3 collective-permute-start.5
  86.9 2.4 %collective-permute-start.6 = (bf16[256,512]{1,0:T(8,128)(2,1)S(1)}, bf16[256,512]{1,0:T(8,128)(2,1)S(1)}, u32[]{:S(2)}, u32[]{:S(2)}) collective-permute-start(bf16[256,512]{1,0:T(8,128)(2,1)S(1)} %get-tuple-element.41), channel_id=1, source_target_pairs={{0,8},{4,12},{8,0},{12,4},{1,9},{5,13},{9,1},{13,5},{2,10},{6,14},... | collective-permute-start | bytes 786440 | tf_op jit(solution)/shard_map/ppermute | solution.py:101
  89.3 1.2 collective-permute-start.7
  90.5 2.1 collective-permute-start.8
  92.5 1.0 collective-permute-done.5
  93.5 6.5 %collective-permute-done.6 = bf16[256,512]{1,0:T(8,128)(2,1)S(1)} collective-permute-done((bf16[256,512]{1,0:T(8,128)(2,1)S(1)}, bf16[256,512]{1,0:T(8,128)(2,1)S(1)}, u32[]{:S(2)}, u32[]{:S(2)}) %collective-permute-start.6) | collective-permute-done | bytes 262176 | tf_op jit(solution)/shard_map/ppermute | solution.py:101
  100.1 0.1 collective-permute-done.7
  100.2 0.2 copy.15
  100.5 0.1 mul.157
  100.6 0.1 copy-done.8
  100.8 0.1 copy-done.9
  100.9 0.5 copy.17
  101.4 0.2 copy.18
  101.6 1.4 maximum_convert_fusion
  102.9 0.3 fusion.23
  103.3 10.7 %all_gather.24 = bf16[256,1536]{1,0:T(8,128)(2,1)S(1)} all-gather(bf16[256,384]{1,0:T(8,128)(2,1)S(1)} %divide_convert_fusion.1), channel_id=1, replica_groups=mesh['segment'=2,'bz'=8,'bx'=4,'my'=2,'mc'=2] {'my','mc'}, dimensions={1}, use_global_device_ids=true | all-gather | bytes 983040 | tf_op jit(solution)/shard_map/all_gather | solution.py:191
  114.1 3.6 %fusion.18 = (f32[256]{0:T(256)S(1)}, bf16[256,1536]{1,0:T(8,128)(2,1)S(1)}) fusion(bf16[384,1536]{1,0:T(8,128)(2,1)} %collective-permute-done.8, bf16[384,1536]{1,0:T(8,128)(2,1)} %collective-permute-done.1, bf16[384,1536]{1,0:T(8,128)(2,1)} %collective-permute-done, bf16[384,1536]{1,0:T(8,128)(2,1)S(1)} %bitcast.111, ...), kind=kOutput, calls=%fused_computation.18 | convolution fusion | flops 1232338688 | bytes 7078912 | tf_op jit(solution)/shard_map/dot_general | solution.py:153
  117.8 0.6 fusion.62
  118.4 0.6 fusion.65
  119.1 4.4 %collective-permute-start.9 = (bf16[256,384]{1,0:T(8,128)(2,1)S(1)}, bf16[256,384]{1,0:T(8,128)(2,1)S(1)}, u32[]{:S(2)}, u32[]{:S(2)}) collective-permute-start(bf16[256,384]{1,0:T(8,128)(2,1)S(1)} %fusion.62), channel_id=1, source_target_pairs={{0,128},{1,129},{2,130},{3,131},{4,132},{5,133},{6,134},{7,135},{8... | collective-permute-start | bytes 589832 | tf_op jit(solution)/shard_map/ppermute | solution.py:23
  123.4 1.3 collective-permute-start.10
  124.7 2.8 %collective-permute-done.9 = bf16[256,384]{1,0:T(8,128)(2,1)S(1)} collective-permute-done((bf16[256,384]{1,0:T(8,128)(2,1)S(1)}, bf16[256,384]{1,0:T(8,128)(2,1)S(1)}, u32[]{:S(2)}, u32[]{:S(2)}) %collective-permute-start.9) | collective-permute-done | bytes 196640 | tf_op jit(solution)/shard_map/ppermute | solution.py:23
  127.5 4.2 %collective-permute-done.10 = bf16[256,384]{1,0:T(8,128)(2,1)S(1)} collective-permute-done((bf16[256,384]{1,0:T(8,128)(2,1)S(1)}, bf16[256,384]{1,0:T(8,128)(2,1)S(1)}, u32[]{:S(2)}, u32[]{:S(2)}) %collective-permute-start.10) | collective-permute-done | bytes 196640 | tf_op jit(solution)/shard_map/ppermute | solution.py:23
  131.7 0.8 pad_maximum_fusion.1
  132.6 1.9 fusion.59
  134.5 12.0 %all_gather.25.q_ref = bf16[1024,384]{1,0:T(8,128)(2,1)S(1)} all-gather(bf16[256,384]{1,0:T(8,128)(2,1)S(1)} %fusion.59), channel_id=1, replica_groups=mesh['segment'=2,'bz'=8,'bx'=4,'my'=2,'mc'=2] {'bx'}, dimensions={0}, use_global_device_ids=true | all-gather | bytes 983040 | tf_op jit(solution)/shard_map/all_gather | solution.py:90
  146.5 30.4 %all-gather.5.cloned.1.call-done.k_ref.v_ref = bf16[2,2048,384]{2,1,0:T(8,128)(2,1)} async-done(((bf16[2,256,384]{2,1,0:T(8,128)(2,1)}), bf16[2,2048,384]{2,1,0:T(8,128)(2,1)}) %all-gather.5.cloned.1.call-update) | async-done | bytes 3145744 | tf_op jit(solution)/shard_map/all_gather | solution.py:91
  176.9 1.9 copy-done.2
  178.8 12.3 %shard_map.101 = bf16[1024,512]{1,0:T(8,128)(2,1)S(1)} custom-call(bf16[1024,384]{1,0:T(8,128)(2,1)S(1)} %all_gather.25.q_ref, bf16[2,2048,384]{2,1,0:T(8,128)(2,1)S(1)} %copy-done.2, bf16[2,2048,384]{2,1,0:T(8,128)(2,1)S(1)} %copy-done.2), custom_call_target="tpu_custom_call" | custom-call | tf_op jit(solution)/shard_map/pallas_call | solution.py:73
  191.1 0.1 dynamic-slice_bitcast_fusion
  191.2 1.3 collective-permute-start.11
  192.5 2.4 %collective-permute-start.12 = (bf16[256,512]{1,0:T(8,128)(2,1)S(1)}, bf16[256,512]{1,0:T(8,128)(2,1)S(1)}, u32[]{:S(2)}, u32[]{:S(2)}) collective-permute-start(bf16[256,512]{1,0:T(8,128)(2,1)S(1)} %get-tuple-element.37), channel_id=1, source_target_pairs={{0,8},{4,12},{8,0},{12,4},{1,9},{5,13},{9,1},{13,5},{2,10},{6,14},... | collective-permute-start | bytes 786440 | tf_op jit(solution)/shard_map/ppermute | solution.py:101
  194.9 1.2 collective-permute-start.13
  196.1 3.1 %collective-permute-done.11 = bf16[256,512]{1,0:T(8,128)(2,1)S(1)} collective-permute-done((bf16[256,512]{1,0:T(8,128)(2,1)S(1)}, bf16[256,512]{1,0:T(8,128)(2,1)S(1)}, u32[]{:S(2)}, u32[]{:S(2)}) %collective-permute-start.11) | collective-permute-done | bytes 262176 | tf_op jit(solution)/shard_map/ppermute | solution.py:101
  199.1 6.5 %collective-permute-done.12 = bf16[256,512]{1,0:T(8,128)(2,1)S(1)} collective-permute-done((bf16[256,512]{1,0:T(8,128)(2,1)S(1)}, bf16[256,512]{1,0:T(8,128)(2,1)S(1)}, u32[]{:S(2)}, u32[]{:S(2)}) %collective-permute-start.12) | collective-permute-done | bytes 262176 | tf_op jit(solution)/shard_map/ppermute | solution.py:101
  205.7 0.1 collective-permute-done.13
  205.8 0.6 copy-done.10
  206.4 0.1 copy-done.11
  206.5 0.2 maximum_convert_fusion.1
  206.7 0.9 maximum_convert_fusion.2
  207.6 0.2 copy.19
  207.9 1.3 mul.172
  209.1 3.0 %copy.21 = f32[4,256,384]{2,1,0:T(8,128)} copy(f32[4,256,384]{1,2,0:T(8,128)} %bitcast.89) | data formatting | bytes 3145728 | tf_op jit(solution)/shard_map/mul | solution.py:112
  212.2 0.2 copy.22
  212.4 1.7 fusion.22
  214.2 10.7 %all_gather.27 = bf16[256,1536]{1,0:T(8,128)(2,1)S(1)} all-gather(bf16[256,384]{1,0:T(8,128)(2,1)S(1)} %divide_convert_fusion), channel_id=1, replica_groups=mesh['segment'=2,'bz'=8,'bx'=4,'my'=2,'mc'=2] {'my','mc'}, dimensions={1}, use_global_device_ids=true | all-gather | bytes 983040 | tf_op jit(solution)/shard_map/all_gather | solution.py:204
  225.0 2.2 fusion.95
  (73 shorter events, 0.9 us)
Async XLA Ops:
  6.5 0.9 copy-start
  6.5 12.7 %copy-start.13 = (f32[1,1536]{1,0:T(1,128)S(1)}, f32[1,1536]{1,0:T(1,128)}, u32[]{:S(2)}) copy-start(f32[1,1536]{1,0:T(1,128)} %param.13) | copy-start | bytes 18436
  6.5 63.9 %all-gather.3.cloned.1.call-start = ((), (), s32[]{:S(2)}) async-start(), calls=%async_computation | async-start | bytes 3538944 | tf_op jit(solution)/shard_map/all_gather | solution.py:91
  19.0 9.5 %copy-start.3 = (bf16[256,1536]{1,0:T(8,128)(2,1)}, bf16[256,1536]{1,0:T(8,128)(2,1)S(1)}, u32[]{:S(2)}) copy-start(bf16[256,1536]{1,0:T(8,128)(2,1)S(1)} %all_gather.21) | copy-start | bytes 2359300
  21.1 5.0 %copy-start.6 = (bf16[384,1536]{1,0:T(8,128)(2,1)S(1)}, bf16[384,1536]{1,0:T(8,128)(2,1)}, u32[]{:S(2)}) copy-start(bf16[384,1536]{1,0:T(8,128)(2,1)} %param.19) | copy-start | bytes 3538948
  24.0 153.0 %all-gather.5.cloned.1.call-start = ((), (), s32[]{:S(2)}) async-start(), calls=%async_computation.1 | async-start | bytes 3538944 | tf_op jit(solution)/shard_map/all_gather | solution.py:91
  24.0 60.7 %collective-permute-start = (bf16[384,1536]{1,0:T(8,128)(2,1)}, bf16[384,1536]{1,0:T(8,128)(2,1)}, u32[]{:S(2)}, u32[]{:S(2)}) collective-permute-start(bf16[384,1536]{1,0:T(8,128)(2,1)} %bitcast.109), channel_id=1, source_target_pairs={{0,2},{2,0},{1,3},{3,1},{4,6},{6,4},{5,7},{7,5},{8,10},{10,8},{9,1... | collective-permute-start | bytes 3538952 | tf_op jit(solution)/shard_map/ppermute | solution.py:129
  25.7 59.0 %collective-permute-start.1 = (bf16[384,1536]{1,0:T(8,128)(2,1)}, bf16[384,1536]{1,0:T(8,128)(2,1)}, u32[]{:S(2)}, u32[]{:S(2)}) collective-permute-start(bf16[384,1536]{1,0:T(8,128)(2,1)} %bitcast.110), channel_id=1, source_target_pairs={{0,1},{1,0},{2,3},{3,2},{4,5},{5,4},{6,7},{7,6},{8,9},{9,8},{10,11... | collective-permute-start | bytes 3538952 | tf_op jit(solution)/shard_map/ppermute | solution.py:130
  27.0 57.7 %collective-permute-start.2 = (bf16[384,384]{1,0:T(8,128)(2,1)S(1)}, bf16[384,384]{1,0:T(8,128)(2,1)S(1)}, u32[]{:S(2)}, u32[]{:S(2)}) collective-permute-start(bf16[384,384]{1,0:T(8,128)(2,1)S(1)} %get-tuple-element.32), channel_id=1, source_target_pairs={{0,1},{1,2},{2,3},{3,0},{4,5},{5,6},{6,7},{7,4},{8,9},{9,10},{10,1... | collective-permute-start | bytes 884744 | tf_op jit(solution)/shard_map/ppermute | solution.py:123
  27.1 57.6 %collective-permute-start.3 = (bf16[384,384]{1,0:T(8,128)(2,1)S(1)}, bf16[384,384]{1,0:T(8,128)(2,1)S(1)}, u32[]{:S(2)}, u32[]{:S(2)}) collective-permute-start(bf16[384,384]{1,0:T(8,128)(2,1)S(1)} %get-tuple-element.34), channel_id=1, source_target_pairs={{0,2},{1,3},{2,0},{3,1},{4,6},{5,7},{6,4},{7,5},{8,10},{9,11},{10,... | collective-permute-start | bytes 884744 | tf_op jit(solution)/shard_map/ppermute | solution.py:123
  28.4 56.3 %collective-permute-start.4 = (bf16[384,384]{1,0:T(8,128)(2,1)S(1)}, bf16[384,384]{1,0:T(8,128)(2,1)S(1)}, u32[]{:S(2)}, u32[]{:S(2)}) collective-permute-start(bf16[384,384]{1,0:T(8,128)(2,1)S(1)} %get-tuple-element.31), channel_id=1, source_target_pairs={{0,3},{1,0},{2,1},{3,2},{4,7},{5,4},{6,5},{7,6},{8,11},{9,8},{10,9... | collective-permute-start | bytes 884744 | tf_op jit(solution)/shard_map/ppermute | solution.py:123
  70.5 1.9 copy-start.1
  84.7 0.9 copy-start.16
  84.7 2.2 copy-start.18
  84.7 0.8 copy-start.20
  85.6 15.0 %copy-start.5 = (bf16[1,256,512]{2,1,0:T(8,128)(2,1)}, bf16[1,256,512]{2,1,0:T(8,128)(2,1)S(1)}, u32[]{:S(2)}) copy-start(bf16[1,256,512]{2,1,0:T(8,128)(2,1)S(1)} %get-tuple-element.39) | copy-start | bytes 786436
  85.6 7.9 %collective-permute-start.5 = (bf16[256,512]{1,0:T(8,128)(2,1)S(1)}, bf16[256,512]{1,0:T(8,128)(2,1)S(1)}, u32[]{:S(2)}, u32[]{:S(2)}) collective-permute-start(bf16[256,512]{1,0:T(8,128)(2,1)S(1)} %get-tuple-element.42), channel_id=1, source_target_pairs={{0,4},{4,8},{8,12},{12,0},{1,5},{5,9},{9,13},{13,1},{2,6},{6,10},{... | collective-permute-start | bytes 786440 | tf_op jit(solution)/shard_map/ppermute | solution.py:101
  86.9 13.2 %collective-permute-start.6 = (bf16[256,512]{1,0:T(8,128)(2,1)S(1)}, bf16[256,512]{1,0:T(8,128)(2,1)S(1)}, u32[]{:S(2)}, u32[]{:S(2)}) collective-permute-start(bf16[256,512]{1,0:T(8,128)(2,1)S(1)} %get-tuple-element.41), channel_id=1, source_target_pairs={{0,8},{4,12},{8,0},{12,4},{1,9},{5,13},{9,1},{13,5},{2,10},{6,14},... | collective-permute-start | bytes 786440 | tf_op jit(solution)/shard_map/ppermute | solution.py:101
  89.3 10.9 %collective-permute-start.7 = (bf16[256,512]{1,0:T(8,128)(2,1)S(1)}, bf16[256,512]{1,0:T(8,128)(2,1)S(1)}, u32[]{:S(2)}, u32[]{:S(2)}) collective-permute-start(bf16[256,512]{1,0:T(8,128)(2,1)S(1)} %get-tuple-element.40), channel_id=1, source_target_pairs={{0,12},{4,0},{8,4},{12,8},{1,13},{5,1},{9,5},{13,9},{2,14},{6,2},{... | collective-permute-start | bytes 786440 | tf_op jit(solution)/shard_map/ppermute | solution.py:101
  90.5 23.6 %collective-permute-start.8 = (bf16[384,1536]{1,0:T(8,128)(2,1)}, bf16[384,1536]{1,0:T(8,128)(2,1)}, u32[]{:S(2)}, u32[]{:S(2)}) collective-permute-start(bf16[384,1536]{1,0:T(8,128)(2,1)} %collective-permute-done), channel_id=1, source_target_pairs={{0,1},{1,0},{2,3},{3,2},{4,5},{5,4},{6,7},{7,6},{8,9},{9,8},{10,11... | collective-permute-start | bytes 3538952 | tf_op jit(solution)/shard_map/ppermute | solution.py:137
  93.5 7.1 %copy-start.7 = (bf16[256,512]{1,0:T(8,128)(2,1)}, bf16[256,512]{1,0:T(8,128)(2,1)S(1)}, u32[]{:S(2)}) copy-start(bf16[256,512]{1,0:T(8,128)(2,1)S(1)} %collective-permute-done.5) | copy-start | bytes 786436
  100.1 0.7 copy-start.8
  100.2 0.7 copy-start.9
  103.2 10.8 %copy-start.4 = (bf16[256,1536]{1,0:T(8,128)(2,1)S(1)}, bf16[256,1536]{1,0:T(8,128)(2,1)}, u32[]{:S(2)}) copy-start(bf16[256,1536]{1,0:T(8,128)(2,1)} %copy-done.3) | copy-start | bytes 2359300
  103.2 10.8 %copy-start.15 = (bf16[1,384,1536]{2,1,0:T(8,128)(2,1)S(1)}, bf16[1,384,1536]{2,1,0:T(8,128)(2,1)}, u32[]{:S(2)}) copy-start(bf16[1,384,1536]{2,1,0:T(8,128)(2,1)} %param.15) | copy-start | bytes 3538948
  114.1 3.7 %copy-start.14 = (bf16[3,1536,384]{2,1,0:T(8,128)(2,1)S(1)}, bf16[3,1536,384]{2,1,0:T(8,128)(2,1)}, u32[]{:S(2)}) copy-start(bf16[3,1536,384]{2,1,0:T(8,128)(2,1)} %param.18) | copy-start | bytes 10616836
  114.1 3.7 %copy-start.22 = (f32[1536]{0:T(1024)S(1)}, f32[1536]{0:T(1024)}, u32[]{:S(2)}) copy-start(f32[1536]{0:T(1024)} %param.17) | copy-start | bytes 18436
  117.7 14.8 %copy-start.24 = (bf16[256,1536]{1,0:T(8,128)(2,1)}, bf16[256,1536]{1,0:T(8,128)(2,1)S(1)}, u32[]{:S(2)}) copy-start(bf16[256,1536]{1,0:T(8,128)(2,1)S(1)} %get-tuple-element.52) | copy-start | bytes 2359300
  118.4 14.1 %copy-start.23 = (f32[1536]{0:T(1024)S(1)}, f32[1536]{0:T(1024)}, u32[]{:S(2)}) copy-start(f32[1536]{0:T(1024)} %param.16) | copy-start | bytes 18436
  119.1 8.4 %collective-permute-start.9 = (bf16[256,384]{1,0:T(8,128)(2,1)S(1)}, bf16[256,384]{1,0:T(8,128)(2,1)S(1)}, u32[]{:S(2)}, u32[]{:S(2)}) collective-permute-start(bf16[256,384]{1,0:T(8,128)(2,1)S(1)} %fusion.62), channel_id=1, source_target_pairs={{0,128},{1,129},{2,130},{3,131},{4,132},{5,133},{6,134},{7,135},{8... | collective-permute-start | bytes 589832 | tf_op jit(solution)/shard_map/ppermute | solution.py:23
  123.4 8.3 %collective-permute-start.10 = (bf16[256,384]{1,0:T(8,128)(2,1)S(1)}, bf16[256,384]{1,0:T(8,128)(2,1)S(1)}, u32[]{:S(2)}, u32[]{:S(2)}) collective-permute-start(bf16[256,384]{1,0:T(8,128)(2,1)S(1)} %fusion.65), channel_id=1, source_target_pairs={{0,128},{1,129},{2,130},{3,131},{4,132},{5,133},{6,134},{7,135},{8... | collective-permute-start | bytes 589832 | tf_op jit(solution)/shard_map/ppermute | solution.py:23
  176.9 1.9 copy-start.2
  191.2 7.9 %collective-permute-start.11 = (bf16[256,512]{1,0:T(8,128)(2,1)S(1)}, bf16[256,512]{1,0:T(8,128)(2,1)S(1)}, u32[]{:S(2)}, u32[]{:S(2)}) collective-permute-start(bf16[256,512]{1,0:T(8,128)(2,1)S(1)} %get-tuple-element.38), channel_id=1, source_target_pairs={{0,4},{4,8},{8,12},{12,0},{1,5},{5,9},{9,13},{13,1},{2,6},{6,10},{... | collective-permute-start | bytes 786440 | tf_op jit(solution)/shard_map/ppermute | solution.py:101
  192.5 13.2 %collective-permute-start.12 = (bf16[256,512]{1,0:T(8,128)(2,1)S(1)}, bf16[256,512]{1,0:T(8,128)(2,1)S(1)}, u32[]{:S(2)}, u32[]{:S(2)}) collective-permute-start(bf16[256,512]{1,0:T(8,128)(2,1)S(1)} %get-tuple-element.37), channel_id=1, source_target_pairs={{0,8},{4,12},{8,0},{12,4},{1,9},{5,13},{9,1},{13,5},{2,10},{6,14},... | collective-permute-start | bytes 786440 | tf_op jit(solution)/shard_map/ppermute | solution.py:101
  194.9 10.9 %collective-permute-start.13 = (bf16[256,512]{1,0:T(8,128)(2,1)S(1)}, bf16[256,512]{1,0:T(8,128)(2,1)S(1)}, u32[]{:S(2)}, u32[]{:S(2)}) collective-permute-start(bf16[256,512]{1,0:T(8,128)(2,1)S(1)} %get-tuple-element.36), channel_id=1, source_target_pairs={{0,12},{4,0},{8,4},{12,8},{1,13},{5,1},{9,5},{13,9},{2,14},{6,2},{... | collective-permute-start | bytes 786440 | tf_op jit(solution)/shard_map/ppermute | solution.py:101
  205.7 0.7 copy-start.10
  205.8 0.7 copy-start.11
  214.1 10.9 %copy-start.12 = (bf16[384,384]{1,0:T(8,128)(2,1)S(1)}, bf16[384,384]{1,0:T(8,128)(2,1)}, u32[]{:S(2)}) copy-start(bf16[384,384]{1,0:T(8,128)(2,1)} %get-tuple-element.23) | copy-start | bytes 884740
  214.1 10.9 %copy-start.17 = (bf16[384,384]{1,0:T(8,128)(2,1)S(1)}, bf16[384,384]{1,0:T(8,128)(2,1)}, u32[]{:S(2)}) copy-start(bf16[384,384]{1,0:T(8,128)(2,1)} %copy-done.16) | copy-start | bytes 884740
  214.1 10.9 %copy-start.19 = (bf16[384,384]{1,0:T(8,128)(2,1)S(1)}, bf16[384,384]{1,0:T(8,128)(2,1)}, u32[]{:S(2)}) copy-start(bf16[384,384]{1,0:T(8,128)(2,1)} %copy-done.18) | copy-start | bytes 884740
  214.1 10.9 %copy-start.21 = (bf16[384,384]{1,0:T(8,128)(2,1)S(1)}, bf16[384,384]{1,0:T(8,128)(2,1)}, u32[]{:S(2)}) copy-start(bf16[384,384]{1,0:T(8,128)(2,1)} %copy-done.20) | copy-start | bytes 884740
Sparse Core Ops, SparseCore 0:
  24.1 46.3 all-gather.2
  132.7 44.2 all-gather.4

commit v10 on v8

--- a/solution.py
+++ b/solution.py
@@ -11,6 +11,7 @@
 HEAD_DIM = 128
 MP = ("my", "mc")
 X_SIZE = 4
+Z_LO = 2
 CORES = 2
 TILE = 256
 STATS = 128
@@ -87,12 +88,12 @@
 def attend(queries, pairs, riders=None):
     rows, width = queries.shape
     heads = width // HEAD_DIM
-    query_block = lax.all_gather(queries, "bx", axis=0, tiled=True)
-    key_block = lax.all_gather(pairs, "bz", axis=1, tiled=True)
+    query_block = lax.all_gather(queries, "qa", axis=0, tiled=True)
+    key_block = lax.all_gather(pairs, ("kz", "kx"), axis=1, tiled=True)
     partial = partial_attend(query_block, key_block)
     if riders is not None:
         partial, riders = lax.optimization_barrier((partial, riders))
-    parts = lax.all_to_all(partial, "bx", 0, 0, tiled=True)
+    parts = lax.all_to_all(partial, "qa", 0, 0, tiled=True)
     parts = parts.reshape(-1, rows, width + STATS).astype(jnp.float32)
     outs = parts[:, :, :width].reshape(-1, rows, heads, HEAD_DIM)
     stats = parts[:, :, width:width + 2 * heads * PARTS].reshape(-1, rows, 2, heads, PARTS)
@@ -203,10 +204,12 @@
 def solution(mesh):
     segments, blocks, parts = (mesh.shape["segment"], mesh.shape["blk"], mesh.shape["mp"])
     split = Mesh(
-        mesh.devices.reshape(segments, blocks // X_SIZE, X_SIZE, parts // CORES, CORES),
-        ("segment", "bz", "bx", "my", "mc"),
-    )
-    rows = ("bz", "bx")
+        mesh.devices.reshape(
+            segments, blocks // (Z_LO * X_SIZE), Z_LO, X_SIZE, parts // CORES, CORES
+        ),
+        ("segment", "qa", "kz", "kx", "my", "mc"),
+    )
+    rows = ("qa", "kz", "kx")
     return jax.shard_map(
         on_device,
         mesh=split,

time: 231 us -> 273 us (1.18); the launches traced: 231 us -> 270 us
  blocking collectives: 54.9 us -> 76.8 us
  waiting for transfers between devices: 92.3 us -> 108 us
    all_gather x2, blocking collectives: 22.7 us -> 48.5 us  [attend(): query_block = lax.all_gather(queries, 'qa', axis=0, tiled=True)]
    all_to_all x2, waiting for transfers between devices: 25.8 us -> 44 us  [attend(): parts = lax.all_to_all(partial, 'qa', 0, 0, tiled=True)]
where the time goes in v10:
time: 273 us; the launch traced here: 270 us
  waiting for transfers between devices  108 us (40%)
  blocking collectives  76.8 us (28%)
  Pallas kernels  24.7 us (9%)
  starting transfers between devices  19 us (7%)
  matrix products  16.2 us (6%)
  between operations  13.7 us (5%)
  local copies, waits for them, and re-layouts  9.29 us (3%)
    all_gather x2, waiting for transfers between devices, attend(): key_block = lax.all_gather(pairs, ('kz', 'kx'), axis=1, tiled=True)  55.8 us
    all_gather x2, blocking collectives, attend(): query_block = lax.all_gather(queries, 'qa', axis=0, tiled=True)  48.5 us
    all_to_all x2, waiting for transfers between devices, attend(): parts = lax.all_to_all(partial, 'qa', 0, 0, tiled=True)  44 us
    pallas_call x2, Pallas kernels, partial_attend(): pl.pallas_call(partial_kernel, grid=(rows // TILE,), in_specs=[pl.BlockSp...  24.7 us
    all_gather x1, blocking collectives, on_device(): embedded_full = lax.all_gather(embedded, MP, axis=1, tiled=True)  10.3 us
    all_gather x1, blocking collectives, on_device(): self_attended = lax.all_gather(self_local, MP, axis=1, tiled=True)  9.32 us
    all_to_all x2, starting transfers between devices, attend(): parts = lax.all_to_all(partial, 'qa', 0, 0, tiled=True)  9.07 us
    dot_general x6, matrix products, project(): jnp.dot(normed, weight, preferred_element_type=jnp.float32)  8.93 us
  transfers between devices with their start and end apart: 11, of which 5 were waited for; matrix products, arithmetic and copies ran while one was open for 2% of the time, Pallas kernels for 5%

profile of v10, /device:TPU:1, one launch (start us, length us, event | category | flops | bytes accessed | tf_op | source)
XLA Modules:
  0.0 269.8 jit_solution(12439314619147283687)
XLA Ops:
  6.5 0.0 copy-start
  6.5 0.0 all-gather.3.cloned.1.call-start
  6.5 0.9 copy-done
  7.5 1.2 fusion.68
  8.7 10.3 %all_gather.21 = bf16[256,1536]{1,0:T(8,128)(2,1)S(1)} all-gather(bf16[256,384]{1,0:T(8,128)(2,1)S(1)} %fusion.68), channel_id=1, replica_groups=mesh['segment'=2,'qa'=4,'kz'=2,'kx'=4,'my'=2,'mc'=2] {'my','mc'}, dimensions={1}, use_global_device_ids=true | all-gather | bytes 983040 | tf_op jit(solution)/shard_map/all_gather | solution.py:175
  19.0 0.2 fusion.19
  19.2 0.0 copy-done.5
  19.2 1.9 fusion.78
  21.1 0.0 copy-start.3
  21.2 2.0 fusion.75
  23.1 0.8 pad_maximum_fusion
  24.0 0.0 all-gather.3.cloned.1.call-update
  24.0 0.2 collective-permute-start.1
  24.3 1.6 collective-permute-start
  25.9 1.0 constant_dynamic-slice_fusion.8
  26.8 0.6 collective-permute-start.4
  27.5 1.1 collective-permute-start.2
  28.6 0.2 collective-permute-start.3
  28.8 1.9 fusion.50
  30.7 25.5 %all_gather.22.q_ref = bf16[1024,384]{1,0:T(8,128)(2,1)S(1)} all-gather(bf16[256,384]{1,0:T(8,128)(2,1)S(1)} %fusion.50), channel_id=1, replica_groups=mesh['segment'=2,'qa'=4,'kz'=2,'kx'=4,'my'=2,'mc'=2] {'qa'}, dimensions={0}, use_global_device_ids=true | all-gather | bytes 983040 | tf_op jit(solution)/shard_map/all_gather | solution.py:91
  56.2 26.6 %all-gather.3.cloned.1.call-done.k_ref.v_ref = bf16[2,2048,384]{2,1,0:T(8,128)(2,1)} async-done(((bf16[2,256,384]{2,1,0:T(8,128)(2,1)}), bf16[2,2048,384]{2,1,0:T(8,128)(2,1)}) %all-gather.3.cloned.1.call-update) | async-done | bytes 3145744 | tf_op jit(solution)/shard_map/all_gather | solution.py:92
  82.8 1.9 copy-done.1
  84.7 12.4 %shard_map.100 = bf16[1024,512]{1,0:T(8,128)(2,1)S(1)} custom-call(bf16[1024,384]{1,0:T(8,128)(2,1)S(1)} %all_gather.22.q_ref, bf16[2,2048,384]{2,1,0:T(8,128)(2,1)S(1)} %copy-done.1, bf16[2,2048,384]{2,1,0:T(8,128)(2,1)S(1)} %copy-done.1), custom_call_target="tpu_custom_call" | custom-call | tf_op jit(solution)/shard_map/pallas_call | solution.py:74
  97.1 0.0 collective-permute-done.4
  97.1 0.0 collective-permute-done.2
  97.1 0.0 collective-permute-done.3
  97.1 0.0 collective-permute-done.1
  97.1 0.0 collective-permute-done
  97.1 1.3 copy.15
  98.5 3.5 %all-to-all-start = ((bf16[4,256,512]{1,2,0:T(8,128)(2,1)}), bf16[4,256,512]{1,2,0:T(8,128)(2,1)S(1)}, u32[]{:S(2)}, u32[]{:S(2)}) async-start(bf16[4,256,512]{1,2,0:T(8,128)(2,1)} %copy.15), calls=%async_computation | async-start | bytes 2097152 | tf_op jit(solution)/shard_map/all_to_all | solution.py:96
  102.0 0.0 all-gather.5.cloned.1.call-start
  102.0 1.9 collective-permute-start.5
  104.0 20.2 %all-to-all-done = bf16[4,256,512]{1,2,0:T(8,128)(2,1)S(1)} async-done(((bf16[4,256,512]{1,2,0:T(8,128)(2,1)}), bf16[4,256,512]{1,2,0:T(8,128)(2,1)S(1)}, u32[]{:S(2)}, u32[]{:S(2)}) %all-to-all-start) | async-done | bytes 1048608 | tf_op jit(solution)/shard_map/all_to_all | solution.py:96
  124.3 0.2 convert_element_type.74
  124.5 0.1 fusion.23
  124.7 0.0 copy-start.7
  124.7 9.3 %all_gather.24 = bf16[256,1536]{0,1:T(8,128)(2,1)S(1)} all-gather(bf16[256,384]{0,1:T(8,128)(2,1)S(1)} %fusion.99), channel_id=1, replica_groups=mesh['segment'=2,'qa'=4,'kz'=2,'kx'=4,'my'=2,'mc'=2] {'my','mc'}, dimensions={1}, use_global_device_ids=true | all-gather | bytes 983040 | tf_op jit(solution)/shard_map/all_gather | solution.py:185
  134.0 0.1 constant_dynamic-slice_fusion.7
  134.1 0.0 collective-permute-done.5
  134.1 0.0 copy-start.6
  134.1 0.0 copy-start.8
  134.1 3.7 %fusion.18 = (f32[256]{0:T(256)S(1)}, bf16[256,1536]{1,0:T(8,128)(2,1)S(1)}) fusion(bf16[384,1536]{1,0:T(8,128)(2,1)} %collective-permute-done.5, bf16[384,1536]{1,0:T(8,128)(2,1)} %collective-permute-done.1, bf16[384,1536]{1,0:T(8,128)(2,1)} %collective-permute-done, bf16[384,1536]{1,0:T(8,128)(2,1)S(1)} %bitcast.101, ...), kind=kOutput, calls=%fused_computation.18 | convolution fusion | flops 1232338688 | bytes 7078912 | tf_op jit(solution)/shard_map/dot_general | solution.py:147
  137.8 0.0 copy-done.6
  137.8 0.0 copy-done.8
  137.8 0.6 fusion.69
  138.5 0.0 copy-start.9
  138.5 0.6 fusion.72
  139.2 4.1 %collective-permute-start.6 = (bf16[2,256,384]{2,1,0:T(8,128)(2,1)S(1)}, bf16[2,256,384]{2,1,0:T(8,128)(2,1)S(1)}, u32[]{:S(2)}, u32[]{:S(2)}) collective-permute-start(bf16[2,256,384]{2,1,0:T(8,128)(2,1)S(1)} %pad_maximum_fusion.1), channel_id=1, source_target_pairs={{0,128},{1,129},{2,130},{3,131},{4,132},{5,133},{6,134},{7,135},{8... | collective-permute-start | bytes 1179656 | tf_op jit(solution)/shard_map/ppermute | solution.py:24
  143.2 8.3 %collective-permute-done.6 = bf16[2,256,384]{2,1,0:T(8,128)(2,1)S(1)} collective-permute-done((bf16[2,256,384]{2,1,0:T(8,128)(2,1)S(1)}, bf16[2,256,384]{2,1,0:T(8,128)(2,1)S(1)}, u32[]{:S(2)}, u32[]{:S(2)}) %collective-permute-start.6) | collective-permute-done | bytes 393248 | tf_op jit(solution)/shard_map/ppermute | solution.py:24
  151.5 0.8 copy-done.4
  152.3 0.0 all-gather.5.cloned.1.call-update
  152.3 1.9 fusion.59
  154.2 23.0 %all_gather.25.q_ref = bf16[1024,384]{1,0:T(8,128)(2,1)S(1)} all-gather(bf16[256,384]{1,0:T(8,128)(2,1)S(1)} %fusion.59), channel_id=1, replica_groups=mesh['segment'=2,'qa'=4,'kz'=2,'kx'=4,'my'=2,'mc'=2] {'qa'}, dimensions={0}, use_global_device_ids=true | all-gather | bytes 983040 | tf_op jit(solution)/shard_map/all_gather | solution.py:91
  177.2 29.2 %all-gather.5.cloned.1.call-done.k_ref.v_ref = bf16[2,2048,384]{2,1,0:T(8,128)(2,1)} async-done(((bf16[2,256,384]{2,1,0:T(8,128)(2,1)}), bf16[2,2048,384]{2,1,0:T(8,128)(2,1)}) %all-gather.5.cloned.1.call-update) | async-done | bytes 3145744 | tf_op jit(solution)/shard_map/all_gather | solution.py:92
  206.4 1.9 copy-done.2
  208.3 12.3 %shard_map.101 = bf16[1024,512]{1,0:T(8,128)(2,1)S(1)} custom-call(bf16[1024,384]{1,0:T(8,128)(2,1)S(1)} %all_gather.25.q_ref, bf16[2,2048,384]{2,1,0:T(8,128)(2,1)S(1)} %copy-done.2, bf16[2,2048,384]{2,1,0:T(8,128)(2,1)S(1)} %copy-done.2), custom_call_target="tpu_custom_call" | custom-call | tf_op jit(solution)/shard_map/pallas_call | solution.py:74
  220.6 1.3 copy.18
  221.9 5.6 %all-to-all-start.1 = ((bf16[4,256,512]{1,2,0:T(8,128)(2,1)}), bf16[4,256,512]{1,2,0:T(8,128)(2,1)S(1)}, u32[]{:S(2)}, u32[]{:S(2)}) async-start(bf16[4,256,512]{1,2,0:T(8,128)(2,1)} %copy.18), calls=%async_computation.1 | async-start | bytes 2097152 | tf_op jit(solution)/shard_map/all_to_all | solution.py:96
  227.4 23.8 %all-to-all-done.1 = bf16[4,256,512]{1,2,0:T(8,128)(2,1)S(1)} async-done(((bf16[4,256,512]{1,2,0:T(8,128)(2,1)}), bf16[4,256,512]{1,2,0:T(8,128)(2,1)S(1)}, u32[]{:S(2)}, u32[]{:S(2)}) %all-to-all-start.1) | async-done | bytes 1048608 | tf_op jit(solution)/shard_map/all_to_all | solution.py:96
  251.4 0.2 convert_element_type.84
  251.6 0.1 fusion.22
  251.8 8.7 %all_gather.27 = bf16[256,1536]{0,1:T(8,128)(2,1)S(1)} all-gather(bf16[256,384]{0,1:T(8,128)(2,1)S(1)} %fusion.98), channel_id=1, replica_groups=mesh['segment'=2,'qa'=4,'kz'=2,'kx'=4,'my'=2,'mc'=2] {'my','mc'}, dimensions={1}, use_global_device_ids=true | all-gather | bytes 983040 | tf_op jit(solution)/shard_map/all_gather | solution.py:196
  260.5 0.1 constant_dynamic-slice_fusion.3
  260.5 2.4 fusion.103
  (25 shorter events, 0.4 us)
Async XLA Ops:
  6.5 0.9 copy-start
  6.5 12.7 %copy-start.5 = (f32[1,1536]{1,0:T(1,128)S(1)}, f32[1,1536]{1,0:T(1,128)}, u32[]{:S(2)}) copy-start(f32[1,1536]{1,0:T(1,128)} %param.13) | copy-start | bytes 18436
  6.5 76.3 %all-gather.3.cloned.1.call-start = ((), (), s32[]{:S(2)}) async-start(), calls=%async_computation.2 | async-start | bytes 3538944 | tf_op jit(solution)/shard_map/all_gather | solution.py:92
  21.1 4.7 %copy-start.3 = (bf16[384,1536]{1,0:T(8,128)(2,1)S(1)}, bf16[384,1536]{1,0:T(8,128)(2,1)}, u32[]{:S(2)}) copy-start(bf16[384,1536]{1,0:T(8,128)(2,1)} %param.19) | copy-start | bytes 3538948
  24.0 73.1 %collective-permute-start.1 = (bf16[384,1536]{1,0:T(8,128)(2,1)}, bf16[384,1536]{1,0:T(8,128)(2,1)}, u32[]{:S(2)}, u32[]{:S(2)}) collective-permute-start(bf16[384,1536]{1,0:T(8,128)(2,1)} %bitcast.99), channel_id=1, source_target_pairs={{0,1},{1,0},{2,3},{3,2},{4,5},{5,4},{6,7},{7,6},{8,9},{9,8},{10,11... | collective-permute-start | bytes 3538952 | tf_op jit(solution)/shard_map/ppermute | solution.py:124
  24.3 72.9 %collective-permute-start = (bf16[384,1536]{1,0:T(8,128)(2,1)}, bf16[384,1536]{1,0:T(8,128)(2,1)}, u32[]{:S(2)}, u32[]{:S(2)}) collective-permute-start(bf16[384,1536]{1,0:T(8,128)(2,1)} %bitcast.100), channel_id=1, source_target_pairs={{0,2},{2,0},{1,3},{3,1},{4,6},{6,4},{5,7},{7,5},{8,10},{10,8},{9,1... | collective-permute-start | bytes 3538952 | tf_op jit(solution)/shard_map/ppermute | solution.py:123
  26.8 70.2 %collective-permute-start.4 = (bf16[384,384]{1,0:T(8,128)(2,1)}, bf16[384,384]{1,0:T(8,128)(2,1)}, u32[]{:S(2)}, u32[]{:S(2)}) collective-permute-start(bf16[384,384]{1,0:T(8,128)(2,1)} %get-tuple-element.31), channel_id=1, source_target_pairs={{0,3},{1,0},{2,1},{3,2},{4,7},{5,4},{6,5},{7,6},{8,11},{9,8},{10,9... | collective-permute-start | bytes 884744 | tf_op jit(solution)/shard_map/ppermute | solution.py:117
  27.5 69.6 %collective-permute-start.2 = (bf16[384,384]{1,0:T(8,128)(2,1)}, bf16[384,384]{1,0:T(8,128)(2,1)}, u32[]{:S(2)}, u32[]{:S(2)}) collective-permute-start(bf16[384,384]{1,0:T(8,128)(2,1)} %get-tuple-element.32), channel_id=1, source_target_pairs={{0,1},{1,2},{2,3},{3,0},{4,5},{5,6},{6,7},{7,4},{8,9},{9,10},{10,1... | collective-permute-start | bytes 884744 | tf_op jit(solution)/shard_map/ppermute | solution.py:117
  28.6 68.5 %collective-permute-start.3 = (bf16[384,384]{1,0:T(8,128)(2,1)S(1)}, bf16[384,384]{1,0:T(8,128)(2,1)}, u32[]{:S(2)}, u32[]{:S(2)}) collective-permute-start(bf16[384,384]{1,0:T(8,128)(2,1)S(1)} %get-tuple-element.34), channel_id=1, source_target_pairs={{0,2},{1,3},{2,0},{3,1},{4,6},{5,7},{6,4},{7,5},{8,10},{9,11},{10,... | collective-permute-start | bytes 884744 | tf_op jit(solution)/shard_map/ppermute | solution.py:117
  82.8 1.9 copy-start.1
  98.5 25.7 %all-to-all-start = ((bf16[4,256,512]{1,2,0:T(8,128)(2,1)}), bf16[4,256,512]{1,2,0:T(8,128)(2,1)S(1)}, u32[]{:S(2)}, u32[]{:S(2)}) async-start(bf16[4,256,512]{1,2,0:T(8,128)(2,1)} %copy.15), calls=%async_computation | async-start | bytes 2097152 | tf_op jit(solution)/shard_map/all_to_all | solution.py:96
  102.0 104.4 %all-gather.5.cloned.1.call-start = ((), (), s32[]{:S(2)}) async-start(), calls=%async_computation.3 | async-start | bytes 3538944 | tf_op jit(solution)/shard_map/all_gather | solution.py:92
  102.0 32.1 %collective-permute-start.5 = (bf16[384,1536]{1,0:T(8,128)(2,1)}, bf16[384,1536]{1,0:T(8,128)(2,1)}, u32[]{:S(2)}, u32[]{:S(2)}) collective-permute-start(bf16[384,1536]{1,0:T(8,128)(2,1)} %collective-permute-done), channel_id=1, source_target_pairs={{0,1},{1,0},{2,3},{3,2},{4,5},{5,4},{6,7},{7,6},{8,9},{9,8},{10,11... | collective-permute-start | bytes 3538952 | tf_op jit(solution)/shard_map/ppermute | solution.py:131
  124.7 9.4 %copy-start.7 = (bf16[1,384,1536]{2,1,0:T(8,128)(2,1)S(1)}, bf16[1,384,1536]{2,1,0:T(8,128)(2,1)}, u32[]{:S(2)}) copy-start(bf16[1,384,1536]{2,1,0:T(8,128)(2,1)} %param.15) | copy-start | bytes 3538948
  134.1 3.7 %copy-start.6 = (bf16[3,1536,384]{2,1,0:T(8,128)(2,1)S(1)}, bf16[3,1536,384]{2,1,0:T(8,128)(2,1)}, u32[]{:S(2)}) copy-start(bf16[3,1536,384]{2,1,0:T(8,128)(2,1)} %param.18) | copy-start | bytes 10616836
  134.1 3.7 %copy-start.8 = (f32[1536]{0:T(1024)S(1)}, f32[1536]{0:T(1024)}, u32[]{:S(2)}) copy-start(f32[1536]{0:T(1024)} %param.17) | copy-start | bytes 18436
  138.5 13.8 %copy-start.9 = (f32[1536]{0:T(1024)S(1)}, f32[1536]{0:T(1024)}, u32[]{:S(2)}) copy-start(f32[1536]{0:T(1024)} %param.16) | copy-start | bytes 18436
  139.2 12.3 %collective-permute-start.6 = (bf16[2,256,384]{2,1,0:T(8,128)(2,1)S(1)}, bf16[2,256,384]{2,1,0:T(8,128)(2,1)S(1)}, u32[]{:S(2)}, u32[]{:S(2)}) collective-permute-start(bf16[2,256,384]{2,1,0:T(8,128)(2,1)S(1)} %pad_maximum_fusion.1), channel_id=1, source_target_pairs={{0,128},{1,129},{2,130},{3,131},{4,132},{5,133},{6,134},{7,135},{8... | collective-permute-start | bytes 1179656 | tf_op jit(solution)/shard_map/ppermute | solution.py:24
  151.5 0.8 copy-start.4
  206.4 1.9 copy-start.2
  221.9 29.4 %all-to-all-start.1 = ((bf16[4,256,512]{1,2,0:T(8,128)(2,1)}), bf16[4,256,512]{1,2,0:T(8,128)(2,1)S(1)}, u32[]{:S(2)}, u32[]{:S(2)}) async-start(bf16[4,256,512]{1,2,0:T(8,128)(2,1)} %copy.18), calls=%async_computation.1 | async-start | bytes 2097152 | tf_op jit(solution)/shard_map/all_to_all | solution.py:96
Sparse Core Ops, SparseCore 0:
  24.1 58.6 all-gather.2
  152.4 53.9 all-gather.4

commit v11 on v8

--- a/solution.py
+++ b/solution.py
@@ -67,29 +67,30 @@
     o_ref[:, heads * HEAD_DIM:] = stats.astype(o_ref.dtype)
 
 
-def partial_attend(queries, pairs):
+def partial_attend(queries, key_block, value_block):
     rows, width = queries.shape
-    keys = pairs.shape[1]
+    keys = key_block.shape[0]
     return pl.pallas_call(
         partial_kernel,
         grid=(rows // TILE,),
         in_specs=[
             pl.BlockSpec((TILE, width), lambda i: (i, 0)),
-            pl.BlockSpec((None, keys, width), lambda i: (0, 0, 0)),
-            pl.BlockSpec((None, keys, width), lambda i: (1, 0, 0)),
+            pl.BlockSpec((keys, width), lambda i: (0, 0)),
+            pl.BlockSpec((keys, width), lambda i: (0, 0)),
         ],
         out_specs=pl.BlockSpec((TILE, width + STATS), lambda i: (i, 0)),
         out_shape=jax.ShapeDtypeStruct((rows, width + STATS), jnp.bfloat16),
         compiler_params=pltpu.CompilerParams(vmem_limit_bytes=48 * 1024 * 1024),
-    )(queries, pairs, pairs)
+    )(queries, key_block, value_block)
 
 
 def attend(queries, pairs, riders=None):
     rows, width = queries.shape
     heads = width // HEAD_DIM
     query_block = lax.all_gather(queries, "bx", axis=0, tiled=True)
-    key_block = lax.all_gather(pairs, "bz", axis=1, tiled=True)
-    partial = partial_attend(query_block, key_block)
+    key_block = lax.all_gather(pairs[0], "bz", axis=0, tiled=True)
+    value_block = lax.all_gather(pairs[1], "bz", axis=0, tiled=True)
+    partial = partial_attend(query_block, key_block, value_block)
     if riders is not None:
         partial, riders = lax.optimization_barrier((partial, riders))
     parts = lax.all_to_all(partial, "bx", 0, 0, tiled=True)

time: 231 us -> 293 us (1.27)
  waiting for transfers between devices: 92.3 us -> 141 us
  blocking collectives: 54.9 us -> 62 us
  starting transfers between devices: 17.7 us -> 21 us
    all_gather x2 -> x4, waiting for transfers between devices: 58.1 us -> 117 us  [the longest x2 59.9 us: attend(): value_block = lax.all_gather(pairs[1], 'bz', axis=0, tiled=True)]
    all_to_all x2, waiting for transfers between devices: 25.8 us -> 15.5 us  [attend(): parts = lax.all_to_all(partial, 'bx', 0, 0, tiled=True)]
    all_gather x1, blocking collectives: 10.8 us -> 14.4 us  [on_device(): lax.all_gather(attend(cross_queries, arrived), MP, axis=1, tiled=True)]
    all_gather x1, blocking collectives: 11.1 us -> 14.7 us  [on_device(): self_attended = lax.all_gather(self_local, MP, axis=1, tiled=True)]
    ppermute x1, starting transfers between devices: 1.52 us -> 4.78 us  [rows_in_order(): far = lax.ppermute(other, 'mc', [(0, 1), (1, 0)])]
    unnamed x20 -> x22, local copies, waits for them, and re-layouts: 5.49 us -> 6.59 us
  transfers between devices with their start and end apart: 11 -> 13, of which waited for: 5 -> 7; matrix products, arithmetic and copies ran while one was open for 2% -> 3% of each run, Pallas kernels for 5% -> 4%
where the time goes in v11:
time: 293 us; the launch traced here: 292 us
  waiting for transfers between devices  141 us (48%)
  blocking collectives  62 us (21%)
  Pallas kernels  24.7 us (8%)
  starting transfers between devices  21 us (7%)
  matrix products  17.6 us (6%)
  between operations  13.4 us (5%)
  local copies, waits for them, and re-layouts  11.2 us (4%)
    all_gather x2, waiting for transfers between devices, attend(): value_block = lax.all_gather(pairs[1], 'bz', axis=0, tiled=True)  59.9 us
    all_gather x2, waiting for transfers between devices, attend(): key_block = lax.all_gather(pairs[0], 'bz', axis=0, tiled=True)  56.6 us
    pallas_call x2, Pallas kernels, partial_attend(): pl.pallas_call(partial_kernel, grid=(rows // TILE,), in_specs=[pl.BlockSp...  24.7 us
    all_gather x2, blocking collectives, attend(): query_block = lax.all_gather(queries, 'bx', axis=0, tiled=True)  22.7 us
    all_to_all x2, waiting for transfers between devices, attend(): parts = lax.all_to_all(partial, 'bx', 0, 0, tiled=True)  15.5 us
    all_gather x1, blocking collectives, on_device(): self_attended = lax.all_gather(self_local, MP, axis=1, tiled=True)  14.7 us
    all_gather x1, blocking collectives, on_device(): lax.all_gather(attend(cross_queries, arrived), MP, axis=1, tiled=True)  14.4 us
    dot_general x6, matrix products, project(): jnp.dot(normed, weight, preferred_element_type=jnp.float32)  10.3 us
  transfers between devices with their start and end apart: 13, of which 7 were waited for; matrix products, arithmetic and copies ran while one was open for 3% of the time, Pallas kernels for 4%

profile of v11, /device:TPU:1, one launch (start us, length us, event | category | flops | bytes accessed | tf_op | source)
XLA Modules:
  0.0 291.9 jit_solution(2091853869458379169)
XLA Ops:
  6.5 0.9 copy-done
  7.5 1.2 fusion.68
  8.7 10.3 %all_gather.27 = bf16[256,1536]{1,0:T(8,128)(2,1)S(1)} all-gather(bf16[256,384]{1,0:T(8,128)(2,1)S(1)} %fusion.68), channel_id=1, replica_groups=mesh['segment'=2,'bz'=8,'bx'=4,'my'=2,'mc'=2] {'my','mc'}, dimensions={1}, use_global_device_ids=true | all-gather | bytes 983040 | tf_op jit(solution)/shard_map/all_gather | solution.py:175
  19.0 0.2 fusion.19
  19.2 2.6 fusion.53
  21.8 0.0 all-gather.7.cloned.1.call-update
  21.8 0.0 copy-start.5
  21.8 0.0 all-gather.9.cloned.1.call-start
  21.9 2.7 fusion.56
  24.6 0.0 all-gather.9.cloned.1.call-update
  24.6 0.3 collective-permute-start.1
  24.9 1.6 collective-permute-start
  26.5 0.9 constant_dynamic-slice_fusion.8
  27.4 0.6 collective-permute-start.4
  28.0 1.1 collective-permute-start.2
  29.2 0.2 collective-permute-start.3
  29.4 1.9 fusion.50
  31.3 11.5 %all_gather.28.q_ref = bf16[1024,384]{1,0:T(8,128)(2,1)S(1)} all-gather(bf16[256,384]{1,0:T(8,128)(2,1)S(1)} %fusion.50), channel_id=1, replica_groups=mesh['segment'=2,'bz'=8,'bx'=4,'my'=2,'mc'=2] {'bx'}, dimensions={0}, use_global_device_ids=true | all-gather | bytes 983040 | tf_op jit(solution)/shard_map/all_gather | solution.py:90
  42.8 16.4 %all-gather.7.cloned.1.call-done.k_ref = bf16[2048,384]{1,0:T(8,128)(2,1)} async-done(((bf16[256,384]{1,0:T(8,128)(2,1)}), bf16[2048,384]{1,0:T(8,128)(2,1)}) %all-gather.7.cloned.1.call-update) | async-done | bytes 1572880 | tf_op jit(solution)/shard_map/all_gather | solution.py:91
  59.2 40.4 %all-gather.9.cloned.1.call-done.v_ref = bf16[2048,384]{1,0:T(8,128)(2,1)} async-done(((bf16[256,384]{1,0:T(8,128)(2,1)}), bf16[2048,384]{1,0:T(8,128)(2,1)}) %all-gather.9.cloned.1.call-update) | async-done | bytes 1572880 | tf_op jit(solution)/shard_map/all_gather | solution.py:92
  99.6 1.4 copy-done.1
  101.0 1.4 copy-done.2
  102.4 12.4 %shard_map.100 = bf16[1024,512]{1,0:T(8,128)(2,1)S(1)} custom-call(bf16[1024,384]{1,0:T(8,128)(2,1)S(1)} %all_gather.28.q_ref, bf16[2048,384]{1,0:T(8,128)(2,1)S(1)} %copy-done.1, bf16[2048,384]{1,0:T(8,128)(2,1)S(1)} %copy-done.2), custom_call_target="tpu_custom_call" | custom-call | tf_op jit(solution)/shard_map/pallas_call | solution.py:73
  114.8 0.0 collective-permute-done.4
  114.8 0.0 collective-permute-done.2
  114.8 0.0 collective-permute-done.3
  114.8 0.0 collective-permute-done
  114.8 1.3 copy.15
  116.2 4.0 %all-to-all-start = ((bf16[4,256,512]{1,2,0:T(8,128)(2,1)}), bf16[4,256,512]{1,2,0:T(8,128)(2,1)S(1)}, u32[]{:S(2)}, u32[]{:S(2)}) async-start(bf16[4,256,512]{1,2,0:T(8,128)(2,1)} %copy.15), calls=%async_computation | async-start | bytes 2097152 | tf_op jit(solution)/shard_map/all_to_all | solution.py:96
  120.1 4.8 %collective-permute-start.5 = (bf16[384,1536]{1,0:T(8,128)(2,1)}, bf16[384,1536]{1,0:T(8,128)(2,1)}, u32[]{:S(2)}, u32[]{:S(2)}) collective-permute-start(bf16[384,1536]{1,0:T(8,128)(2,1)} %collective-permute-done), channel_id=1, source_target_pairs={{0,1},{1,0},{2,3},{3,2},{4,5},{5,4},{6,7},{7,6},{8,9},{9,8},{10,11... | collective-permute-start | bytes 3538952 | tf_op jit(solution)/shard_map/ppermute | solution.py:131
  124.9 5.3 %all-to-all-done = bf16[4,256,512]{1,2,0:T(8,128)(2,1)S(1)} async-done(((bf16[4,256,512]{1,2,0:T(8,128)(2,1)}), bf16[4,256,512]{1,2,0:T(8,128)(2,1)S(1)}, u32[]{:S(2)}, u32[]{:S(2)}) %all-to-all-start) | async-done | bytes 1048608 | tf_op jit(solution)/shard_map/all_to_all | solution.py:96
  130.4 0.2 convert_element_type.74
  130.6 0.1 fusion.23
  130.7 0.0 copy-start.8
  130.8 14.7 %all_gather.31 = bf16[256,1536]{0,1:T(8,128)(2,1)S(1)} all-gather(bf16[256,384]{0,1:T(8,128)(2,1)S(1)} %fusion.93), channel_id=1, replica_groups=mesh['segment'=2,'bz'=8,'bx'=4,'my'=2,'mc'=2] {'my','mc'}, dimensions={1}, use_global_device_ids=true | all-gather | bytes 983040 | tf_op jit(solution)/shard_map/all_gather | solution.py:185
  145.4 0.1 constant_dynamic-slice_fusion.7
  145.5 0.0 collective-permute-done.5
  145.5 0.0 copy-start.7
  145.5 0.0 copy-start.9
  145.5 3.7 %fusion.18 = (f32[256]{0:T(256)S(1)}, bf16[256,1536]{1,0:T(8,128)(2,1)S(1)}) fusion(bf16[384,1536]{1,0:T(8,128)(2,1)} %collective-permute-done.5, bf16[384,1536]{1,0:T(8,128)(2,1)} %collective-permute-done.1, bf16[384,1536]{1,0:T(8,128)(2,1)} %collective-permute-done, bf16[384,1536]{1,0:T(8,128)(2,1)S(1)} %bitcast.97, ...), kind=kOutput, calls=%fused_computation.18 | convolution fusion | flops 1232338688 | bytes 7078912 | tf_op jit(solution)/shard_map/dot_general | solution.py:147
  149.2 0.6 fusion.69
  149.9 0.6 fusion.72
  150.5 0.0 copy-start.10
  150.6 4.4 %collective-permute-start.6 = (bf16[2,256,384]{2,1,0:T(8,128)(2,1)S(1)}, bf16[2,256,384]{2,1,0:T(8,128)(2,1)S(1)}, u32[]{:S(2)}, u32[]{:S(2)}) collective-permute-start(bf16[2,256,384]{2,1,0:T(8,128)(2,1)S(1)} %pad_maximum_fusion), channel_id=1, source_target_pairs={{0,128},{1,129},{2,130},{3,131},{4,132},{5,133},{6,134},{7,135},{8... | collective-permute-start | bytes 1179656 | tf_op jit(solution)/shard_map/ppermute | solution.py:23
  154.9 8.3 %collective-permute-done.6 = bf16[2,256,384]{2,1,0:T(8,128)(2,1)S(1)} collective-permute-done((bf16[2,256,384]{2,1,0:T(8,128)(2,1)S(1)}, bf16[2,256,384]{2,1,0:T(8,128)(2,1)S(1)}, u32[]{:S(2)}, u32[]{:S(2)}) %collective-permute-start.6) | collective-permute-done | bytes 393248 | tf_op jit(solution)/shard_map/ppermute | solution.py:23
  163.2 0.8 fusion.117
  164.0 0.0 all-gather.13.cloned.1.call-update
  164.0 0.0 all-gather.11.cloned.1.call-start
  164.1 0.5 all-gather.11.cloned.1.call-update
  164.6 1.9 fusion.59
  166.5 11.2 %all_gather.32.q_ref = bf16[1024,384]{1,0:T(8,128)(2,1)S(1)} all-gather(bf16[256,384]{1,0:T(8,128)(2,1)S(1)} %fusion.59), channel_id=1, replica_groups=mesh['segment'=2,'bz'=8,'bx'=4,'my'=2,'mc'=2] {'bx'}, dimensions={0}, use_global_device_ids=true | all-gather | bytes 983040 | tf_op jit(solution)/shard_map/all_gather | solution.py:90
  177.7 19.5 %all-gather.13.cloned.1.call-done = bf16[1,2048,384]{2,1,0:T(8,128)(2,1)} async-done(((bf16[1,256,384]{2,1,0:T(8,128)(2,1)}), bf16[1,2048,384]{2,1,0:T(8,128)(2,1)}) %all-gather.13.cloned.1.call-update) | async-done | bytes 1572880 | tf_op jit(solution)/shard_map/all_gather | solution.py:92
  197.3 40.2 %all-gather.11.cloned.1.call-done = bf16[1,2048,384]{2,1,0:T(8,128)(2,1)} async-done(((bf16[1,256,384]{2,1,0:T(8,128)(2,1)}), bf16[1,2048,384]{2,1,0:T(8,128)(2,1)}) %all-gather.11.cloned.1.call-update) | async-done | bytes 1572880 | tf_op jit(solution)/shard_map/all_gather | solution.py:91
  237.4 1.4 copy-done.3
  238.9 1.4 copy-done.4
  240.3 12.3 %shard_map.101 = bf16[1024,512]{1,0:T(8,128)(2,1)S(1)} custom-call(bf16[1024,384]{1,0:T(8,128)(2,1)S(1)} %all_gather.32.q_ref, bf16[2048,384]{1,0:T(8,128)(2,1)S(1)} %bitcast.91, bf16[2048,384]{1,0:T(8,128)(2,1)S(1)} %bitcast.90), custom_call_target="tpu_custom_call" | custom-call | tf_op jit(solution)/shard_map/pallas_call | solution.py:73
  252.6 1.3 copy.18
  253.9 4.0 %all-to-all-start.1 = ((bf16[4,256,512]{1,2,0:T(8,128)(2,1)}), bf16[4,256,512]{1,2,0:T(8,128)(2,1)S(1)}, u32[]{:S(2)}, u32[]{:S(2)}) async-start(bf16[4,256,512]{1,2,0:T(8,128)(2,1)} %copy.18), calls=%async_computation.1 | async-start | bytes 2097152 | tf_op jit(solution)/shard_map/all_to_all | solution.py:96
  257.9 10.1 %all-to-all-done.1 = bf16[4,256,512]{1,2,0:T(8,128)(2,1)S(1)} async-done(((bf16[4,256,512]{1,2,0:T(8,128)(2,1)}), bf16[4,256,512]{1,2,0:T(8,128)(2,1)S(1)}, u32[]{:S(2)}, u32[]{:S(2)}) %all-to-all-start.1) | async-done | bytes 1048608 | tf_op jit(solution)/shard_map/all_to_all | solution.py:96
  268.1 0.2 convert_element_type.84
  268.3 0.1 fusion.22
  268.5 14.4 %all_gather.35 = bf16[256,1536]{0,1:T(8,128)(2,1)S(1)} all-gather(bf16[256,384]{0,1:T(8,128)(2,1)S(1)} %fusion.92), channel_id=1, replica_groups=mesh['segment'=2,'bz'=8,'bx'=4,'my'=2,'mc'=2] {'my','mc'}, dimensions={1}, use_global_device_ids=true | all-gather | bytes 983040 | tf_op jit(solution)/shard_map/all_gather | solution.py:196
  282.9 0.1 constant_dynamic-slice_fusion.3
  282.9 2.4 fusion.97
  (33 shorter events, 0.4 us)
Async XLA Ops:
  6.5 0.9 copy-start
  6.5 12.7 %copy-start.6 = (f32[1,1536]{1,0:T(1,128)S(1)}, f32[1,1536]{1,0:T(1,128)}, u32[]{:S(2)}) copy-start(f32[1,1536]{1,0:T(1,128)} %param.13) | copy-start | bytes 18436
  6.5 52.6 %all-gather.7.cloned.1.call-start = ((), (), s32[]{:S(2)}) async-start(), calls=%async_computation.2 | async-start | bytes 1769472 | tf_op jit(solution)/shard_map/all_gather | solution.py:91
  21.8 4.6 %copy-start.5 = (bf16[384,1536]{1,0:T(8,128)(2,1)S(1)}, bf16[384,1536]{1,0:T(8,128)(2,1)}, u32[]{:S(2)}) copy-start(bf16[384,1536]{1,0:T(8,128)(2,1)} %param.19) | copy-start | bytes 3538948
  21.8 77.7 %all-gather.9.cloned.1.call-start = ((), (), s32[]{:S(2)}) async-start(), calls=%async_computation.3 | async-start | bytes 1769472 | tf_op jit(solution)/shard_map/all_gather | solution.py:92
  24.6 90.2 %collective-permute-start.1 = (bf16[384,1536]{1,0:T(8,128)(2,1)}, bf16[384,1536]{1,0:T(8,128)(2,1)}, u32[]{:S(2)}, u32[]{:S(2)}) collective-permute-start(bf16[384,1536]{1,0:T(8,128)(2,1)} %bitcast.95), channel_id=1, source_target_pairs={{0,1},{1,0},{2,3},{3,2},{4,5},{5,4},{6,7},{7,6},{8,9},{9,8},{10,11... | collective-permute-start | bytes 3538952 | tf_op jit(solution)/shard_map/ppermute | solution.py:124
  24.9 89.9 %collective-permute-start = (bf16[384,1536]{1,0:T(8,128)(2,1)}, bf16[384,1536]{1,0:T(8,128)(2,1)}, u32[]{:S(2)}, u32[]{:S(2)}) collective-permute-start(bf16[384,1536]{1,0:T(8,128)(2,1)} %bitcast.96), channel_id=1, source_target_pairs={{0,2},{2,0},{1,3},{3,1},{4,6},{6,4},{5,7},{7,5},{8,10},{10,8},{9,1... | collective-permute-start | bytes 3538952 | tf_op jit(solution)/shard_map/ppermute | solution.py:123
  27.4 87.3 %collective-permute-start.4 = (bf16[384,384]{1,0:T(8,128)(2,1)}, bf16[384,384]{1,0:T(8,128)(2,1)}, u32[]{:S(2)}, u32[]{:S(2)}) collective-permute-start(bf16[384,384]{1,0:T(8,128)(2,1)} %get-tuple-element.31), channel_id=1, source_target_pairs={{0,3},{1,0},{2,1},{3,2},{4,7},{5,4},{6,5},{7,6},{8,11},{9,8},{10,9... | collective-permute-start | bytes 884744 | tf_op jit(solution)/shard_map/ppermute | solution.py:117
  28.0 86.7 %collective-permute-start.2 = (bf16[384,384]{1,0:T(8,128)(2,1)}, bf16[384,384]{1,0:T(8,128)(2,1)}, u32[]{:S(2)}, u32[]{:S(2)}) collective-permute-start(bf16[384,384]{1,0:T(8,128)(2,1)} %get-tuple-element.32), channel_id=1, source_target_pairs={{0,1},{1,2},{2,3},{3,0},{4,5},{5,6},{6,7},{7,4},{8,9},{9,10},{10,1... | collective-permute-start | bytes 884744 | tf_op jit(solution)/shard_map/ppermute | solution.py:117
  29.2 85.6 %collective-permute-start.3 = (bf16[384,384]{1,0:T(8,128)(2,1)S(1)}, bf16[384,384]{1,0:T(8,128)(2,1)}, u32[]{:S(2)}, u32[]{:S(2)}) collective-permute-start(bf16[384,384]{1,0:T(8,128)(2,1)S(1)} %get-tuple-element.34), channel_id=1, source_target_pairs={{0,2},{1,3},{2,0},{3,1},{4,6},{5,7},{6,4},{7,5},{8,10},{9,11},{10,... | collective-permute-start | bytes 884744 | tf_op jit(solution)/shard_map/ppermute | solution.py:117
  99.6 1.4 copy-start.1
  101.0 1.4 copy-start.2
  116.2 14.1 %all-to-all-start = ((bf16[4,256,512]{1,2,0:T(8,128)(2,1)}), bf16[4,256,512]{1,2,0:T(8,128)(2,1)S(1)}, u32[]{:S(2)}, u32[]{:S(2)}) async-start(bf16[4,256,512]{1,2,0:T(8,128)(2,1)} %copy.15), calls=%async_computation | async-start | bytes 2097152 | tf_op jit(solution)/shard_map/all_to_all | solution.py:96
  120.1 77.1 %all-gather.13.cloned.1.call-start = ((), (), s32[]{:S(2)}) async-start(), calls=%async_computation.5 | async-start | bytes 1769472 | tf_op jit(solution)/shard_map/all_gather | solution.py:92
  120.1 25.4 %collective-permute-start.5 = (bf16[384,1536]{1,0:T(8,128)(2,1)}, bf16[384,1536]{1,0:T(8,128)(2,1)}, u32[]{:S(2)}, u32[]{:S(2)}) collective-permute-start(bf16[384,1536]{1,0:T(8,128)(2,1)} %collective-permute-done), channel_id=1, source_target_pairs={{0,1},{1,0},{2,3},{3,2},{4,5},{5,4},{6,7},{7,6},{8,9},{9,8},{10,11... | collective-permute-start | bytes 3538952 | tf_op jit(solution)/shard_map/ppermute | solution.py:131
  130.7 14.8 %copy-start.8 = (bf16[1,384,1536]{2,1,0:T(8,128)(2,1)S(1)}, bf16[1,384,1536]{2,1,0:T(8,128)(2,1)}, u32[]{:S(2)}) copy-start(bf16[1,384,1536]{2,1,0:T(8,128)(2,1)} %param.15) | copy-start | bytes 3538948
  145.5 3.7 %copy-start.7 = (bf16[3,1536,384]{2,1,0:T(8,128)(2,1)S(1)}, bf16[3,1536,384]{2,1,0:T(8,128)(2,1)}, u32[]{:S(2)}) copy-start(bf16[3,1536,384]{2,1,0:T(8,128)(2,1)} %param.18) | copy-start | bytes 10616836
  145.5 3.7 %copy-start.9 = (f32[1536]{0:T(1024)S(1)}, f32[1536]{0:T(1024)}, u32[]{:S(2)}) copy-start(f32[1536]{0:T(1024)} %param.17) | copy-start | bytes 18436
  150.5 14.1 %copy-start.10 = (f32[1536]{0:T(1024)S(1)}, f32[1536]{0:T(1024)}, u32[]{:S(2)}) copy-start(f32[1536]{0:T(1024)} %param.16) | copy-start | bytes 18436
  150.6 12.6 %collective-permute-start.6 = (bf16[2,256,384]{2,1,0:T(8,128)(2,1)S(1)}, bf16[2,256,384]{2,1,0:T(8,128)(2,1)S(1)}, u32[]{:S(2)}, u32[]{:S(2)}) collective-permute-start(bf16[2,256,384]{2,1,0:T(8,128)(2,1)S(1)} %pad_maximum_fusion), channel_id=1, source_target_pairs={{0,128},{1,129},{2,130},{3,131},{4,132},{5,133},{6,134},{7,135},{8... | collective-permute-start | bytes 1179656 | tf_op jit(solution)/shard_map/ppermute | solution.py:23
  164.0 73.4 %all-gather.11.cloned.1.call-start = ((), (), s32[]{:S(2)}) async-start(), calls=%async_computation.4 | async-start | bytes 1769472 | tf_op jit(solution)/shard_map/all_gather | solution.py:91
  237.4 1.4 copy-start.3
  238.9 1.4 copy-start.4
  253.9 14.1 %all-to-all-start.1 = ((bf16[4,256,512]{1,2,0:T(8,128)(2,1)}), bf16[4,256,512]{1,2,0:T(8,128)(2,1)S(1)}, u32[]{:S(2)}, u32[]{:S(2)}) async-start(bf16[4,256,512]{1,2,0:T(8,128)(2,1)} %copy.18), calls=%async_computation.1 | async-start | bytes 2097152 | tf_op jit(solution)/shard_map/all_to_all | solution.py:96
Sparse Core Ops, SparseCore 0:
  22.0 37.1 all-gather.6
  61.0 38.5 all-gather.8
  164.1 33.0 all-gather.12
  198.9 38.5 all-gather.10

commit v12 on v8

--- a/solution.py
+++ b/solution.py
@@ -53,10 +53,11 @@
         scores = lax.dot_general(
             q_ref[:, cols], k_ref[:, cols], (((1,), (1,)), ((), ())),
             preferred_element_type=jnp.float32,
-        ) * (1.0 / math.sqrt(HEAD_DIM))
+        )
         largest = jnp.max(scores, axis=1, keepdims=True)
-        weights = jnp.exp(scores - largest)
+        weights = jnp.exp2((scores - largest) * (math.log2(math.e) / math.sqrt(HEAD_DIM)))
         summed = jnp.sum(weights, axis=1, keepdims=True)
+        largest = largest * (1.0 / math.sqrt(HEAD_DIM))
         o_ref[:, cols] = jnp.dot(
             weights.astype(jnp.bfloat16), v_ref[:, cols], preferred_element_type=jnp.float32
         ).astype(o_ref.dtype)

time: 231 us -> 229 us (level)
  Pallas kernels: 24.7 us -> 22 us
    pallas_call x2, Pallas kernels: 24.7 us -> 22 us  [partial_attend(): pl.pallas_call(partial_kernel, grid=(rows // TILE,), in_specs=[pl.BlockSp...]
where the time goes in v12:
time: 229 us; the launch traced here: 228 us
  waiting for transfers between devices  92.3 us (40%)
  blocking collectives  54.9 us (24%)
  Pallas kernels  22 us (10%)
  starting transfers between devices  17.7 us (8%)
  matrix products  16.2 us (7%)
  between operations  13.7 us (6%)
  local copies, waits for them, and re-layouts  9.29 us (4%)
    all_gather x2, waiting for transfers between devices, attend(): key_block = lax.all_gather(pairs, 'bz', axis=1, tiled=True)  58.2 us
    all_to_all x2, waiting for transfers between devices, attend(): parts = lax.all_to_all(partial, 'bx', 0, 0, tiled=True)  25.8 us
    all_gather x2, blocking collectives, attend(): query_block = lax.all_gather(queries, 'bx', axis=0, tiled=True)  22.7 us
    pallas_call x2, Pallas kernels, partial_attend(): pl.pallas_call(partial_kernel, grid=(rows // TILE,), in_specs=[pl.BlockSp...  22 us
    all_gather x1, blocking collectives, on_device(): self_attended = lax.all_gather(self_local, MP, axis=1, tiled=True)  11.1 us
    all_gather x1, blocking collectives, on_device(): lax.all_gather(attend(cross_queries, arrived), MP, axis=1, tiled=True)  10.8 us
    all_gather x1, blocking collectives, on_device(): embedded_full = lax.all_gather(embedded, MP, axis=1, tiled=True)  10.3 us
    dot_general x6, matrix products, project(): jnp.dot(normed, weight, preferred_element_type=jnp.float32)  8.93 us
  transfers between devices with their start and end apart: 11, of which 5 were waited for; matrix products, arithmetic and copies ran while one was open for 2% of the time, Pallas kernels for 5%

profile of v12, /device:TPU:1, one launch (start us, length us, event | category | flops | bytes accessed | tf_op | source)
XLA Modules:
  0.0 228.1 jit_solution(17785650959406841411)
XLA Ops:
  6.5 0.0 copy-start
  6.5 0.0 all-gather.3.cloned.1.call-start
  6.5 0.9 copy-done
  7.5 1.2 fusion.68
  8.7 10.3 %all_gather.21 = bf16[256,1536]{1,0:T(8,128)(2,1)S(1)} all-gather(bf16[256,384]{1,0:T(8,128)(2,1)S(1)} %fusion.68), channel_id=1, replica_groups=mesh['segment'=2,'bz'=8,'bx'=4,'my'=2,'mc'=2] {'my','mc'}, dimensions={1}, use_global_device_ids=true | all-gather | bytes 983040 | tf_op jit(solution)/shard_map/all_gather | solution.py:175
  19.0 0.2 fusion.19
  19.2 0.0 copy-done.5
  19.2 1.9 fusion.78
  21.1 0.0 copy-start.3
  21.2 2.0 fusion.75
  23.1 0.8 pad_maximum_fusion
  24.0 0.0 all-gather.3.cloned.1.call-update
  24.0 0.2 collective-permute-start.1
  24.3 1.6 collective-permute-start
  25.9 0.0 copy-done.3
  25.9 1.0 constant_dynamic-slice_fusion.8
  26.8 0.6 collective-permute-start.4
  27.5 1.1 collective-permute-start.2
  28.6 0.2 collective-permute-start.3
  28.8 1.9 fusion.50
  30.7 11.9 %all_gather.22.q_ref = bf16[1024,384]{1,0:T(8,128)(2,1)S(1)} all-gather(bf16[256,384]{1,0:T(8,128)(2,1)S(1)} %fusion.50), channel_id=1, replica_groups=mesh['segment'=2,'bz'=8,'bx'=4,'my'=2,'mc'=2] {'bx'}, dimensions={0}, use_global_device_ids=true | all-gather | bytes 983040 | tf_op jit(solution)/shard_map/all_gather | solution.py:91
  42.6 27.9 %all-gather.3.cloned.1.call-done.k_ref.v_ref = bf16[2,2048,384]{2,1,0:T(8,128)(2,1)} async-done(((bf16[2,256,384]{2,1,0:T(8,128)(2,1)}), bf16[2,2048,384]{2,1,0:T(8,128)(2,1)}) %all-gather.3.cloned.1.call-update) | async-done | bytes 3145744 | tf_op jit(solution)/shard_map/all_gather | solution.py:92
  70.5 1.9 copy-done.1
  72.4 11.0 %shard_map.100 = bf16[1024,512]{1,0:T(8,128)(2,1)S(1)} custom-call(bf16[1024,384]{1,0:T(8,128)(2,1)S(1)} %all_gather.22.q_ref, bf16[2,2048,384]{2,1,0:T(8,128)(2,1)S(1)} %copy-done.1, bf16[2,2048,384]{2,1,0:T(8,128)(2,1)S(1)} %copy-done.1), custom_call_target="tpu_custom_call" | custom-call | tf_op jit(solution)/shard_map/pallas_call | solution.py:74
  83.4 0.0 collective-permute-done.4
  83.4 0.0 collective-permute-done.2
  83.4 0.0 collective-permute-done.3
  83.5 0.0 collective-permute-done.1
  83.5 0.0 collective-permute-done
  83.5 1.3 copy.15
  84.8 4.0 %all-to-all-start = ((bf16[4,256,512]{1,2,0:T(8,128)(2,1)}), bf16[4,256,512]{1,2,0:T(8,128)(2,1)S(1)}, u32[]{:S(2)}, u32[]{:S(2)}) async-start(bf16[4,256,512]{1,2,0:T(8,128)(2,1)} %copy.15), calls=%async_computation | async-start | bytes 2097152 | tf_op jit(solution)/shard_map/all_to_all | solution.py:96
  88.8 0.0 all-gather.5.cloned.1.call-start
  88.8 1.5 collective-permute-start.5
  90.3 12.2 %all-to-all-done = bf16[4,256,512]{1,2,0:T(8,128)(2,1)S(1)} async-done(((bf16[4,256,512]{1,2,0:T(8,128)(2,1)}), bf16[4,256,512]{1,2,0:T(8,128)(2,1)S(1)}, u32[]{:S(2)}, u32[]{:S(2)}) %all-to-all-start) | async-done | bytes 1048608 | tf_op jit(solution)/shard_map/all_to_all | solution.py:96
  102.6 0.2 convert_element_type.74
  102.8 0.1 fusion.23
  102.9 0.0 copy-start.7
  103.0 11.1 %all_gather.24 = bf16[256,1536]{0,1:T(8,128)(2,1)S(1)} all-gather(bf16[256,384]{0,1:T(8,128)(2,1)S(1)} %fusion.99), channel_id=1, replica_groups=mesh['segment'=2,'bz'=8,'bx'=4,'my'=2,'mc'=2] {'my','mc'}, dimensions={1}, use_global_device_ids=true | all-gather | bytes 983040 | tf_op jit(solution)/shard_map/all_gather | solution.py:185
  114.1 0.1 constant_dynamic-slice_fusion.7
  114.1 0.0 collective-permute-done.5
  114.2 0.0 copy-done.7
  114.2 0.0 copy-start.6
  114.2 0.0 copy-start.8
  114.2 3.7 %fusion.18 = (f32[256]{0:T(256)S(1)}, bf16[256,1536]{1,0:T(8,128)(2,1)S(1)}) fusion(bf16[384,1536]{1,0:T(8,128)(2,1)} %collective-permute-done.5, bf16[384,1536]{1,0:T(8,128)(2,1)} %collective-permute-done.1, bf16[384,1536]{1,0:T(8,128)(2,1)} %collective-permute-done, bf16[384,1536]{1,0:T(8,128)(2,1)S(1)} %bitcast.101, ...), kind=kOutput, calls=%fused_computation.18 | convolution fusion | flops 1232338688 | bytes 7078912 | tf_op jit(solution)/shard_map/dot_general | solution.py:147
  117.9 0.6 fusion.69
  118.5 0.0 copy-start.9
  118.5 0.6 fusion.72
  119.2 4.4 %collective-permute-start.6 = (bf16[2,256,384]{2,1,0:T(8,128)(2,1)S(1)}, bf16[2,256,384]{2,1,0:T(8,128)(2,1)S(1)}, u32[]{:S(2)}, u32[]{:S(2)}) collective-permute-start(bf16[2,256,384]{2,1,0:T(8,128)(2,1)S(1)} %pad_maximum_fusion.1), channel_id=1, source_target_pairs={{0,128},{1,129},{2,130},{3,131},{4,132},{5,133},{6,134},{7,135},{8... | collective-permute-start | bytes 1179656 | tf_op jit(solution)/shard_map/ppermute | solution.py:23
  123.6 8.3 %collective-permute-done.6 = bf16[2,256,384]{2,1,0:T(8,128)(2,1)S(1)} collective-permute-done((bf16[2,256,384]{2,1,0:T(8,128)(2,1)S(1)}, bf16[2,256,384]{2,1,0:T(8,128)(2,1)S(1)}, u32[]{:S(2)}, u32[]{:S(2)}) %collective-permute-start.6) | collective-permute-done | bytes 393248 | tf_op jit(solution)/shard_map/ppermute | solution.py:23
  131.9 0.8 copy-done.4
  132.6 0.0 all-gather.5.cloned.1.call-update
  132.6 1.9 fusion.59
  134.5 10.8 %all_gather.25.q_ref = bf16[1024,384]{1,0:T(8,128)(2,1)S(1)} all-gather(bf16[256,384]{1,0:T(8,128)(2,1)S(1)} %fusion.59), channel_id=1, replica_groups=mesh['segment'=2,'bz'=8,'bx'=4,'my'=2,'mc'=2] {'bx'}, dimensions={0}, use_global_device_ids=true | all-gather | bytes 983040 | tf_op jit(solution)/shard_map/all_gather | solution.py:91
  145.4 30.2 %all-gather.5.cloned.1.call-done.k_ref.v_ref = bf16[2,2048,384]{2,1,0:T(8,128)(2,1)} async-done(((bf16[2,256,384]{2,1,0:T(8,128)(2,1)}), bf16[2,2048,384]{2,1,0:T(8,128)(2,1)}) %all-gather.5.cloned.1.call-update) | async-done | bytes 3145744 | tf_op jit(solution)/shard_map/all_gather | solution.py:92
  175.6 1.9 copy-done.2
  177.5 11.0 %shard_map.101 = bf16[1024,512]{1,0:T(8,128)(2,1)S(1)} custom-call(bf16[1024,384]{1,0:T(8,128)(2,1)S(1)} %all_gather.25.q_ref, bf16[2,2048,384]{2,1,0:T(8,128)(2,1)S(1)} %copy-done.2, bf16[2,2048,384]{2,1,0:T(8,128)(2,1)S(1)} %copy-done.2), custom_call_target="tpu_custom_call" | custom-call | tf_op jit(solution)/shard_map/pallas_call | solution.py:74
  188.5 1.3 copy.18
  189.8 4.0 %all-to-all-start.1 = ((bf16[4,256,512]{1,2,0:T(8,128)(2,1)}), bf16[4,256,512]{1,2,0:T(8,128)(2,1)S(1)}, u32[]{:S(2)}, u32[]{:S(2)}) async-start(bf16[4,256,512]{1,2,0:T(8,128)(2,1)} %copy.18), calls=%async_computation.1 | async-start | bytes 2097152 | tf_op jit(solution)/shard_map/all_to_all | solution.py:96
  193.8 13.7 %all-to-all-done.1 = bf16[4,256,512]{1,2,0:T(8,128)(2,1)S(1)} async-done(((bf16[4,256,512]{1,2,0:T(8,128)(2,1)}), bf16[4,256,512]{1,2,0:T(8,128)(2,1)S(1)}, u32[]{:S(2)}, u32[]{:S(2)}) %all-to-all-start.1) | async-done | bytes 1048608 | tf_op jit(solution)/shard_map/all_to_all | solution.py:96
  207.6 0.2 convert_element_type.84
  207.8 0.1 fusion.22
  208.0 10.8 %all_gather.27 = bf16[256,1536]{0,1:T(8,128)(2,1)S(1)} all-gather(bf16[256,384]{0,1:T(8,128)(2,1)S(1)} %fusion.98), channel_id=1, replica_groups=mesh['segment'=2,'bz'=8,'bx'=4,'my'=2,'mc'=2] {'my','mc'}, dimensions={1}, use_global_device_ids=true | all-gather | bytes 983040 | tf_op jit(solution)/shard_map/all_gather | solution.py:196
  218.8 0.1 constant_dynamic-slice_fusion.3
  218.8 2.4 %fusion.103 = bf16[1,256,384]{2,1,0:T(8,128)(2,1)} fusion(bf16[256,1536]{1,0:T(8,128)(2,1)S(1)} %get-tuple-element.44, s32[]{:T(128)S(6)} %select_n.65, pred[]{:T(512)S(6)} %eq.20, bf16[384,384]{1,0:T(8,128)(2,1)} %collective-permute-done.4, bf16[384,384]{1,0:T(8,128)(2,1)} %collective-permute-done.3, bf16[384,384]{1,0:T(8,128)(2,1)} %collective-permute-done.2, ...), kind=kOutput, calls=%fused_computation.89 | convolution fusion | flops 310247424 | bytes 2359301 | tf_op jit(solution)/shard_map/dot_general | solution.py:147
  (25 shorter events, 0.4 us)
Async XLA Ops:
  6.5 0.9 copy-start
  6.5 12.7 %copy-start.5 = (f32[1,1536]{1,0:T(1,128)S(1)}, f32[1,1536]{1,0:T(1,128)}, u32[]{:S(2)}) copy-start(f32[1,1536]{1,0:T(1,128)} %param.13) | copy-start | bytes 18436
  6.5 64.0 %all-gather.3.cloned.1.call-start = ((), (), s32[]{:S(2)}) async-start(), calls=%async_computation.2 | async-start | bytes 3538944 | tf_op jit(solution)/shard_map/all_gather | solution.py:92
  21.1 4.7 %copy-start.3 = (bf16[384,1536]{1,0:T(8,128)(2,1)S(1)}, bf16[384,1536]{1,0:T(8,128)(2,1)}, u32[]{:S(2)}) copy-start(bf16[384,1536]{1,0:T(8,128)(2,1)} %param.19) | copy-start | bytes 3538948
  24.0 59.5 %collective-permute-start.1 = (bf16[384,1536]{1,0:T(8,128)(2,1)}, bf16[384,1536]{1,0:T(8,128)(2,1)}, u32[]{:S(2)}, u32[]{:S(2)}) collective-permute-start(bf16[384,1536]{1,0:T(8,128)(2,1)} %bitcast.99), channel_id=1, source_target_pairs={{0,1},{1,0},{2,3},{3,2},{4,5},{5,4},{6,7},{7,6},{8,9},{9,8},{10,11... | collective-permute-start | bytes 3538952 | tf_op jit(solution)/shard_map/ppermute | solution.py:124
  24.3 59.2 %collective-permute-start = (bf16[384,1536]{1,0:T(8,128)(2,1)}, bf16[384,1536]{1,0:T(8,128)(2,1)}, u32[]{:S(2)}, u32[]{:S(2)}) collective-permute-start(bf16[384,1536]{1,0:T(8,128)(2,1)} %bitcast.100), channel_id=1, source_target_pairs={{0,2},{2,0},{1,3},{3,1},{4,6},{6,4},{5,7},{7,5},{8,10},{10,8},{9,1... | collective-permute-start | bytes 3538952 | tf_op jit(solution)/shard_map/ppermute | solution.py:123
  26.8 56.6 %collective-permute-start.4 = (bf16[384,384]{1,0:T(8,128)(2,1)}, bf16[384,384]{1,0:T(8,128)(2,1)}, u32[]{:S(2)}, u32[]{:S(2)}) collective-permute-start(bf16[384,384]{1,0:T(8,128)(2,1)} %get-tuple-element.31), channel_id=1, source_target_pairs={{0,3},{1,0},{2,1},{3,2},{4,7},{5,4},{6,5},{7,6},{8,11},{9,8},{10,9... | collective-permute-start | bytes 884744 | tf_op jit(solution)/shard_map/ppermute | solution.py:117
  27.5 56.0 %collective-permute-start.2 = (bf16[384,384]{1,0:T(8,128)(2,1)}, bf16[384,384]{1,0:T(8,128)(2,1)}, u32[]{:S(2)}, u32[]{:S(2)}) collective-permute-start(bf16[384,384]{1,0:T(8,128)(2,1)} %get-tuple-element.32), channel_id=1, source_target_pairs={{0,1},{1,2},{2,3},{3,0},{4,5},{5,6},{6,7},{7,4},{8,9},{9,10},{10,1... | collective-permute-start | bytes 884744 | tf_op jit(solution)/shard_map/ppermute | solution.py:117
  28.6 54.9 %collective-permute-start.3 = (bf16[384,384]{1,0:T(8,128)(2,1)S(1)}, bf16[384,384]{1,0:T(8,128)(2,1)}, u32[]{:S(2)}, u32[]{:S(2)}) collective-permute-start(bf16[384,384]{1,0:T(8,128)(2,1)S(1)} %get-tuple-element.34), channel_id=1, source_target_pairs={{0,2},{1,3},{2,0},{3,1},{4,6},{5,7},{6,4},{7,5},{8,10},{9,11},{10,... | collective-permute-start | bytes 884744 | tf_op jit(solution)/shard_map/ppermute | solution.py:117
  70.5 1.9 copy-start.1
  84.8 17.6 %all-to-all-start = ((bf16[4,256,512]{1,2,0:T(8,128)(2,1)}), bf16[4,256,512]{1,2,0:T(8,128)(2,1)S(1)}, u32[]{:S(2)}, u32[]{:S(2)}) async-start(bf16[4,256,512]{1,2,0:T(8,128)(2,1)} %copy.15), calls=%async_computation | async-start | bytes 2097152 | tf_op jit(solution)/shard_map/all_to_all | solution.py:96
  88.8 86.8 %all-gather.5.cloned.1.call-start = ((), (), s32[]{:S(2)}) async-start(), calls=%async_computation.3 | async-start | bytes 3538944 | tf_op jit(solution)/shard_map/all_gather | solution.py:92
  88.8 25.4 %collective-permute-start.5 = (bf16[384,1536]{1,0:T(8,128)(2,1)}, bf16[384,1536]{1,0:T(8,128)(2,1)}, u32[]{:S(2)}, u32[]{:S(2)}) collective-permute-start(bf16[384,1536]{1,0:T(8,128)(2,1)} %collective-permute-done), channel_id=1, source_target_pairs={{0,1},{1,0},{2,3},{3,2},{4,5},{5,4},{6,7},{7,6},{8,9},{9,8},{10,11... | collective-permute-start | bytes 3538952 | tf_op jit(solution)/shard_map/ppermute | solution.py:131
  102.9 11.2 %copy-start.7 = (bf16[1,384,1536]{2,1,0:T(8,128)(2,1)S(1)}, bf16[1,384,1536]{2,1,0:T(8,128)(2,1)}, u32[]{:S(2)}) copy-start(bf16[1,384,1536]{2,1,0:T(8,128)(2,1)} %param.15) | copy-start | bytes 3538948
  114.2 3.7 %copy-start.6 = (bf16[3,1536,384]{2,1,0:T(8,128)(2,1)S(1)}, bf16[3,1536,384]{2,1,0:T(8,128)(2,1)}, u32[]{:S(2)}) copy-start(bf16[3,1536,384]{2,1,0:T(8,128)(2,1)} %param.18) | copy-start | bytes 10616836
  114.2 3.7 %copy-start.8 = (f32[1536]{0:T(1024)S(1)}, f32[1536]{0:T(1024)}, u32[]{:S(2)}) copy-start(f32[1536]{0:T(1024)} %param.17) | copy-start | bytes 18436
  118.5 14.1 %copy-start.9 = (f32[1536]{0:T(1024)S(1)}, f32[1536]{0:T(1024)}, u32[]{:S(2)}) copy-start(f32[1536]{0:T(1024)} %param.16) | copy-start | bytes 18436
  119.2 12.6 %collective-permute-start.6 = (bf16[2,256,384]{2,1,0:T(8,128)(2,1)S(1)}, bf16[2,256,384]{2,1,0:T(8,128)(2,1)S(1)}, u32[]{:S(2)}, u32[]{:S(2)}) collective-permute-start(bf16[2,256,384]{2,1,0:T(8,128)(2,1)S(1)} %pad_maximum_fusion.1), channel_id=1, source_target_pairs={{0,128},{1,129},{2,130},{3,131},{4,132},{5,133},{6,134},{7,135},{8... | collective-permute-start | bytes 1179656 | tf_op jit(solution)/shard_map/ppermute | solution.py:23
  131.9 0.8 copy-start.4
  175.6 1.9 copy-start.2
  189.8 17.6 %all-to-all-start.1 = ((bf16[4,256,512]{1,2,0:T(8,128)(2,1)}), bf16[4,256,512]{1,2,0:T(8,128)(2,1)S(1)}, u32[]{:S(2)}, u32[]{:S(2)}) async-start(bf16[4,256,512]{1,2,0:T(8,128)(2,1)} %copy.18), calls=%async_computation.1 | async-start | bytes 2097152 | tf_op jit(solution)/shard_map/all_to_all | solution.py:96
Sparse Core Ops, SparseCore 0:
  24.1 46.3 all-gather.2
  132.8 42.8 all-gather.4

commit v13 on v12

--- a/solution.py
+++ b/solution.py
@@ -12,7 +12,7 @@
 MP = ("my", "mc")
 X_SIZE = 4
 CORES = 2
-TILE = 256
+TILE = 512
 STATS = 128
 PARTS = 3
 

time: 229 us -> 228 us (level)
  no operation moved by 1% of the time
where the time goes in v13:
time: 228 us
  waiting for transfers between devices  92.3 us (40%)
  blocking collectives  54.7 us (24%)
  Pallas kernels  22 us (10%)
  starting transfers between devices  17.7 us (8%)
  matrix products  16.2 us (7%)
  between operations  13.7 us (6%)
  local copies, waits for them, and re-layouts  9.29 us (4%)
    all_gather x2, waiting for transfers between devices, attend(): key_block = lax.all_gather(pairs, 'bz', axis=1, tiled=True)  58.1 us
    all_to_all x2, waiting for transfers between devices, attend(): parts = lax.all_to_all(partial, 'bx', 0, 0, tiled=True)  25.8 us
    all_gather x2, blocking collectives, attend(): query_block = lax.all_gather(queries, 'bx', axis=0, tiled=True)  22.7 us
    pallas_call x2, Pallas kernels, partial_attend(): pl.pallas_call(partial_kernel, grid=(rows // TILE,), in_specs=[pl.BlockSp...  22 us
    all_gather x1, blocking collectives, on_device(): self_attended = lax.all_gather(self_local, MP, axis=1, tiled=True)  10.9 us
    all_gather x1, blocking collectives, on_device(): lax.all_gather(attend(cross_queries, arrived), MP, axis=1, tiled=True)  10.8 us
    all_gather x1, blocking collectives, on_device(): embedded_full = lax.all_gather(embedded, MP, axis=1, tiled=True)  10.3 us
    dot_general x6, matrix products, project(): jnp.dot(normed, weight, preferred_element_type=jnp.float32)  8.93 us
  transfers between devices with their start and end apart: 11, of which 5 were waited for; matrix products, arithmetic and copies ran while one was open for 2% of the time, Pallas kernels for 5%

profile of v13, /device:TPU:1, one launch (start us, length us, event | category | flops | bytes accessed | tf_op | source)
XLA Modules:
  0.0 227.9 jit_solution(8113805516459104779)
XLA Ops:
  6.5 0.0 copy-start
  6.5 0.0 all-gather.3.cloned.1.call-start
  6.5 0.9 copy-done
  7.5 1.2 fusion.68
  8.7 10.3 %all_gather.21 = bf16[256,1536]{1,0:T(8,128)(2,1)S(1)} all-gather(bf16[256,384]{1,0:T(8,128)(2,1)S(1)} %fusion.68), channel_id=1, replica_groups=mesh['segment'=2,'bz'=8,'bx'=4,'my'=2,'mc'=2] {'my','mc'}, dimensions={1}, use_global_device_ids=true | all-gather | bytes 983040 | tf_op jit(solution)/shard_map/all_gather | solution.py:175
  19.0 0.2 fusion.19
  19.2 0.0 copy-done.5
  19.2 1.9 fusion.78
  21.1 0.0 copy-start.3
  21.2 2.0 fusion.75
  23.1 0.8 pad_maximum_fusion
  24.0 0.0 all-gather.3.cloned.1.call-update
  24.0 0.2 collective-permute-start.1
  24.3 1.6 collective-permute-start
  25.9 0.0 copy-done.3
  25.9 1.0 constant_dynamic-slice_fusion.8
  26.8 0.6 collective-permute-start.4
  27.5 1.1 collective-permute-start.2
  28.6 0.2 collective-permute-start.3
  28.8 1.9 fusion.50
  30.7 11.9 %all_gather.22.q_ref = bf16[1024,384]{1,0:T(8,128)(2,1)S(1)} all-gather(bf16[256,384]{1,0:T(8,128)(2,1)S(1)} %fusion.50), channel_id=1, replica_groups=mesh['segment'=2,'bz'=8,'bx'=4,'my'=2,'mc'=2] {'bx'}, dimensions={0}, use_global_device_ids=true | all-gather | bytes 983040 | tf_op jit(solution)/shard_map/all_gather | solution.py:91
  42.6 27.9 %all-gather.3.cloned.1.call-done.k_ref.v_ref = bf16[2,2048,384]{2,1,0:T(8,128)(2,1)} async-done(((bf16[2,256,384]{2,1,0:T(8,128)(2,1)}), bf16[2,2048,384]{2,1,0:T(8,128)(2,1)}) %all-gather.3.cloned.1.call-update) | async-done | bytes 3145744 | tf_op jit(solution)/shard_map/all_gather | solution.py:92
  70.5 1.9 copy-done.1
  72.4 11.1 %shard_map.100 = bf16[1024,512]{1,0:T(8,128)(2,1)S(1)} custom-call(bf16[1024,384]{1,0:T(8,128)(2,1)S(1)} %all_gather.22.q_ref, bf16[2,2048,384]{2,1,0:T(8,128)(2,1)S(1)} %copy-done.1, bf16[2,2048,384]{2,1,0:T(8,128)(2,1)S(1)} %copy-done.1), custom_call_target="tpu_custom_call" | custom-call | tf_op jit(solution)/shard_map/pallas_call | solution.py:74
  83.5 0.0 collective-permute-done.4
  83.5 0.0 collective-permute-done.2
  83.5 0.0 collective-permute-done.3
  83.5 0.0 collective-permute-done.1
  83.5 0.0 collective-permute-done
  83.6 1.3 copy.15
  84.9 4.0 %all-to-all-start = ((bf16[4,256,512]{1,2,0:T(8,128)(2,1)}), bf16[4,256,512]{1,2,0:T(8,128)(2,1)S(1)}, u32[]{:S(2)}, u32[]{:S(2)}) async-start(bf16[4,256,512]{1,2,0:T(8,128)(2,1)} %copy.15), calls=%async_computation | async-start | bytes 2097152 | tf_op jit(solution)/shard_map/all_to_all | solution.py:96
  88.8 0.0 all-gather.5.cloned.1.call-start
  88.9 1.5 collective-permute-start.5
  90.4 12.1 %all-to-all-done = bf16[4,256,512]{1,2,0:T(8,128)(2,1)S(1)} async-done(((bf16[4,256,512]{1,2,0:T(8,128)(2,1)}), bf16[4,256,512]{1,2,0:T(8,128)(2,1)S(1)}, u32[]{:S(2)}, u32[]{:S(2)}) %all-to-all-start) | async-done | bytes 1048608 | tf_op jit(solution)/shard_map/all_to_all | solution.py:96
  102.7 0.2 convert_element_type.74
  102.8 0.1 fusion.23
  103.0 0.0 copy-start.7
  103.0 10.9 %all_gather.24 = bf16[256,1536]{0,1:T(8,128)(2,1)S(1)} all-gather(bf16[256,384]{0,1:T(8,128)(2,1)S(1)} %fusion.99), channel_id=1, replica_groups=mesh['segment'=2,'bz'=8,'bx'=4,'my'=2,'mc'=2] {'my','mc'}, dimensions={1}, use_global_device_ids=true | all-gather | bytes 983040 | tf_op jit(solution)/shard_map/all_gather | solution.py:185
  114.0 0.1 constant_dynamic-slice_fusion.7
  114.0 0.0 collective-permute-done.5
  114.0 0.0 copy-done.7
  114.1 0.0 copy-start.6
  114.1 0.0 copy-start.8
  114.1 3.7 %fusion.18 = (f32[256]{0:T(256)S(1)}, bf16[256,1536]{1,0:T(8,128)(2,1)S(1)}) fusion(bf16[384,1536]{1,0:T(8,128)(2,1)} %collective-permute-done.5, bf16[384,1536]{1,0:T(8,128)(2,1)} %collective-permute-done.1, bf16[384,1536]{1,0:T(8,128)(2,1)} %collective-permute-done, bf16[384,1536]{1,0:T(8,128)(2,1)S(1)} %bitcast.101, ...), kind=kOutput, calls=%fused_computation.18 | convolution fusion | flops 1232338688 | bytes 7078912 | tf_op jit(solution)/shard_map/dot_general | solution.py:147
  117.8 0.6 fusion.69
  118.4 0.0 copy-start.9
  118.4 0.6 fusion.72
  119.1 4.4 %collective-permute-start.6 = (bf16[2,256,384]{2,1,0:T(8,128)(2,1)S(1)}, bf16[2,256,384]{2,1,0:T(8,128)(2,1)S(1)}, u32[]{:S(2)}, u32[]{:S(2)}) collective-permute-start(bf16[2,256,384]{2,1,0:T(8,128)(2,1)S(1)} %pad_maximum_fusion.1), channel_id=1, source_target_pairs={{0,128},{1,129},{2,130},{3,131},{4,132},{5,133},{6,134},{7,135},{8... | collective-permute-start | bytes 1179656 | tf_op jit(solution)/shard_map/ppermute | solution.py:23
  123.5 8.3 %collective-permute-done.6 = bf16[2,256,384]{2,1,0:T(8,128)(2,1)S(1)} collective-permute-done((bf16[2,256,384]{2,1,0:T(8,128)(2,1)S(1)}, bf16[2,256,384]{2,1,0:T(8,128)(2,1)S(1)}, u32[]{:S(2)}, u32[]{:S(2)}) %collective-permute-start.6) | collective-permute-done | bytes 393248 | tf_op jit(solution)/shard_map/ppermute | solution.py:23
  131.8 0.8 copy-done.4
  132.5 0.0 all-gather.5.cloned.1.call-update
  132.5 1.9 fusion.59
  134.4 10.8 %all_gather.25.q_ref = bf16[1024,384]{1,0:T(8,128)(2,1)S(1)} all-gather(bf16[256,384]{1,0:T(8,128)(2,1)S(1)} %fusion.59), channel_id=1, replica_groups=mesh['segment'=2,'bz'=8,'bx'=4,'my'=2,'mc'=2] {'bx'}, dimensions={0}, use_global_device_ids=true | all-gather | bytes 983040 | tf_op jit(solution)/shard_map/all_gather | solution.py:91
  145.3 30.2 %all-gather.5.cloned.1.call-done.k_ref.v_ref = bf16[2,2048,384]{2,1,0:T(8,128)(2,1)} async-done(((bf16[2,256,384]{2,1,0:T(8,128)(2,1)}), bf16[2,2048,384]{2,1,0:T(8,128)(2,1)}) %all-gather.5.cloned.1.call-update) | async-done | bytes 3145744 | tf_op jit(solution)/shard_map/all_gather | solution.py:92
  175.5 1.9 copy-done.2
  177.4 10.9 %shard_map.101 = bf16[1024,512]{1,0:T(8,128)(2,1)S(1)} custom-call(bf16[1024,384]{1,0:T(8,128)(2,1)S(1)} %all_gather.25.q_ref, bf16[2,2048,384]{2,1,0:T(8,128)(2,1)S(1)} %copy-done.2, bf16[2,2048,384]{2,1,0:T(8,128)(2,1)S(1)} %copy-done.2), custom_call_target="tpu_custom_call" | custom-call | tf_op jit(solution)/shard_map/pallas_call | solution.py:74
  188.3 1.3 copy.18
  189.6 4.0 %all-to-all-start.1 = ((bf16[4,256,512]{1,2,0:T(8,128)(2,1)}), bf16[4,256,512]{1,2,0:T(8,128)(2,1)S(1)}, u32[]{:S(2)}, u32[]{:S(2)}) async-start(bf16[4,256,512]{1,2,0:T(8,128)(2,1)} %copy.18), calls=%async_computation.1 | async-start | bytes 2097152 | tf_op jit(solution)/shard_map/all_to_all | solution.py:96
  193.6 13.7 %all-to-all-done.1 = bf16[4,256,512]{1,2,0:T(8,128)(2,1)S(1)} async-done(((bf16[4,256,512]{1,2,0:T(8,128)(2,1)}), bf16[4,256,512]{1,2,0:T(8,128)(2,1)S(1)}, u32[]{:S(2)}, u32[]{:S(2)}) %all-to-all-start.1) | async-done | bytes 1048608 | tf_op jit(solution)/shard_map/all_to_all | solution.py:96
  207.4 0.2 convert_element_type.84
  207.6 0.1 fusion.22
  207.8 10.8 %all_gather.27 = bf16[256,1536]{0,1:T(8,128)(2,1)S(1)} all-gather(bf16[256,384]{0,1:T(8,128)(2,1)S(1)} %fusion.98), channel_id=1, replica_groups=mesh['segment'=2,'bz'=8,'bx'=4,'my'=2,'mc'=2] {'my','mc'}, dimensions={1}, use_global_device_ids=true | all-gather | bytes 983040 | tf_op jit(solution)/shard_map/all_gather | solution.py:196
  218.6 0.1 constant_dynamic-slice_fusion.3
  218.6 2.4 %fusion.103 = bf16[1,256,384]{2,1,0:T(8,128)(2,1)} fusion(bf16[256,1536]{1,0:T(8,128)(2,1)S(1)} %get-tuple-element.44, s32[]{:T(128)S(6)} %select_n.65, pred[]{:T(512)S(6)} %eq.20, bf16[384,384]{1,0:T(8,128)(2,1)} %collective-permute-done.4, bf16[384,384]{1,0:T(8,128)(2,1)} %collective-permute-done.3, bf16[384,384]{1,0:T(8,128)(2,1)} %collective-permute-done.2, ...), kind=kOutput, calls=%fused_computation.89 | convolution fusion | flops 310247424 | bytes 2359301 | tf_op jit(solution)/shard_map/dot_general | solution.py:147
  (25 shorter events, 0.4 us)
Async XLA Ops:
  6.5 0.9 copy-start
  6.5 12.7 %copy-start.5 = (f32[1,1536]{1,0:T(1,128)S(1)}, f32[1,1536]{1,0:T(1,128)}, u32[]{:S(2)}) copy-start(f32[1,1536]{1,0:T(1,128)} %param.13) | copy-start | bytes 18436
  6.5 64.0 %all-gather.3.cloned.1.call-start = ((), (), s32[]{:S(2)}) async-start(), calls=%async_computation.2 | async-start | bytes 3538944 | tf_op jit(solution)/shard_map/all_gather | solution.py:92
  21.1 4.7 %copy-start.3 = (bf16[384,1536]{1,0:T(8,128)(2,1)S(1)}, bf16[384,1536]{1,0:T(8,128)(2,1)}, u32[]{:S(2)}) copy-start(bf16[384,1536]{1,0:T(8,128)(2,1)} %param.19) | copy-start | bytes 3538948
  24.0 59.5 %collective-permute-start.1 = (bf16[384,1536]{1,0:T(8,128)(2,1)}, bf16[384,1536]{1,0:T(8,128)(2,1)}, u32[]{:S(2)}, u32[]{:S(2)}) collective-permute-start(bf16[384,1536]{1,0:T(8,128)(2,1)} %bitcast.99), channel_id=1, source_target_pairs={{0,1},{1,0},{2,3},{3,2},{4,5},{5,4},{6,7},{7,6},{8,9},{9,8},{10,11... | collective-permute-start | bytes 3538952 | tf_op jit(solution)/shard_map/ppermute | solution.py:124
  24.3 59.3 %collective-permute-start = (bf16[384,1536]{1,0:T(8,128)(2,1)}, bf16[384,1536]{1,0:T(8,128)(2,1)}, u32[]{:S(2)}, u32[]{:S(2)}) collective-permute-start(bf16[384,1536]{1,0:T(8,128)(2,1)} %bitcast.100), channel_id=1, source_target_pairs={{0,2},{2,0},{1,3},{3,1},{4,6},{6,4},{5,7},{7,5},{8,10},{10,8},{9,1... | collective-permute-start | bytes 3538952 | tf_op jit(solution)/shard_map/ppermute | solution.py:123
  26.8 56.7 %collective-permute-start.4 = (bf16[384,384]{1,0:T(8,128)(2,1)}, bf16[384,384]{1,0:T(8,128)(2,1)}, u32[]{:S(2)}, u32[]{:S(2)}) collective-permute-start(bf16[384,384]{1,0:T(8,128)(2,1)} %get-tuple-element.31), channel_id=1, source_target_pairs={{0,3},{1,0},{2,1},{3,2},{4,7},{5,4},{6,5},{7,6},{8,11},{9,8},{10,9... | collective-permute-start | bytes 884744 | tf_op jit(solution)/shard_map/ppermute | solution.py:117
  27.5 56.1 %collective-permute-start.2 = (bf16[384,384]{1,0:T(8,128)(2,1)}, bf16[384,384]{1,0:T(8,128)(2,1)}, u32[]{:S(2)}, u32[]{:S(2)}) collective-permute-start(bf16[384,384]{1,0:T(8,128)(2,1)} %get-tuple-element.32), channel_id=1, source_target_pairs={{0,1},{1,2},{2,3},{3,0},{4,5},{5,6},{6,7},{7,4},{8,9},{9,10},{10,1... | collective-permute-start | bytes 884744 | tf_op jit(solution)/shard_map/ppermute | solution.py:117
  28.6 54.9 %collective-permute-start.3 = (bf16[384,384]{1,0:T(8,128)(2,1)S(1)}, bf16[384,384]{1,0:T(8,128)(2,1)}, u32[]{:S(2)}, u32[]{:S(2)}) collective-permute-start(bf16[384,384]{1,0:T(8,128)(2,1)S(1)} %get-tuple-element.34), channel_id=1, source_target_pairs={{0,2},{1,3},{2,0},{3,1},{4,6},{5,7},{6,4},{7,5},{8,10},{9,11},{10,... | collective-permute-start | bytes 884744 | tf_op jit(solution)/shard_map/ppermute | solution.py:117
  70.5 1.9 copy-start.1
  84.9 17.6 %all-to-all-start = ((bf16[4,256,512]{1,2,0:T(8,128)(2,1)}), bf16[4,256,512]{1,2,0:T(8,128)(2,1)S(1)}, u32[]{:S(2)}, u32[]{:S(2)}) async-start(bf16[4,256,512]{1,2,0:T(8,128)(2,1)} %copy.15), calls=%async_computation | async-start | bytes 2097152 | tf_op jit(solution)/shard_map/all_to_all | solution.py:96
  88.8 86.6 %all-gather.5.cloned.1.call-start = ((), (), s32[]{:S(2)}) async-start(), calls=%async_computation.3 | async-start | bytes 3538944 | tf_op jit(solution)/shard_map/all_gather | solution.py:92
  88.9 25.2 %collective-permute-start.5 = (bf16[384,1536]{1,0:T(8,128)(2,1)}, bf16[384,1536]{1,0:T(8,128)(2,1)}, u32[]{:S(2)}, u32[]{:S(2)}) collective-permute-start(bf16[384,1536]{1,0:T(8,128)(2,1)} %collective-permute-done), channel_id=1, source_target_pairs={{0,1},{1,0},{2,3},{3,2},{4,5},{5,4},{6,7},{7,6},{8,9},{9,8},{10,11... | collective-permute-start | bytes 3538952 | tf_op jit(solution)/shard_map/ppermute | solution.py:131
  103.0 11.1 %copy-start.7 = (bf16[1,384,1536]{2,1,0:T(8,128)(2,1)S(1)}, bf16[1,384,1536]{2,1,0:T(8,128)(2,1)}, u32[]{:S(2)}) copy-start(bf16[1,384,1536]{2,1,0:T(8,128)(2,1)} %param.15) | copy-start | bytes 3538948
  114.1 3.7 %copy-start.6 = (bf16[3,1536,384]{2,1,0:T(8,128)(2,1)S(1)}, bf16[3,1536,384]{2,1,0:T(8,128)(2,1)}, u32[]{:S(2)}) copy-start(bf16[3,1536,384]{2,1,0:T(8,128)(2,1)} %param.18) | copy-start | bytes 10616836
  114.1 3.7 %copy-start.8 = (f32[1536]{0:T(1024)S(1)}, f32[1536]{0:T(1024)}, u32[]{:S(2)}) copy-start(f32[1536]{0:T(1024)} %param.17) | copy-start | bytes 18436
  118.4 14.1 %copy-start.9 = (f32[1536]{0:T(1024)S(1)}, f32[1536]{0:T(1024)}, u32[]{:S(2)}) copy-start(f32[1536]{0:T(1024)} %param.16) | copy-start | bytes 18436
  119.1 12.6 %collective-permute-start.6 = (bf16[2,256,384]{2,1,0:T(8,128)(2,1)S(1)}, bf16[2,256,384]{2,1,0:T(8,128)(2,1)S(1)}, u32[]{:S(2)}, u32[]{:S(2)}) collective-permute-start(bf16[2,256,384]{2,1,0:T(8,128)(2,1)S(1)} %pad_maximum_fusion.1), channel_id=1, source_target_pairs={{0,128},{1,129},{2,130},{3,131},{4,132},{5,133},{6,134},{7,135},{8... | collective-permute-start | bytes 1179656 | tf_op jit(solution)/shard_map/ppermute | solution.py:23
  131.8 0.8 copy-start.4
  175.5 1.9 copy-start.2
  189.6 17.6 %all-to-all-start.1 = ((bf16[4,256,512]{1,2,0:T(8,128)(2,1)}), bf16[4,256,512]{1,2,0:T(8,128)(2,1)S(1)}, u32[]{:S(2)}, u32[]{:S(2)}) async-start(bf16[4,256,512]{1,2,0:T(8,128)(2,1)} %copy.18), calls=%async_computation.1 | async-start | bytes 2097152 | tf_op jit(solution)/shard_map/all_to_all | solution.py:96
Sparse Core Ops, SparseCore 0:
  24.1 46.3 all-gather.2
  132.7 42.7 all-gather.4

commit v14 on v12

--- a/solution.py
+++ b/solution.py
@@ -137,6 +137,10 @@
     ]
 
 
+def mp_gather_flat(value):
+    return lax.all_gather(value, MP, axis=1, tiled=True)
+
+
 def project_out(attended_full, blocks):
     width = blocks[0][1].shape[0]
     pieces = [
@@ -192,12 +196,14 @@
     memory_pairs = jnp.stack(
         [project(memory_normed, cross_weights[1]), project(memory_normed, cross_weights[2])]
     )
-    arrived = shifted(memory_pairs, "segment", 1)
-    crossed = lax.all_gather(attend(cross_queries, arrived), MP, axis=1, tiled=True)
+    voxel_queries = shifted(cross_queries, "segment", -1)
+    voxel_part = shifted(hidden_part, "segment", -1)
+    crossed = mp_gather_flat(attend(voxel_queries, memory_pairs))
     decoded = (
-        hidden_part.astype(jnp.float32) + project_out(crossed, cross_blocks)
+        voxel_part.astype(jnp.float32) + project_out(crossed, cross_blocks)
     ).astype(jnp.bfloat16)
-    chosen = jnp.where(lax.axis_index("segment") == 0, hidden_part, decoded)
+    returned = shifted(decoded, "segment", 1)
+    chosen = jnp.where(lax.axis_index("segment") == 0, hidden_part, returned)
     return chosen[None]
 
 

time: 229 us -> 223 us (0.974)
  waiting for transfers between devices: 92.3 us -> 82.5 us
  starting transfers between devices: 17.7 us -> 20.4 us
    all_gather x2, waiting for transfers between devices: 58.2 us -> 45.5 us  [attend(): key_block = lax.all_gather(pairs, 'bz', axis=1, tiled=True)]
    ppermute x1 -> x3, waiting for transfers between devices: 8.27 us -> 12.5 us  [shifted(): lax.ppermute(value, axis, [(source, source + steps) for source in range(i...]
    ppermute x1 -> x3, starting transfers between devices: 4.36 us -> 6.94 us  [shifted(): lax.ppermute(value, axis, [(source, source + steps) for source in range(i...]
    unnamed x20 -> x22, local copies, waits for them, and re-layouts: 5.49 us -> 4.74 us
  transfers between devices with their start and end apart: 11 -> 13, of which waited for: 5 -> 6; matrix products, arithmetic and copies ran while one was open for 2% -> 3% of each run, Pallas kernels for 5% -> 5%
where the time goes in v14:
time: 223 us; the launch traced here: 222 us
  waiting for transfers between devices  82.5 us (37%)
  blocking collectives  55.7 us (25%)
  Pallas kernels  22 us (10%)
  starting transfers between devices  20.4 us (9%)
  matrix products  15.6 us (7%)
  between operations  13.8 us (6%)
  local copies, waits for them, and re-layouts  8.51 us (4%)
  other arithmetic  3.45 us (2%)
    all_gather x2, waiting for transfers between devices, attend(): key_block = lax.all_gather(pairs, 'bz', axis=1, tiled=True)  45.5 us
    all_to_all x2, waiting for transfers between devices, attend(): parts = lax.all_to_all(partial, 'bx', 0, 0, tiled=True)  24.5 us
    all_gather x2, blocking collectives, attend(): query_block = lax.all_gather(queries, 'bx', axis=0, tiled=True)  23.5 us
    pallas_call x2, Pallas kernels, partial_attend(): pl.pallas_call(partial_kernel, grid=(rows // TILE,), in_specs=[pl.BlockSp...  22 us
    ppermute x3, waiting for transfers between devices, shifted(): lax.ppermute(value, axis, [(source, source + steps) for source in range(i...  12.5 us
    all_gather x1, blocking collectives, on_device(): self_attended = lax.all_gather(self_local, MP, axis=1, tiled=True)  11.1 us
    all_gather x1, blocking collectives, mp_gather_flat(): return lax.all_gather(value, MP, axis=1, tiled=True)  10.8 us
    all_gather x1, blocking collectives, on_device(): embedded_full = lax.all_gather(embedded, MP, axis=1, tiled=True)  10.3 us
  transfers between devices with their start and end apart: 13, of which 6 were waited for; matrix products, arithmetic and copies ran while one was open for 3% of the time, Pallas kernels for 5%

profile of v14, /device:TPU:1, one launch (start us, length us, event | category | flops | bytes accessed | tf_op | source)
XLA Modules:
  0.0 221.9 jit_solution(16630496111963009955)
XLA Ops:
  6.5 0.9 copy-done
  7.5 1.2 fusion.68
  8.7 10.3 %all_gather.21 = bf16[256,1536]{1,0:T(8,128)(2,1)S(1)} all-gather(bf16[256,384]{1,0:T(8,128)(2,1)S(1)} %fusion.68), channel_id=1, replica_groups=mesh['segment'=2,'bz'=8,'bx'=4,'my'=2,'mc'=2] {'my','mc'}, dimensions={1}, use_global_device_ids=true | all-gather | bytes 983040 | tf_op jit(solution)/shard_map/all_gather | solution.py:179
  19.0 0.2 fusion.19
  19.2 1.9 fusion.78
  21.1 0.0 copy-start.3
  21.2 2.0 fusion.75
  23.1 0.8 pad_maximum_fusion
  24.0 0.0 all-gather.3.cloned.1.call-update
  24.0 0.2 collective-permute-start.1
  24.2 1.6 collective-permute-start
  25.8 0.9 constant_dynamic-slice_fusion.9
  26.8 0.6 collective-permute-start.4
  27.4 1.1 collective-permute-start.2
  28.5 0.2 collective-permute-start.3
  28.8 1.9 fusion.50
  30.7 11.9 %all_gather.22.q_ref = bf16[1024,384]{1,0:T(8,128)(2,1)S(1)} all-gather(bf16[256,384]{1,0:T(8,128)(2,1)S(1)} %fusion.50), channel_id=1, replica_groups=mesh['segment'=2,'bz'=8,'bx'=4,'my'=2,'mc'=2] {'bx'}, dimensions={0}, use_global_device_ids=true | all-gather | bytes 983040 | tf_op jit(solution)/shard_map/all_gather | solution.py:91
  42.5 27.9 %all-gather.3.cloned.1.call-done.k_ref.v_ref = bf16[2,2048,384]{2,1,0:T(8,128)(2,1)} async-done(((bf16[2,256,384]{2,1,0:T(8,128)(2,1)}), bf16[2,2048,384]{2,1,0:T(8,128)(2,1)}) %all-gather.3.cloned.1.call-update) | async-done | bytes 3145744 | tf_op jit(solution)/shard_map/all_gather | solution.py:92
  70.5 1.9 copy-done.1
  72.4 11.0 %shard_map.100 = bf16[1024,512]{1,0:T(8,128)(2,1)S(1)} custom-call(bf16[1024,384]{1,0:T(8,128)(2,1)S(1)} %all_gather.22.q_ref, bf16[2,2048,384]{2,1,0:T(8,128)(2,1)S(1)} %copy-done.1, bf16[2,2048,384]{2,1,0:T(8,128)(2,1)S(1)} %copy-done.1), custom_call_target="tpu_custom_call" | custom-call | tf_op jit(solution)/shard_map/pallas_call | solution.py:74
  83.4 0.0 collective-permute-done.4
  83.4 0.0 collective-permute-done.2
  83.4 0.0 collective-permute-done.3
  83.4 0.0 collective-permute-done.1
  83.4 0.0 collective-permute-done
  83.4 1.3 copy.15
  84.8 4.0 %all-to-all-start = ((bf16[4,256,512]{1,2,0:T(8,128)(2,1)}), bf16[4,256,512]{1,2,0:T(8,128)(2,1)S(1)}, u32[]{:S(2)}, u32[]{:S(2)}) async-start(bf16[4,256,512]{1,2,0:T(8,128)(2,1)} %copy.15), calls=%async_computation | async-start | bytes 2097152 | tf_op jit(solution)/shard_map/all_to_all | solution.py:96
  88.7 1.5 collective-permute-start.5
  90.2 12.2 %all-to-all-done = bf16[4,256,512]{1,2,0:T(8,128)(2,1)S(1)} async-done(((bf16[4,256,512]{1,2,0:T(8,128)(2,1)}), bf16[4,256,512]{1,2,0:T(8,128)(2,1)S(1)}, u32[]{:S(2)}, u32[]{:S(2)}) %all-to-all-start) | async-done | bytes 1048608 | tf_op jit(solution)/shard_map/all_to_all | solution.py:96
  102.6 0.2 convert_element_type.74
  102.7 0.1 fusion.23
  102.9 0.0 copy-start.8
  102.9 11.1 %all_gather.24 = bf16[256,1536]{0,1:T(8,128)(2,1)S(1)} all-gather(bf16[256,384]{0,1:T(8,128)(2,1)S(1)} %fusion.99), channel_id=1, replica_groups=mesh['segment'=2,'bz'=8,'bx'=4,'my'=2,'mc'=2] {'my','mc'}, dimensions={1}, use_global_device_ids=true | all-gather | bytes 983040 | tf_op jit(solution)/shard_map/all_gather | solution.py:189
  114.0 0.1 constant_dynamic-slice_fusion.8
  114.1 0.0 collective-permute-done.5
  114.1 0.0 copy-start.7
  114.1 0.0 copy-start.9
  114.1 3.7 %fusion.18 = (f32[256]{0:T(256)S(1)}, bf16[256,1536]{1,0:T(8,128)(2,1)S(1)}) fusion(bf16[384,1536]{1,0:T(8,128)(2,1)} %collective-permute-done.5, bf16[384,1536]{1,0:T(8,128)(2,1)} %collective-permute-done.1, bf16[384,1536]{1,0:T(8,128)(2,1)} %collective-permute-done, bf16[384,1536]{1,0:T(8,128)(2,1)S(1)} %bitcast.101, ...), kind=kOutput, calls=%fused_computation.18 | convolution fusion | flops 1232338688 | bytes 7078912 | tf_op jit(solution)/shard_map/dot_general | solution.py:151
  117.8 0.0 copy-done.7
  117.8 0.6 fusion.69
  118.5 0.0 copy-start.10
  118.5 0.6 fusion.72
  119.1 0.8 pad_maximum_fusion.1
  119.9 0.0 all-gather.5.cloned.1.call-update
  120.0 1.9 fusion.59
  121.9 1.3 collective-permute-start.7
  123.2 8.4 %collective-permute-done.7 = bf16[256,384]{1,0:T(8,128)(2,1)S(1)} collective-permute-done((bf16[256,384]{1,0:T(8,128)(2,1)S(1)}, bf16[256,384]{1,0:T(8,128)(2,1)S(1)}, u32[]{:S(2)}, u32[]{:S(2)}) %collective-permute-start.7) | collective-permute-done | bytes 196640 | tf_op jit(solution)/shard_map/ppermute | solution.py:23
  131.6 11.6 %all_gather.25.q_ref = bf16[1024,384]{1,0:T(8,128)(2,1)S(1)} all-gather(bf16[256,384]{1,0:T(8,128)(2,1)S(1)} %collective-permute-done.7), channel_id=1, replica_groups=mesh['segment'=2,'bz'=8,'bx'=4,'my'=2,'mc'=2] {'bx'}, dimensions={0}, use_global_device_ids=true | all-gather | bytes 983040 | tf_op jit(solution)/shard_map/all_gather | solution.py:91
  143.2 17.6 %all-gather.5.cloned.1.call-done.k_ref.v_ref = bf16[2,2048,384]{2,1,0:T(8,128)(2,1)} async-done(((bf16[2,256,384]{2,1,0:T(8,128)(2,1)}), bf16[2,2048,384]{2,1,0:T(8,128)(2,1)}) %all-gather.5.cloned.1.call-update) | async-done | bytes 3145744 | tf_op jit(solution)/shard_map/all_gather | solution.py:92
  160.8 1.9 copy-done.2
  162.7 11.0 %shard_map.101 = bf16[1024,512]{1,0:T(8,128)(2,1)S(1)} custom-call(bf16[1024,384]{1,0:T(8,128)(2,1)S(1)} %all_gather.25.q_ref, bf16[2,2048,384]{2,1,0:T(8,128)(2,1)S(1)} %copy-done.2, bf16[2,2048,384]{2,1,0:T(8,128)(2,1)S(1)} %copy-done.2), custom_call_target="tpu_custom_call" | custom-call | tf_op jit(solution)/shard_map/pallas_call | solution.py:74
  173.7 1.3 copy.18
  175.0 4.1 %all-to-all-start.1 = ((bf16[4,256,512]{1,2,0:T(8,128)(2,1)}), bf16[4,256,512]{1,2,0:T(8,128)(2,1)S(1)}, u32[]{:S(2)}, u32[]{:S(2)}) async-start(bf16[4,256,512]{1,2,0:T(8,128)(2,1)} %copy.18), calls=%async_computation.1 | async-start | bytes 2097152 | tf_op jit(solution)/shard_map/all_to_all | solution.py:96
  179.1 1.3 collective-permute-start.6
  180.4 12.3 %all-to-all-done.1 = bf16[4,256,512]{1,2,0:T(8,128)(2,1)S(1)} async-done(((bf16[4,256,512]{1,2,0:T(8,128)(2,1)}), bf16[4,256,512]{1,2,0:T(8,128)(2,1)S(1)}, u32[]{:S(2)}, u32[]{:S(2)}) %all-to-all-start.1) | async-done | bytes 1048608 | tf_op jit(solution)/shard_map/all_to_all | solution.py:96
  192.9 0.2 convert_element_type.84
  193.1 0.1 fusion.22
  193.3 10.8 %all_gather.27 = bf16[256,1536]{0,1:T(8,128)(2,1)S(1)} all-gather(bf16[256,384]{0,1:T(8,128)(2,1)S(1)} %fusion.98), channel_id=1, replica_groups=mesh['segment'=2,'bz'=8,'bx'=4,'my'=2,'mc'=2] {'my','mc'}, dimensions={1}, use_global_device_ids=true | all-gather | bytes 983040 | tf_op jit(solution)/shard_map/all_gather | solution.py:141
  204.1 0.1 constant_dynamic-slice_fusion.3
  204.1 0.0 collective-permute-done.6
  204.1 1.7 add_convert_fusion
  205.9 4.4 %collective-permute-start.8 = (bf16[256,384]{1,0:T(8,128)(2,1)S(1)}, bf16[256,384]{1,0:T(8,128)(2,1)S(1)}, u32[]{:S(2)}, u32[]{:S(2)}) collective-permute-start(bf16[256,384]{1,0:T(8,128)(2,1)S(1)} %add_convert_fusion), channel_id=1, source_target_pairs={{0,128},{1,129},{2,130},{3,131},{4,132},{5,133},{6,134},{7,135},{8... | collective-permute-start | bytes 589832 | tf_op jit(solution)/shard_map/ppermute | solution.py:23
  210.3 4.1 %collective-permute-done.8 = bf16[256,384]{1,0:T(8,128)(2,1)S(1)} collective-permute-done((bf16[256,384]{1,0:T(8,128)(2,1)S(1)}, bf16[256,384]{1,0:T(8,128)(2,1)S(1)}, u32[]{:S(2)}, u32[]{:S(2)}) %collective-permute-start.8) | collective-permute-done | bytes 196640 | tf_op jit(solution)/shard_map/ppermute | solution.py:23
  214.3 0.7 select_bitcast_fusion
  (33 shorter events, 0.4 us)
Async XLA Ops:
  6.5 0.9 copy-start
  6.5 12.7 %copy-start.6 = (f32[1,1536]{1,0:T(1,128)S(1)}, f32[1,1536]{1,0:T(1,128)}, u32[]{:S(2)}) copy-start(f32[1,1536]{1,0:T(1,128)} %param.13) | copy-start | bytes 18436
  6.5 63.9 %all-gather.3.cloned.1.call-start = ((), (), s32[]{:S(2)}) async-start(), calls=%async_computation.2 | async-start | bytes 3538944 | tf_op jit(solution)/shard_map/all_gather | solution.py:92
  21.1 4.7 %copy-start.3 = (bf16[384,1536]{1,0:T(8,128)(2,1)S(1)}, bf16[384,1536]{1,0:T(8,128)(2,1)}, u32[]{:S(2)}) copy-start(bf16[384,1536]{1,0:T(8,128)(2,1)} %param.19) | copy-start | bytes 3538948
  24.0 59.4 %collective-permute-start.1 = (bf16[384,1536]{1,0:T(8,128)(2,1)}, bf16[384,1536]{1,0:T(8,128)(2,1)}, u32[]{:S(2)}, u32[]{:S(2)}) collective-permute-start(bf16[384,1536]{1,0:T(8,128)(2,1)} %bitcast.99), channel_id=1, source_target_pairs={{0,1},{1,0},{2,3},{3,2},{4,5},{5,4},{6,7},{7,6},{8,9},{9,8},{10,11... | collective-permute-start | bytes 3538952 | tf_op jit(solution)/shard_map/ppermute | solution.py:124
  24.2 59.2 %collective-permute-start = (bf16[384,1536]{1,0:T(8,128)(2,1)}, bf16[384,1536]{1,0:T(8,128)(2,1)}, u32[]{:S(2)}, u32[]{:S(2)}) collective-permute-start(bf16[384,1536]{1,0:T(8,128)(2,1)} %bitcast.100), channel_id=1, source_target_pairs={{0,2},{2,0},{1,3},{3,1},{4,6},{6,4},{5,7},{7,5},{8,10},{10,8},{9,1... | collective-permute-start | bytes 3538952 | tf_op jit(solution)/shard_map/ppermute | solution.py:123
  26.8 56.6 %collective-permute-start.4 = (bf16[384,384]{1,0:T(8,128)(2,1)}, bf16[384,384]{1,0:T(8,128)(2,1)}, u32[]{:S(2)}, u32[]{:S(2)}) collective-permute-start(bf16[384,384]{1,0:T(8,128)(2,1)} %get-tuple-element.31), channel_id=1, source_target_pairs={{0,3},{1,0},{2,1},{3,2},{4,7},{5,4},{6,5},{7,6},{8,11},{9,8},{10,9... | collective-permute-start | bytes 884744 | tf_op jit(solution)/shard_map/ppermute | solution.py:117
  27.4 56.0 %collective-permute-start.2 = (bf16[384,384]{1,0:T(8,128)(2,1)}, bf16[384,384]{1,0:T(8,128)(2,1)}, u32[]{:S(2)}, u32[]{:S(2)}) collective-permute-start(bf16[384,384]{1,0:T(8,128)(2,1)} %get-tuple-element.32), channel_id=1, source_target_pairs={{0,1},{1,2},{2,3},{3,0},{4,5},{5,6},{6,7},{7,4},{8,9},{9,10},{10,1... | collective-permute-start | bytes 884744 | tf_op jit(solution)/shard_map/ppermute | solution.py:117
  28.5 54.9 %collective-permute-start.3 = (bf16[384,384]{1,0:T(8,128)(2,1)S(1)}, bf16[384,384]{1,0:T(8,128)(2,1)}, u32[]{:S(2)}, u32[]{:S(2)}) collective-permute-start(bf16[384,384]{1,0:T(8,128)(2,1)S(1)} %get-tuple-element.34), channel_id=1, source_target_pairs={{0,2},{1,3},{2,0},{3,1},{4,6},{5,7},{6,4},{7,5},{8,10},{9,11},{10,... | collective-permute-start | bytes 884744 | tf_op jit(solution)/shard_map/ppermute | solution.py:117
  70.5 1.9 copy-start.1
  84.8 17.7 %all-to-all-start = ((bf16[4,256,512]{1,2,0:T(8,128)(2,1)}), bf16[4,256,512]{1,2,0:T(8,128)(2,1)S(1)}, u32[]{:S(2)}, u32[]{:S(2)}) async-start(bf16[4,256,512]{1,2,0:T(8,128)(2,1)} %copy.15), calls=%async_computation | async-start | bytes 2097152 | tf_op jit(solution)/shard_map/all_to_all | solution.py:96
  88.7 72.1 %all-gather.5.cloned.1.call-start = ((), (), s32[]{:S(2)}) async-start(), calls=%async_computation.3 | async-start | bytes 3538944 | tf_op jit(solution)/shard_map/all_gather | solution.py:92
  88.7 25.4 %collective-permute-start.5 = (bf16[384,1536]{1,0:T(8,128)(2,1)}, bf16[384,1536]{1,0:T(8,128)(2,1)}, u32[]{:S(2)}, u32[]{:S(2)}) collective-permute-start(bf16[384,1536]{1,0:T(8,128)(2,1)} %collective-permute-done), channel_id=1, source_target_pairs={{0,1},{1,0},{2,3},{3,2},{4,5},{5,4},{6,7},{7,6},{8,9},{9,8},{10,11... | collective-permute-start | bytes 3538952 | tf_op jit(solution)/shard_map/ppermute | solution.py:131
  102.9 11.2 %copy-start.8 = (bf16[1,384,1536]{2,1,0:T(8,128)(2,1)S(1)}, bf16[1,384,1536]{2,1,0:T(8,128)(2,1)}, u32[]{:S(2)}) copy-start(bf16[1,384,1536]{2,1,0:T(8,128)(2,1)} %param.15) | copy-start | bytes 3538948
  114.1 3.7 %copy-start.7 = (bf16[3,1536,384]{2,1,0:T(8,128)(2,1)S(1)}, bf16[3,1536,384]{2,1,0:T(8,128)(2,1)}, u32[]{:S(2)}) copy-start(bf16[3,1536,384]{2,1,0:T(8,128)(2,1)} %param.18) | copy-start | bytes 10616836
  114.1 3.7 %copy-start.9 = (f32[1536]{0:T(1024)S(1)}, f32[1536]{0:T(1024)}, u32[]{:S(2)}) copy-start(f32[1536]{0:T(1024)} %param.17) | copy-start | bytes 18436
  117.8 2.2 copy-start.4
  118.5 1.5 copy-start.10
  121.9 9.7 %collective-permute-start.7 = (bf16[256,384]{1,0:T(8,128)(2,1)S(1)}, bf16[256,384]{1,0:T(8,128)(2,1)S(1)}, u32[]{:S(2)}, u32[]{:S(2)}) collective-permute-start(bf16[256,384]{1,0:T(8,128)(2,1)S(1)} %fusion.59), channel_id=1, source_target_pairs={{128,0},{129,1},{130,2},{131,3},{132,4},{133,5},{134,6},{135,7},{1... | collective-permute-start | bytes 589832 | tf_op jit(solution)/shard_map/ppermute | solution.py:23
  160.8 1.9 copy-start.2
  175.0 4.1 %copy-start.5 = (bf16[256,1536]{1,0:T(8,128)(2,1)S(1)}, bf16[256,1536]{1,0:T(8,128)(2,1)}, u32[]{:S(2)}) copy-start(bf16[256,1536]{1,0:T(8,128)(2,1)} %copy-done.4) | copy-start | bytes 2359300
  175.0 17.8 %all-to-all-start.1 = ((bf16[4,256,512]{1,2,0:T(8,128)(2,1)}), bf16[4,256,512]{1,2,0:T(8,128)(2,1)S(1)}, u32[]{:S(2)}, u32[]{:S(2)}) async-start(bf16[4,256,512]{1,2,0:T(8,128)(2,1)} %copy.18), calls=%async_computation.1 | async-start | bytes 2097152 | tf_op jit(solution)/shard_map/all_to_all | solution.py:96
  179.1 25.0 %collective-permute-start.6 = (bf16[256,384]{1,0:T(8,128)(2,1)S(1)}, bf16[256,384]{1,0:T(8,128)(2,1)S(1)}, u32[]{:S(2)}, u32[]{:S(2)}) collective-permute-start(bf16[256,384]{1,0:T(8,128)(2,1)S(1)} %constant_dynamic-slice_fusion.4), channel_id=1, source_target_pairs={{128,0},{129,1},{130,2},{131,3},{132,4},{133,5},{134,6},{135,7},{1... | collective-permute-start | bytes 589832 | tf_op jit(solution)/shard_map/ppermute | solution.py:23
  205.9 8.4 %collective-permute-start.8 = (bf16[256,384]{1,0:T(8,128)(2,1)S(1)}, bf16[256,384]{1,0:T(8,128)(2,1)S(1)}, u32[]{:S(2)}, u32[]{:S(2)}) collective-permute-start(bf16[256,384]{1,0:T(8,128)(2,1)S(1)} %add_convert_fusion), channel_id=1, source_target_pairs={{0,128},{1,129},{2,130},{3,131},{4,132},{5,133},{6,134},{7,135},{8... | collective-permute-start | bytes 589832 | tf_op jit(solution)/shard_map/ppermute | solution.py:23
Sparse Core Ops, SparseCore 0:
  24.1 46.3 all-gather.2
  120.1 40.6 all-gather.4

commit v15 on v14

--- a/solution.py
+++ b/solution.py
@@ -85,7 +85,7 @@
     )(queries, pairs, pairs)
 
 
-def attend(queries, pairs, riders=None):
+def attend(queries, pairs, riders=None, by_permutes=False):
     rows, width = queries.shape
     heads = width // HEAD_DIM
     query_block = lax.all_gather(queries, "bx", axis=0, tiled=True)
@@ -93,7 +93,18 @@
     partial = partial_attend(query_block, key_block)
     if riders is not None:
         partial, riders = lax.optimization_barrier((partial, riders))
-    parts = lax.all_to_all(partial, "bx", 0, 0, tiled=True)
+    if by_permutes:
+        count = lax.axis_size("bx")
+        me = lax.axis_index("bx")
+        chunks = [lax.dynamic_slice_in_dim(partial, me * rows, rows, axis=0)]
+        for step in range(1, count):
+            piece = lax.dynamic_slice_in_dim(partial, ((me + step) % count) * rows, rows, axis=0)
+            chunks.append(
+                lax.ppermute(piece, "bx", [(j, (j + step) % count) for j in range(count)])
+            )
+        parts = jnp.stack(chunks)
+    else:
+        parts = lax.all_to_all(partial, "bx", 0, 0, tiled=True)
     parts = parts.reshape(-1, rows, width + STATS).astype(jnp.float32)
     outs = parts[:, :, :width].reshape(-1, rows, heads, HEAD_DIM)
     stats = parts[:, :, width:width + 2 * heads * PARTS].reshape(-1, rows, 2, heads, PARTS)
@@ -183,7 +194,7 @@
         [project(normed, self_weights[0, 1]), project(normed, self_weights[0, 2])]
     )
     self_local, (self_other, self_near, cross_blocks) = attend(
-        self_queries, self_pairs, (self_other, self_near, cross_blocks)
+        self_queries, self_pairs, (self_other, self_near, cross_blocks), by_permutes=True
     )
     self_blocks = rows_in_order(self_out[0], self_other, self_near)
     self_attended = lax.all_gather(self_local, MP, axis=1, tiled=True)

time: 223 us -> 222 us (level)
  waiting for transfers between devices: 82.5 us -> 79.2 us
    all_to_all x2 -> x1, waiting for transfers between devices: 24.5 us -> 12.3 us  [attend(): parts = lax.all_to_all(partial, 'bx', 0, 0, tiled=True)]
    ppermute x0 -> x3, waiting for transfers between devices: none -> 7.63 us  [attend(): lax.ppermute(piece, 'bx', [(j, (j + step) % count) for j in range(count)])]
    ppermute x0 -> x3, starting transfers between devices: none -> 4.85 us  [attend(): lax.ppermute(piece, 'bx', [(j, (j + step) % count) for j in range(count)])]
    all_to_all x2 -> x1, starting transfers between devices: 8.08 us -> 3.97 us  [attend(): parts = lax.all_to_all(partial, 'bx', 0, 0, tiled=True)]
    unnamed x22 -> x44, local copies, waits for them, and re-layouts: 4.74 us -> 5.87 us
  transfers between devices with their start and end apart: 13 -> 15, of which waited for: 6 -> 8; matrix products, arithmetic and copies ran while one was open for 3% -> 4% of each run, Pallas kernels for 5% -> 5%
where the time goes in v15:
time: 222 us; the launch traced here: 221 us
  waiting for transfers between devices  79.2 us (36%)
  blocking collectives  55.9 us (25%)
  Pallas kernels  22 us (10%)
  starting transfers between devices  21.5 us (10%)
  matrix products  14.4 us (6%)
  between operations  13.9 us (6%)
  local copies, waits for them, and re-layouts  9.26 us (4%)
  other arithmetic  4.84 us (2%)
    all_gather x2, waiting for transfers between devices, attend(): key_block = lax.all_gather(pairs, 'bz', axis=1, tiled=True)  46.7 us
    all_gather x2, blocking collectives, attend(): query_block = lax.all_gather(queries, 'bx', axis=0, tiled=True)  24.1 us
    pallas_call x2, Pallas kernels, partial_attend(): pl.pallas_call(partial_kernel, grid=(rows // TILE,), in_specs=[pl.BlockSp...  22 us
    ppermute x3, waiting for transfers between devices, shifted(): lax.ppermute(value, axis, [(source, source + steps) for source in range(i...  12.5 us
    all_to_all x1, waiting for transfers between devices, attend(): parts = lax.all_to_all(partial, 'bx', 0, 0, tiled=True)  12.3 us
    all_gather x1, blocking collectives, mp_gather_flat(): return lax.all_gather(value, MP, axis=1, tiled=True)  10.9 us
    all_gather x1, blocking collectives, on_device(): self_attended = lax.all_gather(self_local, MP, axis=1, tiled=True)  10.6 us
    all_gather x1, blocking collectives, on_device(): embedded_full = lax.all_gather(embedded, MP, axis=1, tiled=True)  10.3 us
  transfers between devices with their start and end apart: 15, of which 8 were waited for; matrix products, arithmetic and copies ran while one was open for 4% of the time, Pallas kernels for 5%

profile of v15, /device:TPU:1, one launch (start us, length us, event | category | flops | bytes accessed | tf_op | source)
XLA Modules:
  0.0 220.9 jit_solution(15021362755075197490)
XLA Ops:
  6.5 0.9 copy-done
  7.5 1.2 fusion.68
  8.7 10.3 %all_gather.21 = bf16[256,1536]{1,0:T(8,128)(2,1)S(1)} all-gather(bf16[256,384]{1,0:T(8,128)(2,1)S(1)} %fusion.68), channel_id=1, replica_groups=mesh['segment'=2,'bz'=8,'bx'=4,'my'=2,'mc'=2] {'my','mc'}, dimensions={1}, use_global_device_ids=true | all-gather | bytes 983040 | tf_op jit(solution)/shard_map/all_gather | solution.py:190
  19.0 0.2 fusion.19
  19.2 1.9 fusion.75
  21.1 2.0 fusion.78
  23.1 0.8 pad_maximum_fusion
  23.9 0.0 all-gather.3.cloned.1.call-update
  23.9 0.0 all-gather.5.cloned.1.call-start
  24.0 1.7 collective-permute-start
  25.7 0.4 collective-permute-start.1
  26.2 0.8 constant_dynamic-slice_fusion.12
  27.0 0.1 collective-permute-start.2
  27.1 1.4 collective-permute-start.3
  28.4 1.9 fusion.50
  30.3 11.8 %all_gather.22.q_ref = bf16[1024,384]{1,0:T(8,128)(2,1)S(1)} all-gather(bf16[256,384]{1,0:T(8,128)(2,1)S(1)} %fusion.50), channel_id=1, replica_groups=mesh['segment'=2,'bz'=8,'bx'=4,'my'=2,'mc'=2] {'bx'}, dimensions={0}, use_global_device_ids=true | all-gather | bytes 983040 | tf_op jit(solution)/shard_map/all_gather | solution.py:91
  42.1 28.4 %all-gather.3.cloned.1.call-done.k_ref.v_ref = bf16[2,2048,384]{2,1,0:T(8,128)(2,1)} async-done(((bf16[2,256,384]{2,1,0:T(8,128)(2,1)}), bf16[2,2048,384]{2,1,0:T(8,128)(2,1)}) %all-gather.3.cloned.1.call-update) | async-done | bytes 3145744 | tf_op jit(solution)/shard_map/all_gather | solution.py:92
  70.4 1.9 copy-done.1
  72.3 11.0 %shard_map.100 = bf16[1024,512]{1,0:T(8,128)(2,1)S(1)} custom-call(bf16[1024,384]{1,0:T(8,128)(2,1)S(1)} %all_gather.22.q_ref, bf16[2,2048,384]{2,1,0:T(8,128)(2,1)S(1)} %copy-done.1, bf16[2,2048,384]{2,1,0:T(8,128)(2,1)S(1)} %copy-done.1), custom_call_target="tpu_custom_call" | custom-call | tf_op jit(solution)/shard_map/pallas_call | solution.py:74
  83.4 0.7 copy-done.14
  84.1 0.1 copy-done.16
  84.1 0.1 copy-done.18
  84.3 0.1 dynamic-slice_bitcast_fusion
  84.4 1.3 collective-permute-start.5
  85.6 2.4 %collective-permute-start.6 = (bf16[256,512]{1,0:T(8,128)(2,1)S(1)}, bf16[256,512]{1,0:T(8,128)(2,1)S(1)}, u32[]{:S(2)}, u32[]{:S(2)}) collective-permute-start(bf16[256,512]{1,0:T(8,128)(2,1)S(1)} %get-tuple-element.37), channel_id=1, source_target_pairs={{0,8},{4,12},{8,0},{12,4},{1,9},{5,13},{9,1},{13,5},{2,10},{6,14},... | collective-permute-start | bytes 786440 | tf_op jit(solution)/shard_map/ppermute | solution.py:103
  88.0 1.2 collective-permute-start.7
  89.2 2.1 collective-permute-start.8
  91.3 1.0 collective-permute-done.5
  92.3 6.5 %collective-permute-done.6 = bf16[256,512]{1,0:T(8,128)(2,1)S(1)} collective-permute-done((bf16[256,512]{1,0:T(8,128)(2,1)S(1)}, bf16[256,512]{1,0:T(8,128)(2,1)S(1)}, u32[]{:S(2)}, u32[]{:S(2)}) %collective-permute-start.6) | collective-permute-done | bytes 262176 | tf_op jit(solution)/shard_map/ppermute | solution.py:103
  98.8 0.1 collective-permute-done.7
  99.0 0.2 copy.15
  99.3 0.1 mul.153
  99.4 0.1 copy-done.8
  99.5 0.1 copy-done.9
  99.6 0.5 copy.17
  100.1 0.2 copy.18
  100.3 1.4 maximum_convert_fusion
  101.7 0.3 fusion.23
  102.0 0.1 divide_convert_fusion
  102.1 10.6 %all_gather.24 = bf16[256,1536]{1,0:T(8,128)(2,1)S(1)} all-gather(bf16[256,384]{1,0:T(8,128)(2,1)S(1)} %divide_convert_fusion), channel_id=1, replica_groups=mesh['segment'=2,'bz'=8,'bx'=4,'my'=2,'mc'=2] {'my','mc'}, dimensions={1}, use_global_device_ids=true | all-gather | bytes 983040 | tf_op jit(solution)/shard_map/all_gather | solution.py:200
  112.7 0.1 constant_dynamic-slice_fusion.8
  112.9 3.6 %fusion.18 = (f32[256]{0:T(256)S(1)}, bf16[256,1536]{1,0:T(8,128)(2,1)S(1)}) fusion(bf16[384,1536]{1,0:T(8,128)(2,1)} %collective-permute-done.8, bf16[384,1536]{1,0:T(8,128)(2,1)} %collective-permute-done.1, bf16[384,1536]{1,0:T(8,128)(2,1)} %collective-permute-done, bf16[384,1536]{1,0:T(8,128)(2,1)S(1)} %bitcast.108, ...), kind=kOutput, calls=%fused_computation.18 | convolution fusion | flops 1232338688 | bytes 7078912 | tf_op jit(solution)/shard_map/dot_general | solution.py:162
  116.5 0.6 fusion.72
  117.2 0.6 fusion.69
  117.8 0.8 pad_maximum_fusion.1
  118.6 1.9 fusion.59
  120.5 1.3 collective-permute-start.10
  121.8 8.4 %collective-permute-done.10 = bf16[256,384]{1,0:T(8,128)(2,1)S(1)} collective-permute-done((bf16[256,384]{1,0:T(8,128)(2,1)S(1)}, bf16[256,384]{1,0:T(8,128)(2,1)S(1)}, u32[]{:S(2)}, u32[]{:S(2)}) %collective-permute-start.10) | collective-permute-done | bytes 196640 | tf_op jit(solution)/shard_map/ppermute | solution.py:23
  130.2 12.3 %all_gather.25.q_ref = bf16[1024,384]{1,0:T(8,128)(2,1)S(1)} all-gather(bf16[256,384]{1,0:T(8,128)(2,1)S(1)} %collective-permute-done.10), channel_id=1, replica_groups=mesh['segment'=2,'bz'=8,'bx'=4,'my'=2,'mc'=2] {'bx'}, dimensions={0}, use_global_device_ids=true | all-gather | bytes 983040 | tf_op jit(solution)/shard_map/all_gather | solution.py:91
  142.5 18.4 %all-gather.5.cloned.1.call-done.k_ref.v_ref = bf16[2,2048,384]{2,1,0:T(8,128)(2,1)} async-done(((bf16[2,256,384]{2,1,0:T(8,128)(2,1)}), bf16[2,2048,384]{2,1,0:T(8,128)(2,1)}) %all-gather.5.cloned.1.call-update) | async-done | bytes 3145744 | tf_op jit(solution)/shard_map/all_gather | solution.py:92
  160.9 1.9 copy-done.2
  162.8 11.0 %shard_map.101 = bf16[1024,512]{1,0:T(8,128)(2,1)S(1)} custom-call(bf16[1024,384]{1,0:T(8,128)(2,1)S(1)} %all_gather.25.q_ref, bf16[2,2048,384]{2,1,0:T(8,128)(2,1)S(1)} %copy-done.2, bf16[2,2048,384]{2,1,0:T(8,128)(2,1)S(1)} %copy-done.2), custom_call_target="tpu_custom_call" | custom-call | tf_op jit(solution)/shard_map/pallas_call | solution.py:74
  173.8 1.3 copy.19
  175.1 4.0 %all-to-all-start = ((bf16[4,256,512]{1,2,0:T(8,128)(2,1)}), bf16[4,256,512]{1,2,0:T(8,128)(2,1)S(1)}, u32[]{:S(2)}, u32[]{:S(2)}) async-start(bf16[4,256,512]{1,2,0:T(8,128)(2,1)} %copy.19), calls=%async_computation | async-start | bytes 2097152 | tf_op jit(solution)/shard_map/all_to_all | solution.py:107
  179.1 1.3 collective-permute-start.9
  180.4 12.3 %all-to-all-done = bf16[4,256,512]{1,2,0:T(8,128)(2,1)S(1)} async-done(((bf16[4,256,512]{1,2,0:T(8,128)(2,1)}), bf16[4,256,512]{1,2,0:T(8,128)(2,1)S(1)}, u32[]{:S(2)}, u32[]{:S(2)}) %all-to-all-start) | async-done | bytes 1048608 | tf_op jit(solution)/shard_map/all_to_all | solution.py:107
  192.9 0.2 convert_element_type.84
  193.0 0.1 fusion.22
  193.2 10.9 %all_gather.27 = bf16[256,1536]{0,1:T(8,128)(2,1)S(1)} all-gather(bf16[256,384]{0,1:T(8,128)(2,1)S(1)} %fusion.98), channel_id=1, replica_groups=mesh['segment'=2,'bz'=8,'bx'=4,'my'=2,'mc'=2] {'my','mc'}, dimensions={1}, use_global_device_ids=true | all-gather | bytes 983040 | tf_op jit(solution)/shard_map/all_gather | solution.py:152
  204.2 0.1 constant_dynamic-slice_fusion.3
  204.3 0.6 add_convert_fusion
  204.9 4.4 %collective-permute-start.11 = (bf16[256,384]{1,0:T(8,128)(2,1)S(1)}, bf16[256,384]{1,0:T(8,128)(2,1)S(1)}, u32[]{:S(2)}, u32[]{:S(2)}) collective-permute-start(bf16[256,384]{1,0:T(8,128)(2,1)S(1)} %add_convert_fusion), channel_id=1, source_target_pairs={{0,128},{1,129},{2,130},{3,131},{4,132},{5,133},{6,134},{7,135},{8... | collective-permute-start | bytes 589832 | tf_op jit(solution)/shard_map/ppermute | solution.py:23
  209.3 4.1 %collective-permute-done.11 = bf16[256,384]{1,0:T(8,128)(2,1)S(1)} collective-permute-done((bf16[256,384]{1,0:T(8,128)(2,1)S(1)}, bf16[256,384]{1,0:T(8,128)(2,1)S(1)}, u32[]{:S(2)}, u32[]{:S(2)}) %collective-permute-start.11) | collective-permute-done | bytes 196640 | tf_op jit(solution)/shard_map/ppermute | solution.py:23
  213.4 0.7 select_bitcast_fusion
  (63 shorter events, 0.5 us)
Async XLA Ops:
  6.5 0.9 copy-start
  6.5 12.7 %copy-start.11 = (f32[1,1536]{1,0:T(1,128)S(1)}, f32[1,1536]{1,0:T(1,128)}, u32[]{:S(2)}) copy-start(f32[1,1536]{1,0:T(1,128)} %param.13) | copy-start | bytes 18436
  6.5 63.9 %all-gather.3.cloned.1.call-start = ((), (), s32[]{:S(2)}) async-start(), calls=%async_computation.1 | async-start | bytes 3538944 | tf_op jit(solution)/shard_map/all_gather | solution.py:92
  19.0 9.5 %copy-start.3 = (bf16[256,1536]{1,0:T(8,128)(2,1)}, bf16[256,1536]{1,0:T(8,128)(2,1)S(1)}, u32[]{:S(2)}) copy-start(bf16[256,1536]{1,0:T(8,128)(2,1)S(1)} %all_gather.21) | copy-start | bytes 2359300
  21.1 5.0 %copy-start.6 = (bf16[384,1536]{1,0:T(8,128)(2,1)S(1)}, bf16[384,1536]{1,0:T(8,128)(2,1)}, u32[]{:S(2)}) copy-start(bf16[384,1536]{1,0:T(8,128)(2,1)} %param.19) | copy-start | bytes 3538948
  23.9 136.9 %all-gather.5.cloned.1.call-start = ((), (), s32[]{:S(2)}) async-start(), calls=%async_computation.2 | async-start | bytes 3538944 | tf_op jit(solution)/shard_map/all_gather | solution.py:92
  24.0 59.4 %collective-permute-start = (bf16[384,1536]{1,0:T(8,128)(2,1)}, bf16[384,1536]{1,0:T(8,128)(2,1)}, u32[]{:S(2)}, u32[]{:S(2)}) collective-permute-start(bf16[384,1536]{1,0:T(8,128)(2,1)} %bitcast.106), channel_id=1, source_target_pairs={{0,2},{2,0},{1,3},{3,1},{4,6},{6,4},{5,7},{7,5},{8,10},{10,8},{9,1... | collective-permute-start | bytes 3538952 | tf_op jit(solution)/shard_map/ppermute | solution.py:134
  25.7 57.7 %collective-permute-start.1 = (bf16[384,1536]{1,0:T(8,128)(2,1)}, bf16[384,1536]{1,0:T(8,128)(2,1)}, u32[]{:S(2)}, u32[]{:S(2)}) collective-permute-start(bf16[384,1536]{1,0:T(8,128)(2,1)} %bitcast.107), channel_id=1, source_target_pairs={{0,1},{1,0},{2,3},{3,2},{4,5},{5,4},{6,7},{7,6},{8,9},{9,8},{10,11... | collective-permute-start | bytes 3538952 | tf_op jit(solution)/shard_map/ppermute | solution.py:135
  27.0 56.3 %collective-permute-start.2 = (bf16[384,384]{1,0:T(8,128)(2,1)S(1)}, bf16[384,384]{1,0:T(8,128)(2,1)S(1)}, u32[]{:S(2)}, u32[]{:S(2)}) collective-permute-start(bf16[384,384]{1,0:T(8,128)(2,1)S(1)} %get-tuple-element.32), channel_id=1, source_target_pairs={{0,1},{1,2},{2,3},{3,0},{4,5},{5,6},{6,7},{7,4},{8,9},{9,10},{10,1... | collective-permute-start | bytes 884744 | tf_op jit(solution)/shard_map/ppermute | solution.py:128
  27.1 56.3 %collective-permute-start.3 = (bf16[384,384]{1,0:T(8,128)(2,1)S(1)}, bf16[384,384]{1,0:T(8,128)(2,1)S(1)}, u32[]{:S(2)}, u32[]{:S(2)}) collective-permute-start(bf16[384,384]{1,0:T(8,128)(2,1)S(1)} %get-tuple-element.34), channel_id=1, source_target_pairs={{0,2},{1,3},{2,0},{3,1},{4,6},{5,7},{6,4},{7,5},{8,10},{9,11},{10,... | collective-permute-start | bytes 884744 | tf_op jit(solution)/shard_map/ppermute | solution.py:128
  28.4 55.0 %collective-permute-start.4 = (bf16[384,384]{1,0:T(8,128)(2,1)S(1)}, bf16[384,384]{1,0:T(8,128)(2,1)S(1)}, u32[]{:S(2)}, u32[]{:S(2)}) collective-permute-start(bf16[384,384]{1,0:T(8,128)(2,1)S(1)} %get-tuple-element.31), channel_id=1, source_target_pairs={{0,3},{1,0},{2,1},{3,2},{4,7},{5,4},{6,5},{7,6},{8,11},{9,8},{10,9... | collective-permute-start | bytes 884744 | tf_op jit(solution)/shard_map/ppermute | solution.py:128
  70.4 1.9 copy-start.1
  83.3 0.7 copy-start.14
  83.4 0.8 copy-start.16
  83.4 0.9 copy-start.18
  84.3 15.0 %copy-start.5 = (bf16[1,256,512]{2,1,0:T(8,128)(2,1)}, bf16[1,256,512]{2,1,0:T(8,128)(2,1)S(1)}, u32[]{:S(2)}) copy-start(bf16[1,256,512]{2,1,0:T(8,128)(2,1)S(1)} %get-tuple-element.35) | copy-start | bytes 786436
  84.4 7.9 %collective-permute-start.5 = (bf16[256,512]{1,0:T(8,128)(2,1)S(1)}, bf16[256,512]{1,0:T(8,128)(2,1)S(1)}, u32[]{:S(2)}, u32[]{:S(2)}) collective-permute-start(bf16[256,512]{1,0:T(8,128)(2,1)S(1)} %get-tuple-element.38), channel_id=1, source_target_pairs={{0,4},{4,8},{8,12},{12,0},{1,5},{5,9},{9,13},{13,1},{2,6},{6,10},{... | collective-permute-start | bytes 786440 | tf_op jit(solution)/shard_map/ppermute | solution.py:103
  85.6 13.2 %collective-permute-start.6 = (bf16[256,512]{1,0:T(8,128)(2,1)S(1)}, bf16[256,512]{1,0:T(8,128)(2,1)S(1)}, u32[]{:S(2)}, u32[]{:S(2)}) collective-permute-start(bf16[256,512]{1,0:T(8,128)(2,1)S(1)} %get-tuple-element.37), channel_id=1, source_target_pairs={{0,8},{4,12},{8,0},{12,4},{1,9},{5,13},{9,1},{13,5},{2,10},{6,14},... | collective-permute-start | bytes 786440 | tf_op jit(solution)/shard_map/ppermute | solution.py:103
  88.0 10.9 %collective-permute-start.7 = (bf16[256,512]{1,0:T(8,128)(2,1)S(1)}, bf16[256,512]{1,0:T(8,128)(2,1)S(1)}, u32[]{:S(2)}, u32[]{:S(2)}) collective-permute-start(bf16[256,512]{1,0:T(8,128)(2,1)S(1)} %get-tuple-element.36), channel_id=1, source_target_pairs={{0,12},{4,0},{8,4},{12,8},{1,13},{5,1},{9,5},{13,9},{2,14},{6,2},{... | collective-permute-start | bytes 786440 | tf_op jit(solution)/shard_map/ppermute | solution.py:103
  89.2 23.6 %collective-permute-start.8 = (bf16[384,1536]{1,0:T(8,128)(2,1)}, bf16[384,1536]{1,0:T(8,128)(2,1)}, u32[]{:S(2)}, u32[]{:S(2)}) collective-permute-start(bf16[384,1536]{1,0:T(8,128)(2,1)} %collective-permute-done), channel_id=1, source_target_pairs={{0,1},{1,0},{2,3},{3,2},{4,5},{5,4},{6,7},{7,6},{8,9},{9,8},{10,11... | collective-permute-start | bytes 3538952 | tf_op jit(solution)/shard_map/ppermute | solution.py:142
  92.3 7.1 %copy-start.7 = (bf16[256,512]{1,0:T(8,128)(2,1)}, bf16[256,512]{1,0:T(8,128)(2,1)S(1)}, u32[]{:S(2)}) copy-start(bf16[256,512]{1,0:T(8,128)(2,1)S(1)} %collective-permute-done.5) | copy-start | bytes 786436
  98.8 0.7 copy-start.8
  98.9 0.7 copy-start.9
  102.0 10.8 %copy-start.4 = (bf16[256,1536]{1,0:T(8,128)(2,1)S(1)}, bf16[256,1536]{1,0:T(8,128)(2,1)}, u32[]{:S(2)}) copy-start(bf16[256,1536]{1,0:T(8,128)(2,1)} %copy-done.3) | copy-start | bytes 2359300
  102.0 10.8 %copy-start.13 = (bf16[1,384,1536]{2,1,0:T(8,128)(2,1)S(1)}, bf16[1,384,1536]{2,1,0:T(8,128)(2,1)}, u32[]{:S(2)}) copy-start(bf16[1,384,1536]{2,1,0:T(8,128)(2,1)} %param.15) | copy-start | bytes 3538948
  112.8 3.7 %copy-start.12 = (bf16[3,1536,384]{2,1,0:T(8,128)(2,1)S(1)}, bf16[3,1536,384]{2,1,0:T(8,128)(2,1)}, u32[]{:S(2)}) copy-start(bf16[3,1536,384]{2,1,0:T(8,128)(2,1)} %param.18) | copy-start | bytes 10616836
  112.8 3.7 %copy-start.20 = (f32[1536]{0:T(1024)S(1)}, f32[1536]{0:T(1024)}, u32[]{:S(2)}) copy-start(f32[1536]{0:T(1024)} %param.17) | copy-start | bytes 18436
  117.1 1.5 copy-start.21
  120.5 9.7 %collective-permute-start.10 = (bf16[256,384]{1,0:T(8,128)(2,1)S(1)}, bf16[256,384]{1,0:T(8,128)(2,1)S(1)}, u32[]{:S(2)}, u32[]{:S(2)}) collective-permute-start(bf16[256,384]{1,0:T(8,128)(2,1)S(1)} %fusion.59), channel_id=1, source_target_pairs={{128,0},{129,1},{130,2},{131,3},{132,4},{133,5},{134,6},{135,7},{1... | collective-permute-start | bytes 589832 | tf_op jit(solution)/shard_map/ppermute | solution.py:23
  160.9 1.9 copy-start.2
  175.1 17.6 %all-to-all-start = ((bf16[4,256,512]{1,2,0:T(8,128)(2,1)}), bf16[4,256,512]{1,2,0:T(8,128)(2,1)S(1)}, u32[]{:S(2)}, u32[]{:S(2)}) async-start(bf16[4,256,512]{1,2,0:T(8,128)(2,1)} %copy.19), calls=%async_computation | async-start | bytes 2097152 | tf_op jit(solution)/shard_map/all_to_all | solution.py:107
  179.1 25.2 %collective-permute-start.9 = (bf16[256,384]{1,0:T(8,128)(2,1)S(1)}, bf16[256,384]{1,0:T(8,128)(2,1)S(1)}, u32[]{:S(2)}, u32[]{:S(2)}) collective-permute-start(bf16[256,384]{1,0:T(8,128)(2,1)S(1)} %constant_dynamic-slice_fusion.4), channel_id=1, source_target_pairs={{128,0},{129,1},{130,2},{131,3},{132,4},{133,5},{134,6},{135,7},{1... | collective-permute-start | bytes 589832 | tf_op jit(solution)/shard_map/ppermute | solution.py:23
  193.2 11.1 %copy-start.10 = (bf16[384,384]{1,0:T(8,128)(2,1)S(1)}, bf16[384,384]{1,0:T(8,128)(2,1)}, u32[]{:S(2)}) copy-start(bf16[384,384]{1,0:T(8,128)(2,1)} %get-tuple-element.23) | copy-start | bytes 884740
  193.2 11.1 %copy-start.15 = (bf16[384,384]{1,0:T(8,128)(2,1)S(1)}, bf16[384,384]{1,0:T(8,128)(2,1)}, u32[]{:S(2)}) copy-start(bf16[384,384]{1,0:T(8,128)(2,1)} %copy-done.14) | copy-start | bytes 884740
  193.2 11.1 %copy-start.17 = (bf16[384,384]{1,0:T(8,128)(2,1)S(1)}, bf16[384,384]{1,0:T(8,128)(2,1)}, u32[]{:S(2)}) copy-start(bf16[384,384]{1,0:T(8,128)(2,1)} %copy-done.16) | copy-start | bytes 884740
  193.2 11.1 %copy-start.19 = (bf16[384,384]{1,0:T(8,128)(2,1)S(1)}, bf16[384,384]{1,0:T(8,128)(2,1)}, u32[]{:S(2)}) copy-start(bf16[384,384]{1,0:T(8,128)(2,1)} %copy-done.18) | copy-start | bytes 884740
  204.9 8.4 %collective-permute-start.11 = (bf16[256,384]{1,0:T(8,128)(2,1)S(1)}, bf16[256,384]{1,0:T(8,128)(2,1)S(1)}, u32[]{:S(2)}, u32[]{:S(2)}) collective-permute-start(bf16[256,384]{1,0:T(8,128)(2,1)S(1)} %add_convert_fusion), channel_id=1, source_target_pairs={{0,128},{1,129},{2,130},{3,131},{4,132},{5,133},{6,134},{7,135},{8... | collective-permute-start | bytes 589832 | tf_op jit(solution)/shard_map/ppermute | solution.py:23
Sparse Core Ops, SparseCore 0:
  24.1 46.3 all-gather.2
  118.7 42.0 all-gather.4

commit v16 on v15

--- a/solution.py
+++ b/solution.py
@@ -209,7 +209,7 @@
     )
     voxel_queries = shifted(cross_queries, "segment", -1)
     voxel_part = shifted(hidden_part, "segment", -1)
-    crossed = mp_gather_flat(attend(voxel_queries, memory_pairs))
+    crossed = mp_gather_flat(attend(voxel_queries, memory_pairs, by_permutes=True))
     decoded = (
         voxel_part.astype(jnp.float32) + project_out(crossed, cross_blocks)
     ).astype(jnp.bfloat16)

time: 222 us -> 227 us (1.023)
  local copies, waits for them, and re-layouts: 9.26 us -> 13.4 us
  waiting for transfers between devices: 79.2 us -> 75.2 us
  other arithmetic: 4.84 us -> 8.3 us
    all_to_all x1 -> x0, waiting for transfers between devices: 12.3 us -> none  [attend(): parts = lax.all_to_all(partial, 'bx', 0, 0, tiled=True)]
    ppermute x3 -> x6, waiting for transfers between devices: 7.63 us -> 16 us  [attend(): lax.ppermute(piece, 'bx', [(j, (j + step) % count) for j in range(count)])]
    ppermute x3 -> x6, starting transfers between devices: 4.85 us -> 9.69 us  [attend(): lax.ppermute(piece, 'bx', [(j, (j + step) % count) for j in range(count)])]
    mul x2 -> x4, local copies, waits for them, and re-layouts: 0.58 us -> 4.9 us  [attend(): merged = jnp.sum(outs * scale[..., None], axis=0) / total[..., None]]
    all_to_all x1 -> x0, starting transfers between devices: 3.97 us -> none  [attend(): parts = lax.all_to_all(partial, 'bx', 0, 0, tiled=True)]
    unnamed x44 -> x50, local copies, waits for them, and re-layouts: 5.87 us -> 6.51 us
  transfers between devices with their start and end apart: 15 -> 17, of which waited for: 8 -> 9; matrix products, arithmetic and copies ran while one was open for 4% -> 7% of each run, Pallas kernels for 5% -> 5%
where the time goes in v16:
time: 227 us; the launch traced here: 226 us
  waiting for transfers between devices  75.2 us (33%)
  blocking collectives  55.5 us (24%)
  starting transfers between devices  22.4 us (10%)
  Pallas kernels  22 us (10%)
  matrix products  15.3 us (7%)
  between operations  13.9 us (6%)
  local copies, waits for them, and re-layouts  13.4 us (6%)
  other arithmetic  8.3 us (4%)
    all_gather x2, waiting for transfers between devices, attend(): key_block = lax.all_gather(pairs, 'bz', axis=1, tiled=True)  46.7 us
    all_gather x2, blocking collectives, attend(): query_block = lax.all_gather(queries, 'bx', axis=0, tiled=True)  24.1 us
    pallas_call x2, Pallas kernels, partial_attend(): pl.pallas_call(partial_kernel, grid=(rows // TILE,), in_specs=[pl.BlockSp...  22 us
    ppermute x6, waiting for transfers between devices, attend(): lax.ppermute(piece, 'bx', [(j, (j + step) % count) for j in range(count)])  16 us
    ppermute x3, waiting for transfers between devices, shifted(): lax.ppermute(value, axis, [(source, source + steps) for source in range(i...  12.5 us
    all_gather x1, blocking collectives, on_device(): self_attended = lax.all_gather(self_local, MP, axis=1, tiled=True)  10.7 us
    all_gather x1, blocking collectives, mp_gather_flat(): return lax.all_gather(value, MP, axis=1, tiled=True)  10.6 us
    all_gather x1, blocking collectives, on_device(): embedded_full = lax.all_gather(embedded, MP, axis=1, tiled=True)  10.3 us
  transfers between devices with their start and end apart: 17, of which 9 were waited for; matrix products, arithmetic and copies ran while one was open for 7% of the time, Pallas kernels for 5%

profile of v16, /device:TPU:1, one launch (start us, length us, event | category | flops | bytes accessed | tf_op | source)
XLA Modules:
  0.0 225.9 jit_solution(3002377928511446167)
XLA Ops:
  6.5 0.9 copy-done
  7.5 1.2 fusion.68
  8.7 10.3 %all_gather.21 = bf16[256,1536]{1,0:T(8,128)(2,1)S(1)} all-gather(bf16[256,384]{1,0:T(8,128)(2,1)S(1)} %fusion.68), channel_id=1, replica_groups=mesh['segment'=2,'bz'=8,'bx'=4,'my'=2,'mc'=2] {'my','mc'}, dimensions={1}, use_global_device_ids=true | all-gather | bytes 983040 | tf_op jit(solution)/shard_map/all_gather | solution.py:190
  19.0 0.2 fusion.19
  19.2 1.9 fusion.75
  21.1 2.0 fusion.78
  23.1 0.8 pad_maximum_fusion
  24.0 1.7 collective-permute-start
  25.7 0.4 collective-permute-start.1
  26.2 0.8 constant_dynamic-slice_fusion.15
  27.1 1.4 collective-permute-start.3
  28.4 1.9 fusion.50
  30.3 11.8 %all_gather.22.q_ref = bf16[1024,384]{1,0:T(8,128)(2,1)S(1)} all-gather(bf16[256,384]{1,0:T(8,128)(2,1)S(1)} %fusion.50), channel_id=1, replica_groups=mesh['segment'=2,'bz'=8,'bx'=4,'my'=2,'mc'=2] {'bx'}, dimensions={0}, use_global_device_ids=true | all-gather | bytes 983040 | tf_op jit(solution)/shard_map/all_gather | solution.py:91
  42.1 28.4 %all-gather.3.cloned.1.call-done.k_ref.v_ref = bf16[2,2048,384]{2,1,0:T(8,128)(2,1)} async-done(((bf16[2,256,384]{2,1,0:T(8,128)(2,1)}), bf16[2,2048,384]{2,1,0:T(8,128)(2,1)}) %all-gather.3.cloned.1.call-update) | async-done | bytes 3145744 | tf_op jit(solution)/shard_map/all_gather | solution.py:92
  70.5 1.9 copy-done.1
  72.3 11.0 %shard_map.100 = bf16[1024,512]{1,0:T(8,128)(2,1)S(1)} custom-call(bf16[1024,384]{1,0:T(8,128)(2,1)S(1)} %all_gather.22.q_ref, bf16[2,2048,384]{2,1,0:T(8,128)(2,1)S(1)} %copy-done.1, bf16[2,2048,384]{2,1,0:T(8,128)(2,1)S(1)} %copy-done.1), custom_call_target="tpu_custom_call" | custom-call | tf_op jit(solution)/shard_map/pallas_call | solution.py:74
  83.4 0.8 copy-done.21
  84.3 1.3 collective-permute-start.5
  85.6 2.4 %collective-permute-start.6 = (bf16[256,512]{1,0:T(8,128)(2,1)S(1)}, bf16[256,512]{1,0:T(8,128)(2,1)S(1)}, u32[]{:S(2)}, u32[]{:S(2)}) collective-permute-start(bf16[256,512]{1,0:T(8,128)(2,1)S(1)} %get-tuple-element.41), channel_id=1, source_target_pairs={{0,8},{4,12},{8,0},{12,4},{1,9},{5,13},{9,1},{13,5},{2,10},{6,14},... | collective-permute-start | bytes 786440 | tf_op jit(solution)/shard_map/ppermute | solution.py:103
  88.0 1.2 collective-permute-start.7
  89.1 2.1 collective-permute-start.8
  91.2 1.0 collective-permute-done.5
  92.2 6.5 %collective-permute-done.6 = bf16[256,512]{1,0:T(8,128)(2,1)S(1)} collective-permute-done((bf16[256,512]{1,0:T(8,128)(2,1)S(1)}, bf16[256,512]{1,0:T(8,128)(2,1)S(1)}, u32[]{:S(2)}, u32[]{:S(2)}) %collective-permute-start.6) | collective-permute-done | bytes 262176 | tf_op jit(solution)/shard_map/ppermute | solution.py:103
  98.7 0.1 collective-permute-done.7
  98.9 0.2 copy.15
  99.2 0.1 mul.157
  99.3 0.1 copy-done.8
  99.4 0.1 copy-done.9
  99.5 0.5 copy.17
  100.0 0.2 copy.18
  100.2 1.4 maximum_convert_fusion
  101.6 0.3 fusion.23
  102.0 10.7 %all_gather.24 = bf16[256,1536]{1,0:T(8,128)(2,1)S(1)} all-gather(bf16[256,384]{1,0:T(8,128)(2,1)S(1)} %divide_convert_fusion.1), channel_id=1, replica_groups=mesh['segment'=2,'bz'=8,'bx'=4,'my'=2,'mc'=2] {'my','mc'}, dimensions={1}, use_global_device_ids=true | all-gather | bytes 983040 | tf_op jit(solution)/shard_map/all_gather | solution.py:200
  112.8 3.6 %fusion.18 = (f32[256]{0:T(256)S(1)}, bf16[256,1536]{1,0:T(8,128)(2,1)S(1)}) fusion(bf16[384,1536]{1,0:T(8,128)(2,1)} %collective-permute-done.8, bf16[384,1536]{1,0:T(8,128)(2,1)} %collective-permute-done.1, bf16[384,1536]{1,0:T(8,128)(2,1)} %collective-permute-done, bf16[384,1536]{1,0:T(8,128)(2,1)S(1)} %bitcast.115, ...), kind=kOutput, calls=%fused_computation.18 | convolution fusion | flops 1232338688 | bytes 7078912 | tf_op jit(solution)/shard_map/dot_general | solution.py:162
  116.4 0.6 fusion.72
  117.1 0.6 fusion.69
  117.7 0.8 pad_maximum_fusion.1
  118.5 1.9 fusion.59
  120.4 1.3 collective-permute-start.10
  121.7 8.4 %collective-permute-done.10 = bf16[256,384]{1,0:T(8,128)(2,1)S(1)} collective-permute-done((bf16[256,384]{1,0:T(8,128)(2,1)S(1)}, bf16[256,384]{1,0:T(8,128)(2,1)S(1)}, u32[]{:S(2)}, u32[]{:S(2)}) %collective-permute-start.10) | collective-permute-done | bytes 196640 | tf_op jit(solution)/shard_map/ppermute | solution.py:23
  130.1 12.3 %all_gather.25.q_ref = bf16[1024,384]{1,0:T(8,128)(2,1)S(1)} all-gather(bf16[256,384]{1,0:T(8,128)(2,1)S(1)} %collective-permute-done.10), channel_id=1, replica_groups=mesh['segment'=2,'bz'=8,'bx'=4,'my'=2,'mc'=2] {'bx'}, dimensions={0}, use_global_device_ids=true | all-gather | bytes 983040 | tf_op jit(solution)/shard_map/all_gather | solution.py:91
  142.4 18.4 %all-gather.5.cloned.1.call-done.k_ref.v_ref = bf16[2,2048,384]{2,1,0:T(8,128)(2,1)} async-done(((bf16[2,256,384]{2,1,0:T(8,128)(2,1)}), bf16[2,2048,384]{2,1,0:T(8,128)(2,1)}) %all-gather.5.cloned.1.call-update) | async-done | bytes 3145744 | tf_op jit(solution)/shard_map/all_gather | solution.py:92
  160.8 1.9 copy-done.2
  162.7 11.0 %shard_map.101 = bf16[1024,512]{1,0:T(8,128)(2,1)S(1)} custom-call(bf16[1024,384]{1,0:T(8,128)(2,1)S(1)} %all_gather.25.q_ref, bf16[2,2048,384]{2,1,0:T(8,128)(2,1)S(1)} %copy-done.2, bf16[2,2048,384]{2,1,0:T(8,128)(2,1)S(1)} %copy-done.2), custom_call_target="tpu_custom_call" | custom-call | tf_op jit(solution)/shard_map/pallas_call | solution.py:74
  173.7 0.1 dynamic-slice_bitcast_fusion
  173.8 1.3 collective-permute-start.11
  175.0 2.4 %collective-permute-start.12 = (bf16[256,512]{1,0:T(8,128)(2,1)S(1)}, bf16[256,512]{1,0:T(8,128)(2,1)S(1)}, u32[]{:S(2)}, u32[]{:S(2)}) collective-permute-start(bf16[256,512]{1,0:T(8,128)(2,1)S(1)} %get-tuple-element.37), channel_id=1, source_target_pairs={{0,8},{4,12},{8,0},{12,4},{1,9},{5,13},{9,1},{13,5},{2,10},{6,14},... | collective-permute-start | bytes 786440 | tf_op jit(solution)/shard_map/ppermute | solution.py:103
  177.4 1.2 collective-permute-start.13
  178.6 1.3 collective-permute-start.9
  179.9 1.7 collective-permute-done.11
  181.7 6.6 %collective-permute-done.12 = bf16[256,512]{1,0:T(8,128)(2,1)S(1)} collective-permute-done((bf16[256,512]{1,0:T(8,128)(2,1)S(1)}, bf16[256,512]{1,0:T(8,128)(2,1)S(1)}, u32[]{:S(2)}, u32[]{:S(2)}) %collective-permute-start.12) | collective-permute-done | bytes 262176 | tf_op jit(solution)/shard_map/ppermute | solution.py:103
  188.3 0.7 copy-done.10
  189.1 0.2 maximum_convert_fusion.1
  189.3 0.9 maximum_convert_fusion.2
  190.2 0.2 copy.19
  190.5 1.3 mul.172
  191.7 3.1 %copy.21 = f32[4,256,384]{2,1,0:T(8,128)} copy(f32[4,256,384]{1,2,0:T(8,128)} %bitcast.95) | data formatting | bytes 3145728 | tf_op jit(solution)/shard_map/mul | solution.py:117
  194.8 0.2 copy.22
  195.0 1.7 fusion.22
  196.8 10.6 %all_gather.27 = bf16[256,1536]{1,0:T(8,128)(2,1)S(1)} all-gather(bf16[256,384]{1,0:T(8,128)(2,1)S(1)} %divide_convert_fusion), channel_id=1, replica_groups=mesh['segment'=2,'bz'=8,'bx'=4,'my'=2,'mc'=2] {'my','mc'}, dimensions={1}, use_global_device_ids=true | all-gather | bytes 983040 | tf_op jit(solution)/shard_map/all_gather | solution.py:152
  207.5 1.5 add_convert_fusion
  209.0 4.4 %collective-permute-start.14 = (bf16[256,384]{1,0:T(8,128)(2,1)S(1)}, bf16[256,384]{1,0:T(8,128)(2,1)S(1)}, u32[]{:S(2)}, u32[]{:S(2)}) collective-permute-start(bf16[256,384]{1,0:T(8,128)(2,1)S(1)} %add_convert_fusion), channel_id=1, source_target_pairs={{0,128},{1,129},{2,130},{3,131},{4,132},{5,133},{6,134},{7,135},{8... | collective-permute-start | bytes 589832 | tf_op jit(solution)/shard_map/ppermute | solution.py:23
  213.4 4.1 %collective-permute-done.14 = bf16[256,384]{1,0:T(8,128)(2,1)S(1)} collective-permute-done((bf16[256,384]{1,0:T(8,128)(2,1)S(1)}, bf16[256,384]{1,0:T(8,128)(2,1)S(1)}, u32[]{:S(2)}, u32[]{:S(2)}) %collective-permute-start.14) | collective-permute-done | bytes 196640 | tf_op jit(solution)/shard_map/ppermute | solution.py:23
  217.5 1.7 select_bitcast_fusion
  (77 shorter events, 1.0 us)
Async XLA Ops:
  6.5 0.9 copy-start
  6.5 12.7 %copy-start.14 = (f32[1,1536]{1,0:T(1,128)S(1)}, f32[1,1536]{1,0:T(1,128)}, u32[]{:S(2)}) copy-start(f32[1,1536]{1,0:T(1,128)} %param.13) | copy-start | bytes 18436
  6.5 63.9 %all-gather.3.cloned.1.call-start = ((), (), s32[]{:S(2)}) async-start(), calls=%async_computation | async-start | bytes 3538944 | tf_op jit(solution)/shard_map/all_gather | solution.py:92
  19.0 9.5 %copy-start.3 = (bf16[256,1536]{1,0:T(8,128)(2,1)}, bf16[256,1536]{1,0:T(8,128)(2,1)S(1)}, u32[]{:S(2)}) copy-start(bf16[256,1536]{1,0:T(8,128)(2,1)S(1)} %all_gather.21) | copy-start | bytes 2359300
  21.1 5.0 %copy-start.6 = (bf16[384,1536]{1,0:T(8,128)(2,1)S(1)}, bf16[384,1536]{1,0:T(8,128)(2,1)}, u32[]{:S(2)}) copy-start(bf16[384,1536]{1,0:T(8,128)(2,1)} %param.19) | copy-start | bytes 3538948
  24.0 136.8 %all-gather.5.cloned.1.call-start = ((), (), s32[]{:S(2)}) async-start(), calls=%async_computation.1 | async-start | bytes 3538944 | tf_op jit(solution)/shard_map/all_gather | solution.py:92
  24.0 59.4 %collective-permute-start = (bf16[384,1536]{1,0:T(8,128)(2,1)}, bf16[384,1536]{1,0:T(8,128)(2,1)}, u32[]{:S(2)}, u32[]{:S(2)}) collective-permute-start(bf16[384,1536]{1,0:T(8,128)(2,1)} %bitcast.113), channel_id=1, source_target_pairs={{0,2},{2,0},{1,3},{3,1},{4,6},{6,4},{5,7},{7,5},{8,10},{10,8},{9,1... | collective-permute-start | bytes 3538952 | tf_op jit(solution)/shard_map/ppermute | solution.py:134
  25.7 57.7 %collective-permute-start.1 = (bf16[384,1536]{1,0:T(8,128)(2,1)}, bf16[384,1536]{1,0:T(8,128)(2,1)}, u32[]{:S(2)}, u32[]{:S(2)}) collective-permute-start(bf16[384,1536]{1,0:T(8,128)(2,1)} %bitcast.114), channel_id=1, source_target_pairs={{0,1},{1,0},{2,3},{3,2},{4,5},{5,4},{6,7},{7,6},{8,9},{9,8},{10,11... | collective-permute-start | bytes 3538952 | tf_op jit(solution)/shard_map/ppermute | solution.py:135
  27.0 56.3 %collective-permute-start.2 = (bf16[384,384]{1,0:T(8,128)(2,1)S(1)}, bf16[384,384]{1,0:T(8,128)(2,1)S(1)}, u32[]{:S(2)}, u32[]{:S(2)}) collective-permute-start(bf16[384,384]{1,0:T(8,128)(2,1)S(1)} %get-tuple-element.32), channel_id=1, source_target_pairs={{0,1},{1,2},{2,3},{3,0},{4,5},{5,6},{6,7},{7,4},{8,9},{9,10},{10,1... | collective-permute-start | bytes 884744 | tf_op jit(solution)/shard_map/ppermute | solution.py:128
  27.1 56.3 %collective-permute-start.3 = (bf16[384,384]{1,0:T(8,128)(2,1)S(1)}, bf16[384,384]{1,0:T(8,128)(2,1)S(1)}, u32[]{:S(2)}, u32[]{:S(2)}) collective-permute-start(bf16[384,384]{1,0:T(8,128)(2,1)S(1)} %get-tuple-element.34), channel_id=1, source_target_pairs={{0,2},{1,3},{2,0},{3,1},{4,6},{5,7},{6,4},{7,5},{8,10},{9,11},{10,... | collective-permute-start | bytes 884744 | tf_op jit(solution)/shard_map/ppermute | solution.py:128
  28.4 55.0 %collective-permute-start.4 = (bf16[384,384]{1,0:T(8,128)(2,1)S(1)}, bf16[384,384]{1,0:T(8,128)(2,1)S(1)}, u32[]{:S(2)}, u32[]{:S(2)}) collective-permute-start(bf16[384,384]{1,0:T(8,128)(2,1)S(1)} %get-tuple-element.31), channel_id=1, source_target_pairs={{0,3},{1,0},{2,1},{3,2},{4,7},{5,4},{6,5},{7,6},{8,11},{9,8},{10,9... | collective-permute-start | bytes 884744 | tf_op jit(solution)/shard_map/ppermute | solution.py:128
  70.5 1.9 copy-start.1
  83.4 0.9 copy-start.17
  83.4 2.2 copy-start.19
  83.4 0.8 copy-start.21
  84.3 15.0 %copy-start.5 = (bf16[1,256,512]{2,1,0:T(8,128)(2,1)}, bf16[1,256,512]{2,1,0:T(8,128)(2,1)S(1)}, u32[]{:S(2)}) copy-start(bf16[1,256,512]{2,1,0:T(8,128)(2,1)S(1)} %get-tuple-element.39) | copy-start | bytes 786436
  84.3 7.9 %collective-permute-start.5 = (bf16[256,512]{1,0:T(8,128)(2,1)S(1)}, bf16[256,512]{1,0:T(8,128)(2,1)S(1)}, u32[]{:S(2)}, u32[]{:S(2)}) collective-permute-start(bf16[256,512]{1,0:T(8,128)(2,1)S(1)} %get-tuple-element.42), channel_id=1, source_target_pairs={{0,4},{4,8},{8,12},{12,0},{1,5},{5,9},{9,13},{13,1},{2,6},{6,10},{... | collective-permute-start | bytes 786440 | tf_op jit(solution)/shard_map/ppermute | solution.py:103
  85.6 13.2 %collective-permute-start.6 = (bf16[256,512]{1,0:T(8,128)(2,1)S(1)}, bf16[256,512]{1,0:T(8,128)(2,1)S(1)}, u32[]{:S(2)}, u32[]{:S(2)}) collective-permute-start(bf16[256,512]{1,0:T(8,128)(2,1)S(1)} %get-tuple-element.41), channel_id=1, source_target_pairs={{0,8},{4,12},{8,0},{12,4},{1,9},{5,13},{9,1},{13,5},{2,10},{6,14},... | collective-permute-start | bytes 786440 | tf_op jit(solution)/shard_map/ppermute | solution.py:103
  88.0 10.9 %collective-permute-start.7 = (bf16[256,512]{1,0:T(8,128)(2,1)S(1)}, bf16[256,512]{1,0:T(8,128)(2,1)S(1)}, u32[]{:S(2)}, u32[]{:S(2)}) collective-permute-start(bf16[256,512]{1,0:T(8,128)(2,1)S(1)} %get-tuple-element.40), channel_id=1, source_target_pairs={{0,12},{4,0},{8,4},{12,8},{1,13},{5,1},{9,5},{13,9},{2,14},{6,2},{... | collective-permute-start | bytes 786440 | tf_op jit(solution)/shard_map/ppermute | solution.py:103
  89.1 23.6 %collective-permute-start.8 = (bf16[384,1536]{1,0:T(8,128)(2,1)}, bf16[384,1536]{1,0:T(8,128)(2,1)}, u32[]{:S(2)}, u32[]{:S(2)}) collective-permute-start(bf16[384,1536]{1,0:T(8,128)(2,1)} %collective-permute-done), channel_id=1, source_target_pairs={{0,1},{1,0},{2,3},{3,2},{4,5},{5,4},{6,7},{7,6},{8,9},{9,8},{10,11... | collective-permute-start | bytes 3538952 | tf_op jit(solution)/shard_map/ppermute | solution.py:142
  92.2 7.1 %copy-start.7 = (bf16[256,512]{1,0:T(8,128)(2,1)}, bf16[256,512]{1,0:T(8,128)(2,1)S(1)}, u32[]{:S(2)}) copy-start(bf16[256,512]{1,0:T(8,128)(2,1)S(1)} %collective-permute-done.5) | copy-start | bytes 786436
  98.7 0.7 copy-start.8
  98.8 0.7 copy-start.9
  101.9 10.8 %copy-start.4 = (bf16[256,1536]{1,0:T(8,128)(2,1)S(1)}, bf16[256,1536]{1,0:T(8,128)(2,1)}, u32[]{:S(2)}) copy-start(bf16[256,1536]{1,0:T(8,128)(2,1)} %copy-done.3) | copy-start | bytes 2359300
  101.9 10.8 %copy-start.16 = (bf16[1,384,1536]{2,1,0:T(8,128)(2,1)S(1)}, bf16[1,384,1536]{2,1,0:T(8,128)(2,1)}, u32[]{:S(2)}) copy-start(bf16[1,384,1536]{2,1,0:T(8,128)(2,1)} %param.15) | copy-start | bytes 3538948
  112.7 3.7 %copy-start.15 = (bf16[3,1536,384]{2,1,0:T(8,128)(2,1)S(1)}, bf16[3,1536,384]{2,1,0:T(8,128)(2,1)}, u32[]{:S(2)}) copy-start(bf16[3,1536,384]{2,1,0:T(8,128)(2,1)} %param.18) | copy-start | bytes 10616836
  112.7 3.7 %copy-start.23 = (f32[1536]{0:T(1024)S(1)}, f32[1536]{0:T(1024)}, u32[]{:S(2)}) copy-start(f32[1536]{0:T(1024)} %param.17) | copy-start | bytes 18436
  116.4 62.2 %copy-start.13 = (bf16[256,1536]{1,0:T(8,128)(2,1)}, bf16[256,1536]{1,0:T(8,128)(2,1)S(1)}, u32[]{:S(2)}) copy-start(bf16[256,1536]{1,0:T(8,128)(2,1)S(1)} %get-tuple-element.52) | copy-start | bytes 2359300
  117.1 1.5 copy-start.24
  120.4 9.7 %collective-permute-start.10 = (bf16[256,384]{1,0:T(8,128)(2,1)S(1)}, bf16[256,384]{1,0:T(8,128)(2,1)S(1)}, u32[]{:S(2)}, u32[]{:S(2)}) collective-permute-start(bf16[256,384]{1,0:T(8,128)(2,1)S(1)} %fusion.59), channel_id=1, source_target_pairs={{128,0},{129,1},{130,2},{131,3},{132,4},{133,5},{134,6},{135,7},{1... | collective-permute-start | bytes 589832 | tf_op jit(solution)/shard_map/ppermute | solution.py:23
  160.8 1.9 copy-start.2
  173.8 7.9 %collective-permute-start.11 = (bf16[256,512]{1,0:T(8,128)(2,1)S(1)}, bf16[256,512]{1,0:T(8,128)(2,1)S(1)}, u32[]{:S(2)}, u32[]{:S(2)}) collective-permute-start(bf16[256,512]{1,0:T(8,128)(2,1)S(1)} %get-tuple-element.38), channel_id=1, source_target_pairs={{0,4},{4,8},{8,12},{12,0},{1,5},{5,9},{9,13},{13,1},{2,6},{6,10},{... | collective-permute-start | bytes 786440 | tf_op jit(solution)/shard_map/ppermute | solution.py:103
  175.0 13.3 %collective-permute-start.12 = (bf16[256,512]{1,0:T(8,128)(2,1)S(1)}, bf16[256,512]{1,0:T(8,128)(2,1)S(1)}, u32[]{:S(2)}, u32[]{:S(2)}) collective-permute-start(bf16[256,512]{1,0:T(8,128)(2,1)S(1)} %get-tuple-element.37), channel_id=1, source_target_pairs={{0,8},{4,12},{8,0},{12,4},{1,9},{5,13},{9,1},{13,5},{2,10},{6,14},... | collective-permute-start | bytes 786440 | tf_op jit(solution)/shard_map/ppermute | solution.py:103
  177.4 10.9 %collective-permute-start.13 = (bf16[256,512]{1,0:T(8,128)(2,1)S(1)}, bf16[256,512]{1,0:T(8,128)(2,1)S(1)}, u32[]{:S(2)}, u32[]{:S(2)}) collective-permute-start(bf16[256,512]{1,0:T(8,128)(2,1)S(1)} %get-tuple-element.36), channel_id=1, source_target_pairs={{0,12},{4,0},{8,4},{12,8},{1,13},{5,1},{9,5},{13,9},{2,14},{6,2},{... | collective-permute-start | bytes 786440 | tf_op jit(solution)/shard_map/ppermute | solution.py:103
  178.6 28.8 %collective-permute-start.9 = (bf16[256,384]{1,0:T(8,128)(2,1)S(1)}, bf16[256,384]{1,0:T(8,128)(2,1)}, u32[]{:S(2)}, u32[]{:S(2)}) collective-permute-start(bf16[256,384]{1,0:T(8,128)(2,1)S(1)} %constant_dynamic-slice_fusion.7), channel_id=1, source_target_pairs={{128,0},{129,1},{130,2},{131,3},{132,4},{133,5},{134,6},{135,7},{1... | collective-permute-start | bytes 589832 | tf_op jit(solution)/shard_map/ppermute | solution.py:23
  188.3 0.7 copy-start.10
  188.3 0.8 copy-start.11
  196.7 10.8 %copy-start.12 = (bf16[384,384]{1,0:T(8,128)(2,1)S(1)}, bf16[384,384]{1,0:T(8,128)(2,1)}, u32[]{:S(2)}) copy-start(bf16[384,384]{1,0:T(8,128)(2,1)} %get-tuple-element.23) | copy-start | bytes 884740
  196.7 10.8 %copy-start.18 = (bf16[384,384]{1,0:T(8,128)(2,1)S(1)}, bf16[384,384]{1,0:T(8,128)(2,1)}, u32[]{:S(2)}) copy-start(bf16[384,384]{1,0:T(8,128)(2,1)} %copy-done.17) | copy-start | bytes 884740
  196.7 10.8 %copy-start.20 = (bf16[384,384]{1,0:T(8,128)(2,1)S(1)}, bf16[384,384]{1,0:T(8,128)(2,1)}, u32[]{:S(2)}) copy-start(bf16[384,384]{1,0:T(8,128)(2,1)} %copy-done.19) | copy-start | bytes 884740
  196.7 10.8 %copy-start.22 = (bf16[384,384]{1,0:T(8,128)(2,1)S(1)}, bf16[384,384]{1,0:T(8,128)(2,1)}, u32[]{:S(2)}) copy-start(bf16[384,384]{1,0:T(8,128)(2,1)} %copy-done.21) | copy-start | bytes 884740
  209.0 8.4 %collective-permute-start.14 = (bf16[256,384]{1,0:T(8,128)(2,1)S(1)}, bf16[256,384]{1,0:T(8,128)(2,1)S(1)}, u32[]{:S(2)}, u32[]{:S(2)}) collective-permute-start(bf16[256,384]{1,0:T(8,128)(2,1)S(1)} %add_convert_fusion), channel_id=1, source_target_pairs={{0,128},{1,129},{2,130},{3,131},{4,132},{5,133},{6,134},{7,135},{8... | collective-permute-start | bytes 589832 | tf_op jit(solution)/shard_map/ppermute | solution.py:23
Sparse Core Ops, SparseCore 0:
  24.1 46.3 all-gather.2
  118.7 42.0 all-gather.4

commit v17 on v15

--- a/solution.py
+++ b/solution.py
@@ -207,8 +207,7 @@
     memory_pairs = jnp.stack(
         [project(memory_normed, cross_weights[1]), project(memory_normed, cross_weights[2])]
     )
-    voxel_queries = shifted(cross_queries, "segment", -1)
-    voxel_part = shifted(hidden_part, "segment", -1)
+    voxel_queries, voxel_part = shifted(jnp.stack([cross_queries, hidden_part]), "segment", -1)
     crossed = mp_gather_flat(attend(voxel_queries, memory_pairs))
     decoded = (
         voxel_part.astype(jnp.float32) + project_out(crossed, cross_blocks)

time: 222 us -> 222 us (level)
    all_gather x2, waiting for transfers between devices: 46.7 us -> 42.4 us  [attend(): key_block = lax.all_gather(pairs, 'bz', axis=1, tiled=True)]
    ppermute x3 -> x2, waiting for transfers between devices: 12.5 us -> 16.7 us  [shifted(): lax.ppermute(value, axis, [(source, source + steps) for source in range(i...]
    ppermute x3 -> x2, starting transfers between devices: 6.95 us -> 5.65 us  [shifted(): lax.ppermute(value, axis, [(source, source + steps) for source in range(i...]
  transfers between devices with their start and end apart: 15 -> 14, of which waited for: 8 -> 8; matrix products, arithmetic and copies ran while one was open for 4% -> 3% of each run, Pallas kernels for 5% -> 5%
where the time goes in v17:
time: 222 us; the launch traced here: 221 us
  waiting for transfers between devices  80.4 us (36%)
  blocking collectives  55.9 us (25%)
  Pallas kernels  22 us (10%)
  starting transfers between devices  20.2 us (9%)
  matrix products  14.3 us (6%)
  between operations  13.9 us (6%)
  local copies, waits for them, and re-layouts  9.26 us (4%)
  other arithmetic  4.89 us (2%)
    all_gather x2, waiting for transfers between devices, attend(): key_block = lax.all_gather(pairs, 'bz', axis=1, tiled=True)  42.4 us
    all_gather x2, blocking collectives, attend(): query_block = lax.all_gather(queries, 'bx', axis=0, tiled=True)  24.1 us
    pallas_call x2, Pallas kernels, partial_attend(): pl.pallas_call(partial_kernel, grid=(rows // TILE,), in_specs=[pl.BlockSp...  22 us
    ppermute x2, waiting for transfers between devices, shifted(): lax.ppermute(value, axis, [(source, source + steps) for source in range(i...  16.7 us
    all_to_all x1, waiting for transfers between devices, attend(): parts = lax.all_to_all(partial, 'bx', 0, 0, tiled=True)  13.7 us
    all_gather x1, blocking collectives, mp_gather_flat(): return lax.all_gather(value, MP, axis=1, tiled=True)  10.9 us
    all_gather x1, blocking collectives, on_device(): self_attended = lax.all_gather(self_local, MP, axis=1, tiled=True)  10.6 us
    all_gather x1, blocking collectives, on_device(): embedded_full = lax.all_gather(embedded, MP, axis=1, tiled=True)  10.3 us
  transfers between devices with their start and end apart: 14, of which 8 were waited for; matrix products, arithmetic and copies ran while one was open for 3% of the time, Pallas kernels for 5%

profile of v17, /device:TPU:1, one launch (start us, length us, event | category | flops | bytes accessed | tf_op | source)
XLA Modules:
  0.0 220.9 jit_solution(2562679006778136217)
XLA Ops:
  6.5 0.9 copy-done
  7.5 1.2 fusion.68
  8.7 10.3 %all_gather.21 = bf16[256,1536]{1,0:T(8,128)(2,1)S(1)} all-gather(bf16[256,384]{1,0:T(8,128)(2,1)S(1)} %fusion.68), channel_id=1, replica_groups=mesh['segment'=2,'bz'=8,'bx'=4,'my'=2,'mc'=2] {'my','mc'}, dimensions={1}, use_global_device_ids=true | all-gather | bytes 983040 | tf_op jit(solution)/shard_map/all_gather | solution.py:190
  19.0 0.2 fusion.19
  19.2 1.9 fusion.78
  21.1 2.0 fusion.81
  23.1 0.8 pad_maximum_fusion
  23.9 0.0 all-gather.4.cloned.1.call-update
  23.9 0.0 all-gather.6.cloned.1.call-start
  24.0 1.7 collective-permute-start
  25.7 0.4 collective-permute-start.1
  26.2 0.8 constant_dynamic-slice_fusion.11
  27.0 0.1 collective-permute-start.2
  27.0 1.4 collective-permute-start.3
  28.4 1.9 fusion.50
  30.3 11.8 %all_gather.22.q_ref = bf16[1024,384]{1,0:T(8,128)(2,1)S(1)} all-gather(bf16[256,384]{1,0:T(8,128)(2,1)S(1)} %fusion.50), channel_id=1, replica_groups=mesh['segment'=2,'bz'=8,'bx'=4,'my'=2,'mc'=2] {'bx'}, dimensions={0}, use_global_device_ids=true | all-gather | bytes 983040 | tf_op jit(solution)/shard_map/all_gather | solution.py:91
  42.1 28.4 %all-gather.4.cloned.1.call-done.k_ref.v_ref = bf16[2,2048,384]{2,1,0:T(8,128)(2,1)} async-done(((bf16[2,256,384]{2,1,0:T(8,128)(2,1)}), bf16[2,2048,384]{2,1,0:T(8,128)(2,1)}) %all-gather.4.cloned.1.call-update) | async-done | bytes 3145744 | tf_op jit(solution)/shard_map/all_gather | solution.py:92
  70.4 1.9 copy-done.1
  72.3 11.0 %shard_map.100 = bf16[1024,512]{1,0:T(8,128)(2,1)S(1)} custom-call(bf16[1024,384]{1,0:T(8,128)(2,1)S(1)} %all_gather.22.q_ref, bf16[2,2048,384]{2,1,0:T(8,128)(2,1)S(1)} %copy-done.1, bf16[2,2048,384]{2,1,0:T(8,128)(2,1)S(1)} %copy-done.1), custom_call_target="tpu_custom_call" | custom-call | tf_op jit(solution)/shard_map/pallas_call | solution.py:74
  83.4 0.6 copy-done.14
  84.1 0.1 copy-done.16
  84.2 0.1 copy-done.18
  84.3 0.1 dynamic-slice_bitcast_fusion
  84.4 1.3 collective-permute-start.5
  85.6 2.4 %collective-permute-start.6 = (bf16[256,512]{1,0:T(8,128)(2,1)S(1)}, bf16[256,512]{1,0:T(8,128)(2,1)S(1)}, u32[]{:S(2)}, u32[]{:S(2)}) collective-permute-start(bf16[256,512]{1,0:T(8,128)(2,1)S(1)} %get-tuple-element.37), channel_id=1, source_target_pairs={{0,8},{4,12},{8,0},{12,4},{1,9},{5,13},{9,1},{13,5},{2,10},{6,14},... | collective-permute-start | bytes 786440 | tf_op jit(solution)/shard_map/ppermute | solution.py:103
  88.0 1.2 collective-permute-start.7
  89.2 2.1 collective-permute-start.8
  91.3 1.0 collective-permute-done.5
  92.3 6.5 %collective-permute-done.6 = bf16[256,512]{1,0:T(8,128)(2,1)S(1)} collective-permute-done((bf16[256,512]{1,0:T(8,128)(2,1)S(1)}, bf16[256,512]{1,0:T(8,128)(2,1)S(1)}, u32[]{:S(2)}, u32[]{:S(2)}) %collective-permute-start.6) | collective-permute-done | bytes 262176 | tf_op jit(solution)/shard_map/ppermute | solution.py:103
  98.8 0.1 collective-permute-done.7
  99.0 0.2 copy.15
  99.3 0.1 mul.153
  99.4 0.1 copy-done.8
  99.5 0.1 copy-done.9
  99.6 0.5 copy.17
  100.1 0.2 copy.18
  100.3 1.4 maximum_convert_fusion
  101.7 0.3 fusion.23
  102.0 0.1 divide_convert_fusion
  102.1 10.6 %all_gather.24 = bf16[256,1536]{1,0:T(8,128)(2,1)S(1)} all-gather(bf16[256,384]{1,0:T(8,128)(2,1)S(1)} %divide_convert_fusion), channel_id=1, replica_groups=mesh['segment'=2,'bz'=8,'bx'=4,'my'=2,'mc'=2] {'my','mc'}, dimensions={1}, use_global_device_ids=true | all-gather | bytes 983040 | tf_op jit(solution)/shard_map/all_gather | solution.py:200
  112.7 0.1 constant_dynamic-slice_fusion.7
  112.8 3.6 %fusion.18 = (f32[256]{0:T(256)S(1)}, bf16[256,1536]{1,0:T(8,128)(2,1)S(1)}) fusion(bf16[384,1536]{1,0:T(8,128)(2,1)} %collective-permute-done.8, bf16[384,1536]{1,0:T(8,128)(2,1)} %collective-permute-done.1, bf16[384,1536]{1,0:T(8,128)(2,1)} %collective-permute-done, bf16[384,1536]{1,0:T(8,128)(2,1)S(1)} %bitcast.121, ...), kind=kOutput, calls=%fused_computation.18 | convolution fusion | flops 1232338688 | bytes 7078912 | tf_op jit(solution)/shard_map/dot_general | solution.py:162
  116.5 0.6 fusion.72
  117.1 0.6 fusion.69
  117.8 0.8 pad_maximum_fusion.2
  118.6 0.0 all-gather.6.cloned.1.call-update
  118.6 1.9 fusion.75
  120.6 1.3 collective-permute-start.9
  121.9 12.6 %collective-permute-done.9 = bf16[2,256,384]{2,1,0:T(8,128)(2,1)S(1)} collective-permute-done((bf16[2,256,384]{2,1,0:T(8,128)(2,1)S(1)}, bf16[2,256,384]{2,1,0:T(8,128)(2,1)S(1)}, u32[]{:S(2)}, u32[]{:S(2)}) %collective-permute-start.9) | collective-permute-done | bytes 393248 | tf_op jit(solution)/shard_map/ppermute | solution.py:23
  134.5 12.3 %all-gather = bf16[1,1024,384]{2,1,0:T(8,128)(2,1)S(1)} all-gather(bf16[1,256,384]{2,1,0:T(8,128)(2,1)S(1)} %unstack.14), channel_id=2, replica_groups=mesh['segment'=2,'bz'=8,'bx'=4,'my'=2,'mc'=2] {'bx'}, dimensions={1}, use_global_device_ids=true | all-gather | bytes 983040 | tf_op jit(solution)/shard_map/all_gather | solution.py:91
  146.8 14.0 %all-gather.6.cloned.1.call-done.k_ref.v_ref = bf16[2,2048,384]{2,1,0:T(8,128)(2,1)} async-done(((bf16[2,256,384]{2,1,0:T(8,128)(2,1)}), bf16[2,2048,384]{2,1,0:T(8,128)(2,1)}) %all-gather.6.cloned.1.call-update) | async-done | bytes 3145744 | tf_op jit(solution)/shard_map/all_gather | solution.py:92
  160.9 1.9 copy-done.2
  162.7 11.0 %shard_map.101 = bf16[1024,512]{1,0:T(8,128)(2,1)S(1)} custom-call(bf16[1024,384]{1,0:T(8,128)(2,1)S(1)} %bitcast.107, bf16[2,2048,384]{2,1,0:T(8,128)(2,1)S(1)} %copy-done.2, bf16[2,2048,384]{2,1,0:T(8,128)(2,1)S(1)} %copy-done.2), custom_call_target="tpu_custom_call" | custom-call | tf_op jit(solution)/shard_map/pallas_call | solution.py:74
  173.7 1.3 copy.19
  175.1 4.0 %all-to-all-start = ((bf16[4,256,512]{1,2,0:T(8,128)(2,1)}), bf16[4,256,512]{1,2,0:T(8,128)(2,1)S(1)}, u32[]{:S(2)}, u32[]{:S(2)}) async-start(bf16[4,256,512]{1,2,0:T(8,128)(2,1)} %copy.19), calls=%async_computation | async-start | bytes 2097152 | tf_op jit(solution)/shard_map/all_to_all | solution.py:107
  179.0 13.7 %all-to-all-done = bf16[4,256,512]{1,2,0:T(8,128)(2,1)S(1)} async-done(((bf16[4,256,512]{1,2,0:T(8,128)(2,1)}), bf16[4,256,512]{1,2,0:T(8,128)(2,1)S(1)}, u32[]{:S(2)}, u32[]{:S(2)}) %all-to-all-start) | async-done | bytes 1048608 | tf_op jit(solution)/shard_map/all_to_all | solution.py:107
  192.8 0.2 convert_element_type.88
  193.0 0.1 fusion.22
  193.2 10.9 %all_gather.27 = bf16[256,1536]{0,1:T(8,128)(2,1)S(1)} all-gather(bf16[256,384]{0,1:T(8,128)(2,1)S(1)} %fusion.102), channel_id=1, replica_groups=mesh['segment'=2,'bz'=8,'bx'=4,'my'=2,'mc'=2] {'my','mc'}, dimensions={1}, use_global_device_ids=true | all-gather | bytes 983040 | tf_op jit(solution)/shard_map/all_gather | solution.py:152
  204.2 0.1 constant_dynamic-slice_fusion.3
  204.3 0.6 fusion.101
  204.9 4.4 %collective-permute-start.10 = (bf16[256,384]{1,0:T(8,128)(2,1)S(1)}, bf16[256,384]{1,0:T(8,128)(2,1)S(1)}, u32[]{:S(2)}, u32[]{:S(2)}) collective-permute-start(bf16[256,384]{1,0:T(8,128)(2,1)S(1)} %fusion.101), channel_id=1, source_target_pairs={{0,128},{1,129},{2,130},{3,131},{4,132},{5,133},{6,134},{7,135},{8... | collective-permute-start | bytes 589832 | tf_op jit(solution)/shard_map/ppermute | solution.py:23
  209.3 4.1 %collective-permute-done.10 = bf16[256,384]{1,0:T(8,128)(2,1)S(1)} collective-permute-done((bf16[256,384]{1,0:T(8,128)(2,1)S(1)}, bf16[256,384]{1,0:T(8,128)(2,1)S(1)}, u32[]{:S(2)}, u32[]{:S(2)}) %collective-permute-start.10) | collective-permute-done | bytes 196640 | tf_op jit(solution)/shard_map/ppermute | solution.py:23
  213.3 0.7 select_bitcast_fusion
  (63 shorter events, 0.5 us)
Async XLA Ops:
  6.5 0.9 copy-start
  6.5 12.7 %copy-start.11 = (f32[1,1536]{1,0:T(1,128)S(1)}, f32[1,1536]{1,0:T(1,128)}, u32[]{:S(2)}) copy-start(f32[1,1536]{1,0:T(1,128)} %param.13) | copy-start | bytes 18436
  6.5 63.9 %all-gather.4.cloned.1.call-start = ((), (), s32[]{:S(2)}) async-start(), calls=%async_computation.1 | async-start | bytes 3538944 | tf_op jit(solution)/shard_map/all_gather | solution.py:92
  19.0 9.5 %copy-start.3 = (bf16[256,1536]{1,0:T(8,128)(2,1)}, bf16[256,1536]{1,0:T(8,128)(2,1)S(1)}, u32[]{:S(2)}) copy-start(bf16[256,1536]{1,0:T(8,128)(2,1)S(1)} %all_gather.21) | copy-start | bytes 2359300
  21.1 5.0 %copy-start.6 = (bf16[384,1536]{1,0:T(8,128)(2,1)S(1)}, bf16[384,1536]{1,0:T(8,128)(2,1)}, u32[]{:S(2)}) copy-start(bf16[384,1536]{1,0:T(8,128)(2,1)} %param.19) | copy-start | bytes 3538948
  23.9 136.9 %all-gather.6.cloned.1.call-start = ((), (), s32[]{:S(2)}) async-start(), calls=%async_computation.2 | async-start | bytes 3538944 | tf_op jit(solution)/shard_map/all_gather | solution.py:92
  24.0 59.4 %collective-permute-start = (bf16[384,1536]{1,0:T(8,128)(2,1)}, bf16[384,1536]{1,0:T(8,128)(2,1)}, u32[]{:S(2)}, u32[]{:S(2)}) collective-permute-start(bf16[384,1536]{1,0:T(8,128)(2,1)} %bitcast.119), channel_id=1, source_target_pairs={{0,2},{2,0},{1,3},{3,1},{4,6},{6,4},{5,7},{7,5},{8,10},{10,8},{9,1... | collective-permute-start | bytes 3538952 | tf_op jit(solution)/shard_map/ppermute | solution.py:134
  25.7 57.7 %collective-permute-start.1 = (bf16[384,1536]{1,0:T(8,128)(2,1)}, bf16[384,1536]{1,0:T(8,128)(2,1)}, u32[]{:S(2)}, u32[]{:S(2)}) collective-permute-start(bf16[384,1536]{1,0:T(8,128)(2,1)} %bitcast.120), channel_id=1, source_target_pairs={{0,1},{1,0},{2,3},{3,2},{4,5},{5,4},{6,7},{7,6},{8,9},{9,8},{10,11... | collective-permute-start | bytes 3538952 | tf_op jit(solution)/shard_map/ppermute | solution.py:135
  27.0 56.4 %collective-permute-start.2 = (bf16[384,384]{1,0:T(8,128)(2,1)S(1)}, bf16[384,384]{1,0:T(8,128)(2,1)S(1)}, u32[]{:S(2)}, u32[]{:S(2)}) collective-permute-start(bf16[384,384]{1,0:T(8,128)(2,1)S(1)} %get-tuple-element.32), channel_id=1, source_target_pairs={{0,1},{1,2},{2,3},{3,0},{4,5},{5,6},{6,7},{7,4},{8,9},{9,10},{10,1... | collective-permute-start | bytes 884744 | tf_op jit(solution)/shard_map/ppermute | solution.py:128
  27.0 56.3 %collective-permute-start.3 = (bf16[384,384]{1,0:T(8,128)(2,1)S(1)}, bf16[384,384]{1,0:T(8,128)(2,1)S(1)}, u32[]{:S(2)}, u32[]{:S(2)}) collective-permute-start(bf16[384,384]{1,0:T(8,128)(2,1)S(1)} %get-tuple-element.34), channel_id=1, source_target_pairs={{0,2},{1,3},{2,0},{3,1},{4,6},{5,7},{6,4},{7,5},{8,10},{9,11},{10,... | collective-permute-start | bytes 884744 | tf_op jit(solution)/shard_map/ppermute | solution.py:128
  28.4 55.0 %collective-permute-start.4 = (bf16[384,384]{1,0:T(8,128)(2,1)S(1)}, bf16[384,384]{1,0:T(8,128)(2,1)S(1)}, u32[]{:S(2)}, u32[]{:S(2)}) collective-permute-start(bf16[384,384]{1,0:T(8,128)(2,1)S(1)} %get-tuple-element.31), channel_id=1, source_target_pairs={{0,3},{1,0},{2,1},{3,2},{4,7},{5,4},{6,5},{7,6},{8,11},{9,8},{10,9... | collective-permute-start | bytes 884744 | tf_op jit(solution)/shard_map/ppermute | solution.py:128
  70.4 1.9 copy-start.1
  83.3 0.7 copy-start.14
  83.4 0.8 copy-start.16
  83.4 0.9 copy-start.18
  84.3 15.0 %copy-start.5 = (bf16[1,256,512]{2,1,0:T(8,128)(2,1)}, bf16[1,256,512]{2,1,0:T(8,128)(2,1)S(1)}, u32[]{:S(2)}) copy-start(bf16[1,256,512]{2,1,0:T(8,128)(2,1)S(1)} %get-tuple-element.35) | copy-start | bytes 786436
  84.4 7.9 %collective-permute-start.5 = (bf16[256,512]{1,0:T(8,128)(2,1)S(1)}, bf16[256,512]{1,0:T(8,128)(2,1)S(1)}, u32[]{:S(2)}, u32[]{:S(2)}) collective-permute-start(bf16[256,512]{1,0:T(8,128)(2,1)S(1)} %get-tuple-element.38), channel_id=1, source_target_pairs={{0,4},{4,8},{8,12},{12,0},{1,5},{5,9},{9,13},{13,1},{2,6},{6,10},{... | collective-permute-start | bytes 786440 | tf_op jit(solution)/shard_map/ppermute | solution.py:103
  85.6 13.2 %collective-permute-start.6 = (bf16[256,512]{1,0:T(8,128)(2,1)S(1)}, bf16[256,512]{1,0:T(8,128)(2,1)S(1)}, u32[]{:S(2)}, u32[]{:S(2)}) collective-permute-start(bf16[256,512]{1,0:T(8,128)(2,1)S(1)} %get-tuple-element.37), channel_id=1, source_target_pairs={{0,8},{4,12},{8,0},{12,4},{1,9},{5,13},{9,1},{13,5},{2,10},{6,14},... | collective-permute-start | bytes 786440 | tf_op jit(solution)/shard_map/ppermute | solution.py:103
  88.0 10.9 %collective-permute-start.7 = (bf16[256,512]{1,0:T(8,128)(2,1)S(1)}, bf16[256,512]{1,0:T(8,128)(2,1)S(1)}, u32[]{:S(2)}, u32[]{:S(2)}) collective-permute-start(bf16[256,512]{1,0:T(8,128)(2,1)S(1)} %get-tuple-element.36), channel_id=1, source_target_pairs={{0,12},{4,0},{8,4},{12,8},{1,13},{5,1},{9,5},{13,9},{2,14},{6,2},{... | collective-permute-start | bytes 786440 | tf_op jit(solution)/shard_map/ppermute | solution.py:103
  89.2 23.6 %collective-permute-start.8 = (bf16[384,1536]{1,0:T(8,128)(2,1)}, bf16[384,1536]{1,0:T(8,128)(2,1)}, u32[]{:S(2)}, u32[]{:S(2)}) collective-permute-start(bf16[384,1536]{1,0:T(8,128)(2,1)} %collective-permute-done), channel_id=1, source_target_pairs={{0,1},{1,0},{2,3},{3,2},{4,5},{5,4},{6,7},{7,6},{8,9},{9,8},{10,11... | collective-permute-start | bytes 3538952 | tf_op jit(solution)/shard_map/ppermute | solution.py:142
  92.3 7.1 %copy-start.7 = (bf16[256,512]{1,0:T(8,128)(2,1)}, bf16[256,512]{1,0:T(8,128)(2,1)S(1)}, u32[]{:S(2)}) copy-start(bf16[256,512]{1,0:T(8,128)(2,1)S(1)} %collective-permute-done.5) | copy-start | bytes 786436
  98.8 0.7 copy-start.8
  98.9 0.7 copy-start.9
  102.0 10.8 %copy-start.4 = (bf16[256,1536]{1,0:T(8,128)(2,1)S(1)}, bf16[256,1536]{1,0:T(8,128)(2,1)}, u32[]{:S(2)}) copy-start(bf16[256,1536]{1,0:T(8,128)(2,1)} %copy-done.3) | copy-start | bytes 2359300
  102.0 10.8 %copy-start.13 = (bf16[1,384,1536]{2,1,0:T(8,128)(2,1)S(1)}, bf16[1,384,1536]{2,1,0:T(8,128)(2,1)}, u32[]{:S(2)}) copy-start(bf16[1,384,1536]{2,1,0:T(8,128)(2,1)} %param.15) | copy-start | bytes 3538948
  112.8 3.7 %copy-start.12 = (bf16[3,1536,384]{2,1,0:T(8,128)(2,1)S(1)}, bf16[3,1536,384]{2,1,0:T(8,128)(2,1)}, u32[]{:S(2)}) copy-start(bf16[3,1536,384]{2,1,0:T(8,128)(2,1)} %param.18) | copy-start | bytes 10616836
  112.8 3.7 %copy-start.20 = (f32[1536]{0:T(1024)S(1)}, f32[1536]{0:T(1024)}, u32[]{:S(2)}) copy-start(f32[1536]{0:T(1024)} %param.17) | copy-start | bytes 18436
  117.8 0.9 copy-start.21
  120.6 13.9 %collective-permute-start.9 = (bf16[2,256,384]{2,1,0:T(8,128)(2,1)S(1)}, bf16[2,256,384]{2,1,0:T(8,128)(2,1)S(1)}, u32[]{:S(2)}, u32[]{:S(2)}) collective-permute-start(bf16[2,256,384]{2,1,0:T(8,128)(2,1)S(1)} %pad_maximum_fusion.1), channel_id=1, source_target_pairs={{128,0},{129,1},{130,2},{131,3},{132,4},{133,5},{134,6},{135,7},{1... | collective-permute-start | bytes 1179656 | tf_op jit(solution)/shard_map/ppermute | solution.py:23
  160.9 1.9 copy-start.2
  175.1 17.6 %all-to-all-start = ((bf16[4,256,512]{1,2,0:T(8,128)(2,1)}), bf16[4,256,512]{1,2,0:T(8,128)(2,1)S(1)}, u32[]{:S(2)}, u32[]{:S(2)}) async-start(bf16[4,256,512]{1,2,0:T(8,128)(2,1)} %copy.19), calls=%async_computation | async-start | bytes 2097152 | tf_op jit(solution)/shard_map/all_to_all | solution.py:107
  193.2 11.1 %copy-start.10 = (bf16[384,384]{1,0:T(8,128)(2,1)S(1)}, bf16[384,384]{1,0:T(8,128)(2,1)}, u32[]{:S(2)}) copy-start(bf16[384,384]{1,0:T(8,128)(2,1)} %get-tuple-element.23) | copy-start | bytes 884740
  193.2 11.1 %copy-start.15 = (bf16[384,384]{1,0:T(8,128)(2,1)S(1)}, bf16[384,384]{1,0:T(8,128)(2,1)}, u32[]{:S(2)}) copy-start(bf16[384,384]{1,0:T(8,128)(2,1)} %copy-done.14) | copy-start | bytes 884740
  193.2 11.1 %copy-start.17 = (bf16[384,384]{1,0:T(8,128)(2,1)S(1)}, bf16[384,384]{1,0:T(8,128)(2,1)}, u32[]{:S(2)}) copy-start(bf16[384,384]{1,0:T(8,128)(2,1)} %copy-done.16) | copy-start | bytes 884740
  193.2 11.1 %copy-start.19 = (bf16[384,384]{1,0:T(8,128)(2,1)S(1)}, bf16[384,384]{1,0:T(8,128)(2,1)}, u32[]{:S(2)}) copy-start(bf16[384,384]{1,0:T(8,128)(2,1)} %copy-done.18) | copy-start | bytes 884740
  204.9 8.4 %collective-permute-start.10 = (bf16[256,384]{1,0:T(8,128)(2,1)S(1)}, bf16[256,384]{1,0:T(8,128)(2,1)S(1)}, u32[]{:S(2)}, u32[]{:S(2)}) collective-permute-start(bf16[256,384]{1,0:T(8,128)(2,1)S(1)} %fusion.101), channel_id=1, source_target_pairs={{0,128},{1,129},{2,130},{3,131},{4,132},{5,133},{6,134},{7,135},{8... | collective-permute-start | bytes 589832 | tf_op jit(solution)/shard_map/ppermute | solution.py:23
Sparse Core Ops, SparseCore 0:
  24.1 46.3 all-gather.3
  118.7 42.1 all-gather.5
